TPU v7x, 128 devices: a whole 4x4x4 slice. The times are simulated.
128 devices in a mesh: chan: 16 (over z, x_lo, core), freq: 8 (over x_hi, y).
Axes of the slice: x: 4 (x_hi: 2, x_lo: 2; x = x_hi * 2 + x_lo), y: 4, z: 4, core: 2. Of those that a mesh axis runs over, the one named last changes fastest.
Arguments:
- records: bfloat16 [67584, 8192], P('freq', 'chan')
- offsets: int32 [512], P('freq'), may hold values from 0 to 8192, as said below
- dead_mask: int32 [8192], P('chan'), may hold values 0 or 1
- band_blocks: int32 [16], P('chan'), may hold values from 0 to 2, as said below
Outputs:
- cross: bfloat16 [3, 32, 8192, 1024], P(None, 'freq', 'chan')
Inputs may be any that keep to these rules, and one draw needn't show every extreme that they name: offsets[s] is the first sample of segment s within time block s // 64 of 8448 samples; all 256 samples of the segment lie in that block. band_blocks[b] is the largest block offset whose cross-spectra are kept for channel block b.
All inputs are finite; a program needn't handle non-finite values. No bound on the sum of `dead_mask` on one device may be relied on, other than what follows from the above.
Results may differ from a plain program's by a relative error of at most 0.0055.
Values may be sent and summed in bfloat16 or wider, within the bound.
No kernel may reach another device: no remote copies, remote signals or barrier semaphores. Data moves between devices by JAX's collectives and lax.ppermute only.
A program may use at most 128 MiB of HBM per device.

v0:
```python
import jax
import jax.numpy as jnp
from jax import lax
from jax.sharding import PartitionSpec as P

SEG_LEN = 256
BINS = 32
FIRST_BIN = 2


EPS_POWER = 1e-06


def from_behind(block, axis, distance):
    devices = range(lax.axis_size(axis))
    route = [(i - distance, i) for i in devices if i - distance in devices]
    return lax.ppermute(block, axis, route)


def dft_table(seg_length, bin_count, first_bin):
    sample_index = jnp.arange(seg_length, dtype=jnp.int32)
    row_index = jnp.arange(2 * bin_count, dtype=jnp.int32)
    harmonic = row_index // 2 + first_bin
    phase_steps = harmonic[:, None] * sample_index[None, :] % seg_length
    phase_angle = 2.0 * jnp.pi / seg_length * phase_steps.astype(jnp.float32)
    hann_taper = 0.5 - 0.5 * jnp.cos(2.0 * jnp.pi / seg_length * sample_index.astype(jnp.float32))
    wave_rows = jnp.where(
        (row_index % 2 == 0)[:, None], jnp.cos(phase_angle), -jnp.sin(phase_angle)
    )
    return (hann_taper[None, :] * wave_rows).astype(jnp.bfloat16)


def local_products(left_panel, partner_panels):
    seg_count = left_panel.shape[2]
    left_real = left_panel[:, 0]
    left_imag = left_panel[:, 1]
    results = []
    for right_panel in partner_panels:
        real_part = jnp.einsum(
            "fpsi,fpsj->fij", left_panel, right_panel, preferred_element_type=jnp.float32
        )
        imag_part = jnp.einsum(
            "fsi,fsj->fij", left_imag, right_panel[:, 0], preferred_element_type=jnp.float32
        ) - jnp.einsum(
            "fsi,fsj->fij", left_real, right_panel[:, 1], preferred_element_type=jnp.float32
        )
        results.append(jnp.concatenate([real_part, imag_part], axis=2) * (1.0 / seg_count))
    return results


def shards(records, offsets, dead_mask, band_blocks):
    dft_rows = dft_table(SEG_LEN, BINS, FIRST_BIN)
    sample_rows = offsets[:, None] + jnp.arange(SEG_LEN, dtype=jnp.int32)[None, :]
    frames = jnp.take(records, sample_rows, axis=0)
    spectra = jnp.einsum("kt,stc->ksc", dft_rows, frames, preferred_element_type=jnp.float32)
    band_power = jnp.sum(spectra * spectra, axis=0) * (1.0 / BINS)
    scaling = dead_mask.astype(jnp.float32)[None, :] / jnp.sqrt(band_power + EPS_POWER)
    whitened = (spectra * scaling[None]).astype(jnp.bfloat16)
    whitened = whitened.reshape(BINS, 2, whitened.shape[1], whitened.shape[2])
    own_panel = lax.all_to_all(whitened, "freq", split_axis=0, concat_axis=2, tiled=True)
    upper_panel = from_behind(own_panel, "chan", -1)
    second_panel = from_behind(own_panel, "chan", -2)
    products = local_products(own_panel, [own_panel, upper_panel, second_panel])
    band_limit = band_blocks[0]
    results = []
    for offset_index, product in enumerate(products):
        keep_flag = (offset_index <= band_limit).astype(jnp.bfloat16)
        results.append(product.astype(jnp.bfloat16) * keep_flag)
    return jnp.stack(results, axis=0)


def solution(mesh):
    in_specs = (P("freq", "chan"), P("freq"), P("chan"), P("chan"))
    out_specs = P(None, "freq", "chan", None)
    return jax.shard_map(shards, mesh=mesh, in_specs=in_specs, out_specs=out_specs, check_vma=False)
```

profile of v0, /device:TPU:34, one launch (start us, length us, event | category | flops | bytes accessed | tf_op | source)
XLA Modules:
  0.0 323.0 jit_solution(17129487919976985947)
XLA Ops:
  0.0 0.7 fusion.16
  0.7 0.7 fusion.22
  1.6 0.7 convert_element_type.70
  2.3 71.2 %gather_fusion = bf16[16384,512]{1,0:T(8,128)(2,1)} fusion(bf16[8448,512]{1,0:T(8,128)(2,1)} %param.4, s32[16384]{0:T(1024)S(1)} %broadcast_clamp_fusion), kind=kCustom, calls=%fused_computation | custom fusion | bytes 33619968 | tf_op jit(solution)/shard_map/jit(_take)/gather | solution.py:54
  73.5 9.3 %multiply_reduce_fusion = (f32[64,512]{1,0:T(8,128)S(1)}, f32[64,64,512]{2,0,1:T(8,128)S(1)}) fusion(bf16[64,256,512]{2,1,0:T(8,128)(2,1)} %bitcast.82, pred[64,256]{1,0:T(8,128)(4,1)S(1)} %fusion.22, s32[64]{0:T(128)S(1)} %fusion.33, f32[256]{0:T(256)S(1)} %multiply_subtract_fusion, pred[64]{0:T(512)(128)(4,1)S(1)} %fusion.32), kind=kOutput, calls=%fused_computation.12 | convolution fusion | flops 1086586880 | bytes 25314624 | tf_op jit(solution)/shard_map/kt,stc->ksc/dot_general | solution.py:55
  82.8 1.6 multiply_convert_fusion
  84.4 2.4 copy.46
  86.8 57.3 %all_to_all.18 = bf16[32,2,64,512]{3,2,1,0:T(8,128)(2,1)S(1)} all-to-all(bf16[32,2,64,512]{3,2,1,0:T(8,128)(2,1)S(1)} %bitcast.83), channel_id=1, replica_groups=mesh['chan'=16,'freq'=8] {'freq'}, dimensions={0} | all-to-all | bytes 8388608 | tf_op jit(solution)/shard_map/all_to_all | solution.py:60
  144.0 2.5 copy.27
  146.6 7.3 %copy.33 = bf16[4,2,512,512]{2,3,1,0:T(8,128)(2,1)} copy(bf16[4,2,512,512]{3,2,1,0:T(8,128)(2,1)} %bitcast.72) | data formatting | bytes 8388608 | tf_op jit(solution)/shard_map/all_to_all | solution.py:60
  153.8 1.9 collective-permute-start
  155.7 2.9 collective-permute-start.1
  159.4 0.0 copy-start
  159.4 3.7 %fusion.12 = f32[4,512,512]{1,2,0:T(8,128)S(1)} fusion(bf16[4,2,512,512]{3,2,1,0:T(8,128)(2,1)} %bitcast.73), kind=kOutput, calls=%fused_computation.31 | convolution fusion | flops 1073741824 | bytes 8388608 | tf_op jit(solution)/shard_map/fsi,fsj->fij/dot_general | solution.py:44
  163.1 0.0 copy-done
  163.1 1.3 subtract_bitcast_fusion.2
  164.4 2.4 convolution_bitcast_fusion.2
  166.8 1.3 fusion.9
  168.1 76.6 %collective-permute-done = bf16[4,2,512,512]{2,3,1,0:T(8,128)(2,1)S(1)} collective-permute-done((bf16[4,2,512,512]{2,3,1,0:T(8,128)(2,1)}, bf16[4,2,512,512]{2,3,1,0:T(8,128)(2,1)S(1)}, u32[]{:S(2)}, u32[]{:S(2)}) %collective-permute-start) | collective-permute-done | bytes 4194336 | tf_op jit(solution)/shard_map/ppermute | solution.py:17
  244.6 1.2 fusion.11
  245.9 1.3 subtract_bitcast_fusion.1
  247.1 2.3 convolution_bitcast_fusion.1
  249.5 1.3 fusion.8
  250.8 43.7 %collective-permute-done.1 = bf16[4,2,512,512]{2,3,1,0:T(8,128)(2,1)S(1)} collective-permute-done((bf16[4,2,512,512]{2,3,1,0:T(8,128)(2,1)}, bf16[4,2,512,512]{2,3,1,0:T(8,128)(2,1)S(1)}, u32[]{:S(2)}, u32[]{:S(2)}) %collective-permute-start.1) | collective-permute-done | bytes 4194336 | tf_op jit(solution)/shard_map/ppermute | solution.py:17
  294.5 1.3 fusion.10
  295.8 2.3 convolution_bitcast_fusion
  298.1 1.3 subtract_bitcast_fusion
  299.4 1.3 fusion.7
  300.7 5.4 %pad_maximum_fusion = bf16[3,4,512,1024]{2,3,1,0:T(8,128)(2,1)} fusion(bf16[1,4,512,1024]{2,3,1,0:T(8,128)(2,1)S(1)} %fusion.7, bf16[1,4,512,1024]{2,3,1,0:T(8,128)(2,1)S(1)} %fusion.8, bf16[1,4,512,1024]{2,3,1,0:T(8,128)(2,1)S(1)} %fusion.9), kind=kLoop, calls=%fused_computation.4 | loop fusion | flops 12582912 | bytes 25165824 | tf_op jit(solution)/shard_map/stack | solution.py:69
  306.1 16.9 %copy.37 = bf16[3,4,512,1024]{3,2,1,0:T(8,128)(2,1)} copy(bf16[3,4,512,1024]{2,3,1,0:T(8,128)(2,1)} %pad_maximum_fusion) | data formatting | bytes 25165824 | tf_op jit(solution)/shard_map/stack | solution.py:69
  (6 shorter events, 0.1 us)
Async XLA Ops:
  153.8 90.8 %collective-permute-start = (bf16[4,2,512,512]{2,3,1,0:T(8,128)(2,1)}, bf16[4,2,512,512]{2,3,1,0:T(8,128)(2,1)S(1)}, u32[]{:S(2)}, u32[]{:S(2)}) collective-permute-start(bf16[4,2,512,512]{2,3,1,0:T(8,128)(2,1)} %copy.33), channel_id=1, source_target_pairs={{8,0},{16,8},{24,16},{32,24},{40,32},{48,40},{56,48},{64,56},{72,6... | collective-permute-start | bytes 12582920 | tf_op jit(solution)/shard_map/ppermute | solution.py:17
  155.7 138.8 %collective-permute-start.1 = (bf16[4,2,512,512]{2,3,1,0:T(8,128)(2,1)}, bf16[4,2,512,512]{2,3,1,0:T(8,128)(2,1)S(1)}, u32[]{:S(2)}, u32[]{:S(2)}) collective-permute-start(bf16[4,2,512,512]{2,3,1,0:T(8,128)(2,1)} %copy.33), channel_id=1, source_target_pairs={{16,0},{24,8},{32,16},{40,24},{48,32},{56,40},{64,48},{72,56},{80,... | collective-permute-start | bytes 12582920 | tf_op jit(solution)/shard_map/ppermute | solution.py:17
  159.4 3.7 %copy-start = (bf16[4,2,8,64,512]{4,3,2,1,0:T(8,128)(2,1)S(1)}, bf16[4,2,8,64,512]{4,3,2,1,0:T(8,128)(2,1)}, u32[]{:S(2)}) copy-start(bf16[4,2,8,64,512]{4,3,2,1,0:T(8,128)(2,1)} %copy.27) | copy-start | bytes 12582916
where the time goes:
time: 324 us; the launch traced here: 323 us
  waiting for transfers between devices  120 us (37%)
  local copies, waits for them, and re-layouts  100 us (31%)
  blocking collectives  57.3 us (18%)
  matrix products  26.3 us (8%)
  other arithmetic  13.2 us (4%)
  starting transfers between devices  4.85 us (1%)
    ppermute x2, waiting for transfers between devices, from_behind(): return lax.ppermute(block, axis, route)  120 us
    gather x1, local copies, waits for them, and re-layouts, shards(): frames = jnp.take(records, sample_rows, axis=0)  71.2 us
    all_to_all x1, blocking collectives, shards(): lax.all_to_all(whitened, 'freq', split_axis=0, concat_axis=2, tiled=True)  57.3 us
    another operation x1, local copies, waits for them, and re-layouts, shards(): return jnp.stack(results, axis=0)  16.9 us
    all_to_all x2, local copies, waits for them, and re-layouts, shards(): lax.all_to_all(whitened, 'freq', split_axis=0, concat_axis=2, tiled=True)  9.79 us
    dot_general x1, matrix products, shards(): jnp.einsum('kt,stc->ksc', dft_rows, frames, preferred_element_type=jnp.fl...  9.27 us
    dot_general x3, matrix products, local_products(): jnp.einsum('fpsi,fpsj->fij', left_panel, right_panel, preferred_element_t...  7.03 us
  transfers between devices with their start and end apart: 2, of which 2 were waited for; matrix products, arithmetic and copies ran while one was open for 5% of the time, Pallas kernels for 0%

commit v1 on v0

--- a/solution.py
+++ b/solution.py
@@ -32,26 +32,20 @@
 
 def local_products(left_panel, partner_panels):
     seg_count = left_panel.shape[2]
-    left_real = left_panel[:, 0]
-    left_imag = left_panel[:, 1]
     results = []
     for right_panel in partner_panels:
-        real_part = jnp.einsum(
-            "fpsi,fpsj->fij", left_panel, right_panel, preferred_element_type=jnp.float32
+        turned = jnp.stack([-right_panel[:, 1], right_panel[:, 0]], axis=1)
+        both = jnp.concatenate([right_panel, turned], axis=3)
+        product = jnp.einsum(
+            "fpsi,fpsj->fij", left_panel, both, preferred_element_type=jnp.float32
         )
-        imag_part = jnp.einsum(
-            "fsi,fsj->fij", left_imag, right_panel[:, 0], preferred_element_type=jnp.float32
-        ) - jnp.einsum(
-            "fsi,fsj->fij", left_real, right_panel[:, 1], preferred_element_type=jnp.float32
-        )
-        results.append(jnp.concatenate([real_part, imag_part], axis=2) * (1.0 / seg_count))
+        results.append(product * (1.0 / seg_count))
     return results
 
 
 def shards(records, offsets, dead_mask, band_blocks):
     dft_rows = dft_table(SEG_LEN, BINS, FIRST_BIN)
-    sample_rows = offsets[:, None] + jnp.arange(SEG_LEN, dtype=jnp.int32)[None, :]
-    frames = jnp.take(records, sample_rows, axis=0)
+    frames = jax.vmap(lambda start: lax.dynamic_slice_in_dim(records, start, SEG_LEN, 0))(offsets)
     spectra = jnp.einsum("kt,stc->ksc", dft_rows, frames, preferred_element_type=jnp.float32)
     band_power = jnp.sum(spectra * spectra, axis=0) * (1.0 / BINS)
     scaling = dead_mask.astype(jnp.float32)[None, :] / jnp.sqrt(band_power + EPS_POWER)

time: 324 us -> 448 us (1.38)
  local copies, waits for them, and re-layouts: 100 us -> 203 us
  other arithmetic: 13.2 us -> 25.4 us
  matrix products: 26.3 us -> 31.4 us
    gather x1 -> x192, local copies, waits for them, and re-layouts: 71.2 us -> 189 us  [shards(): frames = jnp.take(records, sample_rows, axis=0)]
    another operation x1 -> x0, local copies, waits for them, and re-layouts: 16.9 us -> none  [shards(): return jnp.stack(results, axis=0)]
    reshape x1 -> x2, local copies, waits for them, and re-layouts: 2.37 us -> 13.7 us  [shards(): whitened = whitened.reshape(BINS, 2, whitened.shape[1], whitened.shape[2])]
    neg x0 -> x3, other arithmetic: none -> 9.85 us  [local_products(): turned = jnp.stack([-right_panel[:, 1], right_panel[:, 0]], axis=1)]
    all_to_all x2 -> x1, local copies, waits for them, and re-layouts: 9.79 us -> 0.96 us  [shards(): lax.all_to_all(whitened, 'freq', split_axis=0, concat_axis=2, tiled=True)]
    dot_general x9 -> x3, matrix products: 17 us -> 23.7 us  [local_products(): jnp.einsum('fpsi,fpsj->fij', left_panel, both, preferred_element_type=jnp...]
    another operation x1, other arithmetic: 5.43 us -> 10.5 us  [shards(): return jnp.stack(results, axis=0)]
  transfers between devices with their start and end apart: 2 -> 2, of which waited for: 2 -> 2; matrix products, arithmetic and copies ran while one was open for 5% -> 3% of each run, Pallas kernels for 0% -> 0%
where the time goes in v1:
time: 448 us; the launch traced here: 445 us
  local copies, waits for them, and re-layouts  203 us (45%)
  waiting for transfers between devices  122 us (27%)
  blocking collectives  57.3 us (13%)
  matrix products  31.4 us (7%)
  other arithmetic  25.4 us (6%)
  starting transfers between devices  4.87 us (1%)
    gather x192, local copies, waits for them, and re-layouts  189 us
    ppermute x2, waiting for transfers between devices, from_behind(): return lax.ppermute(block, axis, route)  122 us
    all_to_all x1, blocking collectives, shards(): lax.all_to_all(whitened, 'freq', split_axis=0, concat_axis=2, tiled=True)  57.3 us
    dot_general x3, matrix products, local_products(): jnp.einsum('fpsi,fpsj->fij', left_panel, both, preferred_element_type=jnp...  23.7 us
    reshape x2, local copies, waits for them, and re-layouts, shards(): whitened = whitened.reshape(BINS, 2, whitened.shape[1], whitened.shape[2])  13.7 us
    another operation x1, other arithmetic, shards(): return jnp.stack(results, axis=0)  10.5 us
    neg x3, other arithmetic, local_products(): turned = jnp.stack([-right_panel[:, 1], right_panel[:, 0]], axis=1)  9.85 us
  transfers between devices with their start and end apart: 2, of which 2 were waited for; matrix products, arithmetic and copies ran while one was open for 3% of the time, Pallas kernels for 0%

profile of v1, /device:TPU:34, one launch (start us, length us, event | category | flops | bytes accessed | tf_op | source)
XLA Modules:
  0.0 444.6 jit_solution(16170170427373988645)
XLA Ops:
  0.7 188.7 %while.1 = (s32[]{:T(128)}, bf16[8448,512]{1,0:T(8,128)(2,1)}, s32[64,2]{0,1:T(2,128)S(1)}, bf16[64,256,512]{2,1,0:T(8,128)(2,1)}, s32[]{:T(128)}) while((s32[]{:T(128)}, bf16[8448,512]{1,0:T(8,128)(2,1)}, s32[64,2]{0,1:T(2,128)S(1)}, bf16[64,256,512]{2,1,0:T(8,128)(2,1)}, s32[]{:T(128)}) %tuple.20), condition=%wide.while_cond, body=%wide.while_body.sunk | while | flops 2 | bytes 525401 | solution.py:48
  16.0 2.3 bitcast_dynamic-update-slice_fusion.2
  33.7 2.3 bitcast_dynamic-update-slice_fusion.2
  51.4 2.4 bitcast_dynamic-update-slice_fusion.2
  54.4 2.3 bitcast_dynamic-update-slice_fusion.2
  57.3 2.4 bitcast_dynamic-update-slice_fusion.2
  75.0 2.3 bitcast_dynamic-update-slice_fusion.2
  80.9 2.3 bitcast_dynamic-update-slice_fusion.2
  92.7 2.4 bitcast_dynamic-update-slice_fusion.2
  95.7 2.3 bitcast_dynamic-update-slice_fusion.2
  98.6 2.3 bitcast_dynamic-update-slice_fusion.2
  101.6 2.4 bitcast_dynamic-update-slice_fusion.2
  142.8 2.3 bitcast_dynamic-update-slice_fusion.2
  145.8 2.4 bitcast_dynamic-update-slice_fusion.2
  148.7 2.3 bitcast_dynamic-update-slice_fusion.2
  151.7 2.4 bitcast_dynamic-update-slice_fusion.2
  166.4 2.4 bitcast_dynamic-update-slice_fusion.2
  187.1 2.3 bitcast_dynamic-update-slice_fusion.2
  190.1 7.7 %multiply_reduce_fusion = (f32[64,512]{1,0:T(8,128)S(1)}, f32[64,64,512]{2,0,1:T(8,128)S(1)}) fusion(bf16[64,256,512]{2,1,0:T(8,128)(2,1)} %get-tuple-element.12, s32[64]{0:T(128)S(1)} %fusion.50, f32[256]{0:T(256)S(1)} %multiply_subtract_fusion, pred[64]{0:T(512)(128)(4,1)S(1)} %fusion.49), kind=kOutput, calls=%fused_computation.28 | convolution fusion | flops 1078198272 | bytes 25298240 | tf_op jit(solution)/shard_map/kt,stc->ksc/dot_general | solution.py:49
  197.8 3.6 multiply_convert_fusion
  201.4 7.2 %reshape.68 = bf16[32,2,64,512]{3,1,0,2:T(2,128)(2,1)} reshape(bf16[64,64,512]{2,0,1:T(8,128)(2,1)} %multiply_convert_fusion) | data formatting | bytes 8388608 | tf_op jit(solution)/shard_map/reshape | solution.py:53
  208.6 6.5 %copy.9 = bf16[32,2,64,512]{3,1,2,0:T(2,128)(2,1)S(1)} copy(bf16[32,2,64,512]{3,1,0,2:T(2,128)(2,1)} %reshape.68) | data formatting | bytes 8388608 | tf_op jit(solution)/shard_map/reshape | solution.py:53
  215.1 57.3 %all_to_all.18 = bf16[32,2,64,512]{3,1,2,0:T(2,128)(2,1)S(1)} all-to-all(bf16[32,2,64,512]{3,1,2,0:T(2,128)(2,1)S(1)} %copy.9), channel_id=1, replica_groups=mesh['chan'=16,'freq'=8] {'freq'}, dimensions={0} | all-to-all | bytes 8388608 | tf_op jit(solution)/shard_map/all_to_all | solution.py:54
  275.3 3.0 collective-permute-start.1
  280.5 7.4 %fusion.22 = bf16[1,4,512,1024]{3,2,1,0:T(8,128)(2,1)} fusion(bf16[4,2,512,512]{3,2,1,0:T(8,128)(2,1)S(1)} %bitcast.63, bf16[4,1,512,512]{3,2,1,0:T(8,128)(2,1)} %get-tuple-element.22, bf16[4,1,512,512]{3,2,1,0:T(8,128)(2,1)S(1)} %get-tuple-element.21, bf16[]{:T(256)} %bitcast.8), kind=kOutput, calls=%fused_computation.30 | convolution fusion | flops 4326424576 | bytes 12582914 | tf_op jit(solution)/shard_map/fpsi,fpsj->fij/dot_general | solution.py:39
  287.9 76.0 %collective-permute-done = bf16[4,2,512,512]{3,2,1,0:T(8,128)(2,1)} collective-permute-done((bf16[4,2,512,512]{3,2,1,0:T(8,128)(2,1)S(1)}, bf16[4,2,512,512]{3,2,1,0:T(8,128)(2,1)}, u32[]{:S(2)}, u32[]{:S(2)}) %collective-permute-start) | collective-permute-done | bytes 4194336 | tf_op jit(solution)/shard_map/ppermute | solution.py:17
  363.9 4.4 %slice_negate_fusion.1 = (bf16[4,1,512,512]{3,2,1,0:T(8,128)(2,1)}, bf16[4,1,512,512]{3,2,1,0:T(8,128)(2,1)}) fusion(bf16[4,2,512,512]{3,2,1,0:T(8,128)(2,1)} %collective-permute-done), kind=kLoop, calls=%fused_computation.36 | loop fusion | flops 1048576 | bytes 8388608 | tf_op jit(solution)/shard_map/neg | solution.py:37
  368.3 45.6 %collective-permute-done.1 = bf16[4,2,512,512]{3,2,1,0:T(8,128)(2,1)} collective-permute-done((bf16[4,2,512,512]{3,2,1,0:T(8,128)(2,1)S(1)}, bf16[4,2,512,512]{3,2,1,0:T(8,128)(2,1)}, u32[]{:S(2)}, u32[]{:S(2)}) %collective-permute-start.1) | collective-permute-done | bytes 4194336 | tf_op jit(solution)/shard_map/ppermute | solution.py:17
  414.0 3.8 slice_negate_fusion
  417.8 8.3 %fusion.24 = bf16[1,4,512,1024]{3,2,1,0:T(8,128)(2,1)} fusion(bf16[4,2,512,512]{3,2,1,0:T(8,128)(2,1)S(1)} %bitcast.64, bf16[4,1,512,512]{3,2,1,0:T(8,128)(2,1)} %get-tuple-element.24, bf16[4,1,512,512]{3,2,1,0:T(8,128)(2,1)} %get-tuple-element.23, bf16[4,2,512,512]{3,2,1,0:T(8,128)(2,1)} %collective-permute-done, bf16[]{:T(256)} %bitcast.12), kind=kOutput, calls=%fused_computation.32 | convolution fusion | flops 4326424576 | bytes 16777218 | tf_op jit(solution)/shard_map/fpsi,fpsj->fij/dot_general | solution.py:39
  426.1 8.0 %fusion.26 = bf16[1,4,512,1024]{3,2,1,0:T(8,128)(2,1)} fusion(bf16[4,2,512,512]{3,2,1,0:T(8,128)(2,1)S(1)} %bitcast.65, bf16[4,1,512,512]{3,2,1,0:T(8,128)(2,1)} %get-tuple-element.26, bf16[4,1,512,512]{3,2,1,0:T(8,128)(2,1)S(1)} %get-tuple-element.25, bf16[4,2,512,512]{3,2,1,0:T(8,128)(2,1)} %collective-permute-done.1, bf16[]{:T(256)} %bitcast.16), kind=kOutput, calls=%fused_computation.34 | convolution fusion | flops 4326424576 | bytes 16777218 | tf_op jit(solution)/shard_map/fpsi,fpsj->fij/dot_general | solution.py:39
  434.1 10.5 %pad_maximum_fusion = bf16[3,4,512,1024]{3,2,1,0:T(8,128)(2,1)} fusion(bf16[1,4,512,1024]{3,2,1,0:T(8,128)(2,1)} %fusion.26, bf16[1,4,512,1024]{3,2,1,0:T(8,128)(2,1)} %fusion.24, bf16[1,4,512,1024]{3,2,1,0:T(8,128)(2,1)} %fusion.22), kind=kLoop, calls=%fused_computation.2 | loop fusion | flops 12582912 | bytes 25165824 | tf_op jit(solution)/shard_map/stack | solution.py:63
  (186 shorter events, 154.5 us)
Async XLA Ops:
  273.4 90.5 %collective-permute-start = (bf16[4,2,512,512]{3,2,1,0:T(8,128)(2,1)S(1)}, bf16[4,2,512,512]{3,2,1,0:T(8,128)(2,1)}, u32[]{:S(2)}, u32[]{:S(2)}) collective-permute-start(bf16[4,2,512,512]{3,2,1,0:T(8,128)(2,1)S(1)} %bitcast.60), channel_id=1, source_target_pairs={{8,0},{16,8},{24,16},{32,24},{40,32},{48,40},{56,48},{64,56},{72,6... | collective-permute-start | bytes 12582920 | tf_op jit(solution)/shard_map/ppermute | solution.py:17
  275.3 138.7 %collective-permute-start.1 = (bf16[4,2,512,512]{3,2,1,0:T(8,128)(2,1)S(1)}, bf16[4,2,512,512]{3,2,1,0:T(8,128)(2,1)}, u32[]{:S(2)}, u32[]{:S(2)}) collective-permute-start(bf16[4,2,512,512]{3,2,1,0:T(8,128)(2,1)S(1)} %bitcast.61), channel_id=1, source_target_pairs={{16,0},{24,8},{32,16},{40,24},{48,32},{56,40},{64,48},{72,56},{80,... | collective-permute-start | bytes 12582920 | tf_op jit(solution)/shard_map/ppermute | solution.py:17

commit v2 on v1

--- a/solution.py
+++ b/solution.py
@@ -1,6 +1,10 @@
+import functools
+
 import jax
 import jax.numpy as jnp
 from jax import lax
+from jax.experimental import pallas as pl
+from jax.experimental.pallas import tpu as pltpu
 from jax.sharding import PartitionSpec as P
 
 SEG_LEN = 256
@@ -30,6 +34,64 @@
     return (hann_taper[None, :] * wave_rows).astype(jnp.bfloat16)
 
 
+def spectra_kernel(seg_count, window, offs_ref, dft_ref, mask_ref, rec_hbm, out_ref, frames, sems):
+    last_start = rec_hbm.shape[0] - window
+    starts = []
+    copies = []
+    for j in range(seg_count):
+        offset = offs_ref[j]
+        start = pl.multiple_of(jnp.minimum((offset // 16) * 16, last_start), 16)
+        starts.append(offset - start)
+        copies.append(
+            pltpu.make_async_copy(rec_hbm.at[pl.ds(start, window)], frames.at[j], sems.at[j])
+        )
+    for copy in copies:
+        copy.start()
+    dft = dft_ref[...]
+    live = mask_ref[...]
+    for j in range(seg_count):
+        shifted = pltpu.roll(dft, starts[j], 1).astype(jnp.bfloat16)
+        copies[j].wait()
+        spec = jnp.dot(shifted, frames[j], preferred_element_type=jnp.float32)
+        power = jnp.sum(spec * spec, axis=0, keepdims=True) * (1.0 / BINS)
+        scale = live / jnp.sqrt(power + EPS_POWER)
+        out_ref[j] = (spec * scale).astype(out_ref.dtype)
+
+
+def whitened_spectra(records, offsets, dead_mask):
+    seg_count = offsets.shape[0]
+    channels = records.shape[1]
+    window = SEG_LEN + 128
+    dft_rows = dft_table(SEG_LEN, BINS, FIRST_BIN)
+    rows = dft_rows.shape[0]
+    padded = jnp.pad(dft_rows.astype(jnp.float32), ((0, 0), (0, window - SEG_LEN)))
+    live = dead_mask.astype(jnp.float32).reshape(1, channels)
+    return pl.pallas_call(
+        functools.partial(spectra_kernel, seg_count, window),
+        out_shape=jax.ShapeDtypeStruct((seg_count, rows, channels), jnp.bfloat16),
+        grid_spec=pltpu.PrefetchScalarGridSpec(
+            num_scalar_prefetch=1,
+            grid=(1,),
+            in_specs=[
+                pl.BlockSpec((rows, window), lambda i, offs: (0, 0)),
+                pl.BlockSpec((1, channels), lambda i, offs: (0, 0)),
+                pl.BlockSpec(memory_space=pl.ANY),
+            ],
+            out_specs=pl.BlockSpec((seg_count, rows, channels), lambda i, offs: (0, 0, 0)),
+            scratch_shapes=[
+                pltpu.VMEM((seg_count, window, channels), records.dtype),
+                pltpu.SemaphoreType.DMA((seg_count,)),
+            ],
+        ),
+        compiler_params=pltpu.CompilerParams(vmem_limit_bytes=56 * 1024 * 1024),
+        cost_estimate=pl.CostEstimate(
+            flops=2 * seg_count * rows * window * channels,
+            bytes_accessed=seg_count * (window + rows) * channels * 2,
+            transcendentals=seg_count * channels,
+        ),
+    )(offsets, padded, live, records)
+
+
 def local_products(left_panel, partner_panels):
     seg_count = left_panel.shape[2]
     results = []
@@ -44,13 +106,9 @@
 
 
 def shards(records, offsets, dead_mask, band_blocks):
-    dft_rows = dft_table(SEG_LEN, BINS, FIRST_BIN)
-    frames = jax.vmap(lambda start: lax.dynamic_slice_in_dim(records, start, SEG_LEN, 0))(offsets)
-    spectra = jnp.einsum("kt,stc->ksc", dft_rows, frames, preferred_element_type=jnp.float32)
-    band_power = jnp.sum(spectra * spectra, axis=0) * (1.0 / BINS)
-    scaling = dead_mask.astype(jnp.float32)[None, :] / jnp.sqrt(band_power + EPS_POWER)
-    whitened = (spectra * scaling[None]).astype(jnp.bfloat16)
-    whitened = whitened.reshape(BINS, 2, whitened.shape[1], whitened.shape[2])
+    per_segment = whitened_spectra(records, offsets, dead_mask)
+    seg_count, rows, channels = per_segment.shape
+    whitened = per_segment.reshape(seg_count, BINS, 2, channels).transpose(1, 2, 0, 3)
     own_panel = lax.all_to_all(whitened, "freq", split_axis=0, concat_axis=2, tiled=True)
     upper_panel = from_behind(own_panel, "chan", -1)
     second_panel = from_behind(own_panel, "chan", -2)

time: 448 us -> 266 us (0.59)
  local copies, waits for them, and re-layouts: 203 us -> 14.7 us
  Pallas kernels: 0 us -> 20.1 us
  matrix products: 31.4 us -> 23.7 us
    gather x192 -> x0, local copies, waits for them, and re-layouts: 189 us -> none
    pallas_call x0 -> x1, Pallas kernels: none -> 20.1 us  [whitened_spectra(): pl.pallas_call(functools.partial(spectra_kernel, seg_count, window), out_...]
    dot_general x1 -> x0, matrix products: 7.69 us -> none  [shards(): jnp.einsum('kt,stc->ksc', dft_rows, frames, preferred_element_type=jnp.fl...]
  transfers between devices with their start and end apart: 2 -> 2, of which waited for: 2 -> 2; matrix products, arithmetic and copies ran while one was open for 3% -> 5% of each run, Pallas kernels for 0% -> 0%
where the time goes in v2:
time: 266 us
  waiting for transfers between devices  122 us (46%)
  blocking collectives  57.2 us (22%)
  matrix products  23.7 us (9%)
  other arithmetic  22.7 us (9%)
  Pallas kernels  20.1 us (8%)
  local copies, waits for them, and re-layouts  14.7 us (6%)
  starting transfers between devices  4.69 us (2%)
    ppermute x2, waiting for transfers between devices, from_behind(): return lax.ppermute(block, axis, route)  122 us
    all_to_all x1, blocking collectives, shards(): lax.all_to_all(whitened, 'freq', split_axis=0, concat_axis=2, tiled=True)  57.2 us
    dot_general x3, matrix products, local_products(): jnp.einsum('fpsi,fpsj->fij', left_panel, both, preferred_element_type=jnp...  23.7 us
    pallas_call x1, Pallas kernels, whitened_spectra(): pl.pallas_call(functools.partial(spectra_kernel, seg_count, window), out_...  20.1 us
    reshape x2, local copies, waits for them, and re-layouts, shards(): per_segment.reshape(seg_count, BINS, 2, channels).transpose(1, 2, 0, 3)  13.7 us
    another operation x1, other arithmetic, shards(): return jnp.stack(results, axis=0)  10.5 us
    neg x3, other arithmetic, local_products(): turned = jnp.stack([-right_panel[:, 1], right_panel[:, 0]], axis=1)  9.85 us
  transfers between devices with their start and end apart: 2, of which 2 were waited for; matrix products, arithmetic and copies ran while one was open for 5% of the time, Pallas kernels for 0%

profile of v2, /device:TPU:34, one launch (start us, length us, event | category | flops | bytes accessed | tf_op | source)
XLA Modules:
  0.0 265.6 jit_solution(17572295241518018944)
XLA Ops:
  0.1 0.3 multiply_convert_fusion
  0.4 0.6 pad_convert_fusion.dft_ref
  1.1 1.3 convert_element_type.49
  2.3 20.1 %shard_map.46 = bf16[64,64,512]{2,1,0:T(8,128)(2,1)} custom-call(s32[64]{0:T(128)} %offs_ref.1, f32[64,384]{1,0:T(8,128)} %pad_convert_fusion.dft_ref, f32[1,512]{1,0:T(1,128)} %bitcast.55, bf16[8448,512]{1,0:T(8,128)(2,1)} %rec_hbm.1), custom_call_target="tpu_custom_call" | custom-call | flops 1610612736 | bytes 29360128 | tf_op jit(solution)/shard_map/pallas_call | solution.py:69
  22.5 7.2 %reshape.51 = bf16[64,32,2,512]{3,2,1,0:T(2,128)(2,1)} reshape(bf16[64,64,512]{2,1,0:T(8,128)(2,1)} %shard_map.46) | data formatting | bytes 8388608 | tf_op jit(solution)/shard_map/reshape | solution.py:111
  29.7 6.5 %copy.21 = bf16[64,32,2,512]{3,2,0,1:T(2,128)(2,1)S(1)} copy(bf16[64,32,2,512]{3,2,1,0:T(2,128)(2,1)} %reshape.51) | data formatting | bytes 8388608 | tf_op jit(solution)/shard_map/reshape | solution.py:111
  36.2 57.2 %all_to_all.18 = bf16[32,2,64,512]{3,1,2,0:T(2,128)(2,1)S(1)} all-to-all(bf16[32,2,64,512]{3,1,2,0:T(2,128)(2,1)S(1)} %bitcast.53), channel_id=1, replica_groups=mesh['chan'=16,'freq'=8] {'freq'}, dimensions={0} | all-to-all | bytes 8388608 | tf_op jit(solution)/shard_map/all_to_all | solution.py:112
  93.4 1.0 copy.10
  94.3 1.9 collective-permute-start
  96.3 2.8 %collective-permute-start.1 = (bf16[4,2,512,512]{3,2,1,0:T(8,128)(2,1)S(1)}, bf16[4,2,512,512]{3,2,1,0:T(8,128)(2,1)}, u32[]{:S(2)}, u32[]{:S(2)}) collective-permute-start(bf16[4,2,512,512]{3,2,1,0:T(8,128)(2,1)S(1)} %bitcast.48), channel_id=1, source_target_pairs={{16,0},{24,8},{32,16},{40,24},{48,32},{56,40},{64,48},{72,56},{80,... | collective-permute-start | bytes 12582920 | tf_op jit(solution)/shard_map/ppermute | solution.py:21
  99.7 1.6 slice_negate_fusion.2
  101.3 7.4 %fusion.22 = bf16[1,4,512,1024]{3,2,1,0:T(8,128)(2,1)} fusion(bf16[4,2,512,512]{3,2,1,0:T(8,128)(2,1)S(1)} %bitcast.50, bf16[4,1,512,512]{3,2,1,0:T(8,128)(2,1)} %get-tuple-element.6, bf16[4,1,512,512]{3,2,1,0:T(8,128)(2,1)S(1)} %get-tuple-element.5, bf16[]{:T(256)} %bitcast.8), kind=kOutput, calls=%fused_computation.26 | convolution fusion | flops 4326424576 | bytes 12582914 | tf_op jit(solution)/shard_map/fpsi,fpsj->fij/dot_general | solution.py:101
  108.7 76.2 %collective-permute-done = bf16[4,2,512,512]{3,2,1,0:T(8,128)(2,1)} collective-permute-done((bf16[4,2,512,512]{3,2,1,0:T(8,128)(2,1)S(1)}, bf16[4,2,512,512]{3,2,1,0:T(8,128)(2,1)}, u32[]{:S(2)}, u32[]{:S(2)}) %collective-permute-start) | collective-permute-done | bytes 4194336 | tf_op jit(solution)/shard_map/ppermute | solution.py:21
  184.8 4.4 %slice_negate_fusion.1 = (bf16[4,1,512,512]{3,2,1,0:T(8,128)(2,1)}, bf16[4,1,512,512]{3,2,1,0:T(8,128)(2,1)}) fusion(bf16[4,2,512,512]{3,2,1,0:T(8,128)(2,1)} %collective-permute-done), kind=kLoop, calls=%fused_computation.33 | loop fusion | flops 1048576 | bytes 8388608 | tf_op jit(solution)/shard_map/neg | solution.py:99
  189.3 45.6 %collective-permute-done.1 = bf16[4,2,512,512]{3,2,1,0:T(8,128)(2,1)} collective-permute-done((bf16[4,2,512,512]{3,2,1,0:T(8,128)(2,1)S(1)}, bf16[4,2,512,512]{3,2,1,0:T(8,128)(2,1)}, u32[]{:S(2)}, u32[]{:S(2)}) %collective-permute-start.1) | collective-permute-done | bytes 4194336 | tf_op jit(solution)/shard_map/ppermute | solution.py:21
  234.9 3.8 %slice_negate_fusion = (bf16[4,1,512,512]{3,2,1,0:T(8,128)(2,1)S(1)}, bf16[4,1,512,512]{3,2,1,0:T(8,128)(2,1)}) fusion(bf16[4,2,512,512]{3,2,1,0:T(8,128)(2,1)} %collective-permute-done.1), kind=kLoop, calls=%fused_computation.32 | loop fusion | flops 1048576 | bytes 8388608 | tf_op jit(solution)/shard_map/neg | solution.py:99
  238.7 8.3 %fusion.24 = bf16[1,4,512,1024]{3,2,1,0:T(8,128)(2,1)} fusion(bf16[4,2,512,512]{3,2,1,0:T(8,128)(2,1)S(1)} %bitcast.51, bf16[4,1,512,512]{3,2,1,0:T(8,128)(2,1)} %get-tuple-element.8, bf16[4,1,512,512]{3,2,1,0:T(8,128)(2,1)} %get-tuple-element.7, bf16[4,2,512,512]{3,2,1,0:T(8,128)(2,1)} %collective-permute-done, bf16[]{:T(256)} %bitcast.12), kind=kOutput, calls=%fused_computation.28 | convolution fusion | flops 4326424576 | bytes 16777218 | tf_op jit(solution)/shard_map/fpsi,fpsj->fij/dot_general | solution.py:101
  247.1 8.0 %fusion.26 = bf16[1,4,512,1024]{3,2,1,0:T(8,128)(2,1)} fusion(bf16[4,2,512,512]{3,2,1,0:T(8,128)(2,1)S(1)} %bitcast.52, bf16[4,1,512,512]{3,2,1,0:T(8,128)(2,1)} %get-tuple-element.10, bf16[4,1,512,512]{3,2,1,0:T(8,128)(2,1)S(1)} %get-tuple-element.9, bf16[4,2,512,512]{3,2,1,0:T(8,128)(2,1)} %collective-permute-done.1, bf16[]{:T(256)} %bitcast.16), kind=kOutput, calls=%fused_computation.30 | convolution fusion | flops 4326424576 | bytes 16777218 | tf_op jit(solution)/shard_map/fpsi,fpsj->fij/dot_general | solution.py:101
  255.1 10.5 %pad_maximum_fusion = bf16[3,4,512,1024]{3,2,1,0:T(8,128)(2,1)} fusion(bf16[1,4,512,1024]{3,2,1,0:T(8,128)(2,1)} %fusion.26, bf16[1,4,512,1024]{3,2,1,0:T(8,128)(2,1)} %fusion.24, bf16[1,4,512,1024]{3,2,1,0:T(8,128)(2,1)} %fusion.22), kind=kLoop, calls=%fused_computation | loop fusion | flops 12582912 | bytes 25165824 | tf_op jit(solution)/shard_map/stack | solution.py:121
  (3 shorter events, 0.1 us)
Async XLA Ops:
  94.3 90.5 %collective-permute-start = (bf16[4,2,512,512]{3,2,1,0:T(8,128)(2,1)S(1)}, bf16[4,2,512,512]{3,2,1,0:T(8,128)(2,1)}, u32[]{:S(2)}, u32[]{:S(2)}) collective-permute-start(bf16[4,2,512,512]{3,2,1,0:T(8,128)(2,1)S(1)} %bitcast.47), channel_id=1, source_target_pairs={{8,0},{16,8},{24,16},{32,24},{40,32},{48,40},{56,48},{64,56},{72,6... | collective-permute-start | bytes 12582920 | tf_op jit(solution)/shard_map/ppermute | solution.py:21
  96.3 138.7 %collective-permute-start.1 = (bf16[4,2,512,512]{3,2,1,0:T(8,128)(2,1)S(1)}, bf16[4,2,512,512]{3,2,1,0:T(8,128)(2,1)}, u32[]{:S(2)}, u32[]{:S(2)}) collective-permute-start(bf16[4,2,512,512]{3,2,1,0:T(8,128)(2,1)S(1)} %bitcast.48), channel_id=1, source_target_pairs={{16,0},{24,8},{32,16},{40,24},{48,32},{56,40},{64,48},{72,56},{80,... | collective-permute-start | bytes 12582920 | tf_op jit(solution)/shard_map/ppermute | solution.py:21

commit v3 on v2

--- a/solution.py
+++ b/solution.py
@@ -10,6 +10,7 @@
 SEG_LEN = 256
 BINS = 32
 FIRST_BIN = 2
+BAND = 2
 
 
 EPS_POWER = 1e-06
@@ -105,14 +106,36 @@
     return results
 
 
+def exchange_panels(whitened, offsets_kept):
+    n_chan = lax.axis_size("chan")
+    n_freq = lax.axis_size("freq")
+    bins, parts, seg_count, channels = whitened.shape
+    groups = whitened.reshape(n_freq, bins // n_freq, parts, seg_count, channels)
+    me = lax.axis_index("freq")
+    pieces = [lax.dynamic_index_in_dim(groups, me ^ g, 0, keepdims=False) for g in range(n_freq)]
+    panels = []
+    for d in range(offsets_kept):
+        received = []
+        for g in range(n_freq):
+            if d == 0 and g == 0:
+                received.append(pieces[0])
+                continue
+            pairs = [
+                (c * n_freq + f, (c - d) * n_freq + (f ^ g))
+                for c in range(d, n_chan)
+                for f in range(n_freq)
+            ]
+            received.append(lax.ppermute(pieces[g], ("chan", "freq"), pairs))
+        panels.append(jnp.concatenate(received, axis=2))
+    return panels
+
+
 def shards(records, offsets, dead_mask, band_blocks):
     per_segment = whitened_spectra(records, offsets, dead_mask)
     seg_count, rows, channels = per_segment.shape
     whitened = per_segment.reshape(seg_count, BINS, 2, channels).transpose(1, 2, 0, 3)
-    own_panel = lax.all_to_all(whitened, "freq", split_axis=0, concat_axis=2, tiled=True)
-    upper_panel = from_behind(own_panel, "chan", -1)
-    second_panel = from_behind(own_panel, "chan", -2)
-    products = local_products(own_panel, [own_panel, upper_panel, second_panel])
+    panels = exchange_panels(whitened, BAND + 1)
+    products = local_products(panels[0], panels)
     band_limit = band_blocks[0]
     results = []
     for offset_index, product in enumerate(products):

time: 266 us -> 290 us (1.090); the launches traced: 266 us -> 285 us
  starting transfers between devices: 4.69 us -> 119 us
  blocking collectives: 57.2 us -> 0 us
  waiting for transfers between devices: 122 us -> 79.4 us
  matrix products: 23.7 us -> 30.6 us
  other arithmetic: 22.7 us -> 17.7 us
    ppermute x2 -> x23, starting transfers between devices: 4.69 us -> 119 us  [exchange_panels(): received.append(lax.ppermute(pieces[g], ('chan', 'freq'), pairs))]
    all_to_all x1 -> x0, blocking collectives: 57.2 us -> none  [shards(): lax.all_to_all(whitened, 'freq', split_axis=0, concat_axis=2, tiled=True)]
    ppermute x2 -> x23, waiting for transfers between devices: 122 us -> 79.4 us  [exchange_panels(): received.append(lax.ppermute(pieces[g], ('chan', 'freq'), pairs))]
    dot_general x3, matrix products: 23.7 us -> 30.6 us  [local_products(): jnp.einsum('fpsi,fpsj->fij', left_panel, both, preferred_element_type=jnp...]
    reshape x2 -> x1, local copies, waits for them, and re-layouts: 13.7 us -> 7.21 us  [shards(): per_segment.reshape(seg_count, BINS, 2, channels).transpose(1, 2, 0, 3)]
    dynamic_slice x0 -> x1, local copies, waits for them, and re-layouts: none -> 5.83 us  [exchange_panels(): lax.dynamic_index_in_dim(groups, me ^ g, 0, keepdims=False)]
    neg x3, other arithmetic: 9.85 us -> 6.34 us  [local_products(): turned = jnp.stack([-right_panel[:, 1], right_panel[:, 0]], axis=1)]
    unnamed x0 -> x37, local copies, waits for them, and re-layouts: none -> 3.08 us
  transfers between devices with their start and end apart: 2 -> 23, of which waited for: 2 -> 13; matrix products, arithmetic and copies ran while one was open for 5% -> 2% of each run, Pallas kernels for 0% -> 0%
where the time goes in v3:
time: 290 us; the launch traced here: 285 us
  starting transfers between devices  119 us (41%)
  waiting for transfers between devices  79.4 us (27%)
  matrix products  30.6 us (11%)
  Pallas kernels  20 us (7%)
  other arithmetic  17.7 us (6%)
  local copies, waits for them, and re-layouts  16.2 us (6%)
    ppermute x23, starting transfers between devices, exchange_panels(): received.append(lax.ppermute(pieces[g], ('chan', 'freq'), pairs))  119 us
    ppermute x23, waiting for transfers between devices, exchange_panels(): received.append(lax.ppermute(pieces[g], ('chan', 'freq'), pairs))  79.4 us
    dot_general x3, matrix products, local_products(): jnp.einsum('fpsi,fpsj->fij', left_panel, both, preferred_element_type=jnp...  30.6 us
    pallas_call x1, Pallas kernels, whitened_spectra(): pl.pallas_call(functools.partial(spectra_kernel, seg_count, window), out_...  20 us
    another operation x1, other arithmetic, shards(): return jnp.stack(results, axis=0)  8.99 us
    reshape x1, local copies, waits for them, and re-layouts, shards(): per_segment.reshape(seg_count, BINS, 2, channels).transpose(1, 2, 0, 3)  7.21 us
    neg x3, other arithmetic, local_products(): turned = jnp.stack([-right_panel[:, 1], right_panel[:, 0]], axis=1)  6.34 us
    dynamic_slice x1, local copies, waits for them, and re-layouts, exchange_panels(): lax.dynamic_index_in_dim(groups, me ^ g, 0, keepdims=False)  5.83 us
  transfers between devices with their start and end apart: 23, of which 13 were waited for; matrix products, arithmetic and copies ran while one was open for 2% of the time, Pallas kernels for 0%

profile of v3, /device:TPU:34, one launch (start us, length us, event | category | flops | bytes accessed | tf_op | source)
XLA Modules:
  0.0 284.6 jit_solution(12433318073298788075)
XLA Ops:
  2.4 20.0 %shard_map.46 = bf16[64,64,512]{2,1,0:T(8,128)(2,1)} custom-call(s32[64]{0:T(128)} %offs_ref.1, f32[64,384]{1,0:T(8,128)} %pad_convert_fusion.dft_ref, f32[1,512]{1,0:T(1,128)} %bitcast.93, bf16[8448,512]{1,0:T(8,128)(2,1)} %rec_hbm.1), custom_call_target="tpu_custom_call" | custom-call | flops 1610612736 | bytes 29360128 | tf_op jit(solution)/shard_map/pallas_call | solution.py:70
  22.4 7.2 %reshape.54 = bf16[64,32,2,512]{3,2,1,0:T(2,128)(2,1)} reshape(bf16[64,64,512]{2,1,0:T(8,128)(2,1)} %shard_map.46) | data formatting | bytes 8388608 | tf_op jit(solution)/shard_map/reshape | solution.py:136
  29.6 5.8 %constant_dynamic-slice_fusion = (bf16[1,4,2,64,512]{4,2,1,0,3:T(2,128)(2,1)S(1)}, bf16[1,4,2,64,512]{4,2,1,0,3:T(2,128)(2,1)S(1)}, bf16[1,4,2,64,512]{4,2,1,0,3...) fusion(bf16[8,4,2,64,512]{4,2,1,0,3:T(2,128)(2,1)} %bitcast.69,, ...), kind=kLoop, calls=%fused_computation.77 | loop fusion | bytes 8388640 | tf_op jit(solution)/shard_map/jit(dynamic_index_in_dim)/dynamic_slice | solution.py:115
  35.6 2.4 collective-permute-start.15
  42.2 3.3 %collective-permute-start.1 = (bf16[4,2,64,512]{3,2,1,0:T(8,128)(2,1)S(1)}, bf16[4,2,64,512]{3,2,1,0:T(8,128)(2,1)S(1)}, u32[]{:S(2)}, u32[]{:S(2)}) collective-permute-start(bf16[4,2,64,512]{3,2,1,0:T(8,128)(2,1)S(1)} %bitcast.85), channel_id=1, source_target_pairs={{0,2},{1,3},{2,0},{3,1},{4,6},{5,7},{6,4},{7,5},{8,10},{9,11},{10,... | collective-permute-start | bytes 1572872 | tf_op jit(solution)/shard_map/ppermute | solution.py:128
  47.5 4.6 %collective-permute-done.15 = bf16[4,2,64,512]{3,2,1,0:T(8,128)(2,1)S(1)} collective-permute-done((bf16[4,2,64,512]{3,2,1,0:T(8,128)(2,1)S(1)}, bf16[4,2,64,512]{3,2,1,0:T(8,128)(2,1)S(1)}, u32[]{:S(2)}, u32[]{:S(2)}) %collective-permute-start.15) | collective-permute-done | bytes 524320 | tf_op jit(solution)/shard_map/ppermute | solution.py:128
  52.1 2.3 collective-permute-start.3
  56.2 4.9 %collective-permute-start.4 = (bf16[4,2,64,512]{3,2,1,0:T(8,128)(2,1)S(1)}, bf16[4,2,64,512]{3,2,1,0:T(8,128)(2,1)S(1)}, u32[]{:S(2)}, u32[]{:S(2)}) collective-permute-start(bf16[4,2,64,512]{3,2,1,0:T(8,128)(2,1)S(1)} %bitcast.76), channel_id=1, source_target_pairs={{0,5},{1,4},{2,7},{3,6},{4,1},{5,0},{6,3},{7,2},{8,13},{9,12},{10,... | collective-permute-start | bytes 1572872 | tf_op jit(solution)/shard_map/ppermute | solution.py:128
  61.1 3.0 %collective-permute-start.5 = (bf16[4,2,64,512]{3,2,1,0:T(8,128)(2,1)S(1)}, bf16[4,2,64,512]{3,2,1,0:T(8,128)(2,1)S(1)}, u32[]{:S(2)}, u32[]{:S(2)}) collective-permute-start(bf16[4,2,64,512]{3,2,1,0:T(8,128)(2,1)S(1)} %bitcast.73), channel_id=1, source_target_pairs={{0,6},{1,7},{2,4},{3,5},{4,2},{5,3},{6,0},{7,1},{8,14},{9,15},{10,... | collective-permute-start | bytes 1572872 | tf_op jit(solution)/shard_map/ppermute | solution.py:128
  64.2 4.6 %collective-permute-done.1 = bf16[4,2,64,512]{3,2,1,0:T(8,128)(2,1)S(1)} collective-permute-done((bf16[4,2,64,512]{3,2,1,0:T(8,128)(2,1)S(1)}, bf16[4,2,64,512]{3,2,1,0:T(8,128)(2,1)S(1)}, u32[]{:S(2)}, u32[]{:S(2)}) %collective-permute-start.1) | collective-permute-done | bytes 524320 | tf_op jit(solution)/shard_map/ppermute | solution.py:128
  72.0 2.4 collective-permute-start.17
  74.4 4.1 %collective-permute-start.18 = (bf16[4,2,64,512]{3,2,1,0:T(8,128)(2,1)S(1)}, bf16[4,2,64,512]{3,2,1,0:T(8,128)(2,1)S(1)}, u32[]{:S(2)}, u32[]{:S(2)}) collective-permute-start(bf16[4,2,64,512]{3,2,1,0:T(8,128)(2,1)S(1)} %bitcast.83), channel_id=1, source_target_pairs={{16,3},{17,2},{18,1},{19,0},{20,7},{21,6},{22,5},{23,4},{24,11},{2... | collective-permute-start | bytes 1572872 | tf_op jit(solution)/shard_map/ppermute | solution.py:128
  78.6 5.5 %collective-permute-done.4 = bf16[4,2,64,512]{3,2,1,0:T(8,128)(2,1)S(1)} collective-permute-done((bf16[4,2,64,512]{3,2,1,0:T(8,128)(2,1)S(1)}, bf16[4,2,64,512]{3,2,1,0:T(8,128)(2,1)S(1)}, u32[]{:S(2)}, u32[]{:S(2)}) %collective-permute-start.4) | collective-permute-done | bytes 524320 | tf_op jit(solution)/shard_map/ppermute | solution.py:128
  86.1 12.3 %collective-permute-done.5 = bf16[4,2,64,512]{3,2,1,0:T(8,128)(2,1)S(1)} collective-permute-done((bf16[4,2,64,512]{3,2,1,0:T(8,128)(2,1)S(1)}, bf16[4,2,64,512]{3,2,1,0:T(8,128)(2,1)S(1)}, u32[]{:S(2)}, u32[]{:S(2)}) %collective-permute-start.5) | collective-permute-done | bytes 524320 | tf_op jit(solution)/shard_map/ppermute | solution.py:128
  100.4 12.9 %collective-permute-done.16 = bf16[4,2,64,512]{3,2,1,0:T(8,128)(2,1)S(1)} collective-permute-done((bf16[4,2,64,512]{3,2,1,0:T(8,128)(2,1)S(1)}, bf16[4,2,64,512]{3,2,1,0:T(8,128)(2,1)S(1)}, u32[]{:S(2)}, u32[]{:S(2)}) %collective-permute-start.16) | collective-permute-done | bytes 524320 | tf_op jit(solution)/shard_map/ppermute | solution.py:128
  113.3 11.5 %collective-permute-start.21 = (bf16[4,2,64,512]{3,2,1,0:T(8,128)(2,1)S(1)}, bf16[4,2,64,512]{3,2,1,0:T(8,128)(2,1)S(1)}, u32[]{:S(2)}, u32[]{:S(2)}) collective-permute-start(bf16[4,2,64,512]{3,2,1,0:T(8,128)(2,1)S(1)} %bitcast.74), channel_id=1, source_target_pairs={{16,6},{17,7},{18,4},{19,5},{20,2},{21,3},{22,0},{23,1},{24,14},{2... | collective-permute-start | bytes 1572872 | tf_op jit(solution)/shard_map/ppermute | solution.py:128
  124.8 9.3 %collective-permute-done.17 = bf16[4,2,64,512]{3,2,1,0:T(8,128)(2,1)S(1)} collective-permute-done((bf16[4,2,64,512]{3,2,1,0:T(8,128)(2,1)S(1)}, bf16[4,2,64,512]{3,2,1,0:T(8,128)(2,1)S(1)}, u32[]{:S(2)}, u32[]{:S(2)}) %collective-permute-start.17) | collective-permute-done | bytes 524320 | tf_op jit(solution)/shard_map/ppermute | solution.py:128
  134.1 14.8 %collective-permute-start.22 = (bf16[4,2,64,512]{3,2,1,0:T(8,128)(2,1)S(1)}, bf16[4,2,64,512]{3,2,1,0:T(8,128)(2,1)S(1)}, u32[]{:S(2)}, u32[]{:S(2)}) collective-permute-start(bf16[4,2,64,512]{3,2,1,0:T(8,128)(2,1)S(1)} %bitcast.70), channel_id=1, source_target_pairs={{16,7},{17,6},{18,5},{19,4},{20,3},{21,2},{22,1},{23,0},{24,15},{2... | collective-permute-start | bytes 1572872 | tf_op jit(solution)/shard_map/ppermute | solution.py:128
  148.9 8.7 %collective-permute-done.18 = bf16[4,2,64,512]{3,2,1,0:T(8,128)(2,1)S(1)} collective-permute-done((bf16[4,2,64,512]{3,2,1,0:T(8,128)(2,1)S(1)}, bf16[4,2,64,512]{3,2,1,0:T(8,128)(2,1)S(1)}, u32[]{:S(2)}, u32[]{:S(2)}) %collective-permute-start.18) | collective-permute-done | bytes 524320 | tf_op jit(solution)/shard_map/ppermute | solution.py:128
  159.6 9.1 %collective-permute-start.9 = (bf16[4,2,64,512]{3,2,1,0:T(8,128)(2,1)S(1)}, bf16[4,2,64,512]{3,2,1,0:T(8,128)(2,1)S(1)}, u32[]{:S(2)}, u32[]{:S(2)}) collective-permute-start(bf16[4,2,64,512]{3,2,1,0:T(8,128)(2,1)S(1)} %bitcast.87), channel_id=1, source_target_pairs={{8,2},{9,3},{10,0},{11,1},{12,6},{13,7},{14,4},{15,5},{16,10},{17,... | collective-permute-start | bytes 1572872 | tf_op jit(solution)/shard_map/ppermute | solution.py:128
  170.8 10.1 %collective-permute-start.11 = (bf16[4,2,64,512]{3,2,1,0:T(8,128)(2,1)S(1)}, bf16[4,2,64,512]{3,2,1,0:T(8,128)(2,1)S(1)}, u32[]{:S(2)}, u32[]{:S(2)}) collective-permute-start(bf16[4,2,64,512]{3,2,1,0:T(8,128)(2,1)S(1)} %bitcast.81), channel_id=1, source_target_pairs={{8,4},{9,5},{10,6},{11,7},{12,0},{13,1},{14,2},{15,3},{16,12},{17,... | collective-permute-start | bytes 1572872 | tf_op jit(solution)/shard_map/ppermute | solution.py:128
  183.0 6.3 %collective-permute-start.6 = (bf16[4,2,64,512]{3,2,1,0:T(8,128)(2,1)S(1)}, bf16[4,2,64,512]{3,2,1,0:T(8,128)(2,1)S(1)}, u32[]{:S(2)}, u32[]{:S(2)}) collective-permute-start(bf16[4,2,64,512]{3,2,1,0:T(8,128)(2,1)S(1)} %bitcast.71), channel_id=1, source_target_pairs={{0,7},{1,6},{2,5},{3,4},{4,3},{5,2},{6,1},{7,0},{8,15},{9,14},{10,... | collective-permute-start | bytes 1572872 | tf_op jit(solution)/shard_map/ppermute | solution.py:128
  189.4 3.2 %collective-permute-start.13 = (bf16[4,2,64,512]{3,2,1,0:T(8,128)(2,1)S(1)}, bf16[4,2,64,512]{3,2,1,0:T(8,128)(2,1)S(1)}, u32[]{:S(2)}, u32[]{:S(2)}) collective-permute-start(bf16[4,2,64,512]{3,2,1,0:T(8,128)(2,1)S(1)} %bitcast.75), channel_id=1, source_target_pairs={{8,6},{9,7},{10,4},{11,5},{12,2},{13,3},{14,0},{15,1},{16,14},{17,... | collective-permute-start | bytes 1572872 | tf_op jit(solution)/shard_map/ppermute | solution.py:128
  194.4 26.1 %collective-permute-start.14 = (bf16[4,2,64,512]{3,2,1,0:T(8,128)(2,1)S(1)}, bf16[4,2,64,512]{3,2,1,0:T(8,128)(2,1)S(1)}, u32[]{:S(2)}, u32[]{:S(2)}) collective-permute-start(bf16[4,2,64,512]{3,2,1,0:T(8,128)(2,1)S(1)} %bitcast.72), channel_id=1, source_target_pairs={{8,7},{9,6},{10,5},{11,4},{12,3},{13,2},{14,1},{15,0},{16,15},{17,... | collective-permute-start | bytes 1572872 | tf_op jit(solution)/shard_map/ppermute | solution.py:128
  220.6 6.4 %collective-permute-done.12 = bf16[4,2,64,512]{3,2,1,0:T(8,128)(2,1)S(1)} collective-permute-done((bf16[4,2,64,512]{3,2,1,0:T(8,128)(2,1)S(1)}, bf16[4,2,64,512]{3,2,1,0:T(8,128)(2,1)S(1)}, u32[]{:S(2)}, u32[]{:S(2)}) %collective-permute-start.12) | collective-permute-done | bytes 524320 | tf_op jit(solution)/shard_map/ppermute | solution.py:128
  228.6 5.1 %collective-permute-done.13 = bf16[4,2,64,512]{3,2,1,0:T(8,128)(2,1)S(1)} collective-permute-done((bf16[4,2,64,512]{3,2,1,0:T(8,128)(2,1)S(1)}, bf16[4,2,64,512]{3,2,1,0:T(8,128)(2,1)S(1)}, u32[]{:S(2)}, u32[]{:S(2)}) %collective-permute-start.13) | collective-permute-done | bytes 524320 | tf_op jit(solution)/shard_map/ppermute | solution.py:128
  233.8 5.6 %collective-permute-done.14 = bf16[4,2,64,512]{3,2,1,0:T(8,128)(2,1)S(1)} collective-permute-done((bf16[4,2,64,512]{3,2,1,0:T(8,128)(2,1)S(1)}, bf16[4,2,64,512]{3,2,1,0:T(8,128)(2,1)S(1)}, u32[]{:S(2)}, u32[]{:S(2)}) %collective-permute-start.14) | collective-permute-done | bytes 524320 | tf_op jit(solution)/shard_map/ppermute | solution.py:128
  241.7 2.4 slice_negate_fusion.2
  245.0 10.6 %fusion.26 = bf16[1,4,512,1024]{3,2,1,0:T(8,128)(2,1)} fusion(bf16[4,2,512,512]{3,2,1,0:T(8,128)(2,1)} %copy-done.1, bf16[4,1,512,512]{3,2,1,0:T(8,128)(2,1)} %get-tuple-element.10, bf16[4,1,512,512]{3,2,1,0:T(8,128)(2,1)S(1)} %get-tuple-element.9, bf16[4,2,512,512]{3,2,1,0:T(8,128)(2,1)} %copy-done, bf16[]{:T(256)} %bitcast.22), kind=kOutput, calls=%fused_computation.30 | convolution fusion | flops 4326424576 | bytes 16777218 | tf_op jit(solution)/shard_map/fpsi,fpsj->fij/dot_general | solution.py:102
  255.6 9.4 %fusion.24 = bf16[1,4,512,1024]{3,2,1,0:T(8,128)(2,1)} fusion(bf16[4,2,512,512]{3,2,1,0:T(8,128)(2,1)} %copy-done.1, bf16[4,1,512,512]{3,2,1,0:T(8,128)(2,1)} %get-tuple-element.8, bf16[4,1,512,512]{3,2,1,0:T(8,128)(2,1)} %get-tuple-element.7, bf16[4,2,512,512]{3,2,1,0:T(8,128)(2,1)S(1)} %constant_dynamic-update-slice_fusion.8, bf16[]{:T(256)} %bitcast.18), kind=kOutput, calls=%fused_computation.28 | convolution fusion | flops 4326424576 | bytes 16777218 | tf_op jit(solution)/shard_map/fpsi,fpsj->fij/dot_general | solution.py:102
  264.9 10.7 %fusion.22 = bf16[1,4,512,1024]{3,2,1,0:T(8,128)(2,1)} fusion(bf16[4,2,512,512]{3,2,1,0:T(8,128)(2,1)} %copy-done.1, bf16[4,1,512,512]{3,2,1,0:T(8,128)(2,1)} %get-tuple-element.6, bf16[4,1,512,512]{3,2,1,0:T(8,128)(2,1)S(1)} %copy-done.3, bf16[]{:T(256)} %bitcast.14), kind=kOutput, calls=%fused_computation.26 | convolution fusion | flops 4326424576 | bytes 12582914 | tf_op jit(solution)/shard_map/fpsi,fpsj->fij/dot_general | solution.py:102
  275.6 9.0 %pad_maximum_fusion = bf16[3,4,512,1024]{3,2,1,0:T(8,128)(2,1)} fusion(bf16[1,4,512,1024]{3,2,1,0:T(8,128)(2,1)S(1)} %copy-done.2, bf16[1,4,512,1024]{3,2,1,0:T(8,128)(2,1)} %fusion.24, bf16[1,4,512,1024]{3,2,1,0:T(8,128)(2,1)} %fusion.22), kind=kLoop, calls=%fused_computation | loop fusion | flops 12582912 | bytes 25165824 | tf_op jit(solution)/shard_map/stack | solution.py:144
  (70 shorter events, 29.6 us)
Async XLA Ops:
  35.6 16.5 %collective-permute-start.15 = (bf16[4,2,64,512]{3,2,1,0:T(8,128)(2,1)S(1)}, bf16[4,2,64,512]{3,2,1,0:T(8,128)(2,1)S(1)}, u32[]{:S(2)}, u32[]{:S(2)}) collective-permute-start(bf16[4,2,64,512]{3,2,1,0:T(8,128)(2,1)S(1)} %bitcast.91), channel_id=1, source_target_pairs={{16,0},{17,1},{18,2},{19,3},{20,4},{21,5},{22,6},{23,7},{24,8},{25... | collective-permute-start | bytes 1572872 | tf_op jit(solution)/shard_map/ppermute | solution.py:128
  38.1 18.1 %collective-permute-start.7 = (bf16[4,2,64,512]{3,2,1,0:T(8,128)(2,1)S(1)}, bf16[4,2,64,512]{3,2,1,0:T(8,128)(2,1)S(1)}, u32[]{:S(2)}, u32[]{:S(2)}) collective-permute-start(bf16[4,2,64,512]{3,2,1,0:T(8,128)(2,1)S(1)} %bitcast.92), channel_id=1, source_target_pairs={{8,0},{9,1},{10,2},{11,3},{12,4},{13,5},{14,6},{15,7},{16,8},{17,9... | collective-permute-start | bytes 1572872 | tf_op jit(solution)/shard_map/ppermute | solution.py:128
  40.4 20.7 %collective-permute-start = (bf16[4,2,64,512]{3,2,1,0:T(8,128)(2,1)S(1)}, bf16[4,2,64,512]{3,2,1,0:T(8,128)(2,1)S(1)}, u32[]{:S(2)}, u32[]{:S(2)}) collective-permute-start(bf16[4,2,64,512]{3,2,1,0:T(8,128)(2,1)S(1)} %bitcast.88), channel_id=1, source_target_pairs={{0,1},{1,0},{2,3},{3,2},{4,5},{5,4},{6,7},{7,6},{8,9},{9,8},{10,11... | collective-permute-start | bytes 1572872 | tf_op jit(solution)/shard_map/ppermute | solution.py:128
  42.2 26.5 %collective-permute-start.1 = (bf16[4,2,64,512]{3,2,1,0:T(8,128)(2,1)S(1)}, bf16[4,2,64,512]{3,2,1,0:T(8,128)(2,1)S(1)}, u32[]{:S(2)}, u32[]{:S(2)}) collective-permute-start(bf16[4,2,64,512]{3,2,1,0:T(8,128)(2,1)S(1)} %bitcast.85), channel_id=1, source_target_pairs={{0,2},{1,3},{2,0},{3,1},{4,6},{5,7},{6,4},{7,5},{8,10},{9,11},{10,... | collective-permute-start | bytes 1572872 | tf_op jit(solution)/shard_map/ppermute | solution.py:128
  45.7 26.3 %collective-permute-start.2 = (bf16[4,2,64,512]{3,2,1,0:T(8,128)(2,1)S(1)}, bf16[4,2,64,512]{3,2,1,0:T(8,128)(2,1)S(1)}, u32[]{:S(2)}, u32[]{:S(2)}) collective-permute-start(bf16[4,2,64,512]{3,2,1,0:T(8,128)(2,1)S(1)} %bitcast.82), channel_id=1, source_target_pairs={{0,3},{1,2},{2,1},{3,0},{4,7},{5,6},{6,5},{7,4},{8,11},{9,10},{10,... | collective-permute-start | bytes 1572872 | tf_op jit(solution)/shard_map/ppermute | solution.py:128
  52.1 22.3 %collective-permute-start.3 = (bf16[4,2,64,512]{3,2,1,0:T(8,128)(2,1)S(1)}, bf16[4,2,64,512]{3,2,1,0:T(8,128)(2,1)S(1)}, u32[]{:S(2)}, u32[]{:S(2)}) collective-permute-start(bf16[4,2,64,512]{3,2,1,0:T(8,128)(2,1)S(1)} %bitcast.79), channel_id=1, source_target_pairs={{0,4},{1,5},{2,6},{3,7},{4,0},{5,1},{6,2},{7,3},{8,12},{9,13},{10,... | collective-permute-start | bytes 1572872 | tf_op jit(solution)/shard_map/ppermute | solution.py:128
  56.2 27.9 %collective-permute-start.4 = (bf16[4,2,64,512]{3,2,1,0:T(8,128)(2,1)S(1)}, bf16[4,2,64,512]{3,2,1,0:T(8,128)(2,1)S(1)}, u32[]{:S(2)}, u32[]{:S(2)}) collective-permute-start(bf16[4,2,64,512]{3,2,1,0:T(8,128)(2,1)S(1)} %bitcast.76), channel_id=1, source_target_pairs={{0,5},{1,4},{2,7},{3,6},{4,1},{5,0},{6,3},{7,2},{8,13},{9,12},{10,... | collective-permute-start | bytes 1572872 | tf_op jit(solution)/shard_map/ppermute | solution.py:128
  61.1 37.3 %collective-permute-start.5 = (bf16[4,2,64,512]{3,2,1,0:T(8,128)(2,1)S(1)}, bf16[4,2,64,512]{3,2,1,0:T(8,128)(2,1)S(1)}, u32[]{:S(2)}, u32[]{:S(2)}) collective-permute-start(bf16[4,2,64,512]{3,2,1,0:T(8,128)(2,1)S(1)} %bitcast.73), channel_id=1, source_target_pairs={{0,6},{1,7},{2,4},{3,5},{4,2},{5,3},{6,0},{7,1},{8,14},{9,15},{10,... | collective-permute-start | bytes 1572872 | tf_op jit(solution)/shard_map/ppermute | solution.py:128
  68.8 44.5 %collective-permute-start.16 = (bf16[4,2,64,512]{3,2,1,0:T(8,128)(2,1)S(1)}, bf16[4,2,64,512]{3,2,1,0:T(8,128)(2,1)S(1)}, u32[]{:S(2)}, u32[]{:S(2)}) collective-permute-start(bf16[4,2,64,512]{3,2,1,0:T(8,128)(2,1)S(1)} %bitcast.89), channel_id=1, source_target_pairs={{16,1},{17,0},{18,3},{19,2},{20,5},{21,4},{22,7},{23,6},{24,9},{25... | collective-permute-start | bytes 1572872 | tf_op jit(solution)/shard_map/ppermute | solution.py:128
  72.0 62.1 %collective-permute-start.17 = (bf16[4,2,64,512]{3,2,1,0:T(8,128)(2,1)S(1)}, bf16[4,2,64,512]{3,2,1,0:T(8,128)(2,1)S(1)}, u32[]{:S(2)}, u32[]{:S(2)}) collective-permute-start(bf16[4,2,64,512]{3,2,1,0:T(8,128)(2,1)S(1)} %bitcast.86), channel_id=1, source_target_pairs={{16,2},{17,3},{18,0},{19,1},{20,6},{21,7},{22,4},{23,5},{24,10},{2... | collective-permute-start | bytes 1572872 | tf_op jit(solution)/shard_map/ppermute | solution.py:128
  74.4 83.3 %collective-permute-start.18 = (bf16[4,2,64,512]{3,2,1,0:T(8,128)(2,1)S(1)}, bf16[4,2,64,512]{3,2,1,0:T(8,128)(2,1)S(1)}, u32[]{:S(2)}, u32[]{:S(2)}) collective-permute-start(bf16[4,2,64,512]{3,2,1,0:T(8,128)(2,1)S(1)} %bitcast.83), channel_id=1, source_target_pairs={{16,3},{17,2},{18,1},{19,0},{20,7},{21,6},{22,5},{23,4},{24,11},{2... | collective-permute-start | bytes 1572872 | tf_op jit(solution)/shard_map/ppermute | solution.py:128
  84.1 75.5 %collective-permute-start.19 = (bf16[4,2,64,512]{3,2,1,0:T(8,128)(2,1)S(1)}, bf16[4,2,64,512]{3,2,1,0:T(8,128)(2,1)S(1)}, u32[]{:S(2)}, u32[]{:S(2)}) collective-permute-start(bf16[4,2,64,512]{3,2,1,0:T(8,128)(2,1)S(1)} %bitcast.80), channel_id=1, source_target_pairs={{16,4},{17,5},{18,6},{19,7},{20,0},{21,1},{22,2},{23,3},{24,12},{2... | collective-permute-start | bytes 1572872 | tf_op jit(solution)/shard_map/ppermute | solution.py:128
  98.4 70.5 %collective-permute-start.20 = (bf16[4,2,64,512]{3,2,1,0:T(8,128)(2,1)S(1)}, bf16[4,2,64,512]{3,2,1,0:T(8,128)(2,1)S(1)}, u32[]{:S(2)}, u32[]{:S(2)}) collective-permute-start(bf16[4,2,64,512]{3,2,1,0:T(8,128)(2,1)S(1)} %bitcast.77), channel_id=1, source_target_pairs={{16,5},{17,4},{18,7},{19,6},{20,1},{21,0},{22,3},{23,2},{24,13},{2... | collective-permute-start | bytes 1572872 | tf_op jit(solution)/shard_map/ppermute | solution.py:128
  113.3 57.6 %collective-permute-start.21 = (bf16[4,2,64,512]{3,2,1,0:T(8,128)(2,1)S(1)}, bf16[4,2,64,512]{3,2,1,0:T(8,128)(2,1)S(1)}, u32[]{:S(2)}, u32[]{:S(2)}) collective-permute-start(bf16[4,2,64,512]{3,2,1,0:T(8,128)(2,1)S(1)} %bitcast.74), channel_id=1, source_target_pairs={{16,6},{17,7},{18,4},{19,5},{20,2},{21,3},{22,0},{23,1},{24,14},{2... | collective-permute-start | bytes 1572872 | tf_op jit(solution)/shard_map/ppermute | solution.py:128
  134.1 46.9 %collective-permute-start.22 = (bf16[4,2,64,512]{3,2,1,0:T(8,128)(2,1)S(1)}, bf16[4,2,64,512]{3,2,1,0:T(8,128)(2,1)S(1)}, u32[]{:S(2)}, u32[]{:S(2)}) collective-permute-start(bf16[4,2,64,512]{3,2,1,0:T(8,128)(2,1)S(1)} %bitcast.70), channel_id=1, source_target_pairs={{16,7},{17,6},{18,5},{19,4},{20,3},{21,2},{22,1},{23,0},{24,15},{2... | collective-permute-start | bytes 1572872 | tf_op jit(solution)/shard_map/ppermute | solution.py:128
  157.7 25.4 %collective-permute-start.8 = (bf16[4,2,64,512]{3,2,1,0:T(8,128)(2,1)S(1)}, bf16[4,2,64,512]{3,2,1,0:T(8,128)(2,1)S(1)}, u32[]{:S(2)}, u32[]{:S(2)}) collective-permute-start(bf16[4,2,64,512]{3,2,1,0:T(8,128)(2,1)S(1)} %bitcast.90), channel_id=1, source_target_pairs={{8,1},{9,0},{10,3},{11,2},{12,5},{13,4},{14,7},{15,6},{16,9},{17,8... | collective-permute-start | bytes 1572872 | tf_op jit(solution)/shard_map/ppermute | solution.py:128
  159.6 29.8 %collective-permute-start.9 = (bf16[4,2,64,512]{3,2,1,0:T(8,128)(2,1)S(1)}, bf16[4,2,64,512]{3,2,1,0:T(8,128)(2,1)S(1)}, u32[]{:S(2)}, u32[]{:S(2)}) collective-permute-start(bf16[4,2,64,512]{3,2,1,0:T(8,128)(2,1)S(1)} %bitcast.87), channel_id=1, source_target_pairs={{8,2},{9,3},{10,0},{11,1},{12,6},{13,7},{14,4},{15,5},{16,10},{17,... | collective-permute-start | bytes 1572872 | tf_op jit(solution)/shard_map/ppermute | solution.py:128
  168.9 25.6 %collective-permute-start.10 = (bf16[4,2,64,512]{3,2,1,0:T(8,128)(2,1)S(1)}, bf16[4,2,64,512]{3,2,1,0:T(8,128)(2,1)S(1)}, u32[]{:S(2)}, u32[]{:S(2)}) collective-permute-start(bf16[4,2,64,512]{3,2,1,0:T(8,128)(2,1)S(1)} %bitcast.84), channel_id=1, source_target_pairs={{8,3},{9,2},{10,1},{11,0},{12,7},{13,6},{14,5},{15,4},{16,11},{17,... | collective-permute-start | bytes 1572872 | tf_op jit(solution)/shard_map/ppermute | solution.py:128
  170.8 49.7 %collective-permute-start.11 = (bf16[4,2,64,512]{3,2,1,0:T(8,128)(2,1)S(1)}, bf16[4,2,64,512]{3,2,1,0:T(8,128)(2,1)S(1)}, u32[]{:S(2)}, u32[]{:S(2)}) collective-permute-start(bf16[4,2,64,512]{3,2,1,0:T(8,128)(2,1)S(1)} %bitcast.81), channel_id=1, source_target_pairs={{8,4},{9,5},{10,6},{11,7},{12,0},{13,1},{14,2},{15,3},{16,12},{17,... | collective-permute-start | bytes 1572872 | tf_op jit(solution)/shard_map/ppermute | solution.py:128
  181.0 45.9 %collective-permute-start.12 = (bf16[4,2,64,512]{3,2,1,0:T(8,128)(2,1)S(1)}, bf16[4,2,64,512]{3,2,1,0:T(8,128)(2,1)S(1)}, u32[]{:S(2)}, u32[]{:S(2)}) collective-permute-start(bf16[4,2,64,512]{3,2,1,0:T(8,128)(2,1)S(1)} %bitcast.78), channel_id=1, source_target_pairs={{8,5},{9,4},{10,7},{11,6},{12,1},{13,0},{14,3},{15,2},{16,13},{17,... | collective-permute-start | bytes 1572872 | tf_op jit(solution)/shard_map/ppermute | solution.py:128
  183.0 45.6 %copy-start = (bf16[4,2,512,512]{3,2,1,0:T(8,128)(2,1)}, bf16[4,2,512,512]{3,2,1,0:T(8,128)(2,1)S(1)}, u32[]{:S(2)}) copy-start(bf16[4,2,512,512]{3,2,1,0:T(8,128)(2,1)S(1)} %constant_dynamic-update-slice_fusion.16) | copy-start | bytes 12582916
  183.0 58.6 %collective-permute-start.6 = (bf16[4,2,64,512]{3,2,1,0:T(8,128)(2,1)S(1)}, bf16[4,2,64,512]{3,2,1,0:T(8,128)(2,1)S(1)}, u32[]{:S(2)}, u32[]{:S(2)}) collective-permute-start(bf16[4,2,64,512]{3,2,1,0:T(8,128)(2,1)S(1)} %bitcast.71), channel_id=1, source_target_pairs={{0,7},{1,6},{2,5},{3,4},{4,3},{5,2},{6,1},{7,0},{8,15},{9,14},{10,... | collective-permute-start | bytes 1572872 | tf_op jit(solution)/shard_map/ppermute | solution.py:128
  189.4 44.3 %collective-permute-start.13 = (bf16[4,2,64,512]{3,2,1,0:T(8,128)(2,1)S(1)}, bf16[4,2,64,512]{3,2,1,0:T(8,128)(2,1)S(1)}, u32[]{:S(2)}, u32[]{:S(2)}) collective-permute-start(bf16[4,2,64,512]{3,2,1,0:T(8,128)(2,1)S(1)} %bitcast.75), channel_id=1, source_target_pairs={{8,6},{9,7},{10,4},{11,5},{12,2},{13,3},{14,0},{15,1},{16,14},{17,... | collective-permute-start | bytes 1572872 | tf_op jit(solution)/shard_map/ppermute | solution.py:128
  194.4 44.9 %collective-permute-start.14 = (bf16[4,2,64,512]{3,2,1,0:T(8,128)(2,1)S(1)}, bf16[4,2,64,512]{3,2,1,0:T(8,128)(2,1)S(1)}, u32[]{:S(2)}, u32[]{:S(2)}) collective-permute-start(bf16[4,2,64,512]{3,2,1,0:T(8,128)(2,1)S(1)} %bitcast.72), channel_id=1, source_target_pairs={{8,7},{9,6},{10,5},{11,4},{12,3},{13,2},{14,1},{15,0},{16,15},{17,... | collective-permute-start | bytes 1572872 | tf_op jit(solution)/shard_map/ppermute | solution.py:128
  241.7 3.3 %copy-start.1 = (bf16[4,2,512,512]{3,2,1,0:T(8,128)(2,1)}, bf16[4,2,512,512]{3,2,1,0:T(8,128)(2,1)S(1)}, u32[]{:S(2)}) copy-start(bf16[4,2,512,512]{3,2,1,0:T(8,128)(2,1)S(1)} %constant_dynamic-update-slice_fusion) | copy-start | bytes 12582916
  255.6 9.4 %copy-start.3 = (bf16[4,1,512,512]{3,2,1,0:T(8,128)(2,1)S(1)}, bf16[4,1,512,512]{3,2,1,0:T(8,128)(2,1)}, u32[]{:S(2)}) copy-start(bf16[4,1,512,512]{3,2,1,0:T(8,128)(2,1)} %get-tuple-element.5) | copy-start | bytes 6291460
  264.9 10.7 %copy-start.2 = (bf16[1,4,512,1024]{3,2,1,0:T(8,128)(2,1)S(1)}, bf16[1,4,512,1024]{3,2,1,0:T(8,128)(2,1)}, u32[]{:S(2)}) copy-start(bf16[1,4,512,1024]{3,2,1,0:T(8,128)(2,1)} %fusion.26) | copy-start | bytes 12582916

commit v4 on v2

--- a/solution.py
+++ b/solution.py
@@ -10,6 +10,7 @@
 SEG_LEN = 256
 BINS = 32
 FIRST_BIN = 2
+BAND = 2
 
 
 EPS_POWER = 1e-06
@@ -105,17 +106,34 @@
     return results
 
 
+def neighbour_panels(own_panel):
+    n_chan = lax.axis_size("chan")
+    second_panel = from_behind(own_panel, "chan", -2)
+    from_sibling = lax.ppermute(own_panel, "chan", [(c + 1, c) for c in range(0, n_chan, 2)])
+    from_forward = lax.ppermute(second_panel, "chan", [(c - 1, c) for c in range(1, n_chan, 2)])
+    odd = lax.axis_index("chan") % 2 == 1
+    upper_panel = jnp.where(odd, from_forward, from_sibling)
+    return upper_panel, second_panel
+
+
 def shards(records, offsets, dead_mask, band_blocks):
     per_segment = whitened_spectra(records, offsets, dead_mask)
     seg_count, rows, channels = per_segment.shape
     whitened = per_segment.reshape(seg_count, BINS, 2, channels).transpose(1, 2, 0, 3)
-    own_panel = lax.all_to_all(whitened, "freq", split_axis=0, concat_axis=2, tiled=True)
-    upper_panel = from_behind(own_panel, "chan", -1)
-    second_panel = from_behind(own_panel, "chan", -2)
-    products = local_products(own_panel, [own_panel, upper_panel, second_panel])
+    n_freq = lax.axis_size("freq")
+    per_device = BINS // n_freq
+    chunks = 2
+    grouped = whitened.reshape(n_freq, chunks, per_device // chunks, 2, seg_count, channels)
+    chunk_products = []
+    for k in range(chunks):
+        part = grouped[:, k].reshape(BINS // chunks, 2, seg_count, channels)
+        own_panel = lax.all_to_all(part, "freq", split_axis=0, concat_axis=2, tiled=True)
+        upper_panel, second_panel = neighbour_panels(own_panel)
+        chunk_products.append(local_products(own_panel, [own_panel, upper_panel, second_panel]))
     band_limit = band_blocks[0]
     results = []
-    for offset_index, product in enumerate(products):
+    for offset_index in range(BAND + 1):
+        product = jnp.concatenate([p[offset_index] for p in chunk_products], axis=0)
         keep_flag = (offset_index <= band_limit).astype(jnp.bfloat16)
         results.append(product.astype(jnp.bfloat16) * keep_flag)
     return jnp.stack(results, axis=0)

time: 266 us -> 222 us (0.83)
  blocking collectives: 57.2 us -> 0 us
  starting transfers between devices: 4.69 us -> 22.7 us
  local copies, waits for them, and re-layouts: 14.7 us -> 25.9 us
  waiting for transfers between devices: 122 us -> 113 us
  other arithmetic: 22.7 us -> 14.9 us
    all_to_all x1 -> x0, blocking collectives: 57.2 us -> none  [shards(): lax.all_to_all(whitened, 'freq', split_axis=0, concat_axis=2, tiled=True)]
    ppermute x2, waiting for transfers between devices: 122 us -> 67.5 us  [from_behind(): return lax.ppermute(block, axis, route)]
    all_to_all x0 -> x2, waiting for transfers between devices: none -> 45.1 us  [shards(): lax.all_to_all(part, 'freq', split_axis=0, concat_axis=2, tiled=True)]
    all_to_all x0 -> x2, starting transfers between devices: none -> 10.4 us  [shards(): lax.all_to_all(part, 'freq', split_axis=0, concat_axis=2, tiled=True)]
    slice x0 -> x1, local copies, waits for them, and re-layouts: none -> 7.18 us  [shards(): part = grouped[:, k].reshape(BINS // chunks, 2, seg_count, channels)]
    unnamed x0 -> x4, local copies, waits for them, and re-layouts: none -> 6.58 us
    reshape x2 -> x1, local copies, waits for them, and re-layouts: 13.7 us -> 7.21 us  [shards(): per_segment.reshape(seg_count, BINS, 2, channels).transpose(1, 2, 0, 3)]
    ppermute x0 -> x4, starting transfers between devices: none -> 5.63 us  [the longest x2 3.04 us: neighbour_panels(): lax.ppermute(second_panel, 'chan', [(c - 1, c) for c in range(1, n_chan,...]
  transfers between devices with their start and end apart: 2 -> 8, of which waited for: 2 -> 4; matrix products, arithmetic and copies ran while one was open for 5% -> 14% of each run, Pallas kernels for 0% -> 0%
where the time goes in v4:
time: 222 us; the launch traced here: 220 us
  waiting for transfers between devices  113 us (51%)
  local copies, waits for them, and re-layouts  25.9 us (12%)
  matrix products  22.8 us (10%)
  starting transfers between devices  22.7 us (10%)
  Pallas kernels  20.4 us (9%)
  other arithmetic  14.9 us (7%)
    ppermute x2, waiting for transfers between devices, from_behind(): return lax.ppermute(block, axis, route)  67.5 us
    all_to_all x2, waiting for transfers between devices, shards(): lax.all_to_all(part, 'freq', split_axis=0, concat_axis=2, tiled=True)  45.1 us
    dot_general x6, matrix products, local_products(): jnp.einsum('fpsi,fpsj->fij', left_panel, both, preferred_element_type=jnp...  22.8 us
    pallas_call x1, Pallas kernels, whitened_spectra(): pl.pallas_call(functools.partial(spectra_kernel, seg_count, window), out_...  20.4 us
    all_to_all x2, starting transfers between devices, shards(): lax.all_to_all(part, 'freq', split_axis=0, concat_axis=2, tiled=True)  10.4 us
    reshape x1, local copies, waits for them, and re-layouts, shards(): per_segment.reshape(seg_count, BINS, 2, channels).transpose(1, 2, 0, 3)  7.21 us
    slice x1, local copies, waits for them, and re-layouts, shards(): part = grouped[:, k].reshape(BINS // chunks, 2, seg_count, channels)  7.18 us
    ppermute x2, starting transfers between devices, from_behind(): return lax.ppermute(block, axis, route)  6.67 us
  transfers between devices with their start and end apart: 8, of which 4 were waited for; matrix products, arithmetic and copies ran while one was open for 14% of the time, Pallas kernels for 0%

profile of v4, /device:TPU:34, one launch (start us, length us, event | category | flops | bytes accessed | tf_op | source)
XLA Modules:
  0.0 220.3 jit_solution(17976057783052525849)
XLA Ops:
  0.1 1.3 convert_element_type.64
  1.7 0.7 pad_convert_fusion.dft_ref
  2.3 20.4 %shard_map.46 = bf16[64,64,512]{2,1,0:T(8,128)(2,1)} custom-call(s32[64]{0:T(128)} %offs_ref.1, f32[64,384]{1,0:T(8,128)} %pad_convert_fusion.dft_ref, f32[1,512]{1,0:T(1,128)} %bitcast.87, bf16[8448,512]{1,0:T(8,128)(2,1)} %rec_hbm.1), custom_call_target="tpu_custom_call" | custom-call | flops 1610612736 | bytes 29360128 | tf_op jit(solution)/shard_map/pallas_call | solution.py:70
  22.8 7.2 %reshape.156 = bf16[64,32,2,512]{3,2,1,0:T(2,128)(2,1)} reshape(bf16[64,64,512]{2,1,0:T(8,128)(2,1)} %shard_map.46) | data formatting | bytes 8388608 | tf_op jit(solution)/shard_map/reshape | solution.py:122
  30.0 7.2 %fusion.86 = (bf16[8,1,2,2,64,512]{5,3,2,1,0,4:T(2,128)(2,1)}, bf16[8,1,2,2,64,512]{5,3,2,1,0,4:T(2,128)(2,1)S(1)}) fusion(bf16[8,2,2,2,64,512]{5,3,2,1,0,4:T(2,128)(2,1)} %bitcast.77), kind=kLoop, calls=%fused_computation.91 | loop fusion | bytes 8388608 | tf_op jit(solution)/shard_map/slice | solution.py:129
  37.2 2.5 %copy.34 = bf16[8,1,2,2,64,512]{5,4,3,2,0,1:T(8,128)(2,1)} copy(bf16[8,1,2,2,64,512]{5,3,2,1,0,4:T(2,128)(2,1)S(1)} %get-tuple-element.6) | data formatting | bytes 4194304
  39.7 5.6 %all-to-all-start.1 = ((bf16[16,2,64,512]{3,2,1,0:T(8,128)(2,1)}), bf16[16,2,64,512]{3,2,1,0:T(8,128)(2,1)S(1)}, u32[]{:S(2)}, u32[]{:S(2)}) async-start(bf16[16,2,64,512]{3,2,1,0:T(8,128)(2,1)} %bitcast.86), calls=%async_computation.1 | async-start | bytes 4194304 | tf_op jit(solution)/shard_map/all_to_all | solution.py:130
  45.3 4.1 %copy.33 = bf16[8,1,2,2,64,512]{5,4,3,2,0,1:T(8,128)(2,1)} copy(bf16[8,1,2,2,64,512]{5,3,2,1,0,4:T(2,128)(2,1)} %get-tuple-element.5) | data formatting | bytes 4194304
  49.4 22.3 %all-to-all-done.1 = bf16[16,2,64,512]{3,2,1,0:T(8,128)(2,1)S(1)} async-done(((bf16[16,2,64,512]{3,2,1,0:T(8,128)(2,1)}), bf16[16,2,64,512]{3,2,1,0:T(8,128)(2,1)S(1)}, u32[]{:S(2)}, u32[]{:S(2)}) %all-to-all-start.1) | async-done | bytes 2097184 | tf_op jit(solution)/shard_map/all_to_all | solution.py:130
  71.7 4.8 %all-to-all-start = ((bf16[16,2,64,512]{3,2,1,0:T(8,128)(2,1)}), bf16[16,2,64,512]{3,2,1,0:T(8,128)(2,1)}, u32[]{:S(2)}, u32[]{:S(2)}) async-start(bf16[16,2,64,512]{3,2,1,0:T(8,128)(2,1)} %bitcast.85), calls=%async_computation | async-start | bytes 4194304 | tf_op jit(solution)/shard_map/all_to_all | solution.py:130
  76.5 1.8 copy.15
  78.3 3.3 %collective-permute-start.3 = (bf16[2,2,512,512]{3,2,1,0:T(8,128)(2,1)S(1)}, bf16[2,2,512,512]{3,2,1,0:T(8,128)(2,1)}, u32[]{:S(2)}, u32[]{:S(2)}) collective-permute-start(bf16[2,2,512,512]{3,2,1,0:T(8,128)(2,1)S(1)} %bitcast.78), channel_id=1, source_target_pairs={{16,0},{24,8},{32,16},{40,24},{48,32},{56,40},{64,48},{72,56},{80,... | collective-permute-start | bytes 6291464 | tf_op jit(solution)/shard_map/ppermute | solution.py:22
  81.7 22.7 %all-to-all-done = bf16[16,2,64,512]{3,2,1,0:T(8,128)(2,1)} async-done(((bf16[16,2,64,512]{3,2,1,0:T(8,128)(2,1)}), bf16[16,2,64,512]{3,2,1,0:T(8,128)(2,1)}, u32[]{:S(2)}, u32[]{:S(2)}) %all-to-all-start) | async-done | bytes 2097184 | tf_op jit(solution)/shard_map/all_to_all | solution.py:130
  104.4 3.1 %copy.12 = bf16[2,2,8,64,512]{4,3,2,1,0:T(8,128)(2,1)} copy(bf16[2,2,8,64,512]{4,3,1,0,2:T(8,128)(2,1)} %bitcast.5) | data formatting | bytes 4194304 | tf_op jit(solution)/shard_map/all_to_all | solution.py:130
  107.5 3.3 %collective-permute-start = (bf16[2,2,512,512]{3,2,1,0:T(8,128)(2,1)}, bf16[2,2,512,512]{3,2,1,0:T(8,128)(2,1)}, u32[]{:S(2)}, u32[]{:S(2)}) collective-permute-start(bf16[2,2,512,512]{3,2,1,0:T(8,128)(2,1)} %bitcast.6), channel_id=1, source_target_pairs={{16,0},{24,8},{32,16},{40,24},{48,32},{56,40},{64,48},{72,56},{80,... | collective-permute-start | bytes 6291464 | tf_op jit(solution)/shard_map/ppermute | solution.py:22
  111.6 1.3 collective-permute-start.5
  112.9 1.3 collective-permute-start.2
  114.3 1.7 slice_negate_fusion.5
  116.0 2.6 %fusion.57 = bf16[1,2,512,1024]{3,2,1,0:T(8,128)(2,1)S(1)} fusion(bf16[2,2,512,512]{3,2,1,0:T(8,128)(2,1)S(1)} %bitcast.81, bf16[2,1,512,512]{3,2,1,0:T(8,128)(2,1)S(1)} %get-tuple-element.10, bf16[2,1,512,512]{3,2,1,0:T(8,128)(2,1)S(1)} %get-tuple-element.9), kind=kOutput, calls=%fused_computation.55 | convolution fusion | flops 2162163712 | bytes 6291456 | tf_op jit(solution)/shard_map/fpsi,fpsj->fij/dot_general | solution.py:102
  118.6 4.6 %fusion.54 = bf16[1,2,512,1024]{3,2,1,0:T(8,128)(2,1)S(1)} fusion(bf16[2,2,512,512]{3,2,1,0:T(8,128)(2,1)} %bitcast.6, bf16[2,1,512,512]{3,2,1,0:T(8,128)(2,1)S(1)} %get-tuple-element.8, bf16[2,1,512,512]{3,2,1,0:T(8,128)(2,1)S(1)} %get-tuple-element.7), kind=kOutput, calls=%fused_computation.54 | convolution fusion | flops 2162163712 | bytes 6291456 | tf_op jit(solution)/shard_map/fpsi,fpsj->fij/dot_general | solution.py:102
  123.2 25.4 %collective-permute-done.3 = bf16[2,2,512,512]{3,2,1,0:T(8,128)(2,1)} collective-permute-done((bf16[2,2,512,512]{3,2,1,0:T(8,128)(2,1)S(1)}, bf16[2,2,512,512]{3,2,1,0:T(8,128)(2,1)}, u32[]{:S(2)}, u32[]{:S(2)}) %collective-permute-start.3) | collective-permute-done | bytes 2097184 | tf_op jit(solution)/shard_map/ppermute | solution.py:22
  148.6 1.4 collective-permute-start.4
  150.0 0.4 maximum_multiply_fusion
  150.4 42.2 %collective-permute-done = bf16[2,2,512,512]{3,2,1,0:T(8,128)(2,1)} collective-permute-done((bf16[2,2,512,512]{3,2,1,0:T(8,128)(2,1)}, bf16[2,2,512,512]{3,2,1,0:T(8,128)(2,1)}, u32[]{:S(2)}, u32[]{:S(2)}) %collective-permute-start) | collective-permute-done | bytes 2097184 | tf_op jit(solution)/shard_map/ppermute | solution.py:22
  192.6 1.6 collective-permute-start.1
  194.2 1.7 slice_negate_fusion
  195.9 1.7 slice_negate_fusion.1
  197.6 4.0 %fusion.69 = bf16[1,2,512,1024]{3,2,1,0:T(8,128)(2,1)S(1)} fusion(bf16[2,2,512,512]{3,2,1,0:T(8,128)(2,1)S(1)} %bitcast.82, bf16[2,1,512,512]{3,2,1,0:T(8,128)(2,1)S(1)} %get-tuple-element.18, bf16[2,1,512,512]{3,2,1,0:T(8,128)(2,1)S(1)} %get-tuple-element.17, bf16[2,2,512,512]{3,2,1,0:T(8,128)(2,1)} %collective-permute-done.3), kind=kOutput, calls=%fused_computation.59 | convolution fusion | flops 2162163712 | bytes 8388608 | tf_op jit(solution)/shard_map/fpsi,fpsj->fij/dot_general | solution.py:102
  201.5 4.6 %fusion.66 = bf16[1,2,512,1024]{3,2,1,0:T(8,128)(2,1)S(1)} fusion(bf16[2,2,512,512]{3,2,1,0:T(8,128)(2,1)} %bitcast.6, bf16[2,1,512,512]{3,2,1,0:T(8,128)(2,1)S(1)} %get-tuple-element.16, bf16[2,1,512,512]{3,2,1,0:T(8,128)(2,1)S(1)} %get-tuple-element.15, bf16[2,2,512,512]{3,2,1,0:T(8,128)(2,1)} %collective-permute-done), kind=kOutput, calls=%fused_computation.58 | convolution fusion | flops 2162163712 | bytes 8388608 | tf_op jit(solution)/shard_map/fpsi,fpsj->fij/dot_general | solution.py:102
  207.3 2.6 %fusion.63 = bf16[1,2,512,1024]{3,2,1,0:T(8,128)(2,1)S(1)} fusion(bf16[2,2,512,512]{3,2,1,0:T(8,128)(2,1)S(1)} %bitcast.83, bf16[2,1,512,512]{3,2,1,0:T(8,128)(2,1)S(1)} %get-tuple-element.14, bf16[2,1,512,512]{3,2,1,0:T(8,128)(2,1)S(1)} %get-tuple-element.13, bf16[2,2,512,512]{3,2,1,0:T(8,128)(2,1)S(1)} %broadcast_select_fusion), kind=kOutput, calls=%fused_computation.57 | convolution fusion | flops 2162163712 | bytes 8388608 | tf_op jit(solution)/shard_map/fpsi,fpsj->fij/dot_general | solution.py:102
  210.0 4.4 %fusion.60 = bf16[1,2,512,1024]{3,2,1,0:T(8,128)(2,1)S(1)} fusion(bf16[2,2,512,512]{3,2,1,0:T(8,128)(2,1)} %bitcast.6, bf16[2,1,512,512]{3,2,1,0:T(8,128)(2,1)S(1)} %get-tuple-element.12, bf16[2,1,512,512]{3,2,1,0:T(8,128)(2,1)S(1)} %get-tuple-element.11, bf16[2,2,512,512]{3,2,1,0:T(8,128)(2,1)S(1)} %broadcast_select_fusion.1), kind=kOutput, calls=%fused_computation.56 | convolution fusion | flops 2162163712 | bytes 8388608 | tf_op jit(solution)/shard_map/fpsi,fpsj->fij/dot_general | solution.py:102
  214.8 5.5 %pad_maximum_fusion = bf16[3,4,512,1024]{3,2,1,0:T(8,128)(2,1)} fusion(bf16[1,4,512,1024]{3,2,1,0:T(8,128)(2,1)S(1)} %maximum_multiply_fusion.2, bf16[1,4,512,1024]{3,2,1,0:T(8,128)(2,1)S(1)} %maximum_multiply_fusion.1, bf16[1,4,512,1024]{3,2,1,0:T(8,128)(2,1)S(1)} %maximum_multiply_fusion), kind=kLoop, calls=%fused_computation | loop fusion | flops 12582912 | bytes 25165824 | tf_op jit(solution)/shard_map/stack | solution.py:139
  (17 shorter events, 2.1 us)
Async XLA Ops:
  39.7 32.1 %all-to-all-start.1 = ((bf16[16,2,64,512]{3,2,1,0:T(8,128)(2,1)}), bf16[16,2,64,512]{3,2,1,0:T(8,128)(2,1)S(1)}, u32[]{:S(2)}, u32[]{:S(2)}) async-start(bf16[16,2,64,512]{3,2,1,0:T(8,128)(2,1)} %bitcast.86), calls=%async_computation.1 | async-start | bytes 4194304 | tf_op jit(solution)/shard_map/all_to_all | solution.py:130
  71.7 4.8 %copy-start = (bf16[16,2,64,512]{3,2,1,0:T(8,128)(2,1)}, bf16[16,2,64,512]{3,2,1,0:T(8,128)(2,1)S(1)}, u32[]{:S(2)}) copy-start(bf16[16,2,64,512]{3,2,1,0:T(8,128)(2,1)S(1)} %all-to-all-done.1) | copy-start | bytes 6291460
  71.7 32.7 %all-to-all-start = ((bf16[16,2,64,512]{3,2,1,0:T(8,128)(2,1)}), bf16[16,2,64,512]{3,2,1,0:T(8,128)(2,1)}, u32[]{:S(2)}, u32[]{:S(2)}) async-start(bf16[16,2,64,512]{3,2,1,0:T(8,128)(2,1)} %bitcast.85), calls=%async_computation | async-start | bytes 4194304 | tf_op jit(solution)/shard_map/all_to_all | solution.py:130
  78.3 70.3 %collective-permute-start.3 = (bf16[2,2,512,512]{3,2,1,0:T(8,128)(2,1)S(1)}, bf16[2,2,512,512]{3,2,1,0:T(8,128)(2,1)}, u32[]{:S(2)}, u32[]{:S(2)}) collective-permute-start(bf16[2,2,512,512]{3,2,1,0:T(8,128)(2,1)S(1)} %bitcast.78), channel_id=1, source_target_pairs={{16,0},{24,8},{32,16},{40,24},{48,32},{56,40},{64,48},{72,56},{80,... | collective-permute-start | bytes 6291464 | tf_op jit(solution)/shard_map/ppermute | solution.py:22
  107.5 85.0 %collective-permute-start = (bf16[2,2,512,512]{3,2,1,0:T(8,128)(2,1)}, bf16[2,2,512,512]{3,2,1,0:T(8,128)(2,1)}, u32[]{:S(2)}, u32[]{:S(2)}) collective-permute-start(bf16[2,2,512,512]{3,2,1,0:T(8,128)(2,1)} %bitcast.6), channel_id=1, source_target_pairs={{16,0},{24,8},{32,16},{40,24},{48,32},{56,40},{64,48},{72,56},{80,... | collective-permute-start | bytes 6291464 | tf_op jit(solution)/shard_map/ppermute | solution.py:22
  111.6 95.0 %collective-permute-start.5 = (bf16[2,2,512,512]{3,2,1,0:T(8,128)(2,1)S(1)}, bf16[2,2,512,512]{3,2,1,0:T(8,128)(2,1)S(1)}, u32[]{:S(2)}, u32[]{:S(2)}) collective-permute-start(bf16[2,2,512,512]{3,2,1,0:T(8,128)(2,1)S(1)} %bitcast.79), channel_id=1, source_target_pairs={{8,0},{24,16},{40,32},{56,48},{72,64},{88,80},{104,96},{120,112},{... | collective-permute-start | bytes 6291464 | tf_op jit(solution)/shard_map/ppermute | solution.py:112
  112.9 94.1 %collective-permute-start.2 = (bf16[2,2,512,512]{3,2,1,0:T(8,128)(2,1)}, bf16[2,2,512,512]{3,2,1,0:T(8,128)(2,1)S(1)}, u32[]{:S(2)}, u32[]{:S(2)}) collective-permute-start(bf16[2,2,512,512]{3,2,1,0:T(8,128)(2,1)} %bitcast.6), channel_id=1, source_target_pairs={{8,0},{24,16},{40,32},{56,48},{72,64},{88,80},{104,96},{120,112},{... | collective-permute-start | bytes 6291464 | tf_op jit(solution)/shard_map/ppermute | solution.py:112
  148.6 58.0 %collective-permute-start.4 = (bf16[2,2,512,512]{3,2,1,0:T(8,128)(2,1)}, bf16[2,2,512,512]{3,2,1,0:T(8,128)(2,1)S(1)}, u32[]{:S(2)}, u32[]{:S(2)}) collective-permute-start(bf16[2,2,512,512]{3,2,1,0:T(8,128)(2,1)} %collective-permute-done.3), channel_id=1, source_target_pairs={{0,8},{16,24},{32,40},{48,56},{64,72},{80,88},{96,104},{112,120},{... | collective-permute-start | bytes 6291464 | tf_op jit(solution)/shard_map/ppermute | solution.py:113
  192.6 14.4 %collective-permute-start.1 = (bf16[2,2,512,512]{3,2,1,0:T(8,128)(2,1)}, bf16[2,2,512,512]{3,2,1,0:T(8,128)(2,1)S(1)}, u32[]{:S(2)}, u32[]{:S(2)}) collective-permute-start(bf16[2,2,512,512]{3,2,1,0:T(8,128)(2,1)} %collective-permute-done), channel_id=1, source_target_pairs={{0,8},{16,24},{32,40},{48,56},{64,72},{80,88},{96,104},{112,120},{... | collective-permute-start | bytes 6291464 | tf_op jit(solution)/shard_map/ppermute | solution.py:113

commit v5 on v4

--- a/solution.py
+++ b/solution.py
@@ -122,7 +122,7 @@
     whitened = per_segment.reshape(seg_count, BINS, 2, channels).transpose(1, 2, 0, 3)
     n_freq = lax.axis_size("freq")
     per_device = BINS // n_freq
-    chunks = 2
+    chunks = 4
     grouped = whitened.reshape(n_freq, chunks, per_device // chunks, 2, seg_count, channels)
     chunk_products = []
     for k in range(chunks):

time: 222 us -> 219 us (0.986)
  blocking collectives: 0 us -> 60.1 us
  waiting for transfers between devices: 113 us -> 59.4 us
  local copies, waits for them, and re-layouts: 25.9 us -> 8.82 us
  other arithmetic: 14.9 us -> 20.1 us
  starting transfers between devices: 22.7 us -> 27.1 us
  matrix products: 22.8 us -> 20.2 us
    all_to_all x0 -> x3, blocking collectives: none -> 60.1 us  [shards(): lax.all_to_all(part, 'freq', split_axis=0, concat_axis=2, tiled=True)]
    all_to_all x2 -> x1, waiting for transfers between devices: 45.1 us -> 0.07 us  [shards(): lax.all_to_all(part, 'freq', split_axis=0, concat_axis=2, tiled=True)]
    ppermute x2 -> x4, waiting for transfers between devices: 67.5 us -> 59.1 us  [from_behind(): return lax.ppermute(block, axis, route)]
    slice x1 -> x0, local copies, waits for them, and re-layouts: 7.18 us -> none  [shards(): part = grouped[:, k].reshape(BINS // chunks, 2, seg_count, channels)]
    unnamed x4 -> x8, local copies, waits for them, and re-layouts: 6.58 us -> 0.02 us
    all_to_all x2 -> x1, starting transfers between devices: 10.4 us -> 4.44 us  [shards(): lax.all_to_all(part, 'freq', split_axis=0, concat_axis=2, tiled=True)]
    ppermute x2 -> x4, starting transfers between devices: 3.04 us -> 7.42 us  [neighbour_panels(): lax.ppermute(second_panel, 'chan', [(c - 1, c) for c in range(1, n_chan,...]
    ppermute x2 -> x4, starting transfers between devices: 6.67 us -> 10.1 us  [from_behind(): return lax.ppermute(block, axis, route)]
  transfers between devices with their start and end apart: 8 -> 13, of which waited for: 4 -> 6; matrix products, arithmetic and copies ran while one was open for 14% -> 14% of each run, Pallas kernels for 0% -> 0%
where the time goes in v5:
time: 219 us; the launch traced here: 217 us
  blocking collectives  60.1 us (27%)
  waiting for transfers between devices  59.4 us (27%)
  starting transfers between devices  27.1 us (12%)
  matrix products  20.2 us (9%)
  other arithmetic  20.1 us (9%)
  Pallas kernels  20 us (9%)
  local copies, waits for them, and re-layouts  8.82 us (4%)
    all_to_all x3, blocking collectives, shards(): lax.all_to_all(part, 'freq', split_axis=0, concat_axis=2, tiled=True)  60.1 us
    ppermute x4, waiting for transfers between devices, from_behind(): return lax.ppermute(block, axis, route)  59.1 us
    dot_general x12, matrix products, local_products(): jnp.einsum('fpsi,fpsj->fij', left_panel, both, preferred_element_type=jnp...  20.2 us
    pallas_call x1, Pallas kernels, whitened_spectra(): pl.pallas_call(functools.partial(spectra_kernel, seg_count, window), out_...  20 us
    ppermute x4, starting transfers between devices, from_behind(): return lax.ppermute(block, axis, route)  10.1 us
    neg x12, other arithmetic, local_products(): turned = jnp.stack([-right_panel[:, 1], right_panel[:, 0]], axis=1)  7.55 us
    ppermute x4, starting transfers between devices, neighbour_panels(): lax.ppermute(second_panel, 'chan', [(c - 1, c) for c in range(1, n_chan,...  7.42 us
    another operation x1, other arithmetic, shards(): return jnp.stack(results, axis=0)  5.46 us
  transfers between devices with their start and end apart: 13, of which 6 were waited for; matrix products, arithmetic and copies ran while one was open for 14% of the time, Pallas kernels for 0%

profile of v5, /device:TPU:34, one launch (start us, length us, event | category | flops | bytes accessed | tf_op | source)
XLA Modules:
  0.0 217.0 jit_solution(10657894884142970527)
XLA Ops:
  2.3 20.0 %shard_map.46 = bf16[64,64,512]{2,1,0:T(8,128)(2,1)} custom-call(s32[64]{0:T(128)} %offs_ref.1, f32[64,384]{1,0:T(8,128)} %pad_convert_fusion.dft_ref, f32[1,512]{1,0:T(1,128)} %bitcast.261, bf16[8448,512]{1,0:T(8,128)(2,1)} %rec_hbm.1), custom_call_target="tpu_custom_call" | custom-call | flops 1610612736 | bytes 29360128 | tf_op jit(solution)/shard_map/pallas_call | solution.py:70
  22.4 4.5 %copy.58 = bf16[64,64,512]{2,0,1:T(8,128)(2,1)S(1)} copy(bf16[64,64,512]{2,1,0:T(8,128)(2,1)} %shard_map.46) | data formatting | bytes 8388608 | tf_op jit(solution)/shard_map/reshape | solution.py:122
  26.9 1.5 slice_bitcast_fusion.3
  28.4 23.7 %all_to_all.72 = bf16[8,2,64,512]{3,2,1,0:T(8,128)(2,1)} all-to-all(bf16[8,2,64,512]{3,2,1,0:T(8,128)(2,1)S(1)} %get-tuple-element.6), channel_id=1, replica_groups=mesh['chan'=16,'freq'=8] {'freq'}, dimensions={0} | all-to-all | bytes 2097152 | tf_op jit(solution)/shard_map/all_to_all | solution.py:130
  52.1 18.5 %all_to_all.73 = bf16[8,2,64,512]{3,2,1,0:T(8,128)(2,1)S(1)} all-to-all(bf16[8,2,64,512]{3,2,1,0:T(8,128)(2,1)S(1)} %get-tuple-element.7), channel_id=1, replica_groups=mesh['chan'=16,'freq'=8] {'freq'}, dimensions={0} | all-to-all | bytes 2097152 | tf_op jit(solution)/shard_map/all_to_all | solution.py:130
  70.6 18.0 %all_to_all.74 = bf16[8,2,64,512]{3,2,1,0:T(8,128)(2,1)S(1)} all-to-all(bf16[8,2,64,512]{3,2,1,0:T(8,128)(2,1)S(1)} %get-tuple-element.8), channel_id=1, replica_groups=mesh['chan'=16,'freq'=8] {'freq'}, dimensions={0} | all-to-all | bytes 2097152 | tf_op jit(solution)/shard_map/all_to_all | solution.py:130
  88.5 4.4 %all-to-all-start = ((bf16[8,2,64,512]{3,2,1,0:T(8,128)(2,1)}), bf16[8,2,64,512]{3,2,1,0:T(8,128)(2,1)}, u32[]{:S(2)}, u32[]{:S(2)}) async-start(bf16[8,2,64,512]{3,2,1,0:T(8,128)(2,1)} %get-tuple-element.5), calls=%async_computation | async-start | bytes 2097152 | tf_op jit(solution)/shard_map/all_to_all | solution.py:130
  93.8 2.8 %collective-permute-start.3 = (bf16[1,2,512,512]{3,2,1,0:T(8,128)(2,1)S(1)}, bf16[1,2,512,512]{3,2,1,0:T(8,128)(2,1)}, u32[]{:S(2)}, u32[]{:S(2)}) collective-permute-start(bf16[1,2,512,512]{3,2,1,0:T(8,128)(2,1)S(1)} %bitcast.230), channel_id=1, source_target_pairs={{16,0},{24,8},{32,16},{40,24},{48,32},{56,40},{64,48},{72,56},{80,... | collective-permute-start | bytes 3145736 | tf_op jit(solution)/shard_map/ppermute | solution.py:22
  96.6 1.3 collective-permute-start.5
  98.0 2.6 %collective-permute-start.6 = (bf16[1,2,512,512]{3,2,1,0:T(8,128)(2,1)S(1)}, bf16[1,2,512,512]{3,2,1,0:T(8,128)(2,1)}, u32[]{:S(2)}, u32[]{:S(2)}) collective-permute-start(bf16[1,2,512,512]{3,2,1,0:T(8,128)(2,1)S(1)} %bitcast.237), channel_id=1, source_target_pairs={{16,0},{24,8},{32,16},{40,24},{48,32},{56,40},{64,48},{72,56},{80,... | collective-permute-start | bytes 3145736 | tf_op jit(solution)/shard_map/ppermute | solution.py:22
  100.6 1.3 collective-permute-start.8
  101.9 1.3 copy.35
  103.2 2.8 %collective-permute-start.9 = (bf16[1,2,512,512]{3,2,1,0:T(8,128)(2,1)S(1)}, bf16[1,2,512,512]{3,2,1,0:T(8,128)(2,1)}, u32[]{:S(2)}, u32[]{:S(2)}) collective-permute-start(bf16[1,2,512,512]{3,2,1,0:T(8,128)(2,1)S(1)} %bitcast.244), channel_id=1, source_target_pairs={{16,0},{24,8},{32,16},{40,24},{48,32},{56,40},{64,48},{72,56},{80,... | collective-permute-start | bytes 3145736 | tf_op jit(solution)/shard_map/ppermute | solution.py:22
  109.4 1.3 copy.26
  110.7 2.6 %fusion.73 = bf16[1,1,512,1024]{3,2,1,0:T(8,128)(2,1)S(1)} fusion(bf16[2,512,512]{2,1,0:T(8,128)(2,1)S(1)} %bitcast.233, bf16[1,1,512,512]{3,2,1,0:T(8,128)(2,1)} %get-tuple-element.12, bf16[1,1,512,512]{3,2,1,0:T(8,128)(2,1)} %get-tuple-element.11, bf16[1,2,512,512]{3,2,1,0:T(8,128)(2,1)S(1)} %bitcast.234), kind=kOutput, calls=%fused_computation.101 | convolution fusion | flops 1081081856 | bytes 4194304 | tf_op jit(solution)/shard_map/fpsi,fpsj->fij/dot_general | solution.py:102
  117.9 12.9 %collective-permute-done.3 = bf16[1,2,512,512]{3,2,1,0:T(8,128)(2,1)} collective-permute-done((bf16[1,2,512,512]{3,2,1,0:T(8,128)(2,1)S(1)}, bf16[1,2,512,512]{3,2,1,0:T(8,128)(2,1)}, u32[]{:S(2)}, u32[]{:S(2)}) %collective-permute-start.3) | collective-permute-done | bytes 1048608 | tf_op jit(solution)/shard_map/ppermute | solution.py:22
  133.3 19.9 %collective-permute-done.6 = bf16[1,2,512,512]{3,2,1,0:T(8,128)(2,1)} collective-permute-done((bf16[1,2,512,512]{3,2,1,0:T(8,128)(2,1)S(1)}, bf16[1,2,512,512]{3,2,1,0:T(8,128)(2,1)}, u32[]{:S(2)}, u32[]{:S(2)}) %collective-permute-start.6) | collective-permute-done | bytes 1048608 | tf_op jit(solution)/shard_map/ppermute | solution.py:22
  153.2 1.9 collective-permute-start
  156.4 2.5 %fusion.81 = bf16[1,1,512,1024]{3,2,1,0:T(8,128)(2,1)S(1)} fusion(bf16[2,512,512]{2,1,0:T(8,128)(2,1)S(1)} %bitcast.235, bf16[1,1,512,512]{3,2,1,0:T(8,128)(2,1)S(1)} %get-tuple-element.28, bf16[1,1,512,512]{3,2,1,0:T(8,128)(2,1)S(1)} %get-tuple-element.27, bf16[1,2,512,512]{3,2,1,0:T(8,128)(2,1)} %collective-permute-done.3), kind=kOutput, calls=%fused_computation.109 | convolution fusion | flops 1081081856 | bytes 4194304 | tf_op jit(solution)/shard_map/fpsi,fpsj->fij/dot_general | solution.py:102
  158.9 16.8 %collective-permute-done.9 = bf16[1,2,512,512]{3,2,1,0:T(8,128)(2,1)} collective-permute-done((bf16[1,2,512,512]{3,2,1,0:T(8,128)(2,1)S(1)}, bf16[1,2,512,512]{3,2,1,0:T(8,128)(2,1)}, u32[]{:S(2)}, u32[]{:S(2)}) %collective-permute-start.9) | collective-permute-done | bytes 1048608 | tf_op jit(solution)/shard_map/ppermute | solution.py:22
  175.7 1.3 collective-permute-start.4
  178.3 2.5 %fusion.82 = bf16[1,1,512,1024]{3,2,1,0:T(8,128)(2,1)S(1)} fusion(bf16[2,512,512]{2,1,0:T(8,128)(2,1)S(1)} %bitcast.242, bf16[1,1,512,512]{3,2,1,0:T(8,128)(2,1)S(1)} %get-tuple-element.30, bf16[1,1,512,512]{3,2,1,0:T(8,128)(2,1)S(1)} %get-tuple-element.29, bf16[1,2,512,512]{3,2,1,0:T(8,128)(2,1)} %collective-permute-done.6), kind=kOutput, calls=%fused_computation.110 | convolution fusion | flops 1081081856 | bytes 4194304 | tf_op jit(solution)/shard_map/fpsi,fpsj->fij/dot_general | solution.py:102
  180.8 2.5 %fusion.83 = bf16[1,1,512,1024]{3,2,1,0:T(8,128)(2,1)S(1)} fusion(bf16[2,512,512]{2,1,0:T(8,128)(2,1)S(1)} %bitcast.249, bf16[1,1,512,512]{3,2,1,0:T(8,128)(2,1)S(1)} %get-tuple-element.32, bf16[1,1,512,512]{3,2,1,0:T(8,128)(2,1)S(1)} %get-tuple-element.31, bf16[1,2,512,512]{3,2,1,0:T(8,128)(2,1)} %collective-permute-done.9), kind=kOutput, calls=%fused_computation.111 | convolution fusion | flops 1081081856 | bytes 4194304 | tf_op jit(solution)/shard_map/fpsi,fpsj->fij/dot_general | solution.py:102
  183.3 9.5 %collective-permute-done = bf16[1,2,512,512]{3,2,1,0:T(8,128)(2,1)S(1)} collective-permute-done((bf16[1,2,512,512]{3,2,1,0:T(8,128)(2,1)S(1)}, bf16[1,2,512,512]{3,2,1,0:T(8,128)(2,1)S(1)}, u32[]{:S(2)}, u32[]{:S(2)}) %collective-permute-start) | collective-permute-done | bytes 1048608 | tf_op jit(solution)/shard_map/ppermute | solution.py:22
  192.8 1.3 collective-permute-start.7
  196.1 1.3 collective-permute-start.2
  197.5 3.2 %collective-permute-start.10 = (bf16[1,2,512,512]{3,2,1,0:T(8,128)(2,1)}, bf16[1,2,512,512]{3,2,1,0:T(8,128)(2,1)S(1)}, u32[]{:S(2)}, u32[]{:S(2)}) collective-permute-start(bf16[1,2,512,512]{3,2,1,0:T(8,128)(2,1)} %collective-permute-done.9), channel_id=1, source_target_pairs={{0,8},{16,24},{32,40},{48,56},{64,72},{80,88},{96,104},{112,120},{... | collective-permute-start | bytes 3145736 | tf_op jit(solution)/shard_map/ppermute | solution.py:113
  200.6 1.3 broadcast_select_fusion.2
  202.0 1.6 collective-permute-start.1
  203.6 1.3 broadcast_select_fusion.1
  208.3 1.3 fusion.79
  211.5 5.5 %pad_maximum_fusion = bf16[3,4,512,1024]{3,2,1,0:T(8,128)(2,1)} fusion(bf16[1,4,512,1024]{3,2,1,0:T(8,128)(2,1)S(1)} %maximum_multiply_fusion.2, bf16[1,4,512,1024]{3,2,1,0:T(8,128)(2,1)S(1)} %maximum_multiply_fusion.1, bf16[1,4,512,1024]{3,2,1,0:T(8,128)(2,1)S(1)} %maximum_multiply_fusion), kind=kLoop, calls=%fused_computation | loop fusion | flops 12582912 | bytes 25165824 | tf_op jit(solution)/shard_map/stack | solution.py:139
  (50 shorter events, 22.7 us)
Async XLA Ops:
  88.5 20.8 %all-to-all-start = ((bf16[8,2,64,512]{3,2,1,0:T(8,128)(2,1)}), bf16[8,2,64,512]{3,2,1,0:T(8,128)(2,1)}, u32[]{:S(2)}, u32[]{:S(2)}) async-start(bf16[8,2,64,512]{3,2,1,0:T(8,128)(2,1)} %get-tuple-element.5), calls=%async_computation | async-start | bytes 2097152 | tf_op jit(solution)/shard_map/all_to_all | solution.py:130
  93.8 37.0 %collective-permute-start.3 = (bf16[1,2,512,512]{3,2,1,0:T(8,128)(2,1)S(1)}, bf16[1,2,512,512]{3,2,1,0:T(8,128)(2,1)}, u32[]{:S(2)}, u32[]{:S(2)}) collective-permute-start(bf16[1,2,512,512]{3,2,1,0:T(8,128)(2,1)S(1)} %bitcast.230), channel_id=1, source_target_pairs={{16,0},{24,8},{32,16},{40,24},{48,32},{56,40},{64,48},{72,56},{80,... | collective-permute-start | bytes 3145736 | tf_op jit(solution)/shard_map/ppermute | solution.py:22
  96.6 99.6 %collective-permute-start.5 = (bf16[1,2,512,512]{3,2,1,0:T(8,128)(2,1)S(1)}, bf16[1,2,512,512]{3,2,1,0:T(8,128)(2,1)}, u32[]{:S(2)}, u32[]{:S(2)}) collective-permute-start(bf16[1,2,512,512]{3,2,1,0:T(8,128)(2,1)S(1)} %bitcast.231), channel_id=1, source_target_pairs={{8,0},{24,16},{40,32},{56,48},{72,64},{88,80},{104,96},{120,112},{... | collective-permute-start | bytes 3145736 | tf_op jit(solution)/shard_map/ppermute | solution.py:112
  98.0 55.3 %collective-permute-start.6 = (bf16[1,2,512,512]{3,2,1,0:T(8,128)(2,1)S(1)}, bf16[1,2,512,512]{3,2,1,0:T(8,128)(2,1)}, u32[]{:S(2)}, u32[]{:S(2)}) collective-permute-start(bf16[1,2,512,512]{3,2,1,0:T(8,128)(2,1)S(1)} %bitcast.237), channel_id=1, source_target_pairs={{16,0},{24,8},{32,16},{40,24},{48,32},{56,40},{64,48},{72,56},{80,... | collective-permute-start | bytes 3145736 | tf_op jit(solution)/shard_map/ppermute | solution.py:22
  100.6 101.4 %collective-permute-start.8 = (bf16[1,2,512,512]{3,2,1,0:T(8,128)(2,1)S(1)}, bf16[1,2,512,512]{3,2,1,0:T(8,128)(2,1)}, u32[]{:S(2)}, u32[]{:S(2)}) collective-permute-start(bf16[1,2,512,512]{3,2,1,0:T(8,128)(2,1)S(1)} %bitcast.238), channel_id=1, source_target_pairs={{8,0},{24,16},{40,32},{56,48},{72,64},{88,80},{104,96},{120,112},{... | collective-permute-start | bytes 3145736 | tf_op jit(solution)/shard_map/ppermute | solution.py:112
  103.2 72.5 %collective-permute-start.9 = (bf16[1,2,512,512]{3,2,1,0:T(8,128)(2,1)S(1)}, bf16[1,2,512,512]{3,2,1,0:T(8,128)(2,1)}, u32[]{:S(2)}, u32[]{:S(2)}) collective-permute-start(bf16[1,2,512,512]{3,2,1,0:T(8,128)(2,1)S(1)} %bitcast.244), channel_id=1, source_target_pairs={{16,0},{24,8},{32,16},{40,24},{48,32},{56,40},{64,48},{72,56},{80,... | collective-permute-start | bytes 3145736 | tf_op jit(solution)/shard_map/ppermute | solution.py:22
  110.7 2.6 %copy-start.2 = (bf16[1,1,512,512]{3,2,1,0:T(8,128)(2,1)S(1)}, bf16[1,1,512,512]{3,2,1,0:T(8,128)(2,1)}, u32[]{:S(2)}) copy-start(bf16[1,1,512,512]{3,2,1,0:T(8,128)(2,1)} %get-tuple-element.13) | copy-start | bytes 1572868
  110.7 2.6 %copy-start.3 = (bf16[1,1,512,512]{3,2,1,0:T(8,128)(2,1)S(1)}, bf16[1,1,512,512]{3,2,1,0:T(8,128)(2,1)}, u32[]{:S(2)}) copy-start(bf16[1,1,512,512]{3,2,1,0:T(8,128)(2,1)} %get-tuple-element.14) | copy-start | bytes 1572868
  113.3 1.3 copy-start
  113.3 1.3 copy-start.1
  130.8 74.3 %collective-permute-start.11 = (bf16[1,2,512,512]{3,2,1,0:T(8,128)(2,1)S(1)}, bf16[1,2,512,512]{3,2,1,0:T(8,128)(2,1)S(1)}, u32[]{:S(2)}, u32[]{:S(2)}) collective-permute-start(bf16[1,2,512,512]{3,2,1,0:T(8,128)(2,1)S(1)} %bitcast.248), channel_id=1, source_target_pairs={{8,0},{24,16},{40,32},{56,48},{72,64},{88,80},{104,96},{120,112},{... | collective-permute-start | bytes 3145736 | tf_op jit(solution)/shard_map/ppermute | solution.py:112
  153.2 39.6 %collective-permute-start = (bf16[1,2,512,512]{3,2,1,0:T(8,128)(2,1)S(1)}, bf16[1,2,512,512]{3,2,1,0:T(8,128)(2,1)S(1)}, u32[]{:S(2)}, u32[]{:S(2)}) collective-permute-start(bf16[1,2,512,512]{3,2,1,0:T(8,128)(2,1)S(1)} %bitcast.254), channel_id=1, source_target_pairs={{16,0},{24,8},{32,16},{40,24},{48,32},{56,40},{64,48},{72,56},{80,... | collective-permute-start | bytes 3145736 | tf_op jit(solution)/shard_map/ppermute | solution.py:22
  175.7 21.7 %collective-permute-start.4 = (bf16[1,2,512,512]{3,2,1,0:T(8,128)(2,1)}, bf16[1,2,512,512]{3,2,1,0:T(8,128)(2,1)S(1)}, u32[]{:S(2)}, u32[]{:S(2)}) collective-permute-start(bf16[1,2,512,512]{3,2,1,0:T(8,128)(2,1)} %collective-permute-done.3), channel_id=1, source_target_pairs={{0,8},{16,24},{32,40},{48,56},{64,72},{80,88},{96,104},{112,120},{... | collective-permute-start | bytes 3145736 | tf_op jit(solution)/shard_map/ppermute | solution.py:113
  192.8 10.8 %collective-permute-start.7 = (bf16[1,2,512,512]{3,2,1,0:T(8,128)(2,1)}, bf16[1,2,512,512]{3,2,1,0:T(8,128)(2,1)S(1)}, u32[]{:S(2)}, u32[]{:S(2)}) collective-permute-start(bf16[1,2,512,512]{3,2,1,0:T(8,128)(2,1)} %collective-permute-done.6), channel_id=1, source_target_pairs={{0,8},{16,24},{32,40},{48,56},{64,72},{80,88},{96,104},{112,120},{... | collective-permute-start | bytes 3145736 | tf_op jit(solution)/shard_map/ppermute | solution.py:113
  196.1 9.2 %collective-permute-start.2 = (bf16[1,2,512,512]{3,2,1,0:T(8,128)(2,1)S(1)}, bf16[1,2,512,512]{3,2,1,0:T(8,128)(2,1)S(1)}, u32[]{:S(2)}, u32[]{:S(2)}) collective-permute-start(bf16[1,2,512,512]{3,2,1,0:T(8,128)(2,1)S(1)} %bitcast.256), channel_id=1, source_target_pairs={{8,0},{24,16},{40,32},{56,48},{72,64},{88,80},{104,96},{120,112},{... | collective-permute-start | bytes 3145736 | tf_op jit(solution)/shard_map/ppermute | solution.py:112
  197.5 7.6 %collective-permute-start.10 = (bf16[1,2,512,512]{3,2,1,0:T(8,128)(2,1)}, bf16[1,2,512,512]{3,2,1,0:T(8,128)(2,1)S(1)}, u32[]{:S(2)}, u32[]{:S(2)}) collective-permute-start(bf16[1,2,512,512]{3,2,1,0:T(8,128)(2,1)} %collective-permute-done.9), channel_id=1, source_target_pairs={{0,8},{16,24},{32,40},{48,56},{64,72},{80,88},{96,104},{112,120},{... | collective-permute-start | bytes 3145736 | tf_op jit(solution)/shard_map/ppermute | solution.py:113
  202.0 3.6 %collective-permute-start.1 = (bf16[1,2,512,512]{3,2,1,0:T(8,128)(2,1)S(1)}, bf16[1,2,512,512]{3,2,1,0:T(8,128)(2,1)S(1)}, u32[]{:S(2)}, u32[]{:S(2)}) collective-permute-start(bf16[1,2,512,512]{3,2,1,0:T(8,128)(2,1)S(1)} %collective-permute-done), channel_id=1, source_target_pairs={{0,8},{16,24},{32,40},{48,56},{64,72},{80,88},{96,104},{112,120},{... | collective-permute-start | bytes 3145736 | tf_op jit(solution)/shard_map/ppermute | solution.py:113

commit v6 on v5

--- a/solution.py
+++ b/solution.py
@@ -113,7 +113,7 @@
     from_forward = lax.ppermute(second_panel, "chan", [(c - 1, c) for c in range(1, n_chan, 2)])
     odd = lax.axis_index("chan") % 2 == 1
     upper_panel = jnp.where(odd, from_forward, from_sibling)
-    return upper_panel, second_panel
+    return upper_panel, second_panel, from_sibling
 
 
 def shards(records, offsets, dead_mask, band_blocks):
@@ -124,11 +124,13 @@
     per_device = BINS // n_freq
     chunks = 4
     grouped = whitened.reshape(n_freq, chunks, per_device // chunks, 2, seg_count, channels)
+    parts = [grouped[:, k].reshape(BINS // chunks, 2, seg_count, channels) for k in range(chunks)]
     chunk_products = []
     for k in range(chunks):
-        part = grouped[:, k].reshape(BINS // chunks, 2, seg_count, channels)
-        own_panel = lax.all_to_all(part, "freq", split_axis=0, concat_axis=2, tiled=True)
-        upper_panel, second_panel = neighbour_panels(own_panel)
+        own_panel = lax.all_to_all(parts[k], "freq", split_axis=0, concat_axis=2, tiled=True)
+        upper_panel, second_panel, from_sibling = neighbour_panels(own_panel)
+        if k + 1 < chunks:
+            _, parts[k + 1] = lax.optimization_barrier((from_sibling, parts[k + 1]))
         chunk_products.append(local_products(own_panel, [own_panel, upper_panel, second_panel]))
     band_limit = band_blocks[0]
     results = []

time: 219 us -> 216 us (0.986)
  blocking collectives: 60.1 us -> 22.8 us
  starting transfers between devices: 27.1 us -> 41.3 us
  waiting for transfers between devices: 59.4 us -> 69.9 us
  matrix products: 20.2 us -> 30.2 us
  other arithmetic: 20.1 us -> 17.6 us
    all_to_all x3 -> x1, blocking collectives: 60.1 us -> 22.8 us  [shards(): lax.all_to_all(parts[k], 'freq', split_axis=0, concat_axis=2, tiled=True)]
    dot_general x12, matrix products: 20.2 us -> 30.2 us  [local_products(): jnp.einsum('fpsi,fpsj->fij', left_panel, both, preferred_element_type=jnp...]
    all_to_all x1 -> x3, waiting for transfers between devices: 0.07 us -> 7.12 us  [shards(): lax.all_to_all(parts[k], 'freq', split_axis=0, concat_axis=2, tiled=True)]
    all_to_all x1 -> x3, starting transfers between devices: 4.44 us -> 11.1 us  [shards(): lax.all_to_all(parts[k], 'freq', split_axis=0, concat_axis=2, tiled=True)]
    ppermute x4, starting transfers between devices: 7.42 us -> 12.2 us  [neighbour_panels(): lax.ppermute(second_panel, 'chan', [(c - 1, c) for c in range(1, n_chan,...]
    unnamed x8 -> x30, local copies, waits for them, and re-layouts: 0.02 us -> 4.02 us
    ppermute x4, waiting for transfers between devices: 59.1 us -> 62.7 us  [from_behind(): return lax.ppermute(block, axis, route)]
    ppermute x4, starting transfers between devices: 10.1 us -> 12.8 us  [from_behind(): return lax.ppermute(block, axis, route)]
  transfers between devices with their start and end apart: 13 -> 15, of which waited for: 6 -> 7; matrix products, arithmetic and copies ran while one was open for 14% -> 18% of each run, Pallas kernels for 0% -> 0%
where the time goes in v6:
time: 216 us; the launch traced here: 214 us
  waiting for transfers between devices  69.9 us (32%)
  starting transfers between devices  41.3 us (19%)
  matrix products  30.2 us (14%)
  blocking collectives  22.8 us (11%)
  Pallas kernels  20.3 us (9%)
  other arithmetic  17.6 us (8%)
  local copies, waits for them, and re-layouts  10.7 us (5%)
    ppermute x4, waiting for transfers between devices, from_behind(): return lax.ppermute(block, axis, route)  62.7 us
    dot_general x12, matrix products, local_products(): jnp.einsum('fpsi,fpsj->fij', left_panel, both, preferred_element_type=jnp...  30.2 us
    all_to_all x1, blocking collectives, shards(): lax.all_to_all(parts[k], 'freq', split_axis=0, concat_axis=2, tiled=True)  22.8 us
    pallas_call x1, Pallas kernels, whitened_spectra(): pl.pallas_call(functools.partial(spectra_kernel, seg_count, window), out_...  20.3 us
    ppermute x4, starting transfers between devices, from_behind(): return lax.ppermute(block, axis, route)  12.8 us
    ppermute x4, starting transfers between devices, neighbour_panels(): lax.ppermute(second_panel, 'chan', [(c - 1, c) for c in range(1, n_chan,...  12.2 us
    all_to_all x3, starting transfers between devices, shards(): lax.all_to_all(parts[k], 'freq', split_axis=0, concat_axis=2, tiled=True)  11.1 us
    neg x12, other arithmetic, local_products(): turned = jnp.stack([-right_panel[:, 1], right_panel[:, 0]], axis=1)  7.58 us
  transfers between devices with their start and end apart: 15, of which 7 were waited for; matrix products, arithmetic and copies ran while one was open for 18% of the time, Pallas kernels for 0%

profile of v6, /device:TPU:34, one launch (start us, length us, event | category | flops | bytes accessed | tf_op | source)
XLA Modules:
  0.0 213.9 jit_solution(7923956228532692662)
XLA Ops:
  2.3 20.3 %shard_map.46 = bf16[64,64,512]{2,1,0:T(8,128)(2,1)} custom-call(s32[64]{0:T(128)} %offs_ref.1, f32[64,384]{1,0:T(8,128)} %pad_convert_fusion.dft_ref, f32[1,512]{1,0:T(1,128)} %bitcast.262, bf16[8448,512]{1,0:T(8,128)(2,1)} %rec_hbm.1), custom_call_target="tpu_custom_call" | custom-call | flops 1610612736 | bytes 29360128 | tf_op jit(solution)/shard_map/pallas_call | solution.py:70
  22.6 4.5 %copy.58 = bf16[64,64,512]{2,0,1:T(8,128)(2,1)S(1)} copy(bf16[64,64,512]{2,1,0:T(8,128)(2,1)} %shard_map.46) | data formatting | bytes 8388608 | tf_op jit(solution)/shard_map/reshape | solution.py:122
  27.1 1.8 slice_bitcast_fusion
  28.9 22.8 %all_to_all.72 = bf16[8,2,64,512]{3,2,1,0:T(8,128)(2,1)S(1)} all-to-all(bf16[8,2,64,512]{3,2,1,0:T(8,128)(2,1)S(1)} %get-tuple-element.14), channel_id=1, replica_groups=mesh['chan'=16,'freq'=8] {'freq'}, dimensions={0} | all-to-all | bytes 2097152 | tf_op jit(solution)/shard_map/all_to_all | solution.py:130
  53.1 3.3 %collective-permute-start.3 = (bf16[1,2,512,512]{3,2,1,0:T(8,128)(2,1)S(1)}, bf16[1,2,512,512]{3,2,1,0:T(8,128)(2,1)}, u32[]{:S(2)}, u32[]{:S(2)}) collective-permute-start(bf16[1,2,512,512]{3,2,1,0:T(8,128)(2,1)S(1)} %bitcast.231), channel_id=1, source_target_pairs={{16,0},{24,8},{32,16},{40,24},{48,32},{56,40},{64,48},{72,56},{80,... | collective-permute-start | bytes 3145736 | tf_op jit(solution)/shard_map/ppermute | solution.py:22
  58.1 3.7 %all-to-all-start.1 = ((bf16[8,2,64,512]{3,2,1,0:T(8,128)(2,1)}), bf16[8,2,64,512]{3,2,1,0:T(8,128)(2,1)S(1)}, u32[]{:S(2)}, u32[]{:S(2)}) async-start(bf16[8,2,64,512]{3,2,1,0:T(8,128)(2,1)} %get-tuple-element.8), calls=%async_computation.1 | async-start | bytes 2097152 | tf_op jit(solution)/shard_map/all_to_all | solution.py:130
  61.9 3.5 %fusion.72 = bf16[1,1,512,1024]{3,2,1,0:T(8,128)(2,1)} fusion(bf16[2,512,512]{2,1,0:T(8,128)(2,1)S(1)} %bitcast.233, bf16[1,1,512,512]{3,2,1,0:T(8,128)(2,1)} %get-tuple-element.16, bf16[1,1,512,512]{3,2,1,0:T(8,128)(2,1)} %get-tuple-element.15, bf16[1,2,512,512]{3,2,1,0:T(8,128)(2,1)S(1)} %bitcast.234), kind=kOutput, calls=%fused_computation.100 | convolution fusion | flops 1081081856 | bytes 4194304 | tf_op jit(solution)/shard_map/fpsi,fpsj->fij/dot_general | solution.py:102
  65.3 16.5 %collective-permute-done.3 = bf16[1,2,512,512]{3,2,1,0:T(8,128)(2,1)} collective-permute-done((bf16[1,2,512,512]{3,2,1,0:T(8,128)(2,1)S(1)}, bf16[1,2,512,512]{3,2,1,0:T(8,128)(2,1)}, u32[]{:S(2)}, u32[]{:S(2)}) %collective-permute-start.3) | collective-permute-done | bytes 1048608 | tf_op jit(solution)/shard_map/ppermute | solution.py:22
  81.8 3.5 %collective-permute-start.4 = (bf16[1,2,512,512]{3,2,1,0:T(8,128)(2,1)}, bf16[1,2,512,512]{3,2,1,0:T(8,128)(2,1)}, u32[]{:S(2)}, u32[]{:S(2)}) collective-permute-start(bf16[1,2,512,512]{3,2,1,0:T(8,128)(2,1)} %collective-permute-done.3), channel_id=1, source_target_pairs={{0,8},{16,24},{32,40},{48,56},{64,72},{80,88},{96,104},{112,120},{... | collective-permute-start | bytes 3145736 | tf_op jit(solution)/shard_map/ppermute | solution.py:113
  86.6 3.5 %fusion.80 = bf16[1,1,512,1024]{3,2,1,0:T(8,128)(2,1)} fusion(bf16[2,512,512]{2,1,0:T(8,128)(2,1)S(1)} %bitcast.235, bf16[1,1,512,512]{3,2,1,0:T(8,128)(2,1)S(1)} %get-tuple-element.32, bf16[1,1,512,512]{3,2,1,0:T(8,128)(2,1)S(1)} %get-tuple-element.31, bf16[1,2,512,512]{3,2,1,0:T(8,128)(2,1)} %collective-permute-done.3), kind=kOutput, calls=%fused_computation.108 | convolution fusion | flops 1081081856 | bytes 4194304 | tf_op jit(solution)/shard_map/fpsi,fpsj->fij/dot_general | solution.py:102
  90.1 1.4 all-to-all-done.1
  91.6 1.3 collective-permute-start.1
  93.0 3.1 %collective-permute-start.5 = (bf16[1,2,512,512]{3,2,1,0:T(8,128)(2,1)S(1)}, bf16[1,2,512,512]{3,2,1,0:T(8,128)(2,1)}, u32[]{:S(2)}, u32[]{:S(2)}) collective-permute-start(bf16[1,2,512,512]{3,2,1,0:T(8,128)(2,1)S(1)} %bitcast.239), channel_id=1, source_target_pairs={{16,0},{24,8},{32,16},{40,24},{48,32},{56,40},{64,48},{72,56},{80,... | collective-permute-start | bytes 3145736 | tf_op jit(solution)/shard_map/ppermute | solution.py:22
  96.2 2.2 %fusion.73 = bf16[1,1,512,1024]{3,2,1,0:T(8,128)(2,1)} fusion(bf16[2,512,512]{2,1,0:T(8,128)(2,1)S(1)} %bitcast.240, bf16[1,1,512,512]{3,2,1,0:T(8,128)(2,1)S(1)} %get-tuple-element.18, bf16[1,1,512,512]{3,2,1,0:T(8,128)(2,1)S(1)} %get-tuple-element.17, bf16[1,2,512,512]{3,2,1,0:T(8,128)(2,1)S(1)} %bitcast.241), kind=kOutput, calls=%fused_computation.101 | convolution fusion | flops 1081081856 | bytes 4194304 | tf_op jit(solution)/shard_map/fpsi,fpsj->fij/dot_general | solution.py:102
  101.0 3.8 %all-to-all-start.2 = ((bf16[8,2,64,512]{3,2,1,0:T(8,128)(2,1)}), bf16[8,2,64,512]{3,2,1,0:T(8,128)(2,1)S(1)}, u32[]{:S(2)}, u32[]{:S(2)}) async-start(bf16[8,2,64,512]{3,2,1,0:T(8,128)(2,1)} %get-tuple-element.9), calls=%async_computation.2 | async-start | bytes 2097152 | tf_op jit(solution)/shard_map/all_to_all | solution.py:130
  104.8 3.8 %fusion.76 = bf16[1,1,512,1024]{3,2,1,0:T(8,128)(2,1)} fusion(bf16[2,512,512]{2,1,0:T(8,128)(2,1)S(1)} %bitcast.236, bf16[1,1,512,512]{3,2,1,0:T(8,128)(2,1)} %get-tuple-element.24, bf16[1,1,512,512]{3,2,1,0:T(8,128)(2,1)} %get-tuple-element.23, bf16[1,2,512,512]{3,2,1,0:T(8,128)(2,1)} %copy-done.1), kind=kOutput, calls=%fused_computation.104 | convolution fusion | flops 1081081856 | bytes 4194304 | tf_op jit(solution)/shard_map/fpsi,fpsj->fij/dot_general | solution.py:102
  108.6 13.1 %collective-permute-done.5 = bf16[1,2,512,512]{3,2,1,0:T(8,128)(2,1)} collective-permute-done((bf16[1,2,512,512]{3,2,1,0:T(8,128)(2,1)S(1)}, bf16[1,2,512,512]{3,2,1,0:T(8,128)(2,1)}, u32[]{:S(2)}, u32[]{:S(2)}) %collective-permute-start.5) | collective-permute-done | bytes 1048608 | tf_op jit(solution)/shard_map/ppermute | solution.py:22
  121.7 3.1 %collective-permute-start.6 = (bf16[1,2,512,512]{3,2,1,0:T(8,128)(2,1)}, bf16[1,2,512,512]{3,2,1,0:T(8,128)(2,1)}, u32[]{:S(2)}, u32[]{:S(2)}) collective-permute-start(bf16[1,2,512,512]{3,2,1,0:T(8,128)(2,1)} %collective-permute-done.5), channel_id=1, source_target_pairs={{0,8},{16,24},{32,40},{48,56},{64,72},{80,88},{96,104},{112,120},{... | collective-permute-start | bytes 3145736 | tf_op jit(solution)/shard_map/ppermute | solution.py:113
  126.1 3.5 %fusion.81 = bf16[1,1,512,1024]{3,2,1,0:T(8,128)(2,1)} fusion(bf16[2,512,512]{2,1,0:T(8,128)(2,1)S(1)} %bitcast.242, bf16[1,1,512,512]{3,2,1,0:T(8,128)(2,1)S(1)} %get-tuple-element.34, bf16[1,1,512,512]{3,2,1,0:T(8,128)(2,1)S(1)} %get-tuple-element.33, bf16[1,2,512,512]{3,2,1,0:T(8,128)(2,1)} %collective-permute-done.5), kind=kOutput, calls=%fused_computation.109 | convolution fusion | flops 1081081856 | bytes 4194304 | tf_op jit(solution)/shard_map/fpsi,fpsj->fij/dot_general | solution.py:102
  129.6 3.6 %all-to-all-done.2 = bf16[8,2,64,512]{3,2,1,0:T(8,128)(2,1)S(1)} async-done(((bf16[8,2,64,512]{3,2,1,0:T(8,128)(2,1)}), bf16[8,2,64,512]{3,2,1,0:T(8,128)(2,1)S(1)}, u32[]{:S(2)}, u32[]{:S(2)}) %all-to-all-start.2) | async-done | bytes 1048608 | tf_op jit(solution)/shard_map/all_to_all | solution.py:130
  134.6 4.3 %collective-permute-start.7 = (bf16[1,2,512,512]{3,2,1,0:T(8,128)(2,1)S(1)}, bf16[1,2,512,512]{3,2,1,0:T(8,128)(2,1)}, u32[]{:S(2)}, u32[]{:S(2)}) collective-permute-start(bf16[1,2,512,512]{3,2,1,0:T(8,128)(2,1)S(1)} %bitcast.246), channel_id=1, source_target_pairs={{16,0},{24,8},{32,16},{40,24},{48,32},{56,40},{64,48},{72,56},{80,... | collective-permute-start | bytes 3145736 | tf_op jit(solution)/shard_map/ppermute | solution.py:22
  138.9 2.3 %fusion.74 = bf16[1,1,512,1024]{3,2,1,0:T(8,128)(2,1)} fusion(bf16[2,512,512]{2,1,0:T(8,128)(2,1)S(1)} %bitcast.247, bf16[1,1,512,512]{3,2,1,0:T(8,128)(2,1)S(1)} %get-tuple-element.20, bf16[1,1,512,512]{3,2,1,0:T(8,128)(2,1)S(1)} %get-tuple-element.19, bf16[1,2,512,512]{3,2,1,0:T(8,128)(2,1)S(1)} %bitcast.248), kind=kOutput, calls=%fused_computation.102 | convolution fusion | flops 1081081856 | bytes 4194304 | tf_op jit(solution)/shard_map/fpsi,fpsj->fij/dot_general | solution.py:102
  143.7 3.6 %all-to-all-start.3 = ((bf16[8,2,64,512]{3,2,1,0:T(8,128)(2,1)}), bf16[8,2,64,512]{3,2,1,0:T(8,128)(2,1)S(1)}, u32[]{:S(2)}, u32[]{:S(2)}) async-start(bf16[8,2,64,512]{3,2,1,0:T(8,128)(2,1)} %get-tuple-element.10), calls=%async_computation.3 | async-start | bytes 2097152 | tf_op jit(solution)/shard_map/all_to_all | solution.py:130
  147.3 3.8 %fusion.77 = bf16[1,1,512,1024]{3,2,1,0:T(8,128)(2,1)} fusion(bf16[2,512,512]{2,1,0:T(8,128)(2,1)S(1)} %bitcast.243, bf16[1,1,512,512]{3,2,1,0:T(8,128)(2,1)} %get-tuple-element.26, bf16[1,1,512,512]{3,2,1,0:T(8,128)(2,1)} %get-tuple-element.25, bf16[1,2,512,512]{3,2,1,0:T(8,128)(2,1)} %copy-done), kind=kOutput, calls=%fused_computation.105 | convolution fusion | flops 1081081856 | bytes 4194304 | tf_op jit(solution)/shard_map/fpsi,fpsj->fij/dot_general | solution.py:102
  151.1 12.9 %collective-permute-done.7 = bf16[1,2,512,512]{3,2,1,0:T(8,128)(2,1)} collective-permute-done((bf16[1,2,512,512]{3,2,1,0:T(8,128)(2,1)S(1)}, bf16[1,2,512,512]{3,2,1,0:T(8,128)(2,1)}, u32[]{:S(2)}, u32[]{:S(2)}) %collective-permute-start.7) | collective-permute-done | bytes 1048608 | tf_op jit(solution)/shard_map/ppermute | solution.py:22
  164.0 3.7 %collective-permute-start.8 = (bf16[1,2,512,512]{3,2,1,0:T(8,128)(2,1)}, bf16[1,2,512,512]{3,2,1,0:T(8,128)(2,1)}, u32[]{:S(2)}, u32[]{:S(2)}) collective-permute-start(bf16[1,2,512,512]{3,2,1,0:T(8,128)(2,1)} %collective-permute-done.7), channel_id=1, source_target_pairs={{0,8},{16,24},{32,40},{48,56},{64,72},{80,88},{96,104},{112,120},{... | collective-permute-start | bytes 3145736 | tf_op jit(solution)/shard_map/ppermute | solution.py:113
  169.0 2.5 %fusion.82 = bf16[1,1,512,1024]{3,2,1,0:T(8,128)(2,1)S(1)} fusion(bf16[2,512,512]{2,1,0:T(8,128)(2,1)S(1)} %bitcast.249, bf16[1,1,512,512]{3,2,1,0:T(8,128)(2,1)S(1)} %get-tuple-element.36, bf16[1,1,512,512]{3,2,1,0:T(8,128)(2,1)S(1)} %get-tuple-element.35, bf16[1,2,512,512]{3,2,1,0:T(8,128)(2,1)} %collective-permute-done.7), kind=kOutput, calls=%fused_computation.110 | convolution fusion | flops 1081081856 | bytes 4194304 | tf_op jit(solution)/shard_map/fpsi,fpsj->fij/dot_general | solution.py:102
  171.5 2.1 all-to-all-done.3
  173.7 2.1 collective-permute-start.9
  181.8 20.3 %collective-permute-done.9 = bf16[1,2,512,512]{3,2,1,0:T(8,128)(2,1)S(1)} collective-permute-done((bf16[1,2,512,512]{3,2,1,0:T(8,128)(2,1)S(1)}, bf16[1,2,512,512]{3,2,1,0:T(8,128)(2,1)S(1)}, u32[]{:S(2)}, u32[]{:S(2)}) %collective-permute-start.9) | collective-permute-done | bytes 1048608 | tf_op jit(solution)/shard_map/ppermute | solution.py:22
  202.0 1.8 collective-permute-start.10
  208.4 5.5 %pad_maximum_fusion = bf16[3,4,512,1024]{3,2,1,0:T(8,128)(2,1)} fusion(bf16[1,4,512,1024]{3,2,1,0:T(8,128)(2,1)S(1)} %maximum_multiply_fusion.2, bf16[1,4,512,1024]{3,2,1,0:T(8,128)(2,1)S(1)} %maximum_multiply_fusion.1, bf16[1,4,512,1024]{3,2,1,0:T(8,128)(2,1)S(1)} %maximum_multiply_fusion), kind=kLoop, calls=%fused_computation | loop fusion | flops 12582912 | bytes 25165824 | tf_op jit(solution)/shard_map/stack | solution.py:141
  (74 shorter events, 25.5 us)
Async XLA Ops:
  51.8 6.3 %collective-permute-start = (bf16[1,2,512,512]{3,2,1,0:T(8,128)(2,1)S(1)}, bf16[1,2,512,512]{3,2,1,0:T(8,128)(2,1)S(1)}, u32[]{:S(2)}, u32[]{:S(2)}) collective-permute-start(bf16[1,2,512,512]{3,2,1,0:T(8,128)(2,1)S(1)} %bitcast.230), channel_id=1, source_target_pairs={{8,0},{24,16},{40,32},{56,48},{72,64},{88,80},{104,96},{120,112},{... | collective-permute-start | bytes 3145736 | tf_op jit(solution)/shard_map/ppermute | solution.py:112
  53.1 28.6 %collective-permute-start.3 = (bf16[1,2,512,512]{3,2,1,0:T(8,128)(2,1)S(1)}, bf16[1,2,512,512]{3,2,1,0:T(8,128)(2,1)}, u32[]{:S(2)}, u32[]{:S(2)}) collective-permute-start(bf16[1,2,512,512]{3,2,1,0:T(8,128)(2,1)S(1)} %bitcast.231), channel_id=1, source_target_pairs={{16,0},{24,8},{32,16},{40,24},{48,32},{56,40},{64,48},{72,56},{80,... | collective-permute-start | bytes 3145736 | tf_op jit(solution)/shard_map/ppermute | solution.py:22
  58.1 7.2 %copy-start.9 = (bf16[1,2,512,512]{3,2,1,0:T(8,128)(2,1)}, bf16[1,2,512,512]{3,2,1,0:T(8,128)(2,1)S(1)}, u32[]{:S(2)}) copy-start(bf16[1,2,512,512]{3,2,1,0:T(8,128)(2,1)S(1)} %collective-permute-done) | copy-start | bytes 3145732
  58.1 33.4 %all-to-all-start.1 = ((bf16[8,2,64,512]{3,2,1,0:T(8,128)(2,1)}), bf16[8,2,64,512]{3,2,1,0:T(8,128)(2,1)S(1)}, u32[]{:S(2)}, u32[]{:S(2)}) async-start(bf16[8,2,64,512]{3,2,1,0:T(8,128)(2,1)} %get-tuple-element.8), calls=%async_computation.1 | async-start | bytes 2097152 | tf_op jit(solution)/shard_map/all_to_all | solution.py:130
  81.8 16.6 %collective-permute-start.4 = (bf16[1,2,512,512]{3,2,1,0:T(8,128)(2,1)}, bf16[1,2,512,512]{3,2,1,0:T(8,128)(2,1)}, u32[]{:S(2)}, u32[]{:S(2)}) collective-permute-start(bf16[1,2,512,512]{3,2,1,0:T(8,128)(2,1)} %collective-permute-done.3), channel_id=1, source_target_pairs={{0,8},{16,24},{32,40},{48,56},{64,72},{80,88},{96,104},{112,120},{... | collective-permute-start | bytes 3145736 | tf_op jit(solution)/shard_map/ppermute | solution.py:113
  91.6 8.1 %collective-permute-start.1 = (bf16[1,2,512,512]{3,2,1,0:T(8,128)(2,1)S(1)}, bf16[1,2,512,512]{3,2,1,0:T(8,128)(2,1)S(1)}, u32[]{:S(2)}, u32[]{:S(2)}) collective-permute-start(bf16[1,2,512,512]{3,2,1,0:T(8,128)(2,1)S(1)} %bitcast.237), channel_id=1, source_target_pairs={{8,0},{24,16},{40,32},{56,48},{72,64},{88,80},{104,96},{120,112},{... | collective-permute-start | bytes 3145736 | tf_op jit(solution)/shard_map/ppermute | solution.py:112
  93.0 28.7 %collective-permute-start.5 = (bf16[1,2,512,512]{3,2,1,0:T(8,128)(2,1)S(1)}, bf16[1,2,512,512]{3,2,1,0:T(8,128)(2,1)}, u32[]{:S(2)}, u32[]{:S(2)}) collective-permute-start(bf16[1,2,512,512]{3,2,1,0:T(8,128)(2,1)S(1)} %bitcast.239), channel_id=1, source_target_pairs={{16,0},{24,8},{32,16},{40,24},{48,32},{56,40},{64,48},{72,56},{80,... | collective-permute-start | bytes 3145736 | tf_op jit(solution)/shard_map/ppermute | solution.py:22
  96.2 2.3 %copy-start.10 = (bf16[1,2,512,512]{3,2,1,0:T(8,128)(2,1)S(1)}, bf16[1,2,512,512]{3,2,1,0:T(8,128)(2,1)}, u32[]{:S(2)}) copy-start(bf16[1,2,512,512]{3,2,1,0:T(8,128)(2,1)} %copy-done.9) | copy-start | bytes 3145732
  98.6 1.4 copy-start.1
  100.0 1.0 copy-start.13
  101.0 32.2 %all-to-all-start.2 = ((bf16[8,2,64,512]{3,2,1,0:T(8,128)(2,1)}), bf16[8,2,64,512]{3,2,1,0:T(8,128)(2,1)S(1)}, u32[]{:S(2)}, u32[]{:S(2)}) async-start(bf16[8,2,64,512]{3,2,1,0:T(8,128)(2,1)} %get-tuple-element.9), calls=%async_computation.2 | async-start | bytes 2097152 | tf_op jit(solution)/shard_map/all_to_all | solution.py:130
  121.7 19.5 %collective-permute-start.6 = (bf16[1,2,512,512]{3,2,1,0:T(8,128)(2,1)}, bf16[1,2,512,512]{3,2,1,0:T(8,128)(2,1)}, u32[]{:S(2)}, u32[]{:S(2)}) collective-permute-start(bf16[1,2,512,512]{3,2,1,0:T(8,128)(2,1)} %collective-permute-done.5), channel_id=1, source_target_pairs={{0,8},{16,24},{32,40},{48,56},{64,72},{80,88},{96,104},{112,120},{... | collective-permute-start | bytes 3145736 | tf_op jit(solution)/shard_map/ppermute | solution.py:113
  133.3 9.3 %collective-permute-start.2 = (bf16[1,2,512,512]{3,2,1,0:T(8,128)(2,1)S(1)}, bf16[1,2,512,512]{3,2,1,0:T(8,128)(2,1)S(1)}, u32[]{:S(2)}, u32[]{:S(2)}) collective-permute-start(bf16[1,2,512,512]{3,2,1,0:T(8,128)(2,1)S(1)} %bitcast.244), channel_id=1, source_target_pairs={{8,0},{24,16},{40,32},{56,48},{72,64},{88,80},{104,96},{120,112},{... | collective-permute-start | bytes 3145736 | tf_op jit(solution)/shard_map/ppermute | solution.py:112
  134.6 29.3 %collective-permute-start.7 = (bf16[1,2,512,512]{3,2,1,0:T(8,128)(2,1)S(1)}, bf16[1,2,512,512]{3,2,1,0:T(8,128)(2,1)}, u32[]{:S(2)}, u32[]{:S(2)}) collective-permute-start(bf16[1,2,512,512]{3,2,1,0:T(8,128)(2,1)S(1)} %bitcast.246), channel_id=1, source_target_pairs={{16,0},{24,8},{32,16},{40,24},{48,32},{56,40},{64,48},{72,56},{80,... | collective-permute-start | bytes 3145736 | tf_op jit(solution)/shard_map/ppermute | solution.py:22
  138.9 2.3 %copy-start.14 = (bf16[1,2,512,512]{3,2,1,0:T(8,128)(2,1)S(1)}, bf16[1,2,512,512]{3,2,1,0:T(8,128)(2,1)}, u32[]{:S(2)}) copy-start(bf16[1,2,512,512]{3,2,1,0:T(8,128)(2,1)} %copy-done.13) | copy-start | bytes 3145732
  141.4 1.3 copy-start
  142.7 1.0 copy-start.11
  143.7 29.9 %all-to-all-start.3 = ((bf16[8,2,64,512]{3,2,1,0:T(8,128)(2,1)}), bf16[8,2,64,512]{3,2,1,0:T(8,128)(2,1)S(1)}, u32[]{:S(2)}, u32[]{:S(2)}) async-start(bf16[8,2,64,512]{3,2,1,0:T(8,128)(2,1)} %get-tuple-element.10), calls=%async_computation.3 | async-start | bytes 2097152 | tf_op jit(solution)/shard_map/all_to_all | solution.py:130
  164.0 15.7 %collective-permute-start.8 = (bf16[1,2,512,512]{3,2,1,0:T(8,128)(2,1)}, bf16[1,2,512,512]{3,2,1,0:T(8,128)(2,1)}, u32[]{:S(2)}, u32[]{:S(2)}) collective-permute-start(bf16[1,2,512,512]{3,2,1,0:T(8,128)(2,1)} %collective-permute-done.7), channel_id=1, source_target_pairs={{0,8},{16,24},{32,40},{48,56},{64,72},{80,88},{96,104},{112,120},{... | collective-permute-start | bytes 3145736 | tf_op jit(solution)/shard_map/ppermute | solution.py:113
  173.7 28.4 %collective-permute-start.9 = (bf16[1,2,512,512]{3,2,1,0:T(8,128)(2,1)S(1)}, bf16[1,2,512,512]{3,2,1,0:T(8,128)(2,1)S(1)}, u32[]{:S(2)}, u32[]{:S(2)}) collective-permute-start(bf16[1,2,512,512]{3,2,1,0:T(8,128)(2,1)S(1)} %bitcast.251), channel_id=1, source_target_pairs={{16,0},{24,8},{32,16},{40,24},{48,32},{56,40},{64,48},{72,56},{80,... | collective-permute-start | bytes 3145736 | tf_op jit(solution)/shard_map/ppermute | solution.py:22
  175.8 30.2 %collective-permute-start.11 = (bf16[1,2,512,512]{3,2,1,0:T(8,128)(2,1)S(1)}, bf16[1,2,512,512]{3,2,1,0:T(8,128)(2,1)S(1)}, u32[]{:S(2)}, u32[]{:S(2)}) collective-permute-start(bf16[1,2,512,512]{3,2,1,0:T(8,128)(2,1)S(1)} %bitcast.252), channel_id=1, source_target_pairs={{8,0},{24,16},{40,32},{56,48},{72,64},{88,80},{104,96},{120,112},{... | collective-permute-start | bytes 3145736 | tf_op jit(solution)/shard_map/ppermute | solution.py:112
  177.2 1.3 copy-start.4
  177.2 1.5 copy-start.5
  177.2 1.8 copy-start.8
  179.0 1.2 copy-start.12
  202.0 4.0 %collective-permute-start.10 = (bf16[1,2,512,512]{3,2,1,0:T(8,128)(2,1)S(1)}, bf16[1,2,512,512]{3,2,1,0:T(8,128)(2,1)S(1)}, u32[]{:S(2)}, u32[]{:S(2)}) collective-permute-start(bf16[1,2,512,512]{3,2,1,0:T(8,128)(2,1)S(1)} %collective-permute-done.9), channel_id=1, source_target_pairs={{0,8},{16,24},{32,40},{48,56},{64,72},{80,88},{96,104},{112,120},{... | collective-permute-start | bytes 3145736 | tf_op jit(solution)/shard_map/ppermute | solution.py:113
  203.9 1.3 copy-start.2
  203.9 1.5 copy-start.6
  206.3 1.3 copy-start.3
  206.3 1.5 copy-start.7

commit v7 on v5

--- a/solution.py
+++ b/solution.py
@@ -106,14 +106,55 @@
     return results
 
 
-def neighbour_panels(own_panel):
+def block_slice(panel, start, size):
+    return lax.dynamic_slice_in_dim(panel, start, size, axis=2)
+
+
+def chunk_exchange(part, seg_count):
     n_chan = lax.axis_size("chan")
-    second_panel = from_behind(own_panel, "chan", -2)
+    n_freq = lax.axis_size("freq")
+    half = n_freq // 2
+    me = lax.axis_index("freq")
+    side = me // half
+    row = me % half
+    crossed = []
+    for gy in range(half):
+        g = half + gy
+        piece = lax.dynamic_index_in_dim(part, me ^ g, 0, keepdims=False)
+        pairs = [
+            (c * n_freq + f, (c - 2) * n_freq + (f ^ g)) for c in range(2, n_chan) for f in range(n_freq)
+        ]
+        crossed.append(lax.ppermute(piece, ("chan", "freq"), pairs))
+    flat = part.reshape((n_freq * part.shape[1],) + part.shape[2:])
+    own_panel = lax.all_to_all(flat, "freq", split_axis=0, concat_axis=2, tiled=True)
+    near = half * seg_count
+    near_own = block_slice(own_panel, side * near, near)
+    near_second = from_behind(near_own, "chan", -2)
+    second_panel = jnp.concatenate([near_second] + crossed, axis=2)
+    far_own = [
+        block_slice(own_panel, (half * (1 - side) + (row ^ gy)) * seg_count, seg_count)
+        for gy in range(half)
+    ]
+    second_left = jnp.concatenate([near_own] + far_own, axis=2)
     from_sibling = lax.ppermute(own_panel, "chan", [(c + 1, c) for c in range(0, n_chan, 2)])
     from_forward = lax.ppermute(second_panel, "chan", [(c - 1, c) for c in range(1, n_chan, 2)])
     odd = lax.axis_index("chan") % 2 == 1
     upper_panel = jnp.where(odd, from_forward, from_sibling)
-    return upper_panel, second_panel
+    upper_left = jnp.where(odd, second_left, own_panel)
+    return [own_panel, upper_left, second_left], [own_panel, upper_panel, second_panel]
+
+
+def products_of(lefts, rights):
+    seg_count = lefts[0].shape[2]
+    results = []
+    for left_panel, right_panel in zip(lefts, rights):
+        turned = jnp.stack([-right_panel[:, 1], right_panel[:, 0]], axis=1)
+        both = jnp.concatenate([right_panel, turned], axis=3)
+        product = jnp.einsum(
+            "fpsi,fpsj->fij", left_panel, both, preferred_element_type=jnp.float32
+        )
+        results.append(product * (1.0 / seg_count))
+    return results
 
 
 def shards(records, offsets, dead_mask, band_blocks):
@@ -122,14 +163,12 @@
     whitened = per_segment.reshape(seg_count, BINS, 2, channels).transpose(1, 2, 0, 3)
     n_freq = lax.axis_size("freq")
     per_device = BINS // n_freq
-    chunks = 4
+    chunks = 1
     grouped = whitened.reshape(n_freq, chunks, per_device // chunks, 2, seg_count, channels)
     chunk_products = []
     for k in range(chunks):
-        part = grouped[:, k].reshape(BINS // chunks, 2, seg_count, channels)
-        own_panel = lax.all_to_all(part, "freq", split_axis=0, concat_axis=2, tiled=True)
-        upper_panel, second_panel = neighbour_panels(own_panel)
-        chunk_products.append(local_products(own_panel, [own_panel, upper_panel, second_panel]))
+        lefts, rights = chunk_exchange(grouped[:, k], seg_count)
+        chunk_products.append(products_of(lefts, rights))
     band_limit = band_blocks[0]
     results = []
     for offset_index in range(BAND + 1):

time: 219 us -> 266 us (1.21)
  waiting for transfers between devices: 59.4 us -> 124 us
  blocking collectives: 60.1 us -> 0 us
  local copies, waits for them, and re-layouts: 8.82 us -> 42.4 us
  matrix products: 20.2 us -> 27.4 us
  starting transfers between devices: 27.1 us -> 30.3 us
    all_to_all x3 -> x0, blocking collectives: 60.1 us -> none  [shards(): lax.all_to_all(part, 'freq', split_axis=0, concat_axis=2, tiled=True)]
    all_to_all x1, waiting for transfers between devices: 0.07 us -> 49 us  [chunk_exchange(): lax.all_to_all(flat, 'freq', split_axis=0, concat_axis=2, tiled=True)]
    ppermute x4 -> x1, waiting for transfers between devices: 59.1 us -> 74.8 us  [from_behind(): return lax.ppermute(block, axis, route)]
    unnamed x8 -> x14, local copies, waits for them, and re-layouts: 0.02 us -> 15.3 us
    reshape x1 -> x2, local copies, waits for them, and re-layouts: 4.53 us -> 15.8 us  [shards(): per_segment.reshape(seg_count, BINS, 2, channels).transpose(1, 2, 0, 3)]
    ppermute x8 -> x6, starting transfers between devices: 12.6 us -> 20.8 us  [the longest x4 12.6 us: chunk_exchange(): crossed.append(lax.ppermute(piece, ('chan', 'freq'), pairs))]
    dot_general x12 -> x3, matrix products: 20.2 us -> 27.4 us  [products_of(): jnp.einsum('fpsi,fpsj->fij', left_panel, both, preferred_element_type=jnp...]
    ppermute x4 -> x1, starting transfers between devices: 10.1 us -> 3.33 us  [from_behind(): return lax.ppermute(block, axis, route)]
  transfers between devices with their start and end apart: 13 -> 8, of which waited for: 6 -> 2; matrix products, arithmetic and copies ran while one was open for 14% -> 17% of each run, Pallas kernels for 0% -> 0%
where the time goes in v7:
time: 266 us; the launch traced here: 264 us
  waiting for transfers between devices  124 us (47%)
  local copies, waits for them, and re-layouts  42.4 us (16%)
  starting transfers between devices  30.3 us (11%)
  matrix products  27.4 us (10%)
  Pallas kernels  20 us (8%)
  other arithmetic  19.7 us (7%)
    ppermute x1, waiting for transfers between devices, from_behind(): return lax.ppermute(block, axis, route)  74.8 us
    all_to_all x1, waiting for transfers between devices, chunk_exchange(): lax.all_to_all(flat, 'freq', split_axis=0, concat_axis=2, tiled=True)  49 us
    dot_general x3, matrix products, products_of(): jnp.einsum('fpsi,fpsj->fij', left_panel, both, preferred_element_type=jnp...  27.4 us
    pallas_call x1, Pallas kernels, whitened_spectra(): pl.pallas_call(functools.partial(spectra_kernel, seg_count, window), out_...  20 us
    reshape x2, local copies, waits for them, and re-layouts, shards(): per_segment.reshape(seg_count, BINS, 2, channels).transpose(1, 2, 0, 3)  15.8 us
    unnamed x14, local copies, waits for them, and re-layouts  15.3 us
    ppermute x4, starting transfers between devices, chunk_exchange(): crossed.append(lax.ppermute(piece, ('chan', 'freq'), pairs))  12.6 us
    neg x3, other arithmetic, products_of(): turned = jnp.stack([-right_panel[:, 1], right_panel[:, 0]], axis=1)  9.27 us
  transfers between devices with their start and end apart: 8, of which 2 were waited for; matrix products, arithmetic and copies ran while one was open for 17% of the time, Pallas kernels for 0%

profile of v7, /device:TPU:34, one launch (start us, length us, event | category | flops | bytes accessed | tf_op | source)
XLA Modules:
  0.0 264.4 jit_solution(16208043929330020480)
XLA Ops:
  1.1 1.3 convert_element_type.49
  2.3 20.0 %shard_map.46 = bf16[64,64,512]{2,1,0:T(8,128)(2,1)} custom-call(s32[64]{0:T(128)} %offs_ref.1, f32[64,384]{1,0:T(8,128)} %pad_convert_fusion.dft_ref, f32[1,512]{1,0:T(1,128)} %bitcast.70, bf16[8448,512]{1,0:T(8,128)(2,1)} %rec_hbm.1), custom_call_target="tpu_custom_call" | custom-call | flops 1610612736 | bytes 29360128 | tf_op jit(solution)/shard_map/pallas_call | solution.py:70
  22.4 7.2 %reshape.51 = bf16[64,32,2,512]{3,2,1,0:T(2,128)(2,1)} reshape(bf16[64,64,512]{2,1,0:T(8,128)(2,1)} %shard_map.46) | data formatting | bytes 8388608 | tf_op jit(solution)/shard_map/reshape | solution.py:163
  29.6 8.6 %copy.41 = bf16[64,32,2,512]{3,2,0,1:T(2,128)(2,1)} copy(bf16[64,32,2,512]{3,2,1,0:T(2,128)(2,1)} %reshape.51) | data formatting | bytes 8388608 | tf_op jit(solution)/shard_map/reshape | solution.py:163
  38.2 6.1 %all-to-all-start = ((bf16[32,2,64,512]{3,1,2,0:T(2,128)(2,1)}), bf16[32,2,64,512]{3,1,2,0:T(2,128)(2,1)}, u32[]{:S(2)}, u32[]{:S(2)}) async-start(bf16[32,2,64,512]{3,1,2,0:T(2,128)(2,1)} %bitcast.65), calls=%async_computation | async-start | bytes 8388608 | tf_op jit(solution)/shard_map/all_to_all | solution.py:129
  44.3 49.0 %all-to-all-done = bf16[32,2,64,512]{3,1,2,0:T(2,128)(2,1)} async-done(((bf16[32,2,64,512]{3,1,2,0:T(2,128)(2,1)}), bf16[32,2,64,512]{3,1,2,0:T(2,128)(2,1)}, u32[]{:S(2)}, u32[]{:S(2)}) %all-to-all-start) | async-done | bytes 4194336 | tf_op jit(solution)/shard_map/all_to_all | solution.py:129
  93.3 5.2 %copy.14 = bf16[8,4,2,64,512]{4,3,0,2,1:T(8,128)(2,1)} copy(bf16[8,4,2,64,512]{4,2,3,1,0:T(2,128)(2,1)} %bitcast.2) | data formatting | bytes 8388608 | tf_op jit(solution)/shard_map/all_to_all | solution.py:129
  98.5 3.3 %constant_dynamic-update-slice_fusion = (bf16[4,2,512,512]{3,2,1,0:T(8,128)(2,1)}, bf16[4,2,256,512]{3,2,1,0:T(8,128)(2,1)S(1)}) fusion(bf16[4,2,512,512]{3,2,1,0:T(8,128)(2,1)} %bitcast.4, s32[]{:T(128)S(6)} %select_n.91), kind=kLoop, calls=%fused_computation.57 | loop fusion | bytes 6291460
  101.8 3.3 %collective-permute-start = (bf16[4,2,256,512]{3,2,1,0:T(8,128)(2,1)S(1)}, bf16[4,2,256,512]{3,2,1,0:T(8,128)(2,1)}, u32[]{:S(2)}, u32[]{:S(2)}) collective-permute-start(bf16[4,2,256,512]{3,2,1,0:T(8,128)(2,1)S(1)} %get-tuple-element.6), channel_id=1, source_target_pairs={{16,0},{24,8},{32,16},{40,24},{48,32},{56,40},{64,48},{72,56},{80,... | collective-permute-start | bytes 6291464 | tf_op jit(solution)/shard_map/ppermute | solution.py:22
  105.2 3.4 %constant_dynamic-slice_fusion = (bf16[1,4,2,64,512]{4,2,1,0,3:T(2,128)(2,1)S(1)}, bf16[1,4,2,64,512]{4,2,1,0,3:T(2,128)(2,1)S(1)}, bf16[1,4,2,64,512]{4,2,1,0,3:T(2,128)(2,1)S(1)}, bf16[1,4,2,64,512]{4,2,1,0,3:T(2,128)(2,1)S(1)}) fusion(bf16[8,4,2,64,512]{4,2,1,0,3:T(2,128)(2,1)} %bitcast.64, s32[]{:T(128)S(6)} %select_n.101, s32[]{:T(128)S(6)} %select_n.100, ...), kind=kLoop, calls=%fused_computation.63 | loop fusion | bytes 4194320 | tf_op jit(solution)/shard_map/jit(dynamic_index_in_dim)/dynamic_slice | solution.py:123
  108.7 3.2 %collective-permute-start.1 = (bf16[4,2,64,512]{3,2,1,0:T(8,128)(2,1)S(1)}, bf16[4,2,64,512]{3,2,1,0:T(8,128)(2,1)S(1)}, u32[]{:S(2)}, u32[]{:S(2)}) collective-permute-start(bf16[4,2,64,512]{3,2,1,0:T(8,128)(2,1)S(1)} %bitcast.69), channel_id=1, source_target_pairs={{16,4},{17,5},{18,6},{19,7},{20,0},{21,1},{22,2},{23,3},{24,12},{2... | collective-permute-start | bytes 1572872 | tf_op jit(solution)/shard_map/ppermute | solution.py:127
  112.1 3.2 %collective-permute-start.2 = (bf16[4,2,64,512]{3,2,1,0:T(8,128)(2,1)S(1)}, bf16[4,2,64,512]{3,2,1,0:T(8,128)(2,1)S(1)}, u32[]{:S(2)}, u32[]{:S(2)}) collective-permute-start(bf16[4,2,64,512]{3,2,1,0:T(8,128)(2,1)S(1)} %bitcast.68), channel_id=1, source_target_pairs={{16,5},{17,4},{18,7},{19,6},{20,1},{21,0},{22,3},{23,2},{24,13},{2... | collective-permute-start | bytes 1572872 | tf_op jit(solution)/shard_map/ppermute | solution.py:127
  115.4 4.3 %collective-permute-start.3 = (bf16[4,2,64,512]{3,2,1,0:T(8,128)(2,1)S(1)}, bf16[4,2,64,512]{3,2,1,0:T(8,128)(2,1)S(1)}, u32[]{:S(2)}, u32[]{:S(2)}) collective-permute-start(bf16[4,2,64,512]{3,2,1,0:T(8,128)(2,1)S(1)} %bitcast.66), channel_id=1, source_target_pairs={{16,6},{17,7},{18,4},{19,5},{20,2},{21,3},{22,0},{23,1},{24,14},{2... | collective-permute-start | bytes 1572872 | tf_op jit(solution)/shard_map/ppermute | solution.py:127
  119.9 1.9 collective-permute-start.4
  121.8 74.8 %collective-permute-done = bf16[4,2,256,512]{3,2,1,0:T(8,128)(2,1)} collective-permute-done((bf16[4,2,256,512]{3,2,1,0:T(8,128)(2,1)S(1)}, bf16[4,2,256,512]{3,2,1,0:T(8,128)(2,1)}, u32[]{:S(2)}, u32[]{:S(2)}) %collective-permute-start) | collective-permute-done | bytes 2097184 | tf_op jit(solution)/shard_map/ppermute | solution.py:22
  196.6 1.3 collective-permute-start.6
  197.9 3.1 %constant_dynamic-update-slice_fusion.5 = bf16[4,2,512,512]{3,2,1,0:T(8,128)(2,1)} fusion(bf16[4,2,256,512]{3,2,1,0:T(8,128)(2,1)} %collective-permute-done), kind=kLoop, calls=%fused_computation.62 | loop fusion | bytes 4194304
  201.0 0.9 constant_dynamic-update-slice_fusion.4
  203.6 0.9 constant_dynamic-update-slice_fusion.1
  204.4 6.9 %collective-permute-start.5 = (bf16[4,2,512,512]{3,2,1,0:T(8,128)(2,1)}, bf16[4,2,512,512]{3,2,1,0:T(8,128)(2,1)}, u32[]{:S(2)}, u32[]{:S(2)}) collective-permute-start(bf16[4,2,512,512]{3,2,1,0:T(8,128)(2,1)} %constant_dynamic-update-slice_fusion.1), channel_id=1, source_target_pairs={{0,8},{16,24},{32,40},{48,56},{64,72},{80,88},{96,104},{112,120},{... | collective-permute-start | bytes 12582920 | tf_op jit(solution)/shard_map/ppermute | solution.py:140
  212.1 1.9 dynamic-slice_dynamic-update-slice_fusion.3
  214.0 1.9 dynamic-slice_dynamic-update-slice_fusion.2
  215.9 1.9 dynamic-slice_dynamic-update-slice_fusion.1
  217.7 1.9 dynamic-slice_dynamic-update-slice_fusion
  219.6 3.8 %slice_negate_fusion.2 = (bf16[4,1,512,512]{3,2,1,0:T(8,128)(2,1)S(1)}, bf16[4,1,512,512]{3,2,1,0:T(8,128)(2,1)}) fusion(bf16[4,2,512,512]{3,2,1,0:T(8,128)(2,1)} %bitcast.4), kind=kLoop, calls=%fused_computation.37 | loop fusion | flops 1048576 | bytes 8388608 | tf_op jit(solution)/shard_map/neg | solution.py:151
  223.4 8.6 %fusion.22 = bf16[1,4,512,1024]{3,2,1,0:T(8,128)(2,1)S(1)} fusion(bf16[4,2,512,512]{3,2,1,0:T(8,128)(2,1)} %bitcast.4, bf16[4,1,512,512]{3,2,1,0:T(8,128)(2,1)} %get-tuple-element.8, bf16[4,1,512,512]{3,2,1,0:T(8,128)(2,1)S(1)} %get-tuple-element.7, bf16[]{:T(256)} %bitcast.8), kind=kOutput, calls=%fused_computation.26 | convolution fusion | flops 4326424576 | bytes 12582914 | tf_op jit(solution)/shard_map/fpsi,fpsj->fij/dot_general | solution.py:153
  232.1 3.8 %slice_negate_fusion = (bf16[4,1,512,512]{3,2,1,0:T(8,128)(2,1)S(1)}, bf16[4,1,512,512]{3,2,1,0:T(8,128)(2,1)}) fusion(bf16[4,2,512,512]{3,2,1,0:T(8,128)(2,1)} %constant_dynamic-update-slice_fusion.1), kind=kLoop, calls=%fused_computation.35 | loop fusion | flops 1048576 | bytes 8388608 | tf_op jit(solution)/shard_map/neg | solution.py:151
  235.9 10.5 %fusion.26 = bf16[1,4,512,1024]{3,2,1,0:T(8,128)(2,1)} fusion(bf16[4,2,512,512]{3,2,1,0:T(8,128)(2,1)} %dynamic-slice_dynamic-update-slice_fusion, bf16[4,1,512,512]{3,2,1,0:T(8,128)(2,1)} %get-tuple-element.12, bf16[4,1,512,512]{3,2,1,0:T(8,128)(2,1)S(1)} %get-tuple-element.11, bf16[4,2,512,512]{3,2,1,0:T(8,128)(2,1)} %constant_dynamic-update-slice_fusion.1, ...), kind=kOutput, calls=%fused_computation.30 | convolution fusion | flops 4326424576 | bytes 16777218 | tf_op jit(solution)/shard_map/fpsi,fpsj->fij/dot_general | solution.py:153
  246.4 2.6 broadcast_select_fusion
  249.1 1.6 slice_negate_fusion.1
  250.7 8.2 %fusion.24 = bf16[1,4,512,1024]{3,2,1,0:T(8,128)(2,1)S(1)} fusion(bf16[4,1,512,512]{3,2,1,0:T(8,128)(2,1)} %get-tuple-element.10, bf16[4,1,512,512]{3,2,1,0:T(8,128)(2,1)S(1)} %get-tuple-element.9, bf16[4,2,512,512]{3,2,1,0:T(8,128)(2,1)S(1)} %broadcast_select_fusion, bf16[4,2,512,512]{3,2,1,0:T(8,128)(2,1)} %dynamic-slice_dynamic-update-slice_fusion, ...), kind=kOutput, calls=%fused_computation.28 | convolution fusion | flops 4328521728 | bytes 20971524 | tf_op jit(solution)/shard_map/fpsi,fpsj->fij/dot_general | solution.py:153
  258.9 5.5 %pad_maximum_fusion = bf16[3,4,512,1024]{3,2,1,0:T(8,128)(2,1)} fusion(bf16[1,4,512,1024]{3,2,1,0:T(8,128)(2,1)S(1)} %copy-done, bf16[1,4,512,1024]{3,2,1,0:T(8,128)(2,1)S(1)} %fusion.24, bf16[1,4,512,1024]{3,2,1,0:T(8,128)(2,1)S(1)} %fusion.22), kind=kLoop, calls=%fused_computation | loop fusion | flops 12582912 | bytes 25165824 | tf_op jit(solution)/shard_map/stack | solution.py:178
  (19 shorter events, 3.4 us)
Async XLA Ops:
  38.2 55.1 %all-to-all-start = ((bf16[32,2,64,512]{3,1,2,0:T(2,128)(2,1)}), bf16[32,2,64,512]{3,1,2,0:T(2,128)(2,1)}, u32[]{:S(2)}, u32[]{:S(2)}) async-start(bf16[32,2,64,512]{3,1,2,0:T(2,128)(2,1)} %bitcast.65), calls=%async_computation | async-start | bytes 8388608 | tf_op jit(solution)/shard_map/all_to_all | solution.py:129
  101.8 94.8 %collective-permute-start = (bf16[4,2,256,512]{3,2,1,0:T(8,128)(2,1)S(1)}, bf16[4,2,256,512]{3,2,1,0:T(8,128)(2,1)}, u32[]{:S(2)}, u32[]{:S(2)}) collective-permute-start(bf16[4,2,256,512]{3,2,1,0:T(8,128)(2,1)S(1)} %get-tuple-element.6), channel_id=1, source_target_pairs={{16,0},{24,8},{32,16},{40,24},{48,32},{56,40},{64,48},{72,56},{80,... | collective-permute-start | bytes 6291464 | tf_op jit(solution)/shard_map/ppermute | solution.py:22
  108.7 92.2 %collective-permute-start.1 = (bf16[4,2,64,512]{3,2,1,0:T(8,128)(2,1)S(1)}, bf16[4,2,64,512]{3,2,1,0:T(8,128)(2,1)S(1)}, u32[]{:S(2)}, u32[]{:S(2)}) collective-permute-start(bf16[4,2,64,512]{3,2,1,0:T(8,128)(2,1)S(1)} %bitcast.69), channel_id=1, source_target_pairs={{16,4},{17,5},{18,6},{19,7},{20,0},{21,1},{22,2},{23,3},{24,12},{2... | collective-permute-start | bytes 1572872 | tf_op jit(solution)/shard_map/ppermute | solution.py:127
  112.1 89.8 %collective-permute-start.2 = (bf16[4,2,64,512]{3,2,1,0:T(8,128)(2,1)S(1)}, bf16[4,2,64,512]{3,2,1,0:T(8,128)(2,1)S(1)}, u32[]{:S(2)}, u32[]{:S(2)}) collective-permute-start(bf16[4,2,64,512]{3,2,1,0:T(8,128)(2,1)S(1)} %bitcast.68), channel_id=1, source_target_pairs={{16,5},{17,4},{18,7},{19,6},{20,1},{21,0},{22,3},{23,2},{24,13},{2... | collective-permute-start | bytes 1572872 | tf_op jit(solution)/shard_map/ppermute | solution.py:127
  115.4 87.3 %collective-permute-start.3 = (bf16[4,2,64,512]{3,2,1,0:T(8,128)(2,1)S(1)}, bf16[4,2,64,512]{3,2,1,0:T(8,128)(2,1)S(1)}, u32[]{:S(2)}, u32[]{:S(2)}) collective-permute-start(bf16[4,2,64,512]{3,2,1,0:T(8,128)(2,1)S(1)} %bitcast.66), channel_id=1, source_target_pairs={{16,6},{17,7},{18,4},{19,5},{20,2},{21,3},{22,0},{23,1},{24,14},{2... | collective-permute-start | bytes 1572872 | tf_op jit(solution)/shard_map/ppermute | solution.py:127
  119.9 83.6 %collective-permute-start.4 = (bf16[4,2,64,512]{3,2,1,0:T(8,128)(2,1)S(1)}, bf16[4,2,64,512]{3,2,1,0:T(8,128)(2,1)S(1)}, u32[]{:S(2)}, u32[]{:S(2)}) collective-permute-start(bf16[4,2,64,512]{3,2,1,0:T(8,128)(2,1)S(1)} %bitcast.67), channel_id=1, source_target_pairs={{16,7},{17,6},{18,5},{19,4},{20,3},{21,2},{22,1},{23,0},{24,15},{2... | collective-permute-start | bytes 1572872 | tf_op jit(solution)/shard_map/ppermute | solution.py:127
  196.6 49.8 %collective-permute-start.6 = (bf16[4,2,512,512]{3,2,1,0:T(8,128)(2,1)}, bf16[4,2,512,512]{3,2,1,0:T(8,128)(2,1)}, u32[]{:S(2)}, u32[]{:S(2)}) collective-permute-start(bf16[4,2,512,512]{3,2,1,0:T(8,128)(2,1)} %bitcast.4), channel_id=1, source_target_pairs={{8,0},{24,16},{40,32},{56,48},{72,64},{88,80},{104,96},{120,112},{... | collective-permute-start | bytes 12582920 | tf_op jit(solution)/shard_map/ppermute | solution.py:139
  204.4 42.0 %collective-permute-start.5 = (bf16[4,2,512,512]{3,2,1,0:T(8,128)(2,1)}, bf16[4,2,512,512]{3,2,1,0:T(8,128)(2,1)}, u32[]{:S(2)}, u32[]{:S(2)}) collective-permute-start(bf16[4,2,512,512]{3,2,1,0:T(8,128)(2,1)} %constant_dynamic-update-slice_fusion.1), channel_id=1, source_target_pairs={{0,8},{16,24},{32,40},{48,56},{64,72},{80,88},{96,104},{112,120},{... | collective-permute-start | bytes 12582920 | tf_op jit(solution)/shard_map/ppermute | solution.py:140
  250.7 8.2 %copy-start = (bf16[1,4,512,1024]{3,2,1,0:T(8,128)(2,1)S(1)}, bf16[1,4,512,1024]{3,2,1,0:T(8,128)(2,1)}, u32[]{:S(2)}) copy-start(bf16[1,4,512,1024]{3,2,1,0:T(8,128)(2,1)} %fusion.26) | copy-start | bytes 12582916

commit v8 on v7

--- a/solution.py
+++ b/solution.py
@@ -117,19 +117,26 @@
     me = lax.axis_index("freq")
     side = me // half
     row = me % half
+    pieces = [lax.dynamic_index_in_dim(part, me ^ (half + gy), 0, keepdims=False) for gy in range(half)]
+    flat = part.reshape((n_freq * part.shape[1],) + part.shape[2:])
+    *pieces, flat = lax.optimization_barrier((*pieces, flat))
     crossed = []
     for gy in range(half):
         g = half + gy
-        piece = lax.dynamic_index_in_dim(part, me ^ g, 0, keepdims=False)
         pairs = [
             (c * n_freq + f, (c - 2) * n_freq + (f ^ g)) for c in range(2, n_chan) for f in range(n_freq)
         ]
-        crossed.append(lax.ppermute(piece, ("chan", "freq"), pairs))
-    flat = part.reshape((n_freq * part.shape[1],) + part.shape[2:])
+        crossed.append(lax.ppermute(pieces[gy], ("chan", "freq"), pairs))
     own_panel = lax.all_to_all(flat, "freq", split_axis=0, concat_axis=2, tiled=True)
     near = half * seg_count
     near_own = block_slice(own_panel, side * near, near)
-    near_second = from_behind(near_own, "chan", -2)
+    chan_me = lax.axis_index("chan")
+    second_chip = (chan_me // 2) % 2 == 1
+    down_z = lax.ppermute(near_own, "chan", [(c, c - 4) for c in range(4, n_chan) if (c // 2) % 2 == 0])
+    outgoing = jnp.where(second_chip, near_own, down_z)
+    across = [(c, c - 2) for c in range(n_chan) if (c // 2) % 2 == 1]
+    across += [(c, c + 2) for c in range(n_chan - 4) if (c // 2) % 2 == 0]
+    near_second = lax.ppermute(outgoing, "chan", across)
     second_panel = jnp.concatenate([near_second] + crossed, axis=2)
     far_own = [
         block_slice(own_panel, (half * (1 - side) + (row ^ gy)) * seg_count, seg_count)
@@ -141,7 +148,7 @@
     odd = lax.axis_index("chan") % 2 == 1
     upper_panel = jnp.where(odd, from_forward, from_sibling)
     upper_left = jnp.where(odd, second_left, own_panel)
-    return [own_panel, upper_left, second_left], [own_panel, upper_panel, second_panel]
+    return [own_panel, upper_left, second_left], [own_panel, upper_panel, second_panel], from_sibling
 
 
 def products_of(lefts, rights):
@@ -163,11 +170,14 @@
     whitened = per_segment.reshape(seg_count, BINS, 2, channels).transpose(1, 2, 0, 3)
     n_freq = lax.axis_size("freq")
     per_device = BINS // n_freq
-    chunks = 1
+    chunks = 2
     grouped = whitened.reshape(n_freq, chunks, per_device // chunks, 2, seg_count, channels)
     chunk_products = []
+    parts = [grouped[:, k] for k in range(chunks)]
     for k in range(chunks):
-        lefts, rights = chunk_exchange(grouped[:, k], seg_count)
+        lefts, rights, from_sibling = chunk_exchange(parts[k], seg_count)
+        if k + 1 < chunks:
+            _, parts[k + 1] = lax.optimization_barrier((from_sibling, parts[k + 1]))
         chunk_products.append(products_of(lefts, rights))
     band_limit = band_blocks[0]
     results = []

time: 266 us -> 241 us (0.906); the launches traced: 264 us -> 236 us
  waiting for transfers between devices: 124 us -> 24.4 us
  starting transfers between devices: 30.3 us -> 77 us
  blocking collectives: 0 us -> 35 us
  matrix products: 27.4 us -> 19.7 us
  other arithmetic: 19.7 us -> 17 us
    ppermute x5 -> x12, waiting for transfers between devices: 74.8 us -> 24.4 us  [the longest x2 24.4 us: chunk_exchange(): near_second = lax.ppermute(outgoing, 'chan', across)]
    all_to_all x1, waiting for transfers between devices: 49 us -> 0.01 us  [chunk_exchange(): lax.all_to_all(flat, 'freq', split_axis=0, concat_axis=2, tiled=True)]
    ppermute x5 -> x12, starting transfers between devices: 15.9 us -> 62.9 us  [the longest x8 33.4 us: chunk_exchange(): crossed.append(lax.ppermute(pieces[gy], ('chan', 'freq'), pairs))]
    all_to_all x0 -> x1, blocking collectives: none -> 35 us  [chunk_exchange(): lax.all_to_all(flat, 'freq', split_axis=0, concat_axis=2, tiled=True)]
    reshape x2 -> x1, local copies, waits for them, and re-layouts: 15.8 us -> 7.2 us  [shards(): per_segment.reshape(seg_count, BINS, 2, channels).transpose(1, 2, 0, 3)]
    dot_general x3 -> x6, matrix products: 27.4 us -> 19.7 us  [products_of(): jnp.einsum('fpsi,fpsj->fij', left_panel, both, preferred_element_type=jnp...]
    unnamed x14 -> x32, local copies, waits for them, and re-layouts: 15.3 us -> 22 us
    slice x0 -> x1, local copies, waits for them, and re-layouts: none -> 6.1 us  [shards(): parts = [grouped[:, k] for k in range(chunks)]]
  transfers between devices with their start and end apart: 8 -> 17, of which waited for: 2 -> 2; matrix products, arithmetic and copies ran while one was open for 17% -> 20% of each run, Pallas kernels for 0% -> 0%
where the time goes in v8:
time: 241 us; the launch traced here: 236 us
  starting transfers between devices  77 us (32%)
  local copies, waits for them, and re-layouts  41.7 us (17%)
  blocking collectives  35 us (15%)
  waiting for transfers between devices  24.4 us (10%)
  Pallas kernels  20 us (8%)
  matrix products  19.7 us (8%)
  other arithmetic  17 us (7%)
    all_to_all x1, blocking collectives, chunk_exchange(): lax.all_to_all(flat, 'freq', split_axis=0, concat_axis=2, tiled=True)  35 us
    ppermute x8, starting transfers between devices, chunk_exchange(): crossed.append(lax.ppermute(pieces[gy], ('chan', 'freq'), pairs))  33.4 us
    ppermute x2, starting transfers between devices, chunk_exchange(): near_second = lax.ppermute(outgoing, 'chan', across)  26.9 us
    ppermute x2, waiting for transfers between devices, chunk_exchange(): near_second = lax.ppermute(outgoing, 'chan', across)  24.4 us
    unnamed x32, local copies, waits for them, and re-layouts  22 us
    pallas_call x1, Pallas kernels, whitened_spectra(): pl.pallas_call(functools.partial(spectra_kernel, seg_count, window), out_...  20 us
    dot_general x6, matrix products, products_of(): jnp.einsum('fpsi,fpsj->fij', left_panel, both, preferred_element_type=jnp...  19.7 us
    reshape x1, local copies, waits for them, and re-layouts, shards(): per_segment.reshape(seg_count, BINS, 2, channels).transpose(1, 2, 0, 3)  7.2 us
  transfers between devices with their start and end apart: 17, of which 2 were waited for; matrix products, arithmetic and copies ran while one was open for 20% of the time, Pallas kernels for 0%

profile of v8, /device:TPU:34, one launch (start us, length us, event | category | flops | bytes accessed | tf_op | source)
XLA Modules:
  0.0 236.0 jit_solution(9938939112645084274)
XLA Ops:
  2.3 20.0 %shard_map.46 = bf16[64,64,512]{2,1,0:T(8,128)(2,1)} custom-call(s32[64]{0:T(128)} %offs_ref.1, f32[64,384]{1,0:T(8,128)} %pad_convert_fusion.dft_ref, f32[1,512]{1,0:T(1,128)} %bitcast.117, bf16[8448,512]{1,0:T(8,128)(2,1)} %rec_hbm.1), custom_call_target="tpu_custom_call" | custom-call | flops 1610612736 | bytes 29360128 | tf_op jit(solution)/shard_map/pallas_call | solution.py:70
  22.4 7.2 %reshape.167 = bf16[64,32,2,512]{3,2,1,0:T(2,128)(2,1)} reshape(bf16[64,64,512]{2,1,0:T(8,128)(2,1)} %shard_map.46) | data formatting | bytes 8388608 | tf_op jit(solution)/shard_map/reshape | solution.py:170
  29.6 6.1 %fusion.94 = (bf16[8,1,2,2,64,512]{5,3,2,1,0,4:T(2,128)(2,1)}, bf16[8,1,2,2,64,512]{5,3,2,1,0,4:T(2,128)(2,1)S(1)}) fusion(bf16[8,2,2,2,64,512]{5,3,2,1,0,4:T(2,128)(2,1)} %bitcast.112), kind=kLoop, calls=%fused_computation.128 | loop fusion | bytes 8388608 | tf_op jit(solution)/shard_map/slice | solution.py:176
  37.8 35.0 %all_to_all.36 = bf16[16,2,64,512]{3,2,1,0:T(8,128)(2,1)S(1)} all-to-all(bf16[16,2,64,512]{3,2,1,0:T(8,128)(2,1)S(1)} %bitcast.115), channel_id=1, replica_groups=mesh['chan'=16,'freq'=8] {'freq'}, dimensions={0} | all-to-all | bytes 4194304 | tf_op jit(solution)/shard_map/all_to_all | solution.py:130
  75.5 1.7 collective-permute-start.1
  77.2 2.2 collective-permute-start.3
  79.4 2.8 %collective-permute-start.4 = (bf16[2,2,64,512]{3,2,1,0:T(8,128)(2,1)}, bf16[2,2,64,512]{3,2,1,0:T(8,128)(2,1)}, u32[]{:S(2)}, u32[]{:S(2)}) collective-permute-start(bf16[2,2,64,512]{3,2,1,0:T(8,128)(2,1)} %get-tuple-element.20), channel_id=1, source_target_pairs={{16,5},{17,4},{18,7},{19,6},{20,1},{21,0},{22,3},{23,2},{24,13},{2... | collective-permute-start | bytes 786440 | tf_op jit(solution)/shard_map/ppermute | solution.py:129
  82.2 3.6 %collective-permute-start.5 = (bf16[2,2,64,512]{3,2,1,0:T(8,128)(2,1)}, bf16[2,2,64,512]{3,2,1,0:T(8,128)(2,1)}, u32[]{:S(2)}, u32[]{:S(2)}) collective-permute-start(bf16[2,2,64,512]{3,2,1,0:T(8,128)(2,1)} %get-tuple-element.21), channel_id=1, source_target_pairs={{16,6},{17,7},{18,4},{19,5},{20,2},{21,3},{22,0},{23,1},{24,14},{2... | collective-permute-start | bytes 786440 | tf_op jit(solution)/shard_map/ppermute | solution.py:129
  86.6 4.1 %copy.38 = bf16[8,1,2,2,64,512]{5,4,3,2,0,1:T(8,128)(2,1)} copy(bf16[8,1,2,2,64,512]{5,3,2,1,0,4:T(2,128)(2,1)} %get-tuple-element.31) | data formatting | bytes 4194304
  92.9 11.4 %collective-permute-start.6 = (bf16[2,2,64,512]{3,2,1,0:T(8,128)(2,1)S(1)}, bf16[2,2,64,512]{3,2,1,0:T(8,128)(2,1)}, u32[]{:S(2)}, u32[]{:S(2)}) collective-permute-start(bf16[2,2,64,512]{3,2,1,0:T(8,128)(2,1)S(1)} %get-tuple-element.22), channel_id=1, source_target_pairs={{16,7},{17,6},{18,5},{19,4},{20,3},{21,2},{22,1},{23,0},{24,15},{2... | collective-permute-start | bytes 786440 | tf_op jit(solution)/shard_map/ppermute | solution.py:129
  105.4 3.7 %collective-permute-start.2 = (bf16[2,2,256,512]{3,2,1,0:T(8,128)(2,1)}, bf16[2,2,256,512]{3,2,1,0:T(8,128)(2,1)S(1)}, u32[]{:S(2)}, u32[]{:S(2)}) collective-permute-start(bf16[2,2,256,512]{3,2,1,0:T(8,128)(2,1)} %broadcast_select_fusion.3), channel_id=1, source_target_pairs={{16,0},{24,8},{48,32},{56,40},{80,64},{88,72},{112,96},{120,104},{... | collective-permute-start | bytes 3145736 | tf_op jit(solution)/shard_map/ppermute | solution.py:139
  110.1 4.4 %all-to-all-start.1 = ((bf16[16,2,64,512]{3,2,1,0:T(8,128)(2,1)}), bf16[16,2,64,512]{3,2,1,0:T(8,128)(2,1)}, u32[]{:S(2)}, u32[]{:S(2)}) async-start(bf16[16,2,64,512]{3,2,1,0:T(8,128)(2,1)} %bitcast.113), calls=%async_computation.1 | async-start | bytes 4194304 | tf_op jit(solution)/shard_map/all_to_all | solution.py:130
  115.2 5.3 %fusion.58 = bf16[1,2,512,1024]{3,2,1,0:T(8,128)(2,1)} fusion(bf16[2,2,512,512]{3,2,1,0:T(8,128)(2,1)S(1)} %bitcast.99, bf16[2,1,512,512]{3,2,1,0:T(8,128)(2,1)} %get-tuple-element.34, bf16[2,1,512,512]{3,2,1,0:T(8,128)(2,1)} %get-tuple-element.33), kind=kOutput, calls=%fused_computation.59 | convolution fusion | flops 2162163712 | bytes 6291456 | tf_op jit(solution)/shard_map/fpsi,fpsj->fij/dot_general | solution.py:160
  122.0 11.0 %collective-permute-done.2 = bf16[2,2,256,512]{3,2,1,0:T(8,128)(2,1)S(1)} collective-permute-done((bf16[2,2,256,512]{3,2,1,0:T(8,128)(2,1)}, bf16[2,2,256,512]{3,2,1,0:T(8,128)(2,1)S(1)}, u32[]{:S(2)}, u32[]{:S(2)}) %collective-permute-start.2) | collective-permute-done | bytes 1048608 | tf_op jit(solution)/shard_map/ppermute | solution.py:139
  133.0 3.4 %collective-permute-start.10 = (bf16[2,2,64,512]{3,2,1,0:T(8,128)(2,1)}, bf16[2,2,64,512]{3,2,1,0:T(8,128)(2,1)}, u32[]{:S(2)}, u32[]{:S(2)}) collective-permute-start(bf16[2,2,64,512]{3,2,1,0:T(8,128)(2,1)} %get-tuple-element.23), channel_id=1, source_target_pairs={{16,4},{17,5},{18,6},{19,7},{20,0},{21,1},{22,2},{23,3},{24,12},{2... | collective-permute-start | bytes 786440 | tf_op jit(solution)/shard_map/ppermute | solution.py:129
  137.4 1.9 collective-permute-start.11
  141.0 6.2 %collective-permute-start.12 = (bf16[2,2,64,512]{3,2,1,0:T(8,128)(2,1)}, bf16[2,2,64,512]{3,2,1,0:T(8,128)(2,1)}, u32[]{:S(2)}, u32[]{:S(2)}) collective-permute-start(bf16[2,2,64,512]{3,2,1,0:T(8,128)(2,1)} %get-tuple-element.25), channel_id=1, source_target_pairs={{16,6},{17,7},{18,4},{19,5},{20,2},{21,3},{22,0},{23,1},{24,14},{2... | collective-permute-start | bytes 786440 | tf_op jit(solution)/shard_map/ppermute | solution.py:129
  148.9 1.7 constant_dynamic-update-slice_fusion.2
  152.2 3.7 %collective-permute-start.7 = (bf16[2,2,512,512]{3,2,1,0:T(8,128)(2,1)}, bf16[2,2,512,512]{3,2,1,0:T(8,128)(2,1)}, u32[]{:S(2)}, u32[]{:S(2)}) collective-permute-start(bf16[2,2,512,512]{3,2,1,0:T(8,128)(2,1)} %constant_dynamic-update-slice_fusion.1), channel_id=1, source_target_pairs={{0,8},{16,24},{32,40},{48,56},{64,72},{80,88},{96,104},{112,120},{... | collective-permute-start | bytes 6291464 | tf_op jit(solution)/shard_map/ppermute | solution.py:147
  155.9 2.6 %slice_negate_fusion.1 = (bf16[2,1,512,512]{3,2,1,0:T(8,128)(2,1)S(1)}, bf16[2,1,512,512]{3,2,1,0:T(8,128)(2,1)}) fusion(bf16[2,2,512,512]{3,2,1,0:T(8,128)(2,1)} %constant_dynamic-update-slice_fusion.1), kind=kLoop, calls=%fused_computation.66 | loop fusion | flops 524288 | bytes 4194304 | tf_op jit(solution)/shard_map/neg | solution.py:158
  158.6 1.8 copy.17
  162.3 4.0 %fusion.64 = bf16[1,2,512,1024]{3,2,1,0:T(8,128)(2,1)S(1)} fusion(bf16[2,2,512,512]{3,2,1,0:T(8,128)(2,1)S(1)} %copy-done.3, bf16[2,1,512,512]{3,2,1,0:T(8,128)(2,1)S(1)} %copy-done.2, bf16[2,1,512,512]{3,2,1,0:T(8,128)(2,1)S(1)} %get-tuple-element.41, bf16[2,2,512,512]{3,2,1,0:T(8,128)(2,1)} %constant_dynamic-update-slice_fusion.1), kind=kOutput, calls=%fused_computation.61 | convolution fusion | flops 2162163712 | bytes 8388608 | tf_op jit(solution)/shard_map/fpsi,fpsj->fij/dot_general | solution.py:160
  167.8 23.2 %collective-permute-start.9 = (bf16[2,2,256,512]{3,2,1,0:T(8,128)(2,1)S(1)}, bf16[2,2,256,512]{3,2,1,0:T(8,128)(2,1)S(1)}, u32[]{:S(2)}, u32[]{:S(2)}) collective-permute-start(bf16[2,2,256,512]{3,2,1,0:T(8,128)(2,1)S(1)} %broadcast_select_fusion.2), channel_id=1, source_target_pairs={{16,0},{24,8},{48,32},{56,40},{80,64},{88,72},{112,96},{120,104},{... | collective-permute-start | bytes 3145736 | tf_op jit(solution)/shard_map/ppermute | solution.py:139
  191.1 2.6 %fusion.61 = bf16[1,2,512,1024]{3,2,1,0:T(8,128)(2,1)S(1)} fusion(bf16[2,2,512,512]{3,2,1,0:T(8,128)(2,1)S(1)} %bitcast.109, bf16[2,1,512,512]{3,2,1,0:T(8,128)(2,1)S(1)} %get-tuple-element.36, bf16[2,1,512,512]{3,2,1,0:T(8,128)(2,1)S(1)} %get-tuple-element.35), kind=kOutput, calls=%fused_computation.60 | convolution fusion | flops 2162163712 | bytes 6291456 | tf_op jit(solution)/shard_map/fpsi,fpsj->fij/dot_general | solution.py:160
  194.7 1.9 collective-permute-start.13
  196.6 1.8 broadcast_select_fusion.1
  198.4 13.4 %collective-permute-done.9 = bf16[2,2,256,512]{3,2,1,0:T(8,128)(2,1)S(1)} collective-permute-done((bf16[2,2,256,512]{3,2,1,0:T(8,128)(2,1)S(1)}, bf16[2,2,256,512]{3,2,1,0:T(8,128)(2,1)S(1)}, u32[]{:S(2)}, u32[]{:S(2)}) %collective-permute-start.9) | collective-permute-done | bytes 1048608 | tf_op jit(solution)/shard_map/ppermute | solution.py:139
  216.2 3.5 %collective-permute-start.14 = (bf16[2,2,512,512]{3,2,1,0:T(8,128)(2,1)S(1)}, bf16[2,2,512,512]{3,2,1,0:T(8,128)(2,1)S(1)}, u32[]{:S(2)}, u32[]{:S(2)}) collective-permute-start(bf16[2,2,512,512]{3,2,1,0:T(8,128)(2,1)S(1)} %constant_dynamic-update-slice_fusion.7), channel_id=1, source_target_pairs={{0,8},{16,24},{32,40},{48,56},{64,72},{80,88},{96,104},{112,120},{... | collective-permute-start | bytes 6291464 | tf_op jit(solution)/shard_map/ppermute | solution.py:147
  219.8 2.6 %fusion.70 = bf16[1,2,512,1024]{3,2,1,0:T(8,128)(2,1)S(1)} fusion(bf16[2,1,512,512]{3,2,1,0:T(8,128)(2,1)S(1)} %get-tuple-element.38, bf16[2,1,512,512]{3,2,1,0:T(8,128)(2,1)S(1)} %get-tuple-element.37, bf16[2,2,512,512]{3,2,1,0:T(8,128)(2,1)S(1)} %broadcast_select_fusion.1, bf16[2,2,512,512]{3,2,1,0:T(8,128)(2,1)S(1)} %copy-done.3, ...), kind=kOutput, calls=%fused_computation.63 | convolution fusion | flops 2163212288 | bytes 10485761 | tf_op jit(solution)/shard_map/fpsi,fpsj->fij/dot_general | solution.py:160
  224.1 2.6 %fusion.67 = bf16[1,2,512,1024]{3,2,1,0:T(8,128)(2,1)S(1)} fusion(bf16[2,2,512,512]{3,2,1,0:T(8,128)(2,1)S(1)} %copy-done.5, bf16[2,1,512,512]{3,2,1,0:T(8,128)(2,1)S(1)} %get-tuple-element.44, bf16[2,1,512,512]{3,2,1,0:T(8,128)(2,1)S(1)} %get-tuple-element.43, bf16[2,2,512,512]{3,2,1,0:T(8,128)(2,1)S(1)} %constant_dynamic-update-slice_fusion.7), kind=kOutput, calls=%fused_computation.62 | convolution fusion | flops 2162163712 | bytes 8388608 | tf_op jit(solution)/shard_map/fpsi,fpsj->fij/dot_general | solution.py:160
  227.5 2.6 %fusion.75 = bf16[1,2,512,1024]{3,2,1,0:T(8,128)(2,1)S(1)} fusion(bf16[2,1,512,512]{3,2,1,0:T(8,128)(2,1)S(1)} %get-tuple-element.40, bf16[2,1,512,512]{3,2,1,0:T(8,128)(2,1)S(1)} %get-tuple-element.39, bf16[2,2,512,512]{3,2,1,0:T(8,128)(2,1)S(1)} %broadcast_select_fusion, bf16[2,2,512,512]{3,2,1,0:T(8,128)(2,1)S(1)} %copy-done.5, ...), kind=kOutput, calls=%fused_computation.64 | convolution fusion | flops 2163212288 | bytes 10485761 | tf_op jit(solution)/shard_map/fpsi,fpsj->fij/dot_general | solution.py:160
  230.6 5.5 %pad_maximum_fusion = bf16[3,4,512,1024]{3,2,1,0:T(8,128)(2,1)} fusion(bf16[1,4,512,1024]{3,2,1,0:T(8,128)(2,1)S(1)} %maximum_multiply_fusion.2, bf16[1,4,512,1024]{3,2,1,0:T(8,128)(2,1)S(1)} %maximum_multiply_fusion.1, bf16[1,4,512,1024]{3,2,1,0:T(8,128)(2,1)S(1)} %maximum_multiply_fusion), kind=kLoop, calls=%fused_computation | loop fusion | flops 12582912 | bytes 25165824 | tf_op jit(solution)/shard_map/stack | solution.py:188
  (72 shorter events, 31.3 us)
Async XLA Ops:
  73.0 32.4 %collective-permute-start = (bf16[2,2,512,512]{3,2,1,0:T(8,128)(2,1)S(1)}, bf16[2,2,512,512]{3,2,1,0:T(8,128)(2,1)}, u32[]{:S(2)}, u32[]{:S(2)}) collective-permute-start(bf16[2,2,512,512]{3,2,1,0:T(8,128)(2,1)S(1)} %bitcast.94), channel_id=1, source_target_pairs={{8,0},{24,16},{40,32},{56,48},{72,64},{88,80},{104,96},{120,112},{... | collective-permute-start | bytes 6291464 | tf_op jit(solution)/shard_map/ppermute | solution.py:146
  75.5 17.4 %collective-permute-start.1 = (bf16[2,2,256,512]{3,2,1,0:T(8,128)(2,1)S(1)}, bf16[2,2,256,512]{3,2,1,0:T(8,128)(2,1)}, u32[]{:S(2)}, u32[]{:S(2)}) collective-permute-start(bf16[2,2,256,512]{3,2,1,0:T(8,128)(2,1)S(1)} %get-tuple-element.28), channel_id=1, source_target_pairs={{32,0},{40,8},{64,32},{72,40},{96,64},{104,72},{33,1},{41,9},{65,3... | collective-permute-start | bytes 3145736 | tf_op jit(solution)/shard_map/ppermute | solution.py:135
  77.2 60.2 %collective-permute-start.3 = (bf16[2,2,64,512]{3,2,1,0:T(8,128)(2,1)}, bf16[2,2,64,512]{3,2,1,0:T(8,128)(2,1)}, u32[]{:S(2)}, u32[]{:S(2)}) collective-permute-start(bf16[2,2,64,512]{3,2,1,0:T(8,128)(2,1)} %get-tuple-element.19), channel_id=1, source_target_pairs={{16,4},{17,5},{18,6},{19,7},{20,0},{21,1},{22,2},{23,3},{24,12},{2... | collective-permute-start | bytes 786440 | tf_op jit(solution)/shard_map/ppermute | solution.py:129
  79.4 61.6 %collective-permute-start.4 = (bf16[2,2,64,512]{3,2,1,0:T(8,128)(2,1)}, bf16[2,2,64,512]{3,2,1,0:T(8,128)(2,1)}, u32[]{:S(2)}, u32[]{:S(2)}) collective-permute-start(bf16[2,2,64,512]{3,2,1,0:T(8,128)(2,1)} %get-tuple-element.20), channel_id=1, source_target_pairs={{16,5},{17,4},{18,7},{19,6},{20,1},{21,0},{22,3},{23,2},{24,13},{2... | collective-permute-start | bytes 786440 | tf_op jit(solution)/shard_map/ppermute | solution.py:129
  82.2 66.7 %collective-permute-start.5 = (bf16[2,2,64,512]{3,2,1,0:T(8,128)(2,1)}, bf16[2,2,64,512]{3,2,1,0:T(8,128)(2,1)}, u32[]{:S(2)}, u32[]{:S(2)}) collective-permute-start(bf16[2,2,64,512]{3,2,1,0:T(8,128)(2,1)} %get-tuple-element.21), channel_id=1, source_target_pairs={{16,6},{17,7},{18,4},{19,5},{20,2},{21,3},{22,0},{23,1},{24,14},{2... | collective-permute-start | bytes 786440 | tf_op jit(solution)/shard_map/ppermute | solution.py:129
  92.9 16.2 %copy-start = (bf16[8,1,2,2,64,512]{5,4,3,2,0,1:T(8,128)(2,1)S(1)}, bf16[8,1,2,2,64,512]{5,4,3,2,0,1:T(8,128)(2,1)}, u32[]{:S(2)}) copy-start(bf16[8,1,2,2,64,512]{5,4,3,2,0,1:T(8,128)(2,1)} %copy.38) | copy-start | bytes 6291460
  92.9 57.7 %collective-permute-start.6 = (bf16[2,2,64,512]{3,2,1,0:T(8,128)(2,1)S(1)}, bf16[2,2,64,512]{3,2,1,0:T(8,128)(2,1)}, u32[]{:S(2)}, u32[]{:S(2)}) collective-permute-start(bf16[2,2,64,512]{3,2,1,0:T(8,128)(2,1)S(1)} %get-tuple-element.22), channel_id=1, source_target_pairs={{16,7},{17,6},{18,5},{19,4},{20,3},{21,2},{22,1},{23,0},{24,15},{2... | collective-permute-start | bytes 786440 | tf_op jit(solution)/shard_map/ppermute | solution.py:129
  105.4 27.6 %collective-permute-start.2 = (bf16[2,2,256,512]{3,2,1,0:T(8,128)(2,1)}, bf16[2,2,256,512]{3,2,1,0:T(8,128)(2,1)S(1)}, u32[]{:S(2)}, u32[]{:S(2)}) collective-permute-start(bf16[2,2,256,512]{3,2,1,0:T(8,128)(2,1)} %broadcast_select_fusion.3), channel_id=1, source_target_pairs={{16,0},{24,8},{48,32},{56,40},{80,64},{88,72},{112,96},{120,104},{... | collective-permute-start | bytes 3145736 | tf_op jit(solution)/shard_map/ppermute | solution.py:139
  110.1 48.4 %all-to-all-start.1 = ((bf16[16,2,64,512]{3,2,1,0:T(8,128)(2,1)}), bf16[16,2,64,512]{3,2,1,0:T(8,128)(2,1)}, u32[]{:S(2)}, u32[]{:S(2)}) async-start(bf16[16,2,64,512]{3,2,1,0:T(8,128)(2,1)} %bitcast.113), calls=%async_computation.1 | async-start | bytes 4194304 | tf_op jit(solution)/shard_map/all_to_all | solution.py:130
  133.0 80.2 %collective-permute-start.10 = (bf16[2,2,64,512]{3,2,1,0:T(8,128)(2,1)}, bf16[2,2,64,512]{3,2,1,0:T(8,128)(2,1)}, u32[]{:S(2)}, u32[]{:S(2)}) collective-permute-start(bf16[2,2,64,512]{3,2,1,0:T(8,128)(2,1)} %get-tuple-element.23), channel_id=1, source_target_pairs={{16,4},{17,5},{18,6},{19,7},{20,0},{21,1},{22,2},{23,3},{24,12},{2... | collective-permute-start | bytes 786440 | tf_op jit(solution)/shard_map/ppermute | solution.py:129
  137.4 76.8 %collective-permute-start.11 = (bf16[2,2,64,512]{3,2,1,0:T(8,128)(2,1)}, bf16[2,2,64,512]{3,2,1,0:T(8,128)(2,1)}, u32[]{:S(2)}, u32[]{:S(2)}) collective-permute-start(bf16[2,2,64,512]{3,2,1,0:T(8,128)(2,1)} %get-tuple-element.24), channel_id=1, source_target_pairs={{16,5},{17,4},{18,7},{19,6},{20,1},{21,0},{22,3},{23,2},{24,13},{2... | collective-permute-start | bytes 786440 | tf_op jit(solution)/shard_map/ppermute | solution.py:129
  141.0 74.2 %collective-permute-start.12 = (bf16[2,2,64,512]{3,2,1,0:T(8,128)(2,1)}, bf16[2,2,64,512]{3,2,1,0:T(8,128)(2,1)}, u32[]{:S(2)}, u32[]{:S(2)}) collective-permute-start(bf16[2,2,64,512]{3,2,1,0:T(8,128)(2,1)} %get-tuple-element.25), channel_id=1, source_target_pairs={{16,6},{17,7},{18,4},{19,5},{20,2},{21,3},{22,0},{23,1},{24,14},{2... | collective-permute-start | bytes 786440 | tf_op jit(solution)/shard_map/ppermute | solution.py:129
  152.2 41.9 %collective-permute-start.7 = (bf16[2,2,512,512]{3,2,1,0:T(8,128)(2,1)}, bf16[2,2,512,512]{3,2,1,0:T(8,128)(2,1)}, u32[]{:S(2)}, u32[]{:S(2)}) collective-permute-start(bf16[2,2,512,512]{3,2,1,0:T(8,128)(2,1)} %constant_dynamic-update-slice_fusion.1), channel_id=1, source_target_pairs={{0,8},{16,24},{32,40},{48,56},{64,72},{80,88},{96,104},{112,120},{... | collective-permute-start | bytes 6291464 | tf_op jit(solution)/shard_map/ppermute | solution.py:147
  160.4 1.2 copy-start.2
  160.4 1.9 copy-start.3
  160.6 7.2 %collective-permute-start.8 = (bf16[2,2,256,512]{3,2,1,0:T(8,128)(2,1)S(1)}, bf16[2,2,256,512]{3,2,1,0:T(8,128)(2,1)S(1)}, u32[]{:S(2)}, u32[]{:S(2)}) collective-permute-start(bf16[2,2,256,512]{3,2,1,0:T(8,128)(2,1)S(1)} %get-tuple-element.30), channel_id=1, source_target_pairs={{32,0},{40,8},{64,32},{72,40},{96,64},{104,72},{33,1},{41,9},{65,3... | collective-permute-start | bytes 3145736 | tf_op jit(solution)/shard_map/ppermute | solution.py:135
  166.4 1.3 copy-start.4
  167.8 44.0 %collective-permute-start.9 = (bf16[2,2,256,512]{3,2,1,0:T(8,128)(2,1)S(1)}, bf16[2,2,256,512]{3,2,1,0:T(8,128)(2,1)S(1)}, u32[]{:S(2)}, u32[]{:S(2)}) collective-permute-start(bf16[2,2,256,512]{3,2,1,0:T(8,128)(2,1)S(1)} %broadcast_select_fusion.2), channel_id=1, source_target_pairs={{16,0},{24,8},{48,32},{56,40},{80,64},{88,72},{112,96},{120,104},{... | collective-permute-start | bytes 3145736 | tf_op jit(solution)/shard_map/ppermute | solution.py:139
  191.1 2.6 %copy-start.1 = (bf16[1,2,512,1024]{3,2,1,0:T(8,128)(2,1)S(1)}, bf16[1,2,512,1024]{3,2,1,0:T(8,128)(2,1)}, u32[]{:S(2)}) copy-start(bf16[1,2,512,1024]{3,2,1,0:T(8,128)(2,1)} %fusion.58) | copy-start | bytes 6291460
  193.7 1.0 copy-start.6
  194.7 21.5 %collective-permute-start.13 = (bf16[2,2,64,512]{3,2,1,0:T(8,128)(2,1)S(1)}, bf16[2,2,64,512]{3,2,1,0:T(8,128)(2,1)S(1)}, u32[]{:S(2)}, u32[]{:S(2)}) collective-permute-start(bf16[2,2,64,512]{3,2,1,0:T(8,128)(2,1)S(1)} %copy-done.6), channel_id=1, source_target_pairs={{16,7},{17,6},{18,5},{19,4},{20,3},{21,2},{22,1},{23,0},{24,15},{2... | collective-permute-start | bytes 786440 | tf_op jit(solution)/shard_map/ppermute | solution.py:129
  211.8 15.3 %collective-permute-start.15 = (bf16[2,2,512,512]{3,2,1,0:T(8,128)(2,1)S(1)}, bf16[2,2,512,512]{3,2,1,0:T(8,128)(2,1)S(1)}, u32[]{:S(2)}, u32[]{:S(2)}) collective-permute-start(bf16[2,2,512,512]{3,2,1,0:T(8,128)(2,1)S(1)} %bitcast.110), channel_id=1, source_target_pairs={{8,0},{24,16},{40,32},{56,48},{72,64},{88,80},{104,96},{120,112},{... | collective-permute-start | bytes 6291464 | tf_op jit(solution)/shard_map/ppermute | solution.py:146
  216.2 10.9 %collective-permute-start.14 = (bf16[2,2,512,512]{3,2,1,0:T(8,128)(2,1)S(1)}, bf16[2,2,512,512]{3,2,1,0:T(8,128)(2,1)S(1)}, u32[]{:S(2)}, u32[]{:S(2)}) collective-permute-start(bf16[2,2,512,512]{3,2,1,0:T(8,128)(2,1)S(1)} %constant_dynamic-update-slice_fusion.7), channel_id=1, source_target_pairs={{0,8},{16,24},{32,40},{48,56},{64,72},{80,88},{96,104},{112,120},{... | collective-permute-start | bytes 6291464 | tf_op jit(solution)/shard_map/ppermute | solution.py:147
  222.5 1.6 copy-start.5

commit v9 on v6

--- a/solution.py
+++ b/solution.py
@@ -122,7 +122,7 @@
     whitened = per_segment.reshape(seg_count, BINS, 2, channels).transpose(1, 2, 0, 3)
     n_freq = lax.axis_size("freq")
     per_device = BINS // n_freq
-    chunks = 4
+    chunks = 2
     grouped = whitened.reshape(n_freq, chunks, per_device // chunks, 2, seg_count, channels)
     parts = [grouped[:, k].reshape(BINS // chunks, 2, seg_count, channels) for k in range(chunks)]
     chunk_products = []

time: 216 us -> 216 us (level)
  starting transfers between devices: 41.3 us -> 18.7 us
  waiting for transfers between devices: 69.9 us -> 89.6 us
  matrix products: 30.2 us -> 17 us
  blocking collectives: 22.8 us -> 34.5 us
  local copies, waits for them, and re-layouts: 10.7 us -> 19.4 us
  other arithmetic: 17.6 us -> 12.9 us
    dot_general x12 -> x6, matrix products: 30.2 us -> 17 us  [local_products(): jnp.einsum('fpsi,fpsj->fij', left_panel, both, preferred_element_type=jnp...]
    all_to_all x1, blocking collectives: 22.8 us -> 34.5 us  [shards(): lax.all_to_all(parts[k], 'freq', split_axis=0, concat_axis=2, tiled=True)]
    all_to_all x3 -> x1, waiting for transfers between devices: 7.12 us -> 17.1 us  [shards(): lax.all_to_all(parts[k], 'freq', split_axis=0, concat_axis=2, tiled=True)]
    ppermute x4 -> x2, waiting for transfers between devices: 62.7 us -> 72.5 us  [from_behind(): return lax.ppermute(block, axis, route)]
    all_to_all x3 -> x1, starting transfers between devices: 11.1 us -> 4.35 us  [shards(): lax.all_to_all(parts[k], 'freq', split_axis=0, concat_axis=2, tiled=True)]
    ppermute x4 -> x2, starting transfers between devices: 12.2 us -> 5.58 us  [neighbour_panels(): lax.ppermute(second_panel, 'chan', [(c - 1, c) for c in range(1, n_chan,...]
    ppermute x4 -> x2, starting transfers between devices: 12.8 us -> 6.22 us  [from_behind(): return lax.ppermute(block, axis, route)]
    slice x0 -> x1, local copies, waits for them, and re-layouts: none -> 5.06 us  [shards(): grouped[:, k].reshape(BINS // chunks, 2, seg_count, channels)]
  transfers between devices with their start and end apart: 15 -> 7, of which waited for: 7 -> 3; matrix products, arithmetic and copies ran while one was open for 18% -> 11% of each run, Pallas kernels for 0% -> 0%
where the time goes in v9:
time: 216 us; the launch traced here: 213 us
  waiting for transfers between devices  89.6 us (41%)
  blocking collectives  34.5 us (16%)
  Pallas kernels  20 us (9%)
  local copies, waits for them, and re-layouts  19.4 us (9%)
  starting transfers between devices  18.7 us (9%)
  matrix products  17 us (8%)
  other arithmetic  12.9 us (6%)
    ppermute x2, waiting for transfers between devices, from_behind(): return lax.ppermute(block, axis, route)  72.5 us
    all_to_all x1, blocking collectives, shards(): lax.all_to_all(parts[k], 'freq', split_axis=0, concat_axis=2, tiled=True)  34.5 us
    pallas_call x1, Pallas kernels, whitened_spectra(): pl.pallas_call(functools.partial(spectra_kernel, seg_count, window), out_...  20 us
    all_to_all x1, waiting for transfers between devices, shards(): lax.all_to_all(parts[k], 'freq', split_axis=0, concat_axis=2, tiled=True)  17.1 us
    dot_general x6, matrix products, local_products(): jnp.einsum('fpsi,fpsj->fij', left_panel, both, preferred_element_type=jnp...  17 us
    reshape x1, local copies, waits for them, and re-layouts, shards(): per_segment.reshape(seg_count, BINS, 2, channels).transpose(1, 2, 0, 3)  7.21 us
    ppermute x2, starting transfers between devices, from_behind(): return lax.ppermute(block, axis, route)  6.22 us
    ppermute x2, starting transfers between devices, neighbour_panels(): lax.ppermute(second_panel, 'chan', [(c - 1, c) for c in range(1, n_chan,...  5.58 us
  transfers between devices with their start and end apart: 7, of which 3 were waited for; matrix products, arithmetic and copies ran while one was open for 11% of the time, Pallas kernels for 0%

profile of v9, /device:TPU:34, one launch (start us, length us, event | category | flops | bytes accessed | tf_op | source)
XLA Modules:
  0.0 213.1 jit_solution(10456677875701049485)
XLA Ops:
  0.1 1.3 convert_element_type.64
  1.7 0.7 pad_convert_fusion.dft_ref
  2.3 20.0 %shard_map.46 = bf16[64,64,512]{2,1,0:T(8,128)(2,1)} custom-call(s32[64]{0:T(128)} %offs_ref.1, f32[64,384]{1,0:T(8,128)} %pad_convert_fusion.dft_ref, f32[1,512]{1,0:T(1,128)} %bitcast.93, bf16[8448,512]{1,0:T(8,128)(2,1)} %rec_hbm.1), custom_call_target="tpu_custom_call" | custom-call | flops 1610612736 | bytes 29360128 | tf_op jit(solution)/shard_map/pallas_call | solution.py:70
  22.4 7.2 %reshape.156 = bf16[64,32,2,512]{3,2,1,0:T(2,128)(2,1)} reshape(bf16[64,64,512]{2,1,0:T(8,128)(2,1)} %shard_map.46) | data formatting | bytes 8388608 | tf_op jit(solution)/shard_map/reshape | solution.py:122
  29.6 5.1 %fusion.86 = (bf16[8,1,2,2,64,512]{5,3,2,1,0,4:T(2,128)(2,1)S(1)}, bf16[8,1,2,2,64,512]{5,3,2,1,0,4:T(2,128)(2,1)S(1)}) fusion(bf16[8,2,2,2,64,512]{5,3,2,1,0,4:T(2,128)(2,1)} %bitcast.77), kind=kLoop, calls=%fused_computation.91 | loop fusion | bytes 8388608 | tf_op jit(solution)/shard_map/slice | solution.py:127
  34.7 1.2 copy.33
  35.8 34.5 %all_to_all.36 = bf16[16,2,64,512]{3,2,1,0:T(8,128)(2,1)S(1)} all-to-all(bf16[16,2,64,512]{3,2,1,0:T(8,128)(2,1)S(1)} %bitcast.91), channel_id=1, replica_groups=mesh['chan'=16,'freq'=8] {'freq'}, dimensions={0} | all-to-all | bytes 4194304 | tf_op jit(solution)/shard_map/all_to_all | solution.py:130
  70.5 1.3 collective-permute-start
  71.8 3.3 %collective-permute-start.1 = (bf16[2,2,512,512]{3,2,1,0:T(8,128)(2,1)S(1)}, bf16[2,2,512,512]{3,2,1,0:T(8,128)(2,1)}, u32[]{:S(2)}, u32[]{:S(2)}) collective-permute-start(bf16[2,2,512,512]{3,2,1,0:T(8,128)(2,1)S(1)} %bitcast.79), channel_id=1, source_target_pairs={{16,0},{24,8},{32,16},{40,24},{48,32},{56,40},{64,48},{72,56},{80,... | collective-permute-start | bytes 6291464 | tf_op jit(solution)/shard_map/ppermute | solution.py:22
  75.1 2.5 %copy.34 = bf16[8,1,2,2,64,512]{5,4,3,2,0,1:T(8,128)(2,1)} copy(bf16[8,1,2,2,64,512]{5,3,2,1,0,4:T(2,128)(2,1)S(1)} %get-tuple-element.7) | data formatting | bytes 4194304
  77.6 1.3 copy-done
  78.9 4.4 %all-to-all-start.1 = ((bf16[16,2,64,512]{3,2,1,0:T(8,128)(2,1)}), bf16[16,2,64,512]{3,2,1,0:T(8,128)(2,1)}, u32[]{:S(2)}, u32[]{:S(2)}) async-start(bf16[16,2,64,512]{3,2,1,0:T(8,128)(2,1)} %bitcast.90), calls=%async_computation.1 | async-start | bytes 4194304 | tf_op jit(solution)/shard_map/all_to_all | solution.py:130
  84.0 1.2 slice_negate_fusion.5
  85.2 37.8 %collective-permute-done.1 = bf16[2,2,512,512]{3,2,1,0:T(8,128)(2,1)} collective-permute-done((bf16[2,2,512,512]{3,2,1,0:T(8,128)(2,1)S(1)}, bf16[2,2,512,512]{3,2,1,0:T(8,128)(2,1)}, u32[]{:S(2)}, u32[]{:S(2)}) %collective-permute-start.1) | collective-permute-done | bytes 2097184 | tf_op jit(solution)/shard_map/ppermute | solution.py:22
  123.0 3.9 %collective-permute-start.2 = (bf16[2,2,512,512]{3,2,1,0:T(8,128)(2,1)}, bf16[2,2,512,512]{3,2,1,0:T(8,128)(2,1)}, u32[]{:S(2)}, u32[]{:S(2)}) collective-permute-start(bf16[2,2,512,512]{3,2,1,0:T(8,128)(2,1)} %collective-permute-done.1), channel_id=1, source_target_pairs={{0,8},{16,24},{32,40},{48,56},{64,72},{80,88},{96,104},{112,120},{... | collective-permute-start | bytes 6291464 | tf_op jit(solution)/shard_map/ppermute | solution.py:113
  126.9 17.1 %all-to-all-done.1 = bf16[16,2,64,512]{3,2,1,0:T(8,128)(2,1)} async-done(((bf16[16,2,64,512]{3,2,1,0:T(8,128)(2,1)}), bf16[16,2,64,512]{3,2,1,0:T(8,128)(2,1)}, u32[]{:S(2)}, u32[]{:S(2)}) %all-to-all-start.1) | async-done | bytes 2097184 | tf_op jit(solution)/shard_map/all_to_all | solution.py:130
  144.0 1.9 copy.15
  145.9 3.0 %collective-permute-start.3 = (bf16[2,2,512,512]{3,2,1,0:T(8,128)(2,1)S(1)}, bf16[2,2,512,512]{3,2,1,0:T(8,128)(2,1)S(1)}, u32[]{:S(2)}, u32[]{:S(2)}) collective-permute-start(bf16[2,2,512,512]{3,2,1,0:T(8,128)(2,1)S(1)} %bitcast.84), channel_id=1, source_target_pairs={{16,0},{24,8},{32,16},{40,24},{48,32},{56,40},{64,48},{72,56},{80,... | collective-permute-start | bytes 6291464 | tf_op jit(solution)/shard_map/ppermute | solution.py:22
  148.9 2.6 %fusion.54 = bf16[1,2,512,1024]{3,2,1,0:T(8,128)(2,1)S(1)} fusion(bf16[2,2,512,512]{3,2,1,0:T(8,128)(2,1)S(1)} %bitcast.81, bf16[2,1,512,512]{3,2,1,0:T(8,128)(2,1)S(1)} %copy-done.2, bf16[2,1,512,512]{3,2,1,0:T(8,128)(2,1)S(1)} %get-tuple-element.9), kind=kOutput, calls=%fused_computation.54 | convolution fusion | flops 2162163712 | bytes 6291456 | tf_op jit(solution)/shard_map/fpsi,fpsj->fij/dot_general | solution.py:102
  151.5 1.7 slice_negate_fusion.1
  153.2 4.0 %fusion.66 = bf16[1,2,512,1024]{3,2,1,0:T(8,128)(2,1)S(1)} fusion(bf16[2,2,512,512]{3,2,1,0:T(8,128)(2,1)S(1)} %bitcast.82, bf16[2,1,512,512]{3,2,1,0:T(8,128)(2,1)S(1)} %get-tuple-element.18, bf16[2,1,512,512]{3,2,1,0:T(8,128)(2,1)S(1)} %get-tuple-element.17, bf16[2,2,512,512]{3,2,1,0:T(8,128)(2,1)} %collective-permute-done.1), kind=kOutput, calls=%fused_computation.58 | convolution fusion | flops 2162163712 | bytes 8388608 | tf_op jit(solution)/shard_map/fpsi,fpsj->fij/dot_general | solution.py:102
  157.1 1.3 collective-permute-start.5
  158.6 2.6 %fusion.57 = bf16[1,2,512,1024]{3,2,1,0:T(8,128)(2,1)S(1)} fusion(bf16[2,2,512,512]{3,2,1,0:T(8,128)(2,1)S(1)} %bitcast.87, bf16[2,1,512,512]{3,2,1,0:T(8,128)(2,1)S(1)} %get-tuple-element.12, bf16[2,1,512,512]{3,2,1,0:T(8,128)(2,1)S(1)} %get-tuple-element.11), kind=kOutput, calls=%fused_computation.55 | convolution fusion | flops 2162163712 | bytes 6291456 | tf_op jit(solution)/shard_map/fpsi,fpsj->fij/dot_general | solution.py:102
  161.2 0.4 maximum_multiply_fusion
  161.6 34.7 %collective-permute-done.3 = bf16[2,2,512,512]{3,2,1,0:T(8,128)(2,1)S(1)} collective-permute-done((bf16[2,2,512,512]{3,2,1,0:T(8,128)(2,1)S(1)}, bf16[2,2,512,512]{3,2,1,0:T(8,128)(2,1)S(1)}, u32[]{:S(2)}, u32[]{:S(2)}) %collective-permute-start.3) | collective-permute-done | bytes 2097184 | tf_op jit(solution)/shard_map/ppermute | solution.py:22
  196.3 1.6 collective-permute-start.4
  198.4 2.6 %fusion.60 = bf16[1,2,512,1024]{3,2,1,0:T(8,128)(2,1)S(1)} fusion(bf16[2,2,512,512]{3,2,1,0:T(8,128)(2,1)S(1)} %bitcast.83, bf16[2,1,512,512]{3,2,1,0:T(8,128)(2,1)S(1)} %get-tuple-element.14, bf16[2,1,512,512]{3,2,1,0:T(8,128)(2,1)S(1)} %get-tuple-element.13, bf16[2,2,512,512]{3,2,1,0:T(8,128)(2,1)S(1)} %broadcast_select_fusion.1), kind=kOutput, calls=%fused_computation.56 | convolution fusion | flops 2162163712 | bytes 8388608 | tf_op jit(solution)/shard_map/fpsi,fpsj->fij/dot_general | solution.py:102
  201.1 2.6 %fusion.69 = bf16[1,2,512,1024]{3,2,1,0:T(8,128)(2,1)S(1)} fusion(bf16[2,2,512,512]{3,2,1,0:T(8,128)(2,1)S(1)} %bitcast.88, bf16[2,1,512,512]{3,2,1,0:T(8,128)(2,1)S(1)} %get-tuple-element.20, bf16[2,1,512,512]{3,2,1,0:T(8,128)(2,1)S(1)} %get-tuple-element.19, bf16[2,2,512,512]{3,2,1,0:T(8,128)(2,1)S(1)} %collective-permute-done.3), kind=kOutput, calls=%fused_computation.59 | convolution fusion | flops 2162163712 | bytes 8388608 | tf_op jit(solution)/shard_map/fpsi,fpsj->fij/dot_general | solution.py:102
  203.7 0.4 maximum_multiply_fusion.2
  204.6 2.6 %fusion.63 = bf16[1,2,512,1024]{3,2,1,0:T(8,128)(2,1)S(1)} fusion(bf16[2,2,512,512]{3,2,1,0:T(8,128)(2,1)S(1)} %bitcast.89, bf16[2,1,512,512]{3,2,1,0:T(8,128)(2,1)S(1)} %get-tuple-element.16, bf16[2,1,512,512]{3,2,1,0:T(8,128)(2,1)S(1)} %get-tuple-element.15, bf16[2,2,512,512]{3,2,1,0:T(8,128)(2,1)S(1)} %broadcast_select_fusion), kind=kOutput, calls=%fused_computation.57 | convolution fusion | flops 2162163712 | bytes 8388608 | tf_op jit(solution)/shard_map/fpsi,fpsj->fij/dot_general | solution.py:102
  207.2 0.4 maximum_multiply_fusion.1
  207.6 5.5 %pad_maximum_fusion = bf16[3,4,512,1024]{3,2,1,0:T(8,128)(2,1)} fusion(bf16[1,4,512,1024]{3,2,1,0:T(8,128)(2,1)S(1)} %maximum_multiply_fusion.2, bf16[1,4,512,1024]{3,2,1,0:T(8,128)(2,1)S(1)} %maximum_multiply_fusion.1, bf16[1,4,512,1024]{3,2,1,0:T(8,128)(2,1)S(1)} %maximum_multiply_fusion), kind=kLoop, calls=%fused_computation | loop fusion | flops 12582912 | bytes 25165824 | tf_op jit(solution)/shard_map/stack | solution.py:141
  (20 shorter events, 1.6 us)
Async XLA Ops:
  70.5 7.1 %collective-permute-start = (bf16[2,2,512,512]{3,2,1,0:T(8,128)(2,1)S(1)}, bf16[2,2,512,512]{3,2,1,0:T(8,128)(2,1)S(1)}, u32[]{:S(2)}, u32[]{:S(2)}) collective-permute-start(bf16[2,2,512,512]{3,2,1,0:T(8,128)(2,1)S(1)} %bitcast.78), channel_id=1, source_target_pairs={{8,0},{24,16},{40,32},{56,48},{72,64},{88,80},{104,96},{120,112},{... | collective-permute-start | bytes 6291464 | tf_op jit(solution)/shard_map/ppermute | solution.py:112
  71.8 51.1 %collective-permute-start.1 = (bf16[2,2,512,512]{3,2,1,0:T(8,128)(2,1)S(1)}, bf16[2,2,512,512]{3,2,1,0:T(8,128)(2,1)}, u32[]{:S(2)}, u32[]{:S(2)}) collective-permute-start(bf16[2,2,512,512]{3,2,1,0:T(8,128)(2,1)S(1)} %bitcast.79), channel_id=1, source_target_pairs={{16,0},{24,8},{32,16},{40,24},{48,32},{56,40},{64,48},{72,56},{80,... | collective-permute-start | bytes 6291464 | tf_op jit(solution)/shard_map/ppermute | solution.py:22
  77.6 1.3 copy-start
  78.9 65.1 %all-to-all-start.1 = ((bf16[16,2,64,512]{3,2,1,0:T(8,128)(2,1)}), bf16[16,2,64,512]{3,2,1,0:T(8,128)(2,1)}, u32[]{:S(2)}, u32[]{:S(2)}) async-start(bf16[16,2,64,512]{3,2,1,0:T(8,128)(2,1)} %bitcast.90), calls=%async_computation.1 | async-start | bytes 4194304 | tf_op jit(solution)/shard_map/all_to_all | solution.py:130
  123.0 75.0 %collective-permute-start.2 = (bf16[2,2,512,512]{3,2,1,0:T(8,128)(2,1)}, bf16[2,2,512,512]{3,2,1,0:T(8,128)(2,1)}, u32[]{:S(2)}, u32[]{:S(2)}) collective-permute-start(bf16[2,2,512,512]{3,2,1,0:T(8,128)(2,1)} %collective-permute-done.1), channel_id=1, source_target_pairs={{0,8},{16,24},{32,40},{48,56},{64,72},{80,88},{96,104},{112,120},{... | collective-permute-start | bytes 6291464 | tf_op jit(solution)/shard_map/ppermute | solution.py:113
  144.0 4.9 %copy-start.2 = (bf16[2,1,512,512]{3,2,1,0:T(8,128)(2,1)S(1)}, bf16[2,1,512,512]{3,2,1,0:T(8,128)(2,1)}, u32[]{:S(2)}) copy-start(bf16[2,1,512,512]{3,2,1,0:T(8,128)(2,1)} %get-tuple-element.10) | copy-start | bytes 3145732
  145.9 50.4 %collective-permute-start.3 = (bf16[2,2,512,512]{3,2,1,0:T(8,128)(2,1)S(1)}, bf16[2,2,512,512]{3,2,1,0:T(8,128)(2,1)S(1)}, u32[]{:S(2)}, u32[]{:S(2)}) collective-permute-start(bf16[2,2,512,512]{3,2,1,0:T(8,128)(2,1)S(1)} %bitcast.84), channel_id=1, source_target_pairs={{16,0},{24,8},{32,16},{40,24},{48,32},{56,40},{64,48},{72,56},{80,... | collective-permute-start | bytes 6291464 | tf_op jit(solution)/shard_map/ppermute | solution.py:22
  157.1 47.1 %collective-permute-start.5 = (bf16[2,2,512,512]{3,2,1,0:T(8,128)(2,1)S(1)}, bf16[2,2,512,512]{3,2,1,0:T(8,128)(2,1)S(1)}, u32[]{:S(2)}, u32[]{:S(2)}) collective-permute-start(bf16[2,2,512,512]{3,2,1,0:T(8,128)(2,1)S(1)} %bitcast.85), channel_id=1, source_target_pairs={{8,0},{24,16},{40,32},{56,48},{72,64},{88,80},{104,96},{120,112},{... | collective-permute-start | bytes 6291464 | tf_op jit(solution)/shard_map/ppermute | solution.py:112
  161.2 36.8 %copy-start.1 = (bf16[2,2,512,512]{3,2,1,0:T(8,128)(2,1)S(1)}, bf16[2,2,512,512]{3,2,1,0:T(8,128)(2,1)}, u32[]{:S(2)}) copy-start(bf16[2,2,512,512]{3,2,1,0:T(8,128)(2,1)} %copy-done) | copy-start | bytes 6291460
  196.3 7.9 %collective-permute-start.4 = (bf16[2,2,512,512]{3,2,1,0:T(8,128)(2,1)S(1)}, bf16[2,2,512,512]{3,2,1,0:T(8,128)(2,1)S(1)}, u32[]{:S(2)}, u32[]{:S(2)}) collective-permute-start(bf16[2,2,512,512]{3,2,1,0:T(8,128)(2,1)S(1)} %collective-permute-done.3), channel_id=1, source_target_pairs={{0,8},{16,24},{32,40},{48,56},{64,72},{80,88},{96,104},{112,120},{... | collective-permute-start | bytes 6291464 | tf_op jit(solution)/shard_map/ppermute | solution.py:113

commit v10 on v9

--- a/solution.py
+++ b/solution.py
@@ -122,7 +122,7 @@
     whitened = per_segment.reshape(seg_count, BINS, 2, channels).transpose(1, 2, 0, 3)
     n_freq = lax.axis_size("freq")
     per_device = BINS // n_freq
-    chunks = 2
+    chunks = 1
     grouped = whitened.reshape(n_freq, chunks, per_device // chunks, 2, seg_count, channels)
     parts = [grouped[:, k].reshape(BINS // chunks, 2, seg_count, channels) for k in range(chunks)]
     chunk_products = []

time: 216 us -> 243 us (1.12); the launches traced: 213 us -> 243 us
  blocking collectives: 34.5 us -> 57.1 us
  matrix products: 17 us -> 29 us
  starting transfers between devices: 18.7 us -> 7.28 us
  other arithmetic: 12.9 us -> 22.1 us
  local copies, waits for them, and re-layouts: 19.4 us -> 16.7 us
    all_to_all x1, blocking collectives: 34.5 us -> 57.1 us  [shards(): lax.all_to_all(parts[k], 'freq', split_axis=0, concat_axis=2, tiled=True)]
    all_to_all x1 -> x0, waiting for transfers between devices: 17.1 us -> none  [shards(): lax.all_to_all(parts[k], 'freq', split_axis=0, concat_axis=2, tiled=True)]
    ppermute x2 -> x1, waiting for transfers between devices: 72.5 us -> 89.5 us  [from_behind(): return lax.ppermute(block, axis, route)]
    dot_general x6 -> x3, matrix products: 17 us -> 29 us  [local_products(): jnp.einsum('fpsi,fpsj->fij', left_panel, both, preferred_element_type=jnp...]
    reshape x1 -> x2, local copies, waits for them, and re-layouts: 7.21 us -> 13.7 us  [shards(): per_segment.reshape(seg_count, BINS, 2, channels).transpose(1, 2, 0, 3)]
    another operation x1, other arithmetic: 5.47 us -> 10.5 us  [shards(): return jnp.stack(results, axis=0)]
    slice x1 -> x0, local copies, waits for them, and re-layouts: 5.06 us -> none  [shards(): grouped[:, k].reshape(BINS // chunks, 2, seg_count, channels)]
    unnamed x8 -> x0, local copies, waits for them, and re-layouts: 4.98 us -> none
  transfers between devices with their start and end apart: 7 -> 3, of which waited for: 3 -> 1; matrix products, arithmetic and copies ran while one was open for 11% -> 10% of each run, Pallas kernels for 0% -> 0%
where the time goes in v10:
time: 243 us
  waiting for transfers between devices  89.5 us (37%)
  blocking collectives  57.1 us (23%)
  matrix products  29 us (12%)
  other arithmetic  22.1 us (9%)
  Pallas kernels  20.2 us (8%)
  local copies, waits for them, and re-layouts  16.7 us (7%)
  starting transfers between devices  7.28 us (3%)
    ppermute x1, waiting for transfers between devices, from_behind(): return lax.ppermute(block, axis, route)  89.5 us
    all_to_all x1, blocking collectives, shards(): lax.all_to_all(parts[k], 'freq', split_axis=0, concat_axis=2, tiled=True)  57.1 us
    dot_general x3, matrix products, local_products(): jnp.einsum('fpsi,fpsj->fij', left_panel, both, preferred_element_type=jnp...  29 us
    pallas_call x1, Pallas kernels, whitened_spectra(): pl.pallas_call(functools.partial(spectra_kernel, seg_count, window), out_...  20.2 us
    reshape x2, local copies, waits for them, and re-layouts, shards(): per_segment.reshape(seg_count, BINS, 2, channels).transpose(1, 2, 0, 3)  13.7 us
    another operation x1, other arithmetic, shards(): return jnp.stack(results, axis=0)  10.5 us
    neg x3, other arithmetic, local_products(): turned = jnp.stack([-right_panel[:, 1], right_panel[:, 0]], axis=1)  6.6 us
  transfers between devices with their start and end apart: 3, of which 1 were waited for; matrix products, arithmetic and copies ran while one was open for 10% of the time, Pallas kernels for 0%

profile of v10, /device:TPU:34, one launch (start us, length us, event | category | flops | bytes accessed | tf_op | source)
XLA Modules:
  0.0 242.7 jit_solution(13016973106736055937)
XLA Ops:
  0.1 0.3 multiply_convert_fusion
  0.4 0.6 pad_convert_fusion.dft_ref
  1.1 1.3 convert_element_type.49
  2.3 20.2 %shard_map.46 = bf16[64,64,512]{2,1,0:T(8,128)(2,1)} custom-call(s32[64]{0:T(128)} %offs_ref.1, f32[64,384]{1,0:T(8,128)} %pad_convert_fusion.dft_ref, f32[1,512]{1,0:T(1,128)} %bitcast.49, bf16[8448,512]{1,0:T(8,128)(2,1)} %rec_hbm.1), custom_call_target="tpu_custom_call" | custom-call | flops 1610612736 | bytes 29360128 | tf_op jit(solution)/shard_map/pallas_call | solution.py:70
  22.5 7.2 %reshape.51 = bf16[64,32,2,512]{3,2,1,0:T(2,128)(2,1)} reshape(bf16[64,64,512]{2,1,0:T(8,128)(2,1)} %shard_map.46) | data formatting | bytes 8388608 | tf_op jit(solution)/shard_map/reshape | solution.py:122
  29.7 6.5 %copy.21 = bf16[64,32,2,512]{3,2,0,1:T(2,128)(2,1)S(1)} copy(bf16[64,32,2,512]{3,2,1,0:T(2,128)(2,1)} %reshape.51) | data formatting | bytes 8388608 | tf_op jit(solution)/shard_map/reshape | solution.py:122
  36.2 57.1 %all_to_all.18 = bf16[32,2,64,512]{3,1,2,0:T(2,128)(2,1)S(1)} all-to-all(bf16[32,2,64,512]{3,1,2,0:T(2,128)(2,1)S(1)} %bitcast.47), channel_id=1, replica_groups=mesh['chan'=16,'freq'=8] {'freq'}, dimensions={0} | all-to-all | bytes 8388608 | tf_op jit(solution)/shard_map/all_to_all | solution.py:130
  93.4 3.0 %copy.10 = bf16[8,4,2,64,512]{4,3,0,2,1:T(8,128)(2,1)} copy(bf16[8,4,2,64,512]{4,2,3,1,0:T(2,128)(2,1)S(1)} %bitcast.48) | data formatting | bytes 8388608 | tf_op jit(solution)/shard_map/all_to_all | solution.py:130
  96.3 2.8 %collective-permute-start = (bf16[4,2,512,512]{3,2,1,0:T(8,128)(2,1)}, bf16[4,2,512,512]{3,2,1,0:T(8,128)(2,1)}, u32[]{:S(2)}, u32[]{:S(2)}) collective-permute-start(bf16[4,2,512,512]{3,2,1,0:T(8,128)(2,1)} %bitcast.4), channel_id=1, source_target_pairs={{16,0},{24,8},{32,16},{40,24},{48,32},{56,40},{64,48},{72,56},{80,... | collective-permute-start | bytes 12582920 | tf_op jit(solution)/shard_map/ppermute | solution.py:22
  99.1 1.3 collective-permute-start.2
  100.4 89.5 %collective-permute-done = bf16[4,2,512,512]{3,2,1,0:T(8,128)(2,1)} collective-permute-done((bf16[4,2,512,512]{3,2,1,0:T(8,128)(2,1)}, bf16[4,2,512,512]{3,2,1,0:T(8,128)(2,1)}, u32[]{:S(2)}, u32[]{:S(2)}) %collective-permute-start) | collective-permute-done | bytes 4194336 | tf_op jit(solution)/shard_map/ppermute | solution.py:22
  189.9 3.2 %collective-permute-start.1 = (bf16[4,2,512,512]{3,2,1,0:T(8,128)(2,1)}, bf16[4,2,512,512]{3,2,1,0:T(8,128)(2,1)}, u32[]{:S(2)}, u32[]{:S(2)}) collective-permute-start(bf16[4,2,512,512]{3,2,1,0:T(8,128)(2,1)} %collective-permute-done), channel_id=1, source_target_pairs={{0,8},{16,24},{32,40},{48,56},{64,72},{80,88},{96,104},{112,120},{... | collective-permute-start | bytes 12582920 | tf_op jit(solution)/shard_map/ppermute | solution.py:113
  193.8 2.5 %slice_negate_fusion.2 = (bf16[4,1,512,512]{3,2,1,0:T(8,128)(2,1)S(1)}, bf16[4,1,512,512]{3,2,1,0:T(8,128)(2,1)S(1)}) fusion(bf16[4,2,512,512]{3,2,1,0:T(8,128)(2,1)} %bitcast.4), kind=kLoop, calls=%fused_computation.35 | loop fusion | flops 1048576 | bytes 8388608 | tf_op jit(solution)/shard_map/neg | solution.py:100
  196.3 9.9 %fusion.22 = bf16[1,4,512,1024]{3,2,1,0:T(8,128)(2,1)} fusion(bf16[4,2,512,512]{3,2,1,0:T(8,128)(2,1)} %bitcast.4, bf16[4,1,512,512]{3,2,1,0:T(8,128)(2,1)S(1)} %get-tuple-element.6, bf16[4,1,512,512]{3,2,1,0:T(8,128)(2,1)S(1)} %get-tuple-element.5, bf16[]{:T(256)} %bitcast.8), kind=kOutput, calls=%fused_computation.26 | convolution fusion | flops 4326424576 | bytes 12582914 | tf_op jit(solution)/shard_map/fpsi,fpsj->fij/dot_general | solution.py:102
  206.3 2.5 %slice_negate_fusion = (bf16[4,1,512,512]{3,2,1,0:T(8,128)(2,1)S(1)}, bf16[4,1,512,512]{3,2,1,0:T(8,128)(2,1)S(1)}) fusion(bf16[4,2,512,512]{3,2,1,0:T(8,128)(2,1)} %collective-permute-done), kind=kLoop, calls=%fused_computation.33 | loop fusion | flops 1048576 | bytes 8388608 | tf_op jit(solution)/shard_map/neg | solution.py:100
  208.8 10.0 %fusion.26 = bf16[1,4,512,1024]{3,2,1,0:T(8,128)(2,1)} fusion(bf16[4,2,512,512]{3,2,1,0:T(8,128)(2,1)} %bitcast.4, bf16[4,1,512,512]{3,2,1,0:T(8,128)(2,1)S(1)} %get-tuple-element.10, bf16[4,1,512,512]{3,2,1,0:T(8,128)(2,1)S(1)} %get-tuple-element.9, bf16[4,2,512,512]{3,2,1,0:T(8,128)(2,1)} %collective-permute-done, bf16[]{:T(256)} %bitcast.16), kind=kOutput, calls=%fused_computation.30 | convolution fusion | flops 4326424576 | bytes 16777218 | tf_op jit(solution)/shard_map/fpsi,fpsj->fij/dot_general | solution.py:102
  218.7 0.0 collective-permute-done.2
  218.7 0.0 collective-permute-done.1
  218.7 2.6 %broadcast_select_fusion = bf16[4,2,512,512]{3,2,1,0:T(8,128)(2,1)S(1)} fusion(bf16[4,2,512,512]{3,2,1,0:T(8,128)(2,1)} %collective-permute-done.1, bf16[4,2,512,512]{3,2,1,0:T(8,128)(2,1)} %collective-permute-done.2, pred[]{:T(512)S(6)} %eq.18), kind=kLoop, calls=%fused_computation.32 | loop fusion | flops 2097152 | bytes 12582913 | tf_op jit(solution)/shard_map/jit(_where)/select_n | solution.py:115
  221.4 1.6 slice_negate_fusion.1
  223.0 9.2 %fusion.24 = bf16[1,4,512,1024]{3,2,1,0:T(8,128)(2,1)} fusion(bf16[4,2,512,512]{3,2,1,0:T(8,128)(2,1)} %bitcast.4, bf16[4,1,512,512]{3,2,1,0:T(8,128)(2,1)} %get-tuple-element.8, bf16[4,1,512,512]{3,2,1,0:T(8,128)(2,1)S(1)} %get-tuple-element.7, bf16[4,2,512,512]{3,2,1,0:T(8,128)(2,1)S(1)} %broadcast_select_fusion, bf16[]{:T(256)} %bitcast.12), kind=kOutput, calls=%fused_computation.28 | convolution fusion | flops 4326424576 | bytes 16777218 | tf_op jit(solution)/shard_map/fpsi,fpsj->fij/dot_general | solution.py:102
  232.1 10.5 %pad_maximum_fusion = bf16[3,4,512,1024]{3,2,1,0:T(8,128)(2,1)} fusion(bf16[1,4,512,1024]{3,2,1,0:T(8,128)(2,1)} %fusion.26, bf16[1,4,512,1024]{3,2,1,0:T(8,128)(2,1)} %fusion.24, bf16[1,4,512,1024]{3,2,1,0:T(8,128)(2,1)} %fusion.22), kind=kLoop, calls=%fused_computation | loop fusion | flops 12582912 | bytes 25165824 | tf_op jit(solution)/shard_map/stack | solution.py:141
  (3 shorter events, 0.1 us)
Async XLA Ops:
  96.3 93.6 %collective-permute-start = (bf16[4,2,512,512]{3,2,1,0:T(8,128)(2,1)}, bf16[4,2,512,512]{3,2,1,0:T(8,128)(2,1)}, u32[]{:S(2)}, u32[]{:S(2)}) collective-permute-start(bf16[4,2,512,512]{3,2,1,0:T(8,128)(2,1)} %bitcast.4), channel_id=1, source_target_pairs={{16,0},{24,8},{32,16},{40,24},{48,32},{56,40},{64,48},{72,56},{80,... | collective-permute-start | bytes 12582920 | tf_op jit(solution)/shard_map/ppermute | solution.py:22
  99.1 119.6 %collective-permute-start.2 = (bf16[4,2,512,512]{3,2,1,0:T(8,128)(2,1)}, bf16[4,2,512,512]{3,2,1,0:T(8,128)(2,1)}, u32[]{:S(2)}, u32[]{:S(2)}) collective-permute-start(bf16[4,2,512,512]{3,2,1,0:T(8,128)(2,1)} %bitcast.4), channel_id=1, source_target_pairs={{8,0},{24,16},{40,32},{56,48},{72,64},{88,80},{104,96},{120,112},{... | collective-permute-start | bytes 12582920 | tf_op jit(solution)/shard_map/ppermute | solution.py:112
  189.9 28.8 %collective-permute-start.1 = (bf16[4,2,512,512]{3,2,1,0:T(8,128)(2,1)}, bf16[4,2,512,512]{3,2,1,0:T(8,128)(2,1)}, u32[]{:S(2)}, u32[]{:S(2)}) collective-permute-start(bf16[4,2,512,512]{3,2,1,0:T(8,128)(2,1)} %collective-permute-done), channel_id=1, source_target_pairs={{0,8},{16,24},{32,40},{48,56},{64,72},{80,88},{96,104},{112,120},{... | collective-permute-start | bytes 12582920 | tf_op jit(solution)/shard_map/ppermute | solution.py:113

commit v11 on v10

--- a/solution.py
+++ b/solution.py
@@ -122,9 +122,14 @@
     whitened = per_segment.reshape(seg_count, BINS, 2, channels).transpose(1, 2, 0, 3)
     n_freq = lax.axis_size("freq")
     per_device = BINS // n_freq
-    chunks = 1
-    grouped = whitened.reshape(n_freq, chunks, per_device // chunks, 2, seg_count, channels)
-    parts = [grouped[:, k].reshape(BINS // chunks, 2, seg_count, channels) for k in range(chunks)]
+    sizes = [1, per_device - 1]
+    chunks = len(sizes)
+    grouped = whitened.reshape(n_freq, per_device, 2, seg_count, channels)
+    bounds = [sum(sizes[:k]) for k in range(chunks + 1)]
+    parts = [
+        grouped[:, bounds[k]:bounds[k + 1]].reshape(n_freq * sizes[k], 2, seg_count, channels)
+        for k in range(chunks)
+    ]
     chunk_products = []
     for k in range(chunks):
         own_panel = lax.all_to_all(parts[k], "freq", split_axis=0, concat_axis=2, tiled=True)

time: 243 us -> 239 us (0.984)
  local copies, waits for them, and re-layouts: 16.7 us -> 7.38 us
  blocking collectives: 57.1 us -> 66 us
  starting transfers between devices: 7.28 us -> 14.2 us
  matrix products: 29 us -> 23.3 us
  other arithmetic: 22.1 us -> 16.8 us
    reshape x2 -> x1, local copies, waits for them, and re-layouts: 13.7 us -> 4.53 us  [shards(): per_segment.reshape(seg_count, BINS, 2, channels).transpose(1, 2, 0, 3)]
    all_to_all x1 -> x2, blocking collectives: 57.1 us -> 66 us  [shards(): lax.all_to_all(parts[k], 'freq', split_axis=0, concat_axis=2, tiled=True)]
    dot_general x3 -> x6, matrix products: 29 us -> 23.3 us  [local_products(): jnp.einsum('fpsi,fpsj->fij', left_panel, both, preferred_element_type=jnp...]
    another operation x1, other arithmetic: 10.5 us -> 5.47 us  [shards(): return jnp.stack(results, axis=0)]
    ppermute x1 -> x2, waiting for transfers between devices: 0.01 us -> 3.11 us  [neighbour_panels(): lax.ppermute(own_panel, 'chan', [(c + 1, c) for c in range(0, n_chan, 2)])]
    ppermute x1 -> x2, waiting for transfers between devices: 89.5 us -> 86.4 us  [from_behind(): return lax.ppermute(block, axis, route)]
    ppermute x1 -> x2, starting transfers between devices: 3.23 us -> 6.25 us  [neighbour_panels(): lax.ppermute(second_panel, 'chan', [(c - 1, c) for c in range(1, n_chan,...]
    ppermute x1 -> x2, starting transfers between devices: 2.76 us -> 5.39 us  [from_behind(): return lax.ppermute(block, axis, route)]
  transfers between devices with their start and end apart: 3 -> 6, of which waited for: 1 -> 2; matrix products, arithmetic and copies ran while one was open for 10% -> 10% of each run, Pallas kernels for 0% -> 0%
where the time goes in v11:
time: 239 us; the launch traced here: 238 us
  waiting for transfers between devices  89.5 us (37%)
  blocking collectives  66 us (28%)
  matrix products  23.3 us (10%)
  Pallas kernels  20.2 us (8%)
  other arithmetic  16.8 us (7%)
  starting transfers between devices  14.2 us (6%)
  local copies, waits for them, and re-layouts  7.38 us (3%)
    ppermute x2, waiting for transfers between devices, from_behind(): return lax.ppermute(block, axis, route)  86.4 us
    all_to_all x2, blocking collectives, shards(): lax.all_to_all(parts[k], 'freq', split_axis=0, concat_axis=2, tiled=True)  66 us
    dot_general x6, matrix products, local_products(): jnp.einsum('fpsi,fpsj->fij', left_panel, both, preferred_element_type=jnp...  23.3 us
    pallas_call x1, Pallas kernels, whitened_spectra(): pl.pallas_call(functools.partial(spectra_kernel, seg_count, window), out_...  20.2 us
    neg x6, other arithmetic, local_products(): turned = jnp.stack([-right_panel[:, 1], right_panel[:, 0]], axis=1)  6.26 us
    ppermute x2, starting transfers between devices, neighbour_panels(): lax.ppermute(second_panel, 'chan', [(c - 1, c) for c in range(1, n_chan,...  6.25 us
    another operation x1, other arithmetic, shards(): return jnp.stack(results, axis=0)  5.47 us
    ppermute x2, starting transfers between devices, from_behind(): return lax.ppermute(block, axis, route)  5.39 us
  transfers between devices with their start and end apart: 6, of which 2 were waited for; matrix products, arithmetic and copies ran while one was open for 10% of the time, Pallas kernels for 0%

profile of v11, /device:TPU:34, one launch (start us, length us, event | category | flops | bytes accessed | tf_op | source)
XLA Modules:
  0.0 238.3 jit_solution(6722223456321070639)
XLA Ops:
  0.1 1.3 convert_element_type.64
  1.7 0.6 pad_convert_fusion.dft_ref
  2.3 20.2 %shard_map.46 = bf16[64,64,512]{2,1,0:T(8,128)(2,1)} custom-call(s32[64]{0:T(128)} %offs_ref.1, f32[64,384]{1,0:T(8,128)} %pad_convert_fusion.dft_ref, f32[1,512]{1,0:T(1,128)} %bitcast.110, bf16[8448,512]{1,0:T(8,128)(2,1)} %rec_hbm.1), custom_call_target="tpu_custom_call" | custom-call | flops 1610612736 | bytes 29360128 | tf_op jit(solution)/shard_map/pallas_call | solution.py:70
  22.5 4.5 %copy.36 = bf16[64,64,512]{2,0,1:T(8,128)(2,1)S(1)} copy(bf16[64,64,512]{2,1,0:T(8,128)(2,1)} %shard_map.46) | data formatting | bytes 8388608 | tf_op jit(solution)/shard_map/reshape | solution.py:122
  27.2 23.4 %all_to_all.36 = bf16[8,2,64,512]{3,2,1,0:T(8,128)(2,1)S(1)} all-to-all(bf16[8,2,64,512]{3,2,1,0:T(8,128)(2,1)S(1)} %slice_bitcast_fusion), channel_id=1, replica_groups=mesh['chan'=16,'freq'=8] {'freq'}, dimensions={0} | all-to-all | bytes 2097152 | tf_op jit(solution)/shard_map/all_to_all | solution.py:135
  50.6 1.1 copy.18
  51.6 1.3 collective-permute-start
  52.9 0.4 slice.59
  53.3 3.1 %collective-permute-done = bf16[1,2,512,512]{3,2,1,0:T(8,128)(2,1)S(1)} collective-permute-done((bf16[1,2,512,512]{3,2,1,0:T(8,128)(2,1)}, bf16[1,2,512,512]{3,2,1,0:T(8,128)(2,1)S(1)}, u32[]{:S(2)}, u32[]{:S(2)}) %collective-permute-start) | collective-permute-done | bytes 1048608 | tf_op jit(solution)/shard_map/ppermute | solution.py:112
  56.4 1.0 copy-done
  57.4 42.6 %all_to_all.37 = bf16[24,2,64,512]{3,2,1,0:T(8,128)(2,1)S(1)} all-to-all(bf16[24,2,64,512]{3,2,1,0:T(8,128)(2,1)S(1)} %bitcast.107), channel_id=1, replica_groups=mesh['chan'=16,'freq'=8] {'freq'}, dimensions={0} | all-to-all | bytes 6291456 | tf_op jit(solution)/shard_map/all_to_all | solution.py:135
  100.3 3.3 %collective-permute-start.3 = (bf16[3,2,512,512]{3,2,1,0:T(8,128)(2,1)S(1)}, bf16[3,2,512,512]{3,2,1,0:T(8,128)(2,1)}, u32[]{:S(2)}, u32[]{:S(2)}) collective-permute-start(bf16[3,2,512,512]{3,2,1,0:T(8,128)(2,1)S(1)} %bitcast.101), channel_id=1, source_target_pairs={{16,0},{24,8},{32,16},{40,24},{48,32},{56,40},{64,48},{72,56},{80,... | collective-permute-start | bytes 9437192 | tf_op jit(solution)/shard_map/ppermute | solution.py:22
  103.6 2.1 collective-permute-start.1
  106.4 1.3 slice_negate_fusion.5
  107.7 86.4 %collective-permute-done.1 = bf16[1,2,512,512]{3,2,1,0:T(8,128)(2,1)} collective-permute-done((bf16[1,2,512,512]{3,2,1,0:T(8,128)(2,1)}, bf16[1,2,512,512]{3,2,1,0:T(8,128)(2,1)}, u32[]{:S(2)}, u32[]{:S(2)}) %collective-permute-start.1) | collective-permute-done | bytes 1048608 | tf_op jit(solution)/shard_map/ppermute | solution.py:22
  194.1 1.3 collective-permute-start.2
  195.5 2.8 %fusion.48 = bf16[1,1,512,1024]{3,2,1,0:T(8,128)(2,1)S(1)} fusion(bf16[2,512,512]{2,1,0:T(8,128)(2,1)} %bitcast.7, bf16[1,1,512,512]{3,2,1,0:T(8,128)(2,1)S(1)} %get-tuple-element.14, bf16[1,1,512,512]{3,2,1,0:T(8,128)(2,1)S(1)} %get-tuple-element.13, bf16[1,2,512,512]{3,2,1,0:T(8,128)(2,1)} %bitcast.9), kind=kOutput, calls=%fused_computation.59 | convolution fusion | flops 1081081856 | bytes 4194304 | tf_op jit(solution)/shard_map/fpsi,fpsj->fij/dot_general | solution.py:102
  198.3 1.3 slice_negate_fusion.3
  199.6 2.9 %fusion.50 = bf16[1,1,512,1024]{3,2,1,0:T(8,128)(2,1)S(1)} fusion(bf16[2,512,512]{2,1,0:T(8,128)(2,1)} %bitcast.7, bf16[1,1,512,512]{3,2,1,0:T(8,128)(2,1)S(1)} %get-tuple-element.18, bf16[1,1,512,512]{3,2,1,0:T(8,128)(2,1)S(1)} %get-tuple-element.17, bf16[1,2,512,512]{3,2,1,0:T(8,128)(2,1)} %collective-permute-done.1), kind=kOutput, calls=%fused_computation.61 | convolution fusion | flops 1081081856 | bytes 4194304 | tf_op jit(solution)/shard_map/fpsi,fpsj->fij/dot_general | solution.py:102
  202.7 1.3 collective-permute-start.5
  204.0 4.9 %collective-permute-start.4 = (bf16[3,2,512,512]{3,2,1,0:T(8,128)(2,1)}, bf16[3,2,512,512]{3,2,1,0:T(8,128)(2,1)}, u32[]{:S(2)}, u32[]{:S(2)}) collective-permute-start(bf16[3,2,512,512]{3,2,1,0:T(8,128)(2,1)} %collective-permute-done.3), channel_id=1, source_target_pairs={{0,8},{16,24},{32,40},{48,56},{64,72},{80,88},{96,104},{112,120},{... | collective-permute-start | bytes 9437192 | tf_op jit(solution)/shard_map/ppermute | solution.py:113
  208.9 3.5 %fusion.49 = bf16[1,1,512,1024]{3,2,1,0:T(8,128)(2,1)} fusion(bf16[2,512,512]{2,1,0:T(8,128)(2,1)} %bitcast.7, bf16[1,1,512,512]{3,2,1,0:T(8,128)(2,1)S(1)} %get-tuple-element.16, bf16[1,1,512,512]{3,2,1,0:T(8,128)(2,1)S(1)} %get-tuple-element.15, bf16[1,2,512,512]{3,2,1,0:T(8,128)(2,1)S(1)} %broadcast_select_fusion.1), kind=kOutput, calls=%fused_computation.60 | convolution fusion | flops 1081081856 | bytes 4194304 | tf_op jit(solution)/shard_map/fpsi,fpsj->fij/dot_general | solution.py:102
  212.6 3.9 %fusion.21 = bf16[1,3,512,1024]{3,2,1,0:T(8,128)(2,1)S(1)} fusion(bf16[3,2,512,512]{3,2,1,0:T(8,128)(2,1)S(1)} %bitcast.104, bf16[3,1,512,512]{3,2,1,0:T(8,128)(2,1)S(1)} %get-tuple-element.8, bf16[3,1,512,512]{3,2,1,0:T(8,128)(2,1)S(1)} %get-tuple-element.7), kind=kOutput, calls=%fused_computation.28 | convolution fusion | flops 3243245568 | bytes 9437184 | tf_op jit(solution)/shard_map/fpsi,fpsj->fij/dot_general | solution.py:102
  216.5 0.4 maximum_multiply_fusion
  216.9 2.1 slice_negate_fusion
  219.0 5.3 %fusion.23 = bf16[1,3,512,1024]{3,2,1,0:T(8,128)(2,1)S(1)} fusion(bf16[3,2,512,512]{3,2,1,0:T(8,128)(2,1)S(1)} %bitcast.105, bf16[3,1,512,512]{3,2,1,0:T(8,128)(2,1)S(1)} %get-tuple-element.12, bf16[3,1,512,512]{3,2,1,0:T(8,128)(2,1)S(1)} %get-tuple-element.11, bf16[3,2,512,512]{3,2,1,0:T(8,128)(2,1)} %collective-permute-done.3), kind=kOutput, calls=%fused_computation.30 | convolution fusion | flops 3243245568 | bytes 12582912 | tf_op jit(solution)/shard_map/fpsi,fpsj->fij/dot_general | solution.py:102
  224.4 0.4 maximum_multiply_fusion.2
  224.8 0.4 broadcast_select_fusion
  225.2 1.3 slice_negate_fusion.1
  226.6 4.8 %fusion.22 = bf16[1,3,512,1024]{3,2,1,0:T(8,128)(2,1)S(1)} fusion(bf16[3,2,512,512]{3,2,1,0:T(8,128)(2,1)S(1)} %bitcast.106, bf16[3,1,512,512]{3,2,1,0:T(8,128)(2,1)} %get-tuple-element.10, bf16[3,1,512,512]{3,2,1,0:T(8,128)(2,1)S(1)} %get-tuple-element.9, bf16[3,2,512,512]{3,2,1,0:T(8,128)(2,1)S(1)} %broadcast_select_fusion), kind=kOutput, calls=%fused_computation.29 | convolution fusion | flops 3243245568 | bytes 12582912 | tf_op jit(solution)/shard_map/fpsi,fpsj->fij/dot_general | solution.py:102
  231.4 1.4 maximum_multiply_fusion.1
  232.9 5.5 %pad_maximum_fusion = bf16[3,4,512,1024]{3,2,1,0:T(8,128)(2,1)} fusion(bf16[1,4,512,1024]{3,2,1,0:T(8,128)(2,1)S(1)} %maximum_multiply_fusion.2, bf16[1,4,512,1024]{3,2,1,0:T(8,128)(2,1)S(1)} %maximum_multiply_fusion.1, bf16[1,4,512,1024]{3,2,1,0:T(8,128)(2,1)S(1)} %maximum_multiply_fusion), kind=kLoop, calls=%fused_computation | loop fusion | flops 12582912 | bytes 25165824 | tf_op jit(solution)/shard_map/stack | solution.py:146
  (16 shorter events, 1.2 us)
Async XLA Ops:
  51.6 4.8 %collective-permute-start = (bf16[1,2,512,512]{3,2,1,0:T(8,128)(2,1)}, bf16[1,2,512,512]{3,2,1,0:T(8,128)(2,1)S(1)}, u32[]{:S(2)}, u32[]{:S(2)}) collective-permute-start(bf16[1,2,512,512]{3,2,1,0:T(8,128)(2,1)} %bitcast.9), channel_id=1, source_target_pairs={{8,0},{24,16},{40,32},{56,48},{72,64},{88,80},{104,96},{120,112},{... | collective-permute-start | bytes 3145736 | tf_op jit(solution)/shard_map/ppermute | solution.py:112
  56.4 1.0 copy-start
  100.3 103.7 %collective-permute-start.3 = (bf16[3,2,512,512]{3,2,1,0:T(8,128)(2,1)S(1)}, bf16[3,2,512,512]{3,2,1,0:T(8,128)(2,1)}, u32[]{:S(2)}, u32[]{:S(2)}) collective-permute-start(bf16[3,2,512,512]{3,2,1,0:T(8,128)(2,1)S(1)} %bitcast.101), channel_id=1, source_target_pairs={{16,0},{24,8},{32,16},{40,24},{48,32},{56,40},{64,48},{72,56},{80,... | collective-permute-start | bytes 9437192 | tf_op jit(solution)/shard_map/ppermute | solution.py:22
  103.6 90.5 %collective-permute-start.1 = (bf16[1,2,512,512]{3,2,1,0:T(8,128)(2,1)}, bf16[1,2,512,512]{3,2,1,0:T(8,128)(2,1)}, u32[]{:S(2)}, u32[]{:S(2)}) collective-permute-start(bf16[1,2,512,512]{3,2,1,0:T(8,128)(2,1)} %bitcast.9), channel_id=1, source_target_pairs={{16,0},{24,8},{32,16},{40,24},{48,32},{56,40},{64,48},{72,56},{80,... | collective-permute-start | bytes 3145736 | tf_op jit(solution)/shard_map/ppermute | solution.py:22
  194.1 8.4 %collective-permute-start.2 = (bf16[1,2,512,512]{3,2,1,0:T(8,128)(2,1)}, bf16[1,2,512,512]{3,2,1,0:T(8,128)(2,1)S(1)}, u32[]{:S(2)}, u32[]{:S(2)}) collective-permute-start(bf16[1,2,512,512]{3,2,1,0:T(8,128)(2,1)} %collective-permute-done.1), channel_id=1, source_target_pairs={{0,8},{16,24},{32,40},{48,56},{64,72},{80,88},{96,104},{112,120},{... | collective-permute-start | bytes 3145736 | tf_op jit(solution)/shard_map/ppermute | solution.py:113
  199.5 2.9 %copy-start.1 = (bf16[1,2,512,512]{3,2,1,0:T(8,128)(2,1)S(1)}, bf16[1,2,512,512]{3,2,1,0:T(8,128)(2,1)}, u32[]{:S(2)}) copy-start(bf16[1,2,512,512]{3,2,1,0:T(8,128)(2,1)} %copy-done) | copy-start | bytes 3145732
  202.7 22.1 %collective-permute-start.5 = (bf16[3,2,512,512]{3,2,1,0:T(8,128)(2,1)S(1)}, bf16[3,2,512,512]{3,2,1,0:T(8,128)(2,1)S(1)}, u32[]{:S(2)}, u32[]{:S(2)}) collective-permute-start(bf16[3,2,512,512]{3,2,1,0:T(8,128)(2,1)S(1)} %bitcast.102), channel_id=1, source_target_pairs={{8,0},{24,16},{40,32},{56,48},{72,64},{88,80},{104,96},{120,112},{... | collective-permute-start | bytes 9437192 | tf_op jit(solution)/shard_map/ppermute | solution.py:112
  204.0 20.8 %collective-permute-start.4 = (bf16[3,2,512,512]{3,2,1,0:T(8,128)(2,1)}, bf16[3,2,512,512]{3,2,1,0:T(8,128)(2,1)}, u32[]{:S(2)}, u32[]{:S(2)}) collective-permute-start(bf16[3,2,512,512]{3,2,1,0:T(8,128)(2,1)} %collective-permute-done.3), channel_id=1, source_target_pairs={{0,8},{16,24},{32,40},{48,56},{64,72},{80,88},{96,104},{112,120},{... | collective-permute-start | bytes 9437192 | tf_op jit(solution)/shard_map/ppermute | solution.py:113

commit v12 on v9

--- a/solution.py
+++ b/solution.py
@@ -59,11 +59,10 @@
         out_ref[j] = (spec * scale).astype(out_ref.dtype)
 
 
-def whitened_spectra(records, offsets, dead_mask):
+def whitened_spectra(records, offsets, dead_mask, dft_rows):
     seg_count = offsets.shape[0]
     channels = records.shape[1]
     window = SEG_LEN + 128
-    dft_rows = dft_table(SEG_LEN, BINS, FIRST_BIN)
     rows = dft_rows.shape[0]
     padded = jnp.pad(dft_rows.astype(jnp.float32), ((0, 0), (0, window - SEG_LEN)))
     live = dead_mask.astype(jnp.float32).reshape(1, channels)
@@ -117,14 +116,16 @@
 
 
 def shards(records, offsets, dead_mask, band_blocks):
-    per_segment = whitened_spectra(records, offsets, dead_mask)
-    seg_count, rows, channels = per_segment.shape
-    whitened = per_segment.reshape(seg_count, BINS, 2, channels).transpose(1, 2, 0, 3)
     n_freq = lax.axis_size("freq")
     per_device = BINS // n_freq
     chunks = 2
-    grouped = whitened.reshape(n_freq, chunks, per_device // chunks, 2, seg_count, channels)
-    parts = [grouped[:, k].reshape(BINS // chunks, 2, seg_count, channels) for k in range(chunks)]
+    per_chunk = per_device // chunks
+    table = dft_table(SEG_LEN, BINS, FIRST_BIN).reshape(n_freq, chunks, per_chunk, 2, SEG_LEN)
+    table = table.transpose(3, 1, 0, 2, 4).reshape(2 * BINS, SEG_LEN)
+    per_segment = whitened_spectra(records, offsets, dead_mask, table)
+    seg_count, rows, channels = per_segment.shape
+    slabs = per_segment.reshape(seg_count, 2, chunks, n_freq * per_chunk, channels)
+    parts = [slabs[:, :, k].transpose(2, 1, 0, 3) for k in range(chunks)]
     chunk_products = []
     for k in range(chunks):
         own_panel = lax.all_to_all(parts[k], "freq", split_axis=0, concat_axis=2, tiled=True)

time: 216 us -> 208 us (0.963)
  local copies, waits for them, and re-layouts: 19.4 us -> 12.6 us
    reshape x1 -> x0, local copies, waits for them, and re-layouts: 7.21 us -> none  [shards(): per_segment.reshape(seg_count, BINS, 2, channels).transpose(1, 2, 0, 3)]
    slice x1, local copies, waits for them, and re-layouts: 5.06 us -> 2.76 us  [shards(): parts = [slabs[:, :, k].transpose(2, 1, 0, 3) for k in range(chunks)]]
  transfers between devices with their start and end apart: 7 -> 7, of which waited for: 3 -> 3; matrix products, arithmetic and copies ran while one was open for 11% -> 12% of each run, Pallas kernels for 0% -> 0%
where the time goes in v12:
time: 208 us; the launch traced here: 206 us
  waiting for transfers between devices  88.8 us (43%)
  blocking collectives  34.4 us (17%)
  Pallas kernels  20.2 us (10%)
  starting transfers between devices  18.7 us (9%)
  matrix products  17 us (8%)
  other arithmetic  13 us (6%)
  local copies, waits for them, and re-layouts  12.6 us (6%)
    ppermute x2, waiting for transfers between devices, from_behind(): return lax.ppermute(block, axis, route)  71.7 us
    all_to_all x1, blocking collectives, shards(): lax.all_to_all(parts[k], 'freq', split_axis=0, concat_axis=2, tiled=True)  34.4 us
    pallas_call x1, Pallas kernels, whitened_spectra(): pl.pallas_call(functools.partial(spectra_kernel, seg_count, window), out_...  20.2 us
    all_to_all x1, waiting for transfers between devices, shards(): lax.all_to_all(parts[k], 'freq', split_axis=0, concat_axis=2, tiled=True)  17.1 us
    dot_general x6, matrix products, local_products(): jnp.einsum('fpsi,fpsj->fij', left_panel, both, preferred_element_type=jnp...  17 us
    unnamed x8, local copies, waits for them, and re-layouts  6.97 us
    ppermute x2, starting transfers between devices, from_behind(): return lax.ppermute(block, axis, route)  6.04 us
    ppermute x2, starting transfers between devices, neighbour_panels(): lax.ppermute(second_panel, 'chan', [(c - 1, c) for c in range(1, n_chan,...  5.58 us
  transfers between devices with their start and end apart: 7, of which 3 were waited for; matrix products, arithmetic and copies ran while one was open for 12% of the time, Pallas kernels for 0%

profile of v12, /device:TPU:34, one launch (start us, length us, event | category | flops | bytes accessed | tf_op | source)
XLA Modules:
  0.0 205.7 jit_solution(14789249024693266362)
XLA Ops:
  0.1 1.3 convert_element_type.70
  2.1 0.7 pad_convert_fusion.dft_ref
  2.7 20.2 %shard_map.46 = bf16[64,64,512]{2,1,0:T(8,128)(2,1)} custom-call(s32[64]{0:T(128)} %offs_ref.1, f32[64,384]{1,0:T(8,128)} %pad_convert_fusion.dft_ref, f32[1,512]{1,0:T(1,128)} %bitcast.105, bf16[8448,512]{1,0:T(8,128)(2,1)} %rec_hbm.1), custom_call_target="tpu_custom_call" | custom-call | flops 1610612736 | bytes 29360128 | tf_op jit(solution)/shard_map/pallas_call | solution.py:69
  22.9 2.8 %fusion.88 = (bf16[64,2,1,16,512]{4,3,2,1,0:T(8,128)(2,1)S(1)}, bf16[64,2,1,16,512]{4,3,2,1,0:T(8,128)(2,1)S(1)}) fusion(bf16[64,2,2,16,512]{4,3,2,1,0:T(8,128)(2,1)} %bitcast.89), kind=kLoop, calls=%fused_computation.94 | loop fusion | bytes 8388608 | tf_op jit(solution)/shard_map/slice | solution.py:128
  25.7 2.2 %copy.48 = bf16[64,2,1,16,512]{4,1,0,3,2:T(2,128)(2,1)S(1)} copy(bf16[64,2,1,16,512]{4,3,2,1,0:T(8,128)(2,1)S(1)} %get-tuple-element.8) | data formatting | bytes 4194304
  27.9 34.4 %all_to_all.36 = bf16[16,2,64,512]{3,1,2,0:T(2,128)(2,1)S(1)} all-to-all(bf16[16,2,64,512]{3,1,2,0:T(2,128)(2,1)S(1)} %bitcast.103), channel_id=1, replica_groups=mesh['chan'=16,'freq'=8] {'freq'}, dimensions={0} | all-to-all | bytes 4194304 | tf_op jit(solution)/shard_map/all_to_all | solution.py:131
  62.3 0.4 copy.22
  62.7 1.5 collective-permute-start
  64.2 3.1 %collective-permute-start.1 = (bf16[2,2,512,512]{3,2,1,0:T(8,128)(2,1)S(1)}, bf16[2,2,512,512]{3,2,1,0:T(8,128)(2,1)}, u32[]{:S(2)}, u32[]{:S(2)}) collective-permute-start(bf16[2,2,512,512]{3,2,1,0:T(8,128)(2,1)S(1)} %bitcast.91), channel_id=1, source_target_pairs={{16,0},{24,8},{32,16},{40,24},{48,32},{56,40},{64,48},{72,56},{80,... | collective-permute-start | bytes 6291464 | tf_op jit(solution)/shard_map/ppermute | solution.py:22
  67.3 3.5 %copy.47 = bf16[64,2,1,16,512]{4,1,0,3,2:T(2,128)(2,1)} copy(bf16[64,2,1,16,512]{4,3,2,1,0:T(8,128)(2,1)S(1)} %get-tuple-element.7) | data formatting | bytes 4194304
  70.8 1.3 copy-done
  72.1 4.4 %all-to-all-start.1 = ((bf16[16,2,64,512]{3,1,2,0:T(2,128)(2,1)}), bf16[16,2,64,512]{3,1,2,0:T(2,128)(2,1)}, u32[]{:S(2)}, u32[]{:S(2)}) async-start(bf16[16,2,64,512]{3,1,2,0:T(2,128)(2,1)} %bitcast.102), calls=%async_computation.1 | async-start | bytes 4194304 | tf_op jit(solution)/shard_map/all_to_all | solution.py:131
  77.2 1.2 slice_negate_fusion.5
  78.3 37.0 %collective-permute-done.1 = bf16[2,2,512,512]{3,2,1,0:T(8,128)(2,1)} collective-permute-done((bf16[2,2,512,512]{3,2,1,0:T(8,128)(2,1)S(1)}, bf16[2,2,512,512]{3,2,1,0:T(8,128)(2,1)}, u32[]{:S(2)}, u32[]{:S(2)}) %collective-permute-start.1) | collective-permute-done | bytes 2097184 | tf_op jit(solution)/shard_map/ppermute | solution.py:22
  115.3 3.9 %collective-permute-start.2 = (bf16[2,2,512,512]{3,2,1,0:T(8,128)(2,1)}, bf16[2,2,512,512]{3,2,1,0:T(8,128)(2,1)}, u32[]{:S(2)}, u32[]{:S(2)}) collective-permute-start(bf16[2,2,512,512]{3,2,1,0:T(8,128)(2,1)} %collective-permute-done.1), channel_id=1, source_target_pairs={{0,8},{16,24},{32,40},{48,56},{64,72},{80,88},{96,104},{112,120},{... | collective-permute-start | bytes 6291464 | tf_op jit(solution)/shard_map/ppermute | solution.py:112
  119.3 17.1 %all-to-all-done.1 = bf16[16,2,64,512]{3,1,2,0:T(2,128)(2,1)} async-done(((bf16[16,2,64,512]{3,1,2,0:T(2,128)(2,1)}), bf16[16,2,64,512]{3,1,2,0:T(2,128)(2,1)}, u32[]{:S(2)}, u32[]{:S(2)}) %all-to-all-start.1) | async-done | bytes 2097184 | tf_op jit(solution)/shard_map/all_to_all | solution.py:131
  136.4 2.1 %copy.25 = bf16[8,2,2,64,512]{4,3,0,2,1:T(8,128)(2,1)S(1)} copy(bf16[8,2,2,64,512]{4,2,3,1,0:T(2,128)(2,1)} %bitcast.13) | data formatting | bytes 4194304 | tf_op jit(solution)/shard_map/all_to_all | solution.py:131
  138.5 3.0 %collective-permute-start.3 = (bf16[2,2,512,512]{3,2,1,0:T(8,128)(2,1)S(1)}, bf16[2,2,512,512]{3,2,1,0:T(8,128)(2,1)S(1)}, u32[]{:S(2)}, u32[]{:S(2)}) collective-permute-start(bf16[2,2,512,512]{3,2,1,0:T(8,128)(2,1)S(1)} %bitcast.96), channel_id=1, source_target_pairs={{16,0},{24,8},{32,16},{40,24},{48,32},{56,40},{64,48},{72,56},{80,... | collective-permute-start | bytes 6291464 | tf_op jit(solution)/shard_map/ppermute | solution.py:22
  141.5 2.6 %fusion.54 = bf16[1,2,512,1024]{3,2,1,0:T(8,128)(2,1)S(1)} fusion(bf16[2,2,512,512]{3,2,1,0:T(8,128)(2,1)S(1)} %bitcast.93, bf16[2,1,512,512]{3,2,1,0:T(8,128)(2,1)S(1)} %copy-done.2, bf16[2,1,512,512]{3,2,1,0:T(8,128)(2,1)S(1)} %get-tuple-element.9), kind=kOutput, calls=%fused_computation.56 | convolution fusion | flops 2162163712 | bytes 6291456 | tf_op jit(solution)/shard_map/fpsi,fpsj->fij/dot_general | solution.py:101
  144.1 1.7 slice_negate_fusion.1
  145.8 4.0 %fusion.66 = bf16[1,2,512,1024]{3,2,1,0:T(8,128)(2,1)S(1)} fusion(bf16[2,2,512,512]{3,2,1,0:T(8,128)(2,1)S(1)} %bitcast.94, bf16[2,1,512,512]{3,2,1,0:T(8,128)(2,1)S(1)} %get-tuple-element.18, bf16[2,1,512,512]{3,2,1,0:T(8,128)(2,1)S(1)} %get-tuple-element.17, bf16[2,2,512,512]{3,2,1,0:T(8,128)(2,1)} %collective-permute-done.1), kind=kOutput, calls=%fused_computation.60 | convolution fusion | flops 2162163712 | bytes 8388608 | tf_op jit(solution)/shard_map/fpsi,fpsj->fij/dot_general | solution.py:101
  149.7 1.3 collective-permute-start.5
  151.2 2.6 %fusion.57 = bf16[1,2,512,1024]{3,2,1,0:T(8,128)(2,1)S(1)} fusion(bf16[2,2,512,512]{3,2,1,0:T(8,128)(2,1)S(1)} %bitcast.99, bf16[2,1,512,512]{3,2,1,0:T(8,128)(2,1)S(1)} %get-tuple-element.12, bf16[2,1,512,512]{3,2,1,0:T(8,128)(2,1)S(1)} %get-tuple-element.11), kind=kOutput, calls=%fused_computation.57 | convolution fusion | flops 2162163712 | bytes 6291456 | tf_op jit(solution)/shard_map/fpsi,fpsj->fij/dot_general | solution.py:101
  153.8 0.4 maximum_multiply_fusion
  154.2 34.7 %collective-permute-done.3 = bf16[2,2,512,512]{3,2,1,0:T(8,128)(2,1)S(1)} collective-permute-done((bf16[2,2,512,512]{3,2,1,0:T(8,128)(2,1)S(1)}, bf16[2,2,512,512]{3,2,1,0:T(8,128)(2,1)S(1)}, u32[]{:S(2)}, u32[]{:S(2)}) %collective-permute-start.3) | collective-permute-done | bytes 2097184 | tf_op jit(solution)/shard_map/ppermute | solution.py:22
  188.9 1.6 collective-permute-start.4
  191.0 2.6 %fusion.60 = bf16[1,2,512,1024]{3,2,1,0:T(8,128)(2,1)S(1)} fusion(bf16[2,2,512,512]{3,2,1,0:T(8,128)(2,1)S(1)} %bitcast.95, bf16[2,1,512,512]{3,2,1,0:T(8,128)(2,1)S(1)} %get-tuple-element.14, bf16[2,1,512,512]{3,2,1,0:T(8,128)(2,1)S(1)} %get-tuple-element.13, bf16[2,2,512,512]{3,2,1,0:T(8,128)(2,1)S(1)} %broadcast_select_fusion.1), kind=kOutput, calls=%fused_computation.58 | convolution fusion | flops 2162163712 | bytes 8388608 | tf_op jit(solution)/shard_map/fpsi,fpsj->fij/dot_general | solution.py:101
  193.7 2.6 %fusion.69 = bf16[1,2,512,1024]{3,2,1,0:T(8,128)(2,1)S(1)} fusion(bf16[2,2,512,512]{3,2,1,0:T(8,128)(2,1)S(1)} %bitcast.100, bf16[2,1,512,512]{3,2,1,0:T(8,128)(2,1)S(1)} %get-tuple-element.20, bf16[2,1,512,512]{3,2,1,0:T(8,128)(2,1)S(1)} %get-tuple-element.19, bf16[2,2,512,512]{3,2,1,0:T(8,128)(2,1)S(1)} %collective-permute-done.3), kind=kOutput, calls=%fused_computation.61 | convolution fusion | flops 2162163712 | bytes 8388608 | tf_op jit(solution)/shard_map/fpsi,fpsj->fij/dot_general | solution.py:101
  196.4 0.4 maximum_multiply_fusion.2
  197.2 2.6 %fusion.63 = bf16[1,2,512,1024]{3,2,1,0:T(8,128)(2,1)S(1)} fusion(bf16[2,2,512,512]{3,2,1,0:T(8,128)(2,1)S(1)} %bitcast.101, bf16[2,1,512,512]{3,2,1,0:T(8,128)(2,1)S(1)} %get-tuple-element.16, bf16[2,1,512,512]{3,2,1,0:T(8,128)(2,1)S(1)} %get-tuple-element.15, bf16[2,2,512,512]{3,2,1,0:T(8,128)(2,1)S(1)} %broadcast_select_fusion), kind=kOutput, calls=%fused_computation.59 | convolution fusion | flops 2162163712 | bytes 8388608 | tf_op jit(solution)/shard_map/fpsi,fpsj->fij/dot_general | solution.py:101
  199.8 0.4 maximum_multiply_fusion.1
  200.2 5.5 %pad_maximum_fusion = bf16[3,4,512,1024]{3,2,1,0:T(8,128)(2,1)} fusion(bf16[1,4,512,1024]{3,2,1,0:T(8,128)(2,1)S(1)} %maximum_multiply_fusion.2, bf16[1,4,512,1024]{3,2,1,0:T(8,128)(2,1)S(1)} %maximum_multiply_fusion.1, bf16[1,4,512,1024]{3,2,1,0:T(8,128)(2,1)S(1)} %maximum_multiply_fusion), kind=kLoop, calls=%fused_computation | loop fusion | flops 12582912 | bytes 25165824 | tf_op jit(solution)/shard_map/stack | solution.py:142
  (25 shorter events, 1.8 us)
Async XLA Ops:
  62.7 8.0 %collective-permute-start = (bf16[2,2,512,512]{3,2,1,0:T(8,128)(2,1)S(1)}, bf16[2,2,512,512]{3,2,1,0:T(8,128)(2,1)S(1)}, u32[]{:S(2)}, u32[]{:S(2)}) collective-permute-start(bf16[2,2,512,512]{3,2,1,0:T(8,128)(2,1)S(1)} %bitcast.90), channel_id=1, source_target_pairs={{8,0},{24,16},{40,32},{56,48},{72,64},{88,80},{104,96},{120,112},{... | collective-permute-start | bytes 6291464 | tf_op jit(solution)/shard_map/ppermute | solution.py:111
  64.2 51.1 %collective-permute-start.1 = (bf16[2,2,512,512]{3,2,1,0:T(8,128)(2,1)S(1)}, bf16[2,2,512,512]{3,2,1,0:T(8,128)(2,1)}, u32[]{:S(2)}, u32[]{:S(2)}) collective-permute-start(bf16[2,2,512,512]{3,2,1,0:T(8,128)(2,1)S(1)} %bitcast.91), channel_id=1, source_target_pairs={{16,0},{24,8},{32,16},{40,24},{48,32},{56,40},{64,48},{72,56},{80,... | collective-permute-start | bytes 6291464 | tf_op jit(solution)/shard_map/ppermute | solution.py:22
  70.8 1.3 copy-start
  72.1 64.2 %all-to-all-start.1 = ((bf16[16,2,64,512]{3,1,2,0:T(2,128)(2,1)}), bf16[16,2,64,512]{3,1,2,0:T(2,128)(2,1)}, u32[]{:S(2)}, u32[]{:S(2)}) async-start(bf16[16,2,64,512]{3,1,2,0:T(2,128)(2,1)} %bitcast.102), calls=%async_computation.1 | async-start | bytes 4194304 | tf_op jit(solution)/shard_map/all_to_all | solution.py:131
  115.3 75.2 %collective-permute-start.2 = (bf16[2,2,512,512]{3,2,1,0:T(8,128)(2,1)}, bf16[2,2,512,512]{3,2,1,0:T(8,128)(2,1)}, u32[]{:S(2)}, u32[]{:S(2)}) collective-permute-start(bf16[2,2,512,512]{3,2,1,0:T(8,128)(2,1)} %collective-permute-done.1), channel_id=1, source_target_pairs={{0,8},{16,24},{32,40},{48,56},{64,72},{80,88},{96,104},{112,120},{... | collective-permute-start | bytes 6291464 | tf_op jit(solution)/shard_map/ppermute | solution.py:112
  136.4 5.1 %copy-start.2 = (bf16[2,1,512,512]{3,2,1,0:T(8,128)(2,1)S(1)}, bf16[2,1,512,512]{3,2,1,0:T(8,128)(2,1)}, u32[]{:S(2)}) copy-start(bf16[2,1,512,512]{3,2,1,0:T(8,128)(2,1)} %get-tuple-element.10) | copy-start | bytes 3145732
  138.5 50.4 %collective-permute-start.3 = (bf16[2,2,512,512]{3,2,1,0:T(8,128)(2,1)S(1)}, bf16[2,2,512,512]{3,2,1,0:T(8,128)(2,1)S(1)}, u32[]{:S(2)}, u32[]{:S(2)}) collective-permute-start(bf16[2,2,512,512]{3,2,1,0:T(8,128)(2,1)S(1)} %bitcast.96), channel_id=1, source_target_pairs={{16,0},{24,8},{32,16},{40,24},{48,32},{56,40},{64,48},{72,56},{80,... | collective-permute-start | bytes 6291464 | tf_op jit(solution)/shard_map/ppermute | solution.py:22
  149.7 47.1 %collective-permute-start.5 = (bf16[2,2,512,512]{3,2,1,0:T(8,128)(2,1)S(1)}, bf16[2,2,512,512]{3,2,1,0:T(8,128)(2,1)S(1)}, u32[]{:S(2)}, u32[]{:S(2)}) collective-permute-start(bf16[2,2,512,512]{3,2,1,0:T(8,128)(2,1)S(1)} %bitcast.97), channel_id=1, source_target_pairs={{8,0},{24,16},{40,32},{56,48},{72,64},{88,80},{104,96},{120,112},{... | collective-permute-start | bytes 6291464 | tf_op jit(solution)/shard_map/ppermute | solution.py:111
  153.8 36.8 %copy-start.1 = (bf16[2,2,512,512]{3,2,1,0:T(8,128)(2,1)S(1)}, bf16[2,2,512,512]{3,2,1,0:T(8,128)(2,1)}, u32[]{:S(2)}) copy-start(bf16[2,2,512,512]{3,2,1,0:T(8,128)(2,1)} %copy-done) | copy-start | bytes 6291460
  188.9 7.9 %collective-permute-start.4 = (bf16[2,2,512,512]{3,2,1,0:T(8,128)(2,1)S(1)}, bf16[2,2,512,512]{3,2,1,0:T(8,128)(2,1)S(1)}, u32[]{:S(2)}, u32[]{:S(2)}) collective-permute-start(bf16[2,2,512,512]{3,2,1,0:T(8,128)(2,1)S(1)} %collective-permute-done.3), channel_id=1, source_target_pairs={{0,8},{16,24},{32,40},{48,56},{64,72},{80,88},{96,104},{112,120},{... | collective-permute-start | bytes 6291464 | tf_op jit(solution)/shard_map/ppermute | solution.py:112

commit v13 on v12

--- a/solution.py
+++ b/solution.py
@@ -118,14 +118,20 @@
 def shards(records, offsets, dead_mask, band_blocks):
     n_freq = lax.axis_size("freq")
     per_device = BINS // n_freq
-    chunks = 2
-    per_chunk = per_device // chunks
-    table = dft_table(SEG_LEN, BINS, FIRST_BIN).reshape(n_freq, chunks, per_chunk, 2, SEG_LEN)
-    table = table.transpose(3, 1, 0, 2, 4).reshape(2 * BINS, SEG_LEN)
+    sizes = [per_device - 1, 1]
+    chunks = len(sizes)
+    bounds = [sum(sizes[:k]) for k in range(chunks + 1)]
+    table = dft_table(SEG_LEN, BINS, FIRST_BIN).reshape(n_freq, per_device, 2, SEG_LEN)
+    table = jnp.concatenate(
+        [table[:, bounds[k]:bounds[k + 1]].reshape(n_freq * sizes[k], 2, SEG_LEN) for k in range(chunks)], axis=0
+    )
+    table = table.transpose(1, 0, 2).reshape(2 * BINS, SEG_LEN)
     per_segment = whitened_spectra(records, offsets, dead_mask, table)
     seg_count, rows, channels = per_segment.shape
-    slabs = per_segment.reshape(seg_count, 2, chunks, n_freq * per_chunk, channels)
-    parts = [slabs[:, :, k].transpose(2, 1, 0, 3) for k in range(chunks)]
+    slabs = per_segment.reshape(seg_count, 2, BINS, channels)
+    parts = [
+        slabs[:, :, n_freq * bounds[k]:n_freq * bounds[k + 1]].transpose(2, 1, 0, 3) for k in range(chunks)
+    ]
     chunk_products = []
     for k in range(chunks):
         own_panel = lax.all_to_all(parts[k], "freq", split_axis=0, concat_axis=2, tiled=True)

time: 208 us -> 211 us (1.014)
  waiting for transfers between devices: 88.8 us -> 67.1 us
  blocking collectives: 34.4 us -> 46.1 us
  other arithmetic: 13 us -> 20 us
  matrix products: 17 us -> 23.5 us
  starting transfers between devices: 18.7 us -> 21.1 us
    all_to_all x1, waiting for transfers between devices: 17.1 us -> 0.01 us  [shards(): lax.all_to_all(parts[k], 'freq', split_axis=0, concat_axis=2, tiled=True)]
    all_to_all x1, blocking collectives: 34.4 us -> 46.1 us  [shards(): lax.all_to_all(parts[k], 'freq', split_axis=0, concat_axis=2, tiled=True)]
    dot_general x6, matrix products: 17 us -> 23.5 us  [local_products(): jnp.einsum('fpsi,fpsj->fij', left_panel, both, preferred_element_type=jnp...]
    ppermute x2, waiting for transfers between devices: 71.7 us -> 67.1 us  [from_behind(): return lax.ppermute(block, axis, route)]
    neg x6, other arithmetic: 3.42 us -> 7.67 us  [local_products(): turned = jnp.stack([-right_panel[:, 1], right_panel[:, 0]], axis=1)]
    ppermute x2, starting transfers between devices: 5.58 us -> 9.08 us  [neighbour_panels(): lax.ppermute(second_panel, 'chan', [(c - 1, c) for c in range(1, n_chan,...]
    unnamed x8 -> x6, local copies, waits for them, and re-layouts: 6.97 us -> 4.61 us
    slice x1 -> x4, local copies, waits for them, and re-layouts: 2.76 us -> 4.45 us  [the longest x2 4.42 us: shards(): slabs[:, :, n_freq * bounds[k]:n_freq * bounds[k + 1]].transpose(2, 1, 0, 3)]
  transfers between devices with their start and end apart: 7 -> 7, of which waited for: 3 -> 2; matrix products, arithmetic and copies ran while one was open for 12% -> 15% of each run, Pallas kernels for 0% -> 0%
where the time goes in v13:
time: 211 us; the launch traced here: 209 us
  waiting for transfers between devices  67.1 us (32%)
  blocking collectives  46.1 us (22%)
  matrix products  23.5 us (11%)
  starting transfers between devices  21.1 us (10%)
  other arithmetic  20 us (9%)
  Pallas kernels  20 us (9%)
  local copies, waits for them, and re-layouts  10.7 us (5%)
    ppermute x2, waiting for transfers between devices, from_behind(): return lax.ppermute(block, axis, route)  67.1 us
    all_to_all x1, blocking collectives, shards(): lax.all_to_all(parts[k], 'freq', split_axis=0, concat_axis=2, tiled=True)  46.1 us
    dot_general x6, matrix products, local_products(): jnp.einsum('fpsi,fpsj->fij', left_panel, both, preferred_element_type=jnp...  23.5 us
    pallas_call x1, Pallas kernels, whitened_spectra(): pl.pallas_call(functools.partial(spectra_kernel, seg_count, window), out_...  20 us
    ppermute x2, starting transfers between devices, neighbour_panels(): lax.ppermute(second_panel, 'chan', [(c - 1, c) for c in range(1, n_chan,...  9.08 us
    neg x6, other arithmetic, local_products(): turned = jnp.stack([-right_panel[:, 1], right_panel[:, 0]], axis=1)  7.67 us
    another operation x1, other arithmetic, shards(): return jnp.stack(results, axis=0)  5.47 us
    ppermute x2, starting transfers between devices, from_behind(): return lax.ppermute(block, axis, route)  5.17 us
  transfers between devices with their start and end apart: 7, of which 2 were waited for; matrix products, arithmetic and copies ran while one was open for 15% of the time, Pallas kernels for 0%

profile of v13, /device:TPU:34, one launch (start us, length us, event | category | flops | bytes accessed | tf_op | source)
XLA Modules:
  0.0 209.5 jit_solution(1050073882052064674)
XLA Ops:
  0.1 1.3 multiply_convert_fusion
  1.4 1.2 convert_element_type.80
  2.7 0.6 pad_convert_fusion.dft_ref
  3.4 20.0 %shard_map.46 = bf16[64,64,512]{2,1,0:T(8,128)(2,1)} custom-call(s32[64]{0:T(128)} %offs_ref.1, f32[64,384]{1,0:T(8,128)} %pad_convert_fusion.dft_ref, f32[1,512]{1,0:T(1,128)} %bitcast.126, bf16[8448,512]{1,0:T(8,128)(2,1)} %rec_hbm.1), custom_call_target="tpu_custom_call" | custom-call | flops 1610612736 | bytes 29360128 | tf_op jit(solution)/shard_map/pallas_call | solution.py:69
  23.5 2.1 %slice.66 = bf16[64,2,24,512]{3,2,1,0:T(8,128)(2,1)S(1)} slice(bf16[64,2,32,512]{3,2,1,0:T(8,128)(2,1)} %bitcast.106), slice={[0:64], [0:2], [0:24], [0:512]} | slice | bytes 6291456 | tf_op jit(solution)/shard_map/slice | solution.py:133
  25.6 1.8 copy.47
  27.3 46.1 %all_to_all.36 = bf16[24,2,64,512]{3,2,1,0:T(8,128)(2,1)S(1)} all-to-all(bf16[24,2,64,512]{3,2,1,0:T(8,128)(2,1)S(1)} %bitcast.114), channel_id=1, replica_groups=mesh['chan'=16,'freq'=8] {'freq'}, dimensions={0} | all-to-all | bytes 6291456 | tf_op jit(solution)/shard_map/all_to_all | solution.py:137
  73.8 1.3 collective-permute-start
  75.1 3.1 %collective-permute-start.1 = (bf16[3,2,512,512]{3,2,1,0:T(8,128)(2,1)S(1)}, bf16[3,2,512,512]{3,2,1,0:T(8,128)(2,1)}, u32[]{:S(2)}, u32[]{:S(2)}) collective-permute-start(bf16[3,2,512,512]{3,2,1,0:T(8,128)(2,1)S(1)} %bitcast.109), channel_id=1, source_target_pairs={{16,0},{24,8},{32,16},{40,24},{48,32},{56,40},{64,48},{72,56},{80,... | collective-permute-start | bytes 9437192 | tf_op jit(solution)/shard_map/ppermute | solution.py:22
  78.2 2.3 %slice.69 = bf16[64,2,8,512]{3,2,1,0:T(8,128)(2,1)} slice(bf16[64,2,32,512]{3,2,1,0:T(8,128)(2,1)} %bitcast.107), slice={[0:64], [0:2], [24:32], [0:512]} | slice | bytes 2097152 | tf_op jit(solution)/shard_map/slice | solution.py:133
  81.2 2.9 %copy.48 = bf16[64,2,8,512]{3,0,1,2:T(8,128)(2,1)} copy(bf16[64,2,8,512]{3,2,1,0:T(8,128)(2,1)} %slice.69) | data formatting | bytes 2097152
  84.0 1.8 slice_negate_fusion.2
  85.9 4.2 %all-to-all-start.1 = ((bf16[8,2,64,512]{3,2,1,0:T(8,128)(2,1)}), bf16[8,2,64,512]{3,2,1,0:T(8,128)(2,1)}, u32[]{:S(2)}, u32[]{:S(2)}) async-start(bf16[8,2,64,512]{3,2,1,0:T(8,128)(2,1)} %bitcast.123), calls=%async_computation.1 | async-start | bytes 2097152 | tf_op jit(solution)/shard_map/all_to_all | solution.py:137
  90.1 7.0 %fusion.21 = bf16[1,3,512,1024]{3,2,1,0:T(8,128)(2,1)} fusion(bf16[3,2,512,512]{3,2,1,0:T(8,128)(2,1)S(1)} %bitcast.111, bf16[3,1,512,512]{3,2,1,0:T(8,128)(2,1)} %get-tuple-element.8, bf16[3,1,512,512]{3,2,1,0:T(8,128)(2,1)} %get-tuple-element.7), kind=kOutput, calls=%fused_computation.28 | convolution fusion | flops 3243245568 | bytes 9437184 | tf_op jit(solution)/shard_map/fpsi,fpsj->fij/dot_general | solution.py:101
  97.1 50.0 %collective-permute-done.1 = bf16[3,2,512,512]{3,2,1,0:T(8,128)(2,1)} collective-permute-done((bf16[3,2,512,512]{3,2,1,0:T(8,128)(2,1)S(1)}, bf16[3,2,512,512]{3,2,1,0:T(8,128)(2,1)}, u32[]{:S(2)}, u32[]{:S(2)}) %collective-permute-start.1) | collective-permute-done | bytes 3145760 | tf_op jit(solution)/shard_map/ppermute | solution.py:22
  147.1 7.4 %collective-permute-start.2 = (bf16[3,2,512,512]{3,2,1,0:T(8,128)(2,1)}, bf16[3,2,512,512]{3,2,1,0:T(8,128)(2,1)}, u32[]{:S(2)}, u32[]{:S(2)}) collective-permute-start(bf16[3,2,512,512]{3,2,1,0:T(8,128)(2,1)} %collective-permute-done.1), channel_id=1, source_target_pairs={{0,8},{16,24},{32,40},{48,56},{64,72},{80,88},{96,104},{112,120},{... | collective-permute-start | bytes 9437192 | tf_op jit(solution)/shard_map/ppermute | solution.py:112
  154.5 3.7 %slice_negate_fusion = (bf16[3,1,512,512]{3,2,1,0:T(8,128)(2,1)}, bf16[3,1,512,512]{3,2,1,0:T(8,128)(2,1)}) fusion(bf16[3,2,512,512]{3,2,1,0:T(8,128)(2,1)} %collective-permute-done.1), kind=kLoop, calls=%fused_computation.57 | loop fusion | flops 786432 | bytes 6291456 | tf_op jit(solution)/shard_map/neg | solution.py:99
  158.3 1.3 copy.28
  159.6 2.0 collective-permute-start.3
  161.6 6.3 %fusion.23 = bf16[1,3,512,1024]{3,2,1,0:T(8,128)(2,1)S(1)} fusion(bf16[3,2,512,512]{3,2,1,0:T(8,128)(2,1)S(1)} %bitcast.112, bf16[3,1,512,512]{3,2,1,0:T(8,128)(2,1)} %get-tuple-element.12, bf16[3,1,512,512]{3,2,1,0:T(8,128)(2,1)} %get-tuple-element.11, bf16[3,2,512,512]{3,2,1,0:T(8,128)(2,1)} %collective-permute-done.1), kind=kOutput, calls=%fused_computation.30 | convolution fusion | flops 3243245568 | bytes 12582912 | tf_op jit(solution)/shard_map/fpsi,fpsj->fij/dot_general | solution.py:101
  167.9 1.3 collective-permute-start.5
  169.3 1.3 fusion.48
  170.6 17.1 %collective-permute-done.3 = bf16[1,2,512,512]{3,2,1,0:T(8,128)(2,1)S(1)} collective-permute-done((bf16[1,2,512,512]{3,2,1,0:T(8,128)(2,1)S(1)}, bf16[1,2,512,512]{3,2,1,0:T(8,128)(2,1)S(1)}, u32[]{:S(2)}, u32[]{:S(2)}) %collective-permute-start.3) | collective-permute-done | bytes 1048608 | tf_op jit(solution)/shard_map/ppermute | solution.py:22
  187.7 1.6 collective-permute-start.4
  189.4 0.4 maximum_multiply_fusion
  189.9 1.3 fusion.50
  191.2 0.4 maximum_multiply_fusion.2
  191.8 2.2 %fusion.49 = bf16[1,1,512,1024]{3,2,1,0:T(8,128)(2,1)} fusion(bf16[2,512,512]{2,1,0:T(8,128)(2,1)S(1)} %bitcast.122, bf16[1,1,512,512]{3,2,1,0:T(8,128)(2,1)S(1)} %get-tuple-element.16, bf16[1,1,512,512]{3,2,1,0:T(8,128)(2,1)S(1)} %get-tuple-element.15, bf16[1,2,512,512]{3,2,1,0:T(8,128)(2,1)S(1)} %broadcast_select_fusion.1), kind=kOutput, calls=%fused_computation.61 | convolution fusion | flops 1081081856 | bytes 4194304 | tf_op jit(solution)/shard_map/fpsi,fpsj->fij/dot_general | solution.py:101
  194.1 2.2 %broadcast_select_fusion = bf16[3,2,512,512]{3,2,1,0:T(8,128)(2,1)S(1)} fusion(bf16[3,2,512,512]{3,2,1,0:T(8,128)(2,1)} %collective-permute-done.2, bf16[3,2,512,512]{3,2,1,0:T(8,128)(2,1)} %collective-permute-done, pred[]{:T(512)S(6)} %eq.22), kind=kLoop, calls=%fused_computation.32 | loop fusion | flops 1572864 | bytes 9437185 | tf_op jit(solution)/shard_map/jit(_where)/select_n | solution.py:114
  196.3 1.9 slice_negate_fusion.1
  198.1 5.4 %fusion.22 = bf16[1,3,512,1024]{3,2,1,0:T(8,128)(2,1)S(1)} fusion(bf16[3,2,512,512]{3,2,1,0:T(8,128)(2,1)S(1)} %bitcast.113, bf16[3,1,512,512]{3,2,1,0:T(8,128)(2,1)} %get-tuple-element.10, bf16[3,1,512,512]{3,2,1,0:T(8,128)(2,1)} %get-tuple-element.9, bf16[3,2,512,512]{3,2,1,0:T(8,128)(2,1)S(1)} %broadcast_select_fusion), kind=kOutput, calls=%fused_computation.29 | convolution fusion | flops 3243245568 | bytes 12582912 | tf_op jit(solution)/shard_map/fpsi,fpsj->fij/dot_general | solution.py:101
  204.0 5.5 %pad_maximum_fusion = bf16[3,4,512,1024]{3,2,1,0:T(8,128)(2,1)} fusion(bf16[1,4,512,1024]{3,2,1,0:T(8,128)(2,1)S(1)} %maximum_multiply_fusion.2, bf16[1,4,512,1024]{3,2,1,0:T(8,128)(2,1)S(1)} %maximum_multiply_fusion.1, bf16[1,4,512,1024]{3,2,1,0:T(8,128)(2,1)S(1)} %maximum_multiply_fusion), kind=kLoop, calls=%fused_computation | loop fusion | flops 12582912 | bytes 25165824 | tf_op jit(solution)/shard_map/stack | solution.py:148
  (23 shorter events, 1.3 us)
Async XLA Ops:
  73.8 12.1 %collective-permute-start = (bf16[3,2,512,512]{3,2,1,0:T(8,128)(2,1)S(1)}, bf16[3,2,512,512]{3,2,1,0:T(8,128)(2,1)}, u32[]{:S(2)}, u32[]{:S(2)}) collective-permute-start(bf16[3,2,512,512]{3,2,1,0:T(8,128)(2,1)S(1)} %bitcast.108), channel_id=1, source_target_pairs={{8,0},{24,16},{40,32},{56,48},{72,64},{88,80},{104,96},{120,112},{... | collective-permute-start | bytes 9437192 | tf_op jit(solution)/shard_map/ppermute | solution.py:111
  75.1 72.0 %collective-permute-start.1 = (bf16[3,2,512,512]{3,2,1,0:T(8,128)(2,1)S(1)}, bf16[3,2,512,512]{3,2,1,0:T(8,128)(2,1)}, u32[]{:S(2)}, u32[]{:S(2)}) collective-permute-start(bf16[3,2,512,512]{3,2,1,0:T(8,128)(2,1)S(1)} %bitcast.109), channel_id=1, source_target_pairs={{16,0},{24,8},{32,16},{40,24},{48,32},{56,40},{64,48},{72,56},{80,... | collective-permute-start | bytes 9437192 | tf_op jit(solution)/shard_map/ppermute | solution.py:22
  85.9 72.4 %all-to-all-start.1 = ((bf16[8,2,64,512]{3,2,1,0:T(8,128)(2,1)}), bf16[8,2,64,512]{3,2,1,0:T(8,128)(2,1)}, u32[]{:S(2)}, u32[]{:S(2)}) async-start(bf16[8,2,64,512]{3,2,1,0:T(8,128)(2,1)} %bitcast.123), calls=%async_computation.1 | async-start | bytes 2097152 | tf_op jit(solution)/shard_map/all_to_all | solution.py:137
  147.1 47.0 %collective-permute-start.2 = (bf16[3,2,512,512]{3,2,1,0:T(8,128)(2,1)}, bf16[3,2,512,512]{3,2,1,0:T(8,128)(2,1)}, u32[]{:S(2)}, u32[]{:S(2)}) collective-permute-start(bf16[3,2,512,512]{3,2,1,0:T(8,128)(2,1)} %collective-permute-done.1), channel_id=1, source_target_pairs={{0,8},{16,24},{32,40},{48,56},{64,72},{80,88},{96,104},{112,120},{... | collective-permute-start | bytes 9437192 | tf_op jit(solution)/shard_map/ppermute | solution.py:112
  159.6 28.1 %collective-permute-start.3 = (bf16[1,2,512,512]{3,2,1,0:T(8,128)(2,1)S(1)}, bf16[1,2,512,512]{3,2,1,0:T(8,128)(2,1)S(1)}, u32[]{:S(2)}, u32[]{:S(2)}) collective-permute-start(bf16[1,2,512,512]{3,2,1,0:T(8,128)(2,1)S(1)} %bitcast.116), channel_id=1, source_target_pairs={{16,0},{24,8},{32,16},{40,24},{48,32},{56,40},{64,48},{72,56},{80,... | collective-permute-start | bytes 3145736 | tf_op jit(solution)/shard_map/ppermute | solution.py:22
  167.9 23.7 %collective-permute-start.5 = (bf16[1,2,512,512]{3,2,1,0:T(8,128)(2,1)S(1)}, bf16[1,2,512,512]{3,2,1,0:T(8,128)(2,1)S(1)}, u32[]{:S(2)}, u32[]{:S(2)}) collective-permute-start(bf16[1,2,512,512]{3,2,1,0:T(8,128)(2,1)S(1)} %bitcast.117), channel_id=1, source_target_pairs={{8,0},{24,16},{40,32},{56,48},{72,64},{88,80},{104,96},{120,112},{... | collective-permute-start | bytes 3145736 | tf_op jit(solution)/shard_map/ppermute | solution.py:111
  169.3 20.1 %copy-start = (bf16[1,3,512,1024]{3,2,1,0:T(8,128)(2,1)S(1)}, bf16[1,3,512,1024]{3,2,1,0:T(8,128)(2,1)}, u32[]{:S(2)}) copy-start(bf16[1,3,512,1024]{3,2,1,0:T(8,128)(2,1)} %fusion.21) | copy-start | bytes 9437188
  187.7 3.9 %collective-permute-start.4 = (bf16[1,2,512,512]{3,2,1,0:T(8,128)(2,1)S(1)}, bf16[1,2,512,512]{3,2,1,0:T(8,128)(2,1)S(1)}, u32[]{:S(2)}, u32[]{:S(2)}) collective-permute-start(bf16[1,2,512,512]{3,2,1,0:T(8,128)(2,1)S(1)} %collective-permute-done.3), channel_id=1, source_target_pairs={{0,8},{16,24},{32,40},{48,56},{64,72},{80,88},{96,104},{112,120},{... | collective-permute-start | bytes 3145736 | tf_op jit(solution)/shard_map/ppermute | solution.py:112
  198.1 5.4 %copy-start.1 = (bf16[1,1,512,1024]{3,2,1,0:T(8,128)(2,1)S(1)}, bf16[1,1,512,1024]{3,2,1,0:T(8,128)(2,1)}, u32[]{:S(2)}) copy-start(bf16[1,1,512,1024]{3,2,1,0:T(8,128)(2,1)} %fusion.49) | copy-start | bytes 3145732

commit v14 on v12

--- a/solution.py
+++ b/solution.py
@@ -105,9 +105,14 @@
     return results
 
 
-def neighbour_panels(own_panel):
+def neighbour_panels(own_panel, flows=1):
     n_chan = lax.axis_size("chan")
-    second_panel = from_behind(own_panel, "chan", -2)
+    if flows == 1:
+        second_panel = from_behind(own_panel, "chan", -2)
+    else:
+        second_panel = jnp.concatenate(
+            [from_behind(own_panel[b:b + 1], "chan", -2) for b in range(own_panel.shape[0])], axis=0
+        )
     from_sibling = lax.ppermute(own_panel, "chan", [(c + 1, c) for c in range(0, n_chan, 2)])
     from_forward = lax.ppermute(second_panel, "chan", [(c - 1, c) for c in range(1, n_chan, 2)])
     odd = lax.axis_index("chan") % 2 == 1
@@ -129,7 +134,7 @@
     chunk_products = []
     for k in range(chunks):
         own_panel = lax.all_to_all(parts[k], "freq", split_axis=0, concat_axis=2, tiled=True)
-        upper_panel, second_panel, from_sibling = neighbour_panels(own_panel)
+        upper_panel, second_panel, from_sibling = neighbour_panels(own_panel, 1 if k + 1 < chunks else 2)
         if k + 1 < chunks:
             _, parts[k + 1] = lax.optimization_barrier((from_sibling, parts[k + 1]))
         chunk_products.append(local_products(own_panel, [own_panel, upper_panel, second_panel]))

time: 208 us -> 211 us (1.014)
  waiting for transfers between devices: 88.8 us -> 81.5 us
  starting transfers between devices: 18.7 us -> 24.4 us
  matrix products: 17 us -> 19.4 us
    all_to_all x1, waiting for transfers between devices: 17.1 us -> 7.55 us  [shards(): lax.all_to_all(parts[k], 'freq', split_axis=0, concat_axis=2, tiled=True)]
    ppermute x2, starting transfers between devices: 5.58 us -> 8.86 us  [neighbour_panels(): lax.ppermute(second_panel, 'chan', [(c - 1, c) for c in range(1, n_chan,...]
    ppermute x2 -> x3, starting transfers between devices: 6.04 us -> 8.46 us  [from_behind(): return lax.ppermute(block, axis, route)]
    dot_general x6, matrix products: 17 us -> 19.4 us  [local_products(): jnp.einsum('fpsi,fpsj->fij', left_panel, both, preferred_element_type=jnp...]
    ppermute x2 -> x3, waiting for transfers between devices: 71.7 us -> 73.9 us  [from_behind(): return lax.ppermute(block, axis, route)]
    unnamed x8 -> x7, local copies, waits for them, and re-layouts: 6.97 us -> 7.3 us
  transfers between devices with their start and end apart: 7 -> 8, of which waited for: 3 -> 4; matrix products, arithmetic and copies ran while one was open for 12% -> 14% of each run, Pallas kernels for 0% -> 0%
where the time goes in v14:
time: 211 us; the launch traced here: 209 us
  waiting for transfers between devices  81.5 us (39%)
  blocking collectives  34.6 us (16%)
  starting transfers between devices  24.4 us (12%)
  Pallas kernels  20.2 us (10%)
  matrix products  19.4 us (9%)
  local copies, waits for them, and re-layouts  14.7 us (7%)
  other arithmetic  13.5 us (6%)
    ppermute x3, waiting for transfers between devices, from_behind(): return lax.ppermute(block, axis, route)  73.9 us
    all_to_all x1, blocking collectives, shards(): lax.all_to_all(parts[k], 'freq', split_axis=0, concat_axis=2, tiled=True)  34.6 us
    pallas_call x1, Pallas kernels, whitened_spectra(): pl.pallas_call(functools.partial(spectra_kernel, seg_count, window), out_...  20.2 us
    dot_general x6, matrix products, local_products(): jnp.einsum('fpsi,fpsj->fij', left_panel, both, preferred_element_type=jnp...  19.4 us
    ppermute x2, starting transfers between devices, neighbour_panels(): lax.ppermute(second_panel, 'chan', [(c - 1, c) for c in range(1, n_chan,...  8.86 us
    ppermute x3, starting transfers between devices, from_behind(): return lax.ppermute(block, axis, route)  8.46 us
    all_to_all x1, waiting for transfers between devices, shards(): lax.all_to_all(parts[k], 'freq', split_axis=0, concat_axis=2, tiled=True)  7.55 us
    unnamed x7, local copies, waits for them, and re-layouts  7.3 us
  transfers between devices with their start and end apart: 8, of which 4 were waited for; matrix products, arithmetic and copies ran while one was open for 14% of the time, Pallas kernels for 0%

profile of v14, /device:TPU:34, one launch (start us, length us, event | category | flops | bytes accessed | tf_op | source)
XLA Modules:
  0.0 209.2 jit_solution(4103069225542546083)
XLA Ops:
  0.1 1.2 convert_element_type.70
  2.0 0.7 pad_convert_fusion.dft_ref
  2.7 20.2 %shard_map.46 = bf16[64,64,512]{2,1,0:T(8,128)(2,1)} custom-call(s32[64]{0:T(128)} %offs_ref.1, f32[64,384]{1,0:T(8,128)} %pad_convert_fusion.dft_ref, f32[1,512]{1,0:T(1,128)} %bitcast.111, bf16[8448,512]{1,0:T(8,128)(2,1)} %rec_hbm.1), custom_call_target="tpu_custom_call" | custom-call | flops 1610612736 | bytes 29360128 | tf_op jit(solution)/shard_map/pallas_call | solution.py:69
  22.9 4.3 %fusion.88 = (bf16[64,2,1,16,512]{4,3,2,1,0:T(8,128)(2,1)}, bf16[64,2,1,16,512]{4,3,2,1,0:T(8,128)(2,1)S(1)}) fusion(bf16[64,2,2,16,512]{4,3,2,1,0:T(8,128)(2,1)} %bitcast.99), kind=kLoop, calls=%fused_computation.97 | loop fusion | bytes 8388608 | tf_op jit(solution)/shard_map/slice | solution.py:133
  27.2 2.2 %copy.50 = bf16[64,2,1,16,512]{4,1,0,3,2:T(2,128)(2,1)S(1)} copy(bf16[64,2,1,16,512]{4,3,2,1,0:T(8,128)(2,1)S(1)} %get-tuple-element.8) | data formatting | bytes 4194304
  29.3 34.6 %all_to_all.36 = bf16[16,2,64,512]{3,1,2,0:T(2,128)(2,1)S(1)} all-to-all(bf16[16,2,64,512]{3,1,2,0:T(2,128)(2,1)S(1)} %bitcast.107), channel_id=1, replica_groups=mesh['chan'=16,'freq'=8] {'freq'}, dimensions={0} | all-to-all | bytes 4194304 | tf_op jit(solution)/shard_map/all_to_all | solution.py:136
  63.9 0.4 copy.22
  64.4 1.5 collective-permute-start
  65.9 3.1 %collective-permute-start.1 = (bf16[2,2,512,512]{3,2,1,0:T(8,128)(2,1)S(1)}, bf16[2,2,512,512]{3,2,1,0:T(8,128)(2,1)}, u32[]{:S(2)}, u32[]{:S(2)}) collective-permute-start(bf16[2,2,512,512]{3,2,1,0:T(8,128)(2,1)S(1)} %bitcast.101), channel_id=1, source_target_pairs={{16,0},{24,8},{32,16},{40,24},{48,32},{56,40},{64,48},{72,56},{80,... | collective-permute-start | bytes 6291464 | tf_op jit(solution)/shard_map/ppermute | solution.py:22
  69.6 5.1 %copy.49 = bf16[64,2,1,16,512]{4,1,0,3,2:T(2,128)(2,1)} copy(bf16[64,2,1,16,512]{4,3,2,1,0:T(8,128)(2,1)} %get-tuple-element.7) | data formatting | bytes 4194304
  74.7 4.4 %all-to-all-start.1 = ((bf16[16,2,64,512]{3,1,2,0:T(2,128)(2,1)}), bf16[16,2,64,512]{3,1,2,0:T(2,128)(2,1)}, u32[]{:S(2)}, u32[]{:S(2)}) async-start(bf16[16,2,64,512]{3,1,2,0:T(2,128)(2,1)} %bitcast.106), calls=%async_computation.1 | async-start | bytes 4194304 | tf_op jit(solution)/shard_map/all_to_all | solution.py:136
  79.2 3.6 %fusion.54 = bf16[1,2,512,1024]{3,2,1,0:T(8,128)(2,1)} fusion(bf16[2,2,512,512]{3,2,1,0:T(8,128)(2,1)S(1)} %bitcast.103, bf16[2,1,512,512]{3,2,1,0:T(8,128)(2,1)S(1)} %get-tuple-element.10, bf16[2,1,512,512]{3,2,1,0:T(8,128)(2,1)S(1)} %get-tuple-element.9), kind=kOutput, calls=%fused_computation.56 | convolution fusion | flops 2162163712 | bytes 6291456 | tf_op jit(solution)/shard_map/fpsi,fpsj->fij/dot_general | solution.py:101
  82.8 32.9 %collective-permute-done.1 = bf16[2,2,512,512]{3,2,1,0:T(8,128)(2,1)} collective-permute-done((bf16[2,2,512,512]{3,2,1,0:T(8,128)(2,1)S(1)}, bf16[2,2,512,512]{3,2,1,0:T(8,128)(2,1)}, u32[]{:S(2)}, u32[]{:S(2)}) %collective-permute-start.1) | collective-permute-done | bytes 2097184 | tf_op jit(solution)/shard_map/ppermute | solution.py:22
  115.7 6.5 %collective-permute-start.2 = (bf16[2,2,512,512]{3,2,1,0:T(8,128)(2,1)}, bf16[2,2,512,512]{3,2,1,0:T(8,128)(2,1)}, u32[]{:S(2)}, u32[]{:S(2)}) collective-permute-start(bf16[2,2,512,512]{3,2,1,0:T(8,128)(2,1)} %collective-permute-done.1), channel_id=1, source_target_pairs={{0,8},{16,24},{32,40},{48,56},{64,72},{80,88},{96,104},{112,120},{... | collective-permute-start | bytes 6291464 | tf_op jit(solution)/shard_map/ppermute | solution.py:117
  122.2 1.7 slice_negate_fusion.1
  123.9 5.3 %fusion.66 = bf16[1,2,512,1024]{3,2,1,0:T(8,128)(2,1)} fusion(bf16[2,2,512,512]{3,2,1,0:T(8,128)(2,1)S(1)} %bitcast.104, bf16[2,1,512,512]{3,2,1,0:T(8,128)(2,1)S(1)} %get-tuple-element.18, bf16[2,1,512,512]{3,2,1,0:T(8,128)(2,1)S(1)} %get-tuple-element.17, bf16[2,2,512,512]{3,2,1,0:T(8,128)(2,1)} %collective-permute-done.1), kind=kOutput, calls=%fused_computation.60 | convolution fusion | flops 2162163712 | bytes 8388608 | tf_op jit(solution)/shard_map/fpsi,fpsj->fij/dot_general | solution.py:101
  129.2 7.6 %all-to-all-done.1 = bf16[16,2,64,512]{3,1,2,0:T(2,128)(2,1)} async-done(((bf16[16,2,64,512]{3,1,2,0:T(2,128)(2,1)}), bf16[16,2,64,512]{3,1,2,0:T(2,128)(2,1)}, u32[]{:S(2)}, u32[]{:S(2)}) %all-to-all-start.1) | async-done | bytes 2097184 | tf_op jit(solution)/shard_map/all_to_all | solution.py:136
  136.8 2.0 copy.51
  139.0 3.0 %collective-permute-start.3 = (bf16[1,2,512,512]{3,2,1,0:T(8,128)(2,1)S(1)}, bf16[1,2,512,512]{3,2,1,0:T(8,128)(2,1)S(1)}, u32[]{:S(2)}, u32[]{:S(2)}) collective-permute-start(bf16[1,2,512,512]{3,2,1,0:T(8,128)(2,1)S(1)} %bitcast.110), channel_id=1, source_target_pairs={{16,0},{24,8},{32,16},{40,24},{48,32},{56,40},{64,48},{72,56},{80,... | collective-permute-start | bytes 3145736 | tf_op jit(solution)/shard_map/ppermute | solution.py:22
  142.0 2.4 %collective-permute-start.4 = (bf16[1,2,512,512]{3,2,1,0:T(8,128)(2,1)S(1)}, bf16[1,2,512,512]{3,2,1,0:T(8,128)(2,1)S(1)}, u32[]{:S(2)}, u32[]{:S(2)}) collective-permute-start(bf16[1,2,512,512]{3,2,1,0:T(8,128)(2,1)S(1)} %bitcast.109), channel_id=1, source_target_pairs={{16,0},{24,8},{32,16},{40,24},{48,32},{56,40},{64,48},{72,56},{80,... | collective-permute-start | bytes 3145736 | tf_op jit(solution)/shard_map/ppermute | solution.py:22
  144.6 1.3 collective-permute-start.6
  145.9 2.6 %fusion.57 = bf16[1,2,512,1024]{3,2,1,0:T(8,128)(2,1)S(1)} fusion(bf16[2,2,512,512]{3,2,1,0:T(8,128)(2,1)S(1)} %bitcast.96, bf16[2,1,512,512]{3,2,1,0:T(8,128)(2,1)S(1)} %get-tuple-element.12, bf16[2,1,512,512]{3,2,1,0:T(8,128)(2,1)S(1)} %get-tuple-element.11), kind=kOutput, calls=%fused_computation.57 | convolution fusion | flops 2162163712 | bytes 6291456 | tf_op jit(solution)/shard_map/fpsi,fpsj->fij/dot_general | solution.py:101
  148.5 0.4 maximum_multiply_fusion
  148.9 18.6 %collective-permute-done.3 = bf16[1,2,512,512]{3,2,1,0:T(8,128)(2,1)S(1)} collective-permute-done((bf16[1,2,512,512]{3,2,1,0:T(8,128)(2,1)S(1)}, bf16[1,2,512,512]{3,2,1,0:T(8,128)(2,1)S(1)}, u32[]{:S(2)}, u32[]{:S(2)}) %collective-permute-start.3) | collective-permute-done | bytes 1048608 | tf_op jit(solution)/shard_map/ppermute | solution.py:22
  167.6 22.4 %collective-permute-done.4 = bf16[1,2,512,512]{3,2,1,0:T(8,128)(2,1)S(1)} collective-permute-done((bf16[1,2,512,512]{3,2,1,0:T(8,128)(2,1)S(1)}, bf16[1,2,512,512]{3,2,1,0:T(8,128)(2,1)S(1)}, u32[]{:S(2)}, u32[]{:S(2)}) %collective-permute-start.4) | collective-permute-done | bytes 1048608 | tf_op jit(solution)/shard_map/ppermute | solution.py:22
  190.1 2.4 %collective-permute-start.5 = (bf16[2,2,512,512]{3,2,1,0:T(8,128)(2,1)S(1)}, bf16[2,2,512,512]{3,2,1,0:T(8,128)(2,1)S(1)}, u32[]{:S(2)}, u32[]{:S(2)}) collective-permute-start(bf16[2,2,512,512]{3,2,1,0:T(8,128)(2,1)S(1)} %constant_dynamic-update-slice_fusion), channel_id=1, source_target_pairs={{0,8},{16,24},{32,40},{48,56},{64,72},{80,88},{96,104},{112,120},{... | collective-permute-start | bytes 6291464 | tf_op jit(solution)/shard_map/ppermute | solution.py:117
  192.5 1.8 broadcast_select_fusion.1
  194.5 2.6 %fusion.60 = bf16[1,2,512,1024]{3,2,1,0:T(8,128)(2,1)S(1)} fusion(bf16[2,2,512,512]{3,2,1,0:T(8,128)(2,1)S(1)} %bitcast.105, bf16[2,1,512,512]{3,2,1,0:T(8,128)(2,1)S(1)} %get-tuple-element.14, bf16[2,1,512,512]{3,2,1,0:T(8,128)(2,1)S(1)} %get-tuple-element.13, bf16[2,2,512,512]{3,2,1,0:T(8,128)(2,1)S(1)} %broadcast_select_fusion.1), kind=kOutput, calls=%fused_computation.58 | convolution fusion | flops 2162163712 | bytes 8388608 | tf_op jit(solution)/shard_map/fpsi,fpsj->fij/dot_general | solution.py:101
  197.2 2.6 %fusion.69 = bf16[1,2,512,1024]{3,2,1,0:T(8,128)(2,1)S(1)} fusion(bf16[2,2,512,512]{3,2,1,0:T(8,128)(2,1)S(1)} %bitcast.97, bf16[2,1,512,512]{3,2,1,0:T(8,128)(2,1)S(1)} %get-tuple-element.20, bf16[2,1,512,512]{3,2,1,0:T(8,128)(2,1)S(1)} %get-tuple-element.19, bf16[2,2,512,512]{3,2,1,0:T(8,128)(2,1)S(1)} %constant_dynamic-update-slice_fusion), kind=kOutput, calls=%fused_computation.61 | convolution fusion | flops 2162163712 | bytes 8388608 | tf_op jit(solution)/shard_map/fpsi,fpsj->fij/dot_general | solution.py:101
  199.9 0.4 maximum_multiply_fusion.2
  200.7 2.6 %fusion.63 = bf16[1,2,512,1024]{3,2,1,0:T(8,128)(2,1)S(1)} fusion(bf16[2,2,512,512]{3,2,1,0:T(8,128)(2,1)S(1)} %bitcast.98, bf16[2,1,512,512]{3,2,1,0:T(8,128)(2,1)S(1)} %get-tuple-element.16, bf16[2,1,512,512]{3,2,1,0:T(8,128)(2,1)S(1)} %get-tuple-element.15, bf16[2,2,512,512]{3,2,1,0:T(8,128)(2,1)S(1)} %broadcast_select_fusion), kind=kOutput, calls=%fused_computation.59 | convolution fusion | flops 2162163712 | bytes 8388608 | tf_op jit(solution)/shard_map/fpsi,fpsj->fij/dot_general | solution.py:101
  203.7 5.5 %pad_maximum_fusion = bf16[3,4,512,1024]{3,2,1,0:T(8,128)(2,1)} fusion(bf16[1,4,512,1024]{3,2,1,0:T(8,128)(2,1)S(1)} %maximum_multiply_fusion.2, bf16[1,4,512,1024]{3,2,1,0:T(8,128)(2,1)S(1)} %maximum_multiply_fusion.1, bf16[1,4,512,1024]{3,2,1,0:T(8,128)(2,1)S(1)} %maximum_multiply_fusion), kind=kLoop, calls=%fused_computation | loop fusion | flops 12582912 | bytes 25165824 | tf_op jit(solution)/shard_map/stack | solution.py:147
  (28 shorter events, 2.5 us)
Async XLA Ops:
  64.4 10.3 %collective-permute-start = (bf16[2,2,512,512]{3,2,1,0:T(8,128)(2,1)S(1)}, bf16[2,2,512,512]{3,2,1,0:T(8,128)(2,1)}, u32[]{:S(2)}, u32[]{:S(2)}) collective-permute-start(bf16[2,2,512,512]{3,2,1,0:T(8,128)(2,1)S(1)} %bitcast.100), channel_id=1, source_target_pairs={{8,0},{24,16},{40,32},{56,48},{72,64},{88,80},{104,96},{120,112},{... | collective-permute-start | bytes 6291464 | tf_op jit(solution)/shard_map/ppermute | solution.py:116
  65.9 49.9 %collective-permute-start.1 = (bf16[2,2,512,512]{3,2,1,0:T(8,128)(2,1)S(1)}, bf16[2,2,512,512]{3,2,1,0:T(8,128)(2,1)}, u32[]{:S(2)}, u32[]{:S(2)}) collective-permute-start(bf16[2,2,512,512]{3,2,1,0:T(8,128)(2,1)S(1)} %bitcast.101), channel_id=1, source_target_pairs={{16,0},{24,8},{32,16},{40,24},{48,32},{56,40},{64,48},{72,56},{80,... | collective-permute-start | bytes 6291464 | tf_op jit(solution)/shard_map/ppermute | solution.py:22
  74.7 62.0 %all-to-all-start.1 = ((bf16[16,2,64,512]{3,1,2,0:T(2,128)(2,1)}), bf16[16,2,64,512]{3,1,2,0:T(2,128)(2,1)}, u32[]{:S(2)}, u32[]{:S(2)}) async-start(bf16[16,2,64,512]{3,1,2,0:T(2,128)(2,1)} %bitcast.106), calls=%async_computation.1 | async-start | bytes 4194304 | tf_op jit(solution)/shard_map/all_to_all | solution.py:136
  115.7 76.7 %collective-permute-start.2 = (bf16[2,2,512,512]{3,2,1,0:T(8,128)(2,1)}, bf16[2,2,512,512]{3,2,1,0:T(8,128)(2,1)}, u32[]{:S(2)}, u32[]{:S(2)}) collective-permute-start(bf16[2,2,512,512]{3,2,1,0:T(8,128)(2,1)} %collective-permute-done.1), channel_id=1, source_target_pairs={{0,8},{16,24},{32,40},{48,56},{64,72},{80,88},{96,104},{112,120},{... | collective-permute-start | bytes 6291464 | tf_op jit(solution)/shard_map/ppermute | solution.py:117
  139.0 28.5 %collective-permute-start.3 = (bf16[1,2,512,512]{3,2,1,0:T(8,128)(2,1)S(1)}, bf16[1,2,512,512]{3,2,1,0:T(8,128)(2,1)S(1)}, u32[]{:S(2)}, u32[]{:S(2)}) collective-permute-start(bf16[1,2,512,512]{3,2,1,0:T(8,128)(2,1)S(1)} %bitcast.110), channel_id=1, source_target_pairs={{16,0},{24,8},{32,16},{40,24},{48,32},{56,40},{64,48},{72,56},{80,... | collective-permute-start | bytes 3145736 | tf_op jit(solution)/shard_map/ppermute | solution.py:22
  142.0 48.0 %collective-permute-start.4 = (bf16[1,2,512,512]{3,2,1,0:T(8,128)(2,1)S(1)}, bf16[1,2,512,512]{3,2,1,0:T(8,128)(2,1)S(1)}, u32[]{:S(2)}, u32[]{:S(2)}) collective-permute-start(bf16[1,2,512,512]{3,2,1,0:T(8,128)(2,1)S(1)} %bitcast.109), channel_id=1, source_target_pairs={{16,0},{24,8},{32,16},{40,24},{48,32},{56,40},{64,48},{72,56},{80,... | collective-permute-start | bytes 3145736 | tf_op jit(solution)/shard_map/ppermute | solution.py:22
  144.6 55.7 %collective-permute-start.6 = (bf16[2,2,512,512]{3,2,1,0:T(8,128)(2,1)S(1)}, bf16[2,2,512,512]{3,2,1,0:T(8,128)(2,1)S(1)}, u32[]{:S(2)}, u32[]{:S(2)}) collective-permute-start(bf16[2,2,512,512]{3,2,1,0:T(8,128)(2,1)S(1)} %bitcast.95), channel_id=1, source_target_pairs={{8,0},{24,16},{40,32},{56,48},{72,64},{88,80},{104,96},{120,112},{... | collective-permute-start | bytes 6291464 | tf_op jit(solution)/shard_map/ppermute | solution.py:116
  145.9 2.6 %copy-start.1 = (bf16[1,2,512,1024]{3,2,1,0:T(8,128)(2,1)S(1)}, bf16[1,2,512,1024]{3,2,1,0:T(8,128)(2,1)}, u32[]{:S(2)}) copy-start(bf16[1,2,512,1024]{3,2,1,0:T(8,128)(2,1)} %fusion.54) | copy-start | bytes 6291460
  190.1 10.2 %collective-permute-start.5 = (bf16[2,2,512,512]{3,2,1,0:T(8,128)(2,1)S(1)}, bf16[2,2,512,512]{3,2,1,0:T(8,128)(2,1)S(1)}, u32[]{:S(2)}, u32[]{:S(2)}) collective-permute-start(bf16[2,2,512,512]{3,2,1,0:T(8,128)(2,1)S(1)} %constant_dynamic-update-slice_fusion), channel_id=1, source_target_pairs={{0,8},{16,24},{32,40},{48,56},{64,72},{80,88},{96,104},{112,120},{... | collective-permute-start | bytes 6291464 | tf_op jit(solution)/shard_map/ppermute | solution.py:117
  197.2 2.6 %copy-start = (bf16[1,2,512,1024]{3,2,1,0:T(8,128)(2,1)S(1)}, bf16[1,2,512,1024]{3,2,1,0:T(8,128)(2,1)}, u32[]{:S(2)}) copy-start(bf16[1,2,512,1024]{3,2,1,0:T(8,128)(2,1)} %fusion.66) | copy-start | bytes 6291460

commit v15 on v12

--- a/solution.py
+++ b/solution.py
@@ -118,7 +118,7 @@
 def shards(records, offsets, dead_mask, band_blocks):
     n_freq = lax.axis_size("freq")
     per_device = BINS // n_freq
-    chunks = 2
+    chunks = 4
     per_chunk = per_device // chunks
     table = dft_table(SEG_LEN, BINS, FIRST_BIN).reshape(n_freq, chunks, per_chunk, 2, SEG_LEN)
     table = table.transpose(3, 1, 0, 2, 4).reshape(2 * BINS, SEG_LEN)

time: 208 us -> 214 us (1.029)
  waiting for transfers between devices: 88.8 us -> 61.5 us
  starting transfers between devices: 18.7 us -> 43.7 us
  matrix products: 17 us -> 29 us
  blocking collectives: 34.4 us -> 23.2 us
  other arithmetic: 13 us -> 17.9 us
    ppermute x2 -> x4, waiting for transfers between devices: 71.7 us -> 56.5 us  [from_behind(): return lax.ppermute(block, axis, route)]
    all_to_all x1 -> x3, waiting for transfers between devices: 17.1 us -> 5 us  [shards(): lax.all_to_all(parts[k], 'freq', split_axis=0, concat_axis=2, tiled=True)]
    dot_general x6 -> x12, matrix products: 17 us -> 29 us  [local_products(): jnp.einsum('fpsi,fpsj->fij', left_panel, both, preferred_element_type=jnp...]
    all_to_all x1, blocking collectives: 34.4 us -> 23.2 us  [shards(): lax.all_to_all(parts[k], 'freq', split_axis=0, concat_axis=2, tiled=True)]
    ppermute x2 -> x4, starting transfers between devices: 5.58 us -> 14.3 us  [neighbour_panels(): lax.ppermute(second_panel, 'chan', [(c - 1, c) for c in range(1, n_chan,...]
    ppermute x2 -> x4, starting transfers between devices: 6.04 us -> 13.1 us  [from_behind(): return lax.ppermute(block, axis, route)]
    all_to_all x1 -> x3, starting transfers between devices: 4.35 us -> 11.1 us  [shards(): lax.all_to_all(parts[k], 'freq', split_axis=0, concat_axis=2, tiled=True)]
    unnamed x8 -> x30, local copies, waits for them, and re-layouts: 6.97 us -> 10.4 us
  transfers between devices with their start and end apart: 7 -> 15, of which waited for: 3 -> 6; matrix products, arithmetic and copies ran while one was open for 12% -> 21% of each run, Pallas kernels for 0% -> 0%
where the time goes in v15:
time: 214 us; the launch traced here: 211 us
  waiting for transfers between devices  61.5 us (29%)
  starting transfers between devices  43.7 us (20%)
  matrix products  29 us (14%)
  blocking collectives  23.2 us (11%)
  Pallas kernels  20.1 us (9%)
  other arithmetic  17.9 us (8%)
  local copies, waits for them, and re-layouts  14.6 us (7%)
    ppermute x4, waiting for transfers between devices, from_behind(): return lax.ppermute(block, axis, route)  56.5 us
    dot_general x12, matrix products, local_products(): jnp.einsum('fpsi,fpsj->fij', left_panel, both, preferred_element_type=jnp...  29 us
    all_to_all x1, blocking collectives, shards(): lax.all_to_all(parts[k], 'freq', split_axis=0, concat_axis=2, tiled=True)  23.2 us
    pallas_call x1, Pallas kernels, whitened_spectra(): pl.pallas_call(functools.partial(spectra_kernel, seg_count, window), out_...  20.1 us
    ppermute x4, starting transfers between devices, neighbour_panels(): lax.ppermute(second_panel, 'chan', [(c - 1, c) for c in range(1, n_chan,...  14.3 us
    ppermute x4, starting transfers between devices, from_behind(): return lax.ppermute(block, axis, route)  13.1 us
    all_to_all x3, starting transfers between devices, shards(): lax.all_to_all(parts[k], 'freq', split_axis=0, concat_axis=2, tiled=True)  11.1 us
    unnamed x30, local copies, waits for them, and re-layouts  10.4 us
  transfers between devices with their start and end apart: 15, of which 6 were waited for; matrix products, arithmetic and copies ran while one was open for 21% of the time, Pallas kernels for 0%

profile of v15, /device:TPU:34, one launch (start us, length us, event | category | flops | bytes accessed | tf_op | source)
XLA Modules:
  0.0 211.2 jit_solution(15171301210243739573)
XLA Ops:
  2.3 20.1 %shard_map.46 = bf16[64,64,512]{2,1,0:T(8,128)(2,1)} custom-call(s32[64]{0:T(128)} %offs_ref.1, f32[64,384]{1,0:T(8,128)} %pad_convert_fusion.dft_ref, f32[1,512]{1,0:T(1,128)} %bitcast.279, bf16[8448,512]{1,0:T(8,128)(2,1)} %rec_hbm.1), custom_call_target="tpu_custom_call" | custom-call | flops 1610612736 | bytes 29360128 | tf_op jit(solution)/shard_map/pallas_call | solution.py:69
  22.5 3.8 %fusion.107 = (bf16[64,2,1,8,512]{4,3,2,1,0:T(8,128)(2,1)}, bf16[64,2,1,8,512]{4,3,2,1,0:T(8,128)(2,1)S(1)}, bf16[64,2,1,8,512]{4,3,2,1,0:T(8,128)(2,1)S(1)}, bf16[64,2,1,8,512]{4,3,2,1,0:T(8,128)(2,1)S(1)}) fusion(bf16[64,2,4,8,512]{4,3,2,1,0:T(8,128)(2,1)} %bitcast.248), kind=kLoop, calls=%fused_computation.165 | loop fusion | bytes 8388608 | tf_op jit(solution)/shard_map/slice | solution.py:128
  26.9 23.2 %all_to_all.72 = bf16[8,2,64,512]{3,2,1,0:T(8,128)(2,1)S(1)} all-to-all(bf16[8,2,64,512]{3,2,1,0:T(8,128)(2,1)S(1)} %bitcast.277), channel_id=1, replica_groups=mesh['chan'=16,'freq'=8] {'freq'}, dimensions={0} | all-to-all | bytes 2097152 | tf_op jit(solution)/shard_map/all_to_all | solution.py:131
  51.4 3.3 %collective-permute-start.3 = (bf16[1,2,512,512]{3,2,1,0:T(8,128)(2,1)S(1)}, bf16[1,2,512,512]{3,2,1,0:T(8,128)(2,1)}, u32[]{:S(2)}, u32[]{:S(2)}) collective-permute-start(bf16[1,2,512,512]{3,2,1,0:T(8,128)(2,1)S(1)} %bitcast.250), channel_id=1, source_target_pairs={{16,0},{24,8},{32,16},{40,24},{48,32},{56,40},{64,48},{72,56},{80,... | collective-permute-start | bytes 3145736 | tf_op jit(solution)/shard_map/ppermute | solution.py:22
  55.4 2.8 %copy.69 = bf16[64,2,1,8,512]{4,0,1,3,2:T(8,128)(2,1)} copy(bf16[64,2,1,8,512]{4,3,2,1,0:T(8,128)(2,1)} %get-tuple-element.11) | data formatting | bytes 2097152
  58.1 1.6 copy.70
  59.7 1.6 copy.71
  61.4 3.7 %all-to-all-start.1 = ((bf16[8,2,64,512]{3,2,1,0:T(8,128)(2,1)}), bf16[8,2,64,512]{3,2,1,0:T(8,128)(2,1)S(1)}, u32[]{:S(2)}, u32[]{:S(2)}) async-start(bf16[8,2,64,512]{3,2,1,0:T(8,128)(2,1)} %bitcast.246), calls=%async_computation.1 | async-start | bytes 2097152 | tf_op jit(solution)/shard_map/all_to_all | solution.py:131
  65.1 2.2 %fusion.72 = bf16[1,1,512,1024]{3,2,1,0:T(8,128)(2,1)} fusion(bf16[2,512,512]{2,1,0:T(8,128)(2,1)S(1)} %bitcast.252, bf16[1,1,512,512]{3,2,1,0:T(8,128)(2,1)S(1)} %get-tuple-element.16, bf16[1,1,512,512]{3,2,1,0:T(8,128)(2,1)S(1)} %get-tuple-element.15, bf16[1,2,512,512]{3,2,1,0:T(8,128)(2,1)S(1)} %bitcast.253), kind=kOutput, calls=%fused_computation.100 | convolution fusion | flops 1081081856 | bytes 4194304 | tf_op jit(solution)/shard_map/fpsi,fpsj->fij/dot_general | solution.py:101
  67.4 11.7 %collective-permute-done.3 = bf16[1,2,512,512]{3,2,1,0:T(8,128)(2,1)} collective-permute-done((bf16[1,2,512,512]{3,2,1,0:T(8,128)(2,1)S(1)}, bf16[1,2,512,512]{3,2,1,0:T(8,128)(2,1)}, u32[]{:S(2)}, u32[]{:S(2)}) %collective-permute-start.3) | collective-permute-done | bytes 1048608 | tf_op jit(solution)/shard_map/ppermute | solution.py:22
  79.1 5.4 %collective-permute-start.4 = (bf16[1,2,512,512]{3,2,1,0:T(8,128)(2,1)}, bf16[1,2,512,512]{3,2,1,0:T(8,128)(2,1)}, u32[]{:S(2)}, u32[]{:S(2)}) collective-permute-start(bf16[1,2,512,512]{3,2,1,0:T(8,128)(2,1)} %collective-permute-done.3), channel_id=1, source_target_pairs={{0,8},{16,24},{32,40},{48,56},{64,72},{80,88},{96,104},{112,120},{... | collective-permute-start | bytes 3145736 | tf_op jit(solution)/shard_map/ppermute | solution.py:112
  85.8 3.5 %fusion.80 = bf16[1,1,512,1024]{3,2,1,0:T(8,128)(2,1)} fusion(bf16[2,512,512]{2,1,0:T(8,128)(2,1)S(1)} %bitcast.254, bf16[1,1,512,512]{3,2,1,0:T(8,128)(2,1)S(1)} %get-tuple-element.32, bf16[1,1,512,512]{3,2,1,0:T(8,128)(2,1)S(1)} %get-tuple-element.31, bf16[1,2,512,512]{3,2,1,0:T(8,128)(2,1)} %collective-permute-done.3), kind=kOutput, calls=%fused_computation.108 | convolution fusion | flops 1081081856 | bytes 4194304 | tf_op jit(solution)/shard_map/fpsi,fpsj->fij/dot_general | solution.py:101
  90.8 2.7 %collective-permute-start.5 = (bf16[1,2,512,512]{3,2,1,0:T(8,128)(2,1)S(1)}, bf16[1,2,512,512]{3,2,1,0:T(8,128)(2,1)}, u32[]{:S(2)}, u32[]{:S(2)}) collective-permute-start(bf16[1,2,512,512]{3,2,1,0:T(8,128)(2,1)S(1)} %bitcast.258), channel_id=1, source_target_pairs={{16,0},{24,8},{32,16},{40,24},{48,32},{56,40},{64,48},{72,56},{80,... | collective-permute-start | bytes 3145736 | tf_op jit(solution)/shard_map/ppermute | solution.py:22
  93.5 2.3 %fusion.73 = bf16[1,1,512,1024]{3,2,1,0:T(8,128)(2,1)} fusion(bf16[2,512,512]{2,1,0:T(8,128)(2,1)S(1)} %bitcast.259, bf16[1,1,512,512]{3,2,1,0:T(8,128)(2,1)S(1)} %get-tuple-element.18, bf16[1,1,512,512]{3,2,1,0:T(8,128)(2,1)S(1)} %get-tuple-element.17, bf16[1,2,512,512]{3,2,1,0:T(8,128)(2,1)S(1)} %bitcast.260), kind=kOutput, calls=%fused_computation.101 | convolution fusion | flops 1081081856 | bytes 4194304 | tf_op jit(solution)/shard_map/fpsi,fpsj->fij/dot_general | solution.py:101
  99.5 3.8 %all-to-all-start.2 = ((bf16[8,2,64,512]{3,2,1,0:T(8,128)(2,1)}), bf16[8,2,64,512]{3,2,1,0:T(8,128)(2,1)S(1)}, u32[]{:S(2)}, u32[]{:S(2)}) async-start(bf16[8,2,64,512]{3,2,1,0:T(8,128)(2,1)} %bitcast.245), calls=%async_computation.2 | async-start | bytes 2097152 | tf_op jit(solution)/shard_map/all_to_all | solution.py:131
  103.3 3.8 %fusion.76 = bf16[1,1,512,1024]{3,2,1,0:T(8,128)(2,1)} fusion(bf16[2,512,512]{2,1,0:T(8,128)(2,1)S(1)} %bitcast.255, bf16[1,1,512,512]{3,2,1,0:T(8,128)(2,1)} %get-tuple-element.24, bf16[1,1,512,512]{3,2,1,0:T(8,128)(2,1)} %get-tuple-element.23, bf16[1,2,512,512]{3,2,1,0:T(8,128)(2,1)} %copy-done), kind=kOutput, calls=%fused_computation.104 | convolution fusion | flops 1081081856 | bytes 4194304 | tf_op jit(solution)/shard_map/fpsi,fpsj->fij/dot_general | solution.py:101
  107.1 12.4 %collective-permute-done.5 = bf16[1,2,512,512]{3,2,1,0:T(8,128)(2,1)} collective-permute-done((bf16[1,2,512,512]{3,2,1,0:T(8,128)(2,1)S(1)}, bf16[1,2,512,512]{3,2,1,0:T(8,128)(2,1)}, u32[]{:S(2)}, u32[]{:S(2)}) %collective-permute-start.5) | collective-permute-done | bytes 1048608 | tf_op jit(solution)/shard_map/ppermute | solution.py:22
  119.5 3.3 %collective-permute-start.6 = (bf16[1,2,512,512]{3,2,1,0:T(8,128)(2,1)}, bf16[1,2,512,512]{3,2,1,0:T(8,128)(2,1)}, u32[]{:S(2)}, u32[]{:S(2)}) collective-permute-start(bf16[1,2,512,512]{3,2,1,0:T(8,128)(2,1)} %collective-permute-done.5), channel_id=1, source_target_pairs={{0,8},{16,24},{32,40},{48,56},{64,72},{80,88},{96,104},{112,120},{... | collective-permute-start | bytes 3145736 | tf_op jit(solution)/shard_map/ppermute | solution.py:112
  124.1 3.5 %fusion.81 = bf16[1,1,512,1024]{3,2,1,0:T(8,128)(2,1)} fusion(bf16[2,512,512]{2,1,0:T(8,128)(2,1)S(1)} %bitcast.261, bf16[1,1,512,512]{3,2,1,0:T(8,128)(2,1)S(1)} %get-tuple-element.34, bf16[1,1,512,512]{3,2,1,0:T(8,128)(2,1)S(1)} %get-tuple-element.33, bf16[1,2,512,512]{3,2,1,0:T(8,128)(2,1)} %collective-permute-done.5), kind=kOutput, calls=%fused_computation.109 | convolution fusion | flops 1081081856 | bytes 4194304 | tf_op jit(solution)/shard_map/fpsi,fpsj->fij/dot_general | solution.py:101
  127.6 2.9 %all-to-all-done.2 = bf16[8,2,64,512]{3,2,1,0:T(8,128)(2,1)S(1)} async-done(((bf16[8,2,64,512]{3,2,1,0:T(8,128)(2,1)}), bf16[8,2,64,512]{3,2,1,0:T(8,128)(2,1)S(1)}, u32[]{:S(2)}, u32[]{:S(2)}) %all-to-all-start.2) | async-done | bytes 1048608 | tf_op jit(solution)/shard_map/all_to_all | solution.py:131
  132.0 4.3 %collective-permute-start.7 = (bf16[1,2,512,512]{3,2,1,0:T(8,128)(2,1)S(1)}, bf16[1,2,512,512]{3,2,1,0:T(8,128)(2,1)}, u32[]{:S(2)}, u32[]{:S(2)}) collective-permute-start(bf16[1,2,512,512]{3,2,1,0:T(8,128)(2,1)S(1)} %bitcast.265), channel_id=1, source_target_pairs={{16,0},{24,8},{32,16},{40,24},{48,32},{56,40},{64,48},{72,56},{80,... | collective-permute-start | bytes 3145736 | tf_op jit(solution)/shard_map/ppermute | solution.py:22
  136.3 2.3 %fusion.74 = bf16[1,1,512,1024]{3,2,1,0:T(8,128)(2,1)} fusion(bf16[2,512,512]{2,1,0:T(8,128)(2,1)S(1)} %bitcast.266, bf16[1,1,512,512]{3,2,1,0:T(8,128)(2,1)S(1)} %get-tuple-element.20, bf16[1,1,512,512]{3,2,1,0:T(8,128)(2,1)S(1)} %get-tuple-element.19, bf16[1,2,512,512]{3,2,1,0:T(8,128)(2,1)S(1)} %bitcast.267), kind=kOutput, calls=%fused_computation.102 | convolution fusion | flops 1081081856 | bytes 4194304 | tf_op jit(solution)/shard_map/fpsi,fpsj->fij/dot_general | solution.py:101
  141.0 3.6 %all-to-all-start.3 = ((bf16[8,2,64,512]{3,2,1,0:T(8,128)(2,1)}), bf16[8,2,64,512]{3,2,1,0:T(8,128)(2,1)S(1)}, u32[]{:S(2)}, u32[]{:S(2)}) async-start(bf16[8,2,64,512]{3,2,1,0:T(8,128)(2,1)} %bitcast.244), calls=%async_computation.3 | async-start | bytes 2097152 | tf_op jit(solution)/shard_map/all_to_all | solution.py:131
  144.6 3.8 %fusion.77 = bf16[1,1,512,1024]{3,2,1,0:T(8,128)(2,1)} fusion(bf16[2,512,512]{2,1,0:T(8,128)(2,1)S(1)} %bitcast.262, bf16[1,1,512,512]{3,2,1,0:T(8,128)(2,1)} %get-tuple-element.26, bf16[1,1,512,512]{3,2,1,0:T(8,128)(2,1)} %get-tuple-element.25, bf16[1,2,512,512]{3,2,1,0:T(8,128)(2,1)} %copy-done.1), kind=kOutput, calls=%fused_computation.105 | convolution fusion | flops 1081081856 | bytes 4194304 | tf_op jit(solution)/shard_map/fpsi,fpsj->fij/dot_general | solution.py:101
  148.4 12.9 %collective-permute-done.7 = bf16[1,2,512,512]{3,2,1,0:T(8,128)(2,1)} collective-permute-done((bf16[1,2,512,512]{3,2,1,0:T(8,128)(2,1)S(1)}, bf16[1,2,512,512]{3,2,1,0:T(8,128)(2,1)}, u32[]{:S(2)}, u32[]{:S(2)}) %collective-permute-start.7) | collective-permute-done | bytes 1048608 | tf_op jit(solution)/shard_map/ppermute | solution.py:22
  161.3 3.7 %collective-permute-start.8 = (bf16[1,2,512,512]{3,2,1,0:T(8,128)(2,1)}, bf16[1,2,512,512]{3,2,1,0:T(8,128)(2,1)}, u32[]{:S(2)}, u32[]{:S(2)}) collective-permute-start(bf16[1,2,512,512]{3,2,1,0:T(8,128)(2,1)} %collective-permute-done.7), channel_id=1, source_target_pairs={{0,8},{16,24},{32,40},{48,56},{64,72},{80,88},{96,104},{112,120},{... | collective-permute-start | bytes 3145736 | tf_op jit(solution)/shard_map/ppermute | solution.py:112
  166.3 2.5 %fusion.82 = bf16[1,1,512,1024]{3,2,1,0:T(8,128)(2,1)S(1)} fusion(bf16[2,512,512]{2,1,0:T(8,128)(2,1)S(1)} %bitcast.268, bf16[1,1,512,512]{3,2,1,0:T(8,128)(2,1)S(1)} %get-tuple-element.36, bf16[1,1,512,512]{3,2,1,0:T(8,128)(2,1)S(1)} %get-tuple-element.35, bf16[1,2,512,512]{3,2,1,0:T(8,128)(2,1)} %collective-permute-done.7), kind=kOutput, calls=%fused_computation.110 | convolution fusion | flops 1081081856 | bytes 4194304 | tf_op jit(solution)/shard_map/fpsi,fpsj->fij/dot_general | solution.py:101
  168.8 2.1 %all-to-all-done.3 = bf16[8,2,64,512]{3,2,1,0:T(8,128)(2,1)S(1)} async-done(((bf16[8,2,64,512]{3,2,1,0:T(8,128)(2,1)}), bf16[8,2,64,512]{3,2,1,0:T(8,128)(2,1)S(1)}, u32[]{:S(2)}, u32[]{:S(2)}) %all-to-all-start.3) | async-done | bytes 1048608 | tf_op jit(solution)/shard_map/all_to_all | solution.py:131
  171.0 2.9 %collective-permute-start.9 = (bf16[1,2,512,512]{3,2,1,0:T(8,128)(2,1)S(1)}, bf16[1,2,512,512]{3,2,1,0:T(8,128)(2,1)S(1)}, u32[]{:S(2)}, u32[]{:S(2)}) collective-permute-start(bf16[1,2,512,512]{3,2,1,0:T(8,128)(2,1)S(1)} %bitcast.270), channel_id=1, source_target_pairs={{16,0},{24,8},{32,16},{40,24},{48,32},{56,40},{64,48},{72,56},{80,... | collective-permute-start | bytes 3145736 | tf_op jit(solution)/shard_map/ppermute | solution.py:22
  179.9 19.5 %collective-permute-done.9 = bf16[1,2,512,512]{3,2,1,0:T(8,128)(2,1)S(1)} collective-permute-done((bf16[1,2,512,512]{3,2,1,0:T(8,128)(2,1)S(1)}, bf16[1,2,512,512]{3,2,1,0:T(8,128)(2,1)S(1)}, u32[]{:S(2)}, u32[]{:S(2)}) %collective-permute-start.9) | collective-permute-done | bytes 1048608 | tf_op jit(solution)/shard_map/ppermute | solution.py:22
  199.4 1.8 collective-permute-start.10
  205.7 5.5 %pad_maximum_fusion = bf16[3,4,512,1024]{3,2,1,0:T(8,128)(2,1)} fusion(bf16[1,4,512,1024]{3,2,1,0:T(8,128)(2,1)S(1)} %maximum_multiply_fusion.2, bf16[1,4,512,1024]{3,2,1,0:T(8,128)(2,1)S(1)} %maximum_multiply_fusion.1, bf16[1,4,512,1024]{3,2,1,0:T(8,128)(2,1)S(1)} %maximum_multiply_fusion), kind=kLoop, calls=%fused_computation | loop fusion | flops 12582912 | bytes 25165824 | tf_op jit(solution)/shard_map/stack | solution.py:142
  (73 shorter events, 27.6 us)
Async XLA Ops:
  50.1 11.2 %collective-permute-start = (bf16[1,2,512,512]{3,2,1,0:T(8,128)(2,1)S(1)}, bf16[1,2,512,512]{3,2,1,0:T(8,128)(2,1)}, u32[]{:S(2)}, u32[]{:S(2)}) collective-permute-start(bf16[1,2,512,512]{3,2,1,0:T(8,128)(2,1)S(1)} %bitcast.249), channel_id=1, source_target_pairs={{8,0},{24,16},{40,32},{56,48},{72,64},{88,80},{104,96},{120,112},{... | collective-permute-start | bytes 3145736 | tf_op jit(solution)/shard_map/ppermute | solution.py:111
  51.4 27.7 %collective-permute-start.3 = (bf16[1,2,512,512]{3,2,1,0:T(8,128)(2,1)S(1)}, bf16[1,2,512,512]{3,2,1,0:T(8,128)(2,1)}, u32[]{:S(2)}, u32[]{:S(2)}) collective-permute-start(bf16[1,2,512,512]{3,2,1,0:T(8,128)(2,1)S(1)} %bitcast.250), channel_id=1, source_target_pairs={{16,0},{24,8},{32,16},{40,24},{48,32},{56,40},{64,48},{72,56},{80,... | collective-permute-start | bytes 3145736 | tf_op jit(solution)/shard_map/ppermute | solution.py:22
  61.4 28.0 %all-to-all-start.1 = ((bf16[8,2,64,512]{3,2,1,0:T(8,128)(2,1)}), bf16[8,2,64,512]{3,2,1,0:T(8,128)(2,1)S(1)}, u32[]{:S(2)}, u32[]{:S(2)}) async-start(bf16[8,2,64,512]{3,2,1,0:T(8,128)(2,1)} %bitcast.246), calls=%async_computation.1 | async-start | bytes 2097152 | tf_op jit(solution)/shard_map/all_to_all | solution.py:131
  79.1 16.6 %collective-permute-start.4 = (bf16[1,2,512,512]{3,2,1,0:T(8,128)(2,1)}, bf16[1,2,512,512]{3,2,1,0:T(8,128)(2,1)}, u32[]{:S(2)}, u32[]{:S(2)}) collective-permute-start(bf16[1,2,512,512]{3,2,1,0:T(8,128)(2,1)} %collective-permute-done.3), channel_id=1, source_target_pairs={{0,8},{16,24},{32,40},{48,56},{64,72},{80,88},{96,104},{112,120},{... | collective-permute-start | bytes 3145736 | tf_op jit(solution)/shard_map/ppermute | solution.py:112
  89.4 8.9 %collective-permute-start.1 = (bf16[1,2,512,512]{3,2,1,0:T(8,128)(2,1)S(1)}, bf16[1,2,512,512]{3,2,1,0:T(8,128)(2,1)S(1)}, u32[]{:S(2)}, u32[]{:S(2)}) collective-permute-start(bf16[1,2,512,512]{3,2,1,0:T(8,128)(2,1)S(1)} %bitcast.256), channel_id=1, source_target_pairs={{8,0},{24,16},{40,32},{56,48},{72,64},{88,80},{104,96},{120,112},{... | collective-permute-start | bytes 3145736 | tf_op jit(solution)/shard_map/ppermute | solution.py:111
  90.8 28.7 %collective-permute-start.5 = (bf16[1,2,512,512]{3,2,1,0:T(8,128)(2,1)S(1)}, bf16[1,2,512,512]{3,2,1,0:T(8,128)(2,1)}, u32[]{:S(2)}, u32[]{:S(2)}) collective-permute-start(bf16[1,2,512,512]{3,2,1,0:T(8,128)(2,1)S(1)} %bitcast.258), channel_id=1, source_target_pairs={{16,0},{24,8},{32,16},{40,24},{48,32},{56,40},{64,48},{72,56},{80,... | collective-permute-start | bytes 3145736 | tf_op jit(solution)/shard_map/ppermute | solution.py:22
  97.1 1.4 copy-start
  98.5 1.0 copy-start.11
  99.5 31.0 %all-to-all-start.2 = ((bf16[8,2,64,512]{3,2,1,0:T(8,128)(2,1)}), bf16[8,2,64,512]{3,2,1,0:T(8,128)(2,1)S(1)}, u32[]{:S(2)}, u32[]{:S(2)}) async-start(bf16[8,2,64,512]{3,2,1,0:T(8,128)(2,1)} %bitcast.245), calls=%async_computation.2 | async-start | bytes 2097152 | tf_op jit(solution)/shard_map/all_to_all | solution.py:131
  119.5 19.1 %collective-permute-start.6 = (bf16[1,2,512,512]{3,2,1,0:T(8,128)(2,1)}, bf16[1,2,512,512]{3,2,1,0:T(8,128)(2,1)}, u32[]{:S(2)}, u32[]{:S(2)}) collective-permute-start(bf16[1,2,512,512]{3,2,1,0:T(8,128)(2,1)} %collective-permute-done.5), channel_id=1, source_target_pairs={{0,8},{16,24},{32,40},{48,56},{64,72},{80,88},{96,104},{112,120},{... | collective-permute-start | bytes 3145736 | tf_op jit(solution)/shard_map/ppermute | solution.py:112
  130.6 9.3 %collective-permute-start.2 = (bf16[1,2,512,512]{3,2,1,0:T(8,128)(2,1)S(1)}, bf16[1,2,512,512]{3,2,1,0:T(8,128)(2,1)S(1)}, u32[]{:S(2)}, u32[]{:S(2)}) collective-permute-start(bf16[1,2,512,512]{3,2,1,0:T(8,128)(2,1)S(1)} %bitcast.263), channel_id=1, source_target_pairs={{8,0},{24,16},{40,32},{56,48},{72,64},{88,80},{104,96},{120,112},{... | collective-permute-start | bytes 3145736 | tf_op jit(solution)/shard_map/ppermute | solution.py:111
  132.0 29.3 %collective-permute-start.7 = (bf16[1,2,512,512]{3,2,1,0:T(8,128)(2,1)S(1)}, bf16[1,2,512,512]{3,2,1,0:T(8,128)(2,1)}, u32[]{:S(2)}, u32[]{:S(2)}) collective-permute-start(bf16[1,2,512,512]{3,2,1,0:T(8,128)(2,1)S(1)} %bitcast.265), channel_id=1, source_target_pairs={{16,0},{24,8},{32,16},{40,24},{48,32},{56,40},{64,48},{72,56},{80,... | collective-permute-start | bytes 3145736 | tf_op jit(solution)/shard_map/ppermute | solution.py:22
  136.3 2.4 %copy-start.12 = (bf16[1,2,512,512]{3,2,1,0:T(8,128)(2,1)S(1)}, bf16[1,2,512,512]{3,2,1,0:T(8,128)(2,1)}, u32[]{:S(2)}) copy-start(bf16[1,2,512,512]{3,2,1,0:T(8,128)(2,1)} %copy-done.11) | copy-start | bytes 3145732
  138.8 1.3 copy-start.1
  140.1 1.0 copy-start.9
  141.0 29.9 %all-to-all-start.3 = ((bf16[8,2,64,512]{3,2,1,0:T(8,128)(2,1)}), bf16[8,2,64,512]{3,2,1,0:T(8,128)(2,1)S(1)}, u32[]{:S(2)}, u32[]{:S(2)}) async-start(bf16[8,2,64,512]{3,2,1,0:T(8,128)(2,1)} %bitcast.244), calls=%async_computation.3 | async-start | bytes 2097152 | tf_op jit(solution)/shard_map/all_to_all | solution.py:131
  161.3 16.5 %collective-permute-start.8 = (bf16[1,2,512,512]{3,2,1,0:T(8,128)(2,1)}, bf16[1,2,512,512]{3,2,1,0:T(8,128)(2,1)}, u32[]{:S(2)}, u32[]{:S(2)}) collective-permute-start(bf16[1,2,512,512]{3,2,1,0:T(8,128)(2,1)} %collective-permute-done.7), channel_id=1, source_target_pairs={{0,8},{16,24},{32,40},{48,56},{64,72},{80,88},{96,104},{112,120},{... | collective-permute-start | bytes 3145736 | tf_op jit(solution)/shard_map/ppermute | solution.py:112
  171.0 28.4 %collective-permute-start.9 = (bf16[1,2,512,512]{3,2,1,0:T(8,128)(2,1)S(1)}, bf16[1,2,512,512]{3,2,1,0:T(8,128)(2,1)S(1)}, u32[]{:S(2)}, u32[]{:S(2)}) collective-permute-start(bf16[1,2,512,512]{3,2,1,0:T(8,128)(2,1)S(1)} %bitcast.270), channel_id=1, source_target_pairs={{16,0},{24,8},{32,16},{40,24},{48,32},{56,40},{64,48},{72,56},{80,... | collective-permute-start | bytes 3145736 | tf_op jit(solution)/shard_map/ppermute | solution.py:22
  173.9 29.5 %collective-permute-start.11 = (bf16[1,2,512,512]{3,2,1,0:T(8,128)(2,1)S(1)}, bf16[1,2,512,512]{3,2,1,0:T(8,128)(2,1)S(1)}, u32[]{:S(2)}, u32[]{:S(2)}) collective-permute-start(bf16[1,2,512,512]{3,2,1,0:T(8,128)(2,1)S(1)} %bitcast.271), channel_id=1, source_target_pairs={{8,0},{24,16},{40,32},{56,48},{72,64},{88,80},{104,96},{120,112},{... | collective-permute-start | bytes 3145736 | tf_op jit(solution)/shard_map/ppermute | solution.py:111
  175.3 1.3 copy-start.4
  175.3 1.5 copy-start.5
  175.3 1.8 copy-start.8
  177.2 1.2 copy-start.10
  199.4 4.0 %collective-permute-start.10 = (bf16[1,2,512,512]{3,2,1,0:T(8,128)(2,1)S(1)}, bf16[1,2,512,512]{3,2,1,0:T(8,128)(2,1)S(1)}, u32[]{:S(2)}, u32[]{:S(2)}) collective-permute-start(bf16[1,2,512,512]{3,2,1,0:T(8,128)(2,1)S(1)} %collective-permute-done.9), channel_id=1, source_target_pairs={{0,8},{16,24},{32,40},{48,56},{64,72},{80,88},{96,104},{112,120},{... | collective-permute-start | bytes 3145736 | tf_op jit(solution)/shard_map/ppermute | solution.py:112
  201.3 1.3 copy-start.2
  201.3 1.5 copy-start.6
  203.6 1.3 copy-start.3
  203.6 1.5 copy-start.7

commit v16 on v12

--- a/solution.py
+++ b/solution.py
@@ -51,7 +51,7 @@
     dft = dft_ref[...]
     live = mask_ref[...]
     for j in range(seg_count):
-        shifted = pltpu.roll(dft, starts[j], 1).astype(jnp.bfloat16)
+        shifted = pltpu.roll(dft, starts[j], 1)[:, :window].astype(jnp.bfloat16)
         copies[j].wait()
         spec = jnp.dot(shifted, frames[j], preferred_element_type=jnp.float32)
         power = jnp.sum(spec * spec, axis=0, keepdims=True) * (1.0 / BINS)
@@ -62,9 +62,9 @@
 def whitened_spectra(records, offsets, dead_mask, dft_rows):
     seg_count = offsets.shape[0]
     channels = records.shape[1]
-    window = SEG_LEN + 128
+    window = SEG_LEN + 16
     rows = dft_rows.shape[0]
-    padded = jnp.pad(dft_rows.astype(jnp.float32), ((0, 0), (0, window - SEG_LEN)))
+    padded = jnp.pad(dft_rows.astype(jnp.float32), ((0, 0), (0, 128)))
     live = dead_mask.astype(jnp.float32).reshape(1, channels)
     return pl.pallas_call(
         functools.partial(spectra_kernel, seg_count, window),
@@ -73,7 +73,7 @@
             num_scalar_prefetch=1,
             grid=(1,),
             in_specs=[
-                pl.BlockSpec((rows, window), lambda i, offs: (0, 0)),
+                pl.BlockSpec((rows, SEG_LEN + 128), lambda i, offs: (0, 0)),
                 pl.BlockSpec((1, channels), lambda i, offs: (0, 0)),
                 pl.BlockSpec(memory_space=pl.ANY),
             ],

time: 208 us -> 208 us (level)
  no operation moved by 1% of the time
where the time goes in v16:
time: 208 us; the launch traced here: 205 us
  waiting for transfers between devices  88.6 us (43%)
  blocking collectives  34.4 us (17%)
  Pallas kernels  19.9 us (10%)
  starting transfers between devices  18.7 us (9%)
  matrix products  17 us (8%)
  other arithmetic  13 us (6%)
  local copies, waits for them, and re-layouts  12.6 us (6%)
    ppermute x2, waiting for transfers between devices, from_behind(): return lax.ppermute(block, axis, route)  71.5 us
    all_to_all x1, blocking collectives, shards(): lax.all_to_all(parts[k], 'freq', split_axis=0, concat_axis=2, tiled=True)  34.4 us
    pallas_call x1, Pallas kernels, whitened_spectra(): pl.pallas_call(functools.partial(spectra_kernel, seg_count, window), out_...  19.9 us
    all_to_all x1, waiting for transfers between devices, shards(): lax.all_to_all(parts[k], 'freq', split_axis=0, concat_axis=2, tiled=True)  17.1 us
    dot_general x6, matrix products, local_products(): jnp.einsum('fpsi,fpsj->fij', left_panel, both, preferred_element_type=jnp...  17 us
    unnamed x8, local copies, waits for them, and re-layouts  6.97 us
    ppermute x2, starting transfers between devices, from_behind(): return lax.ppermute(block, axis, route)  6.23 us
    ppermute x2, starting transfers between devices, neighbour_panels(): lax.ppermute(second_panel, 'chan', [(c - 1, c) for c in range(1, n_chan,...  5.58 us
  transfers between devices with their start and end apart: 7, of which 3 were waited for; matrix products, arithmetic and copies ran while one was open for 12% of the time, Pallas kernels for 0%

profile of v16, /device:TPU:34, one launch (start us, length us, event | category | flops | bytes accessed | tf_op | source)
XLA Modules:
  0.0 205.2 jit_solution(14238415141365629921)
XLA Ops:
  0.1 1.3 convert_element_type.70
  2.1 0.7 pad_convert_fusion.dft_ref
  2.7 19.9 %shard_map.46 = bf16[64,64,512]{2,1,0:T(8,128)(2,1)} custom-call(s32[64]{0:T(128)} %offs_ref.1, f32[64,384]{1,0:T(8,128)} %pad_convert_fusion.dft_ref, f32[1,512]{1,0:T(1,128)} %bitcast.105, bf16[8448,512]{1,0:T(8,128)(2,1)} %rec_hbm.1), custom_call_target="tpu_custom_call" | custom-call | flops 1140850688 | bytes 22020096 | tf_op jit(solution)/shard_map/pallas_call | solution.py:69
  22.6 2.8 %fusion.88 = (bf16[64,2,1,16,512]{4,3,2,1,0:T(8,128)(2,1)S(1)}, bf16[64,2,1,16,512]{4,3,2,1,0:T(8,128)(2,1)S(1)}) fusion(bf16[64,2,2,16,512]{4,3,2,1,0:T(8,128)(2,1)} %bitcast.89), kind=kLoop, calls=%fused_computation.94 | loop fusion | bytes 8388608 | tf_op jit(solution)/shard_map/slice | solution.py:128
  25.4 2.2 %copy.48 = bf16[64,2,1,16,512]{4,1,0,3,2:T(2,128)(2,1)S(1)} copy(bf16[64,2,1,16,512]{4,3,2,1,0:T(8,128)(2,1)S(1)} %get-tuple-element.8) | data formatting | bytes 4194304
  27.6 34.4 %all_to_all.36 = bf16[16,2,64,512]{3,1,2,0:T(2,128)(2,1)S(1)} all-to-all(bf16[16,2,64,512]{3,1,2,0:T(2,128)(2,1)S(1)} %bitcast.103), channel_id=1, replica_groups=mesh['chan'=16,'freq'=8] {'freq'}, dimensions={0} | all-to-all | bytes 4194304 | tf_op jit(solution)/shard_map/all_to_all | solution.py:131
  62.0 0.4 copy.22
  62.4 1.3 collective-permute-start
  63.7 3.3 %collective-permute-start.1 = (bf16[2,2,512,512]{3,2,1,0:T(8,128)(2,1)S(1)}, bf16[2,2,512,512]{3,2,1,0:T(8,128)(2,1)}, u32[]{:S(2)}, u32[]{:S(2)}) collective-permute-start(bf16[2,2,512,512]{3,2,1,0:T(8,128)(2,1)S(1)} %bitcast.91), channel_id=1, source_target_pairs={{16,0},{24,8},{32,16},{40,24},{48,32},{56,40},{64,48},{72,56},{80,... | collective-permute-start | bytes 6291464 | tf_op jit(solution)/shard_map/ppermute | solution.py:22
  67.0 3.5 %copy.47 = bf16[64,2,1,16,512]{4,1,0,3,2:T(2,128)(2,1)} copy(bf16[64,2,1,16,512]{4,3,2,1,0:T(8,128)(2,1)S(1)} %get-tuple-element.7) | data formatting | bytes 4194304
  70.5 1.3 copy-done
  71.8 4.4 %all-to-all-start.1 = ((bf16[16,2,64,512]{3,1,2,0:T(2,128)(2,1)}), bf16[16,2,64,512]{3,1,2,0:T(2,128)(2,1)}, u32[]{:S(2)}, u32[]{:S(2)}) async-start(bf16[16,2,64,512]{3,1,2,0:T(2,128)(2,1)} %bitcast.102), calls=%async_computation.1 | async-start | bytes 4194304 | tf_op jit(solution)/shard_map/all_to_all | solution.py:131
  76.8 1.2 slice_negate_fusion.5
  78.0 36.8 %collective-permute-done.1 = bf16[2,2,512,512]{3,2,1,0:T(8,128)(2,1)} collective-permute-done((bf16[2,2,512,512]{3,2,1,0:T(8,128)(2,1)S(1)}, bf16[2,2,512,512]{3,2,1,0:T(8,128)(2,1)}, u32[]{:S(2)}, u32[]{:S(2)}) %collective-permute-start.1) | collective-permute-done | bytes 2097184 | tf_op jit(solution)/shard_map/ppermute | solution.py:22
  114.8 3.9 %collective-permute-start.2 = (bf16[2,2,512,512]{3,2,1,0:T(8,128)(2,1)}, bf16[2,2,512,512]{3,2,1,0:T(8,128)(2,1)}, u32[]{:S(2)}, u32[]{:S(2)}) collective-permute-start(bf16[2,2,512,512]{3,2,1,0:T(8,128)(2,1)} %collective-permute-done.1), channel_id=1, source_target_pairs={{0,8},{16,24},{32,40},{48,56},{64,72},{80,88},{96,104},{112,120},{... | collective-permute-start | bytes 6291464 | tf_op jit(solution)/shard_map/ppermute | solution.py:112
  118.8 17.1 %all-to-all-done.1 = bf16[16,2,64,512]{3,1,2,0:T(2,128)(2,1)} async-done(((bf16[16,2,64,512]{3,1,2,0:T(2,128)(2,1)}), bf16[16,2,64,512]{3,1,2,0:T(2,128)(2,1)}, u32[]{:S(2)}, u32[]{:S(2)}) %all-to-all-start.1) | async-done | bytes 2097184 | tf_op jit(solution)/shard_map/all_to_all | solution.py:131
  135.9 2.1 %copy.25 = bf16[8,2,2,64,512]{4,3,0,2,1:T(8,128)(2,1)S(1)} copy(bf16[8,2,2,64,512]{4,2,3,1,0:T(2,128)(2,1)} %bitcast.13) | data formatting | bytes 4194304 | tf_op jit(solution)/shard_map/all_to_all | solution.py:131
  138.0 3.0 %collective-permute-start.3 = (bf16[2,2,512,512]{3,2,1,0:T(8,128)(2,1)S(1)}, bf16[2,2,512,512]{3,2,1,0:T(8,128)(2,1)S(1)}, u32[]{:S(2)}, u32[]{:S(2)}) collective-permute-start(bf16[2,2,512,512]{3,2,1,0:T(8,128)(2,1)S(1)} %bitcast.96), channel_id=1, source_target_pairs={{16,0},{24,8},{32,16},{40,24},{48,32},{56,40},{64,48},{72,56},{80,... | collective-permute-start | bytes 6291464 | tf_op jit(solution)/shard_map/ppermute | solution.py:22
  141.0 2.6 %fusion.54 = bf16[1,2,512,1024]{3,2,1,0:T(8,128)(2,1)S(1)} fusion(bf16[2,2,512,512]{3,2,1,0:T(8,128)(2,1)S(1)} %bitcast.93, bf16[2,1,512,512]{3,2,1,0:T(8,128)(2,1)S(1)} %copy-done.2, bf16[2,1,512,512]{3,2,1,0:T(8,128)(2,1)S(1)} %get-tuple-element.9), kind=kOutput, calls=%fused_computation.56 | convolution fusion | flops 2162163712 | bytes 6291456 | tf_op jit(solution)/shard_map/fpsi,fpsj->fij/dot_general | solution.py:101
  143.6 1.7 slice_negate_fusion.1
  145.3 4.0 %fusion.66 = bf16[1,2,512,1024]{3,2,1,0:T(8,128)(2,1)S(1)} fusion(bf16[2,2,512,512]{3,2,1,0:T(8,128)(2,1)S(1)} %bitcast.94, bf16[2,1,512,512]{3,2,1,0:T(8,128)(2,1)S(1)} %get-tuple-element.18, bf16[2,1,512,512]{3,2,1,0:T(8,128)(2,1)S(1)} %get-tuple-element.17, bf16[2,2,512,512]{3,2,1,0:T(8,128)(2,1)} %collective-permute-done.1), kind=kOutput, calls=%fused_computation.60 | convolution fusion | flops 2162163712 | bytes 8388608 | tf_op jit(solution)/shard_map/fpsi,fpsj->fij/dot_general | solution.py:101
  149.2 1.3 collective-permute-start.5
  150.7 2.6 %fusion.57 = bf16[1,2,512,1024]{3,2,1,0:T(8,128)(2,1)S(1)} fusion(bf16[2,2,512,512]{3,2,1,0:T(8,128)(2,1)S(1)} %bitcast.99, bf16[2,1,512,512]{3,2,1,0:T(8,128)(2,1)S(1)} %get-tuple-element.12, bf16[2,1,512,512]{3,2,1,0:T(8,128)(2,1)S(1)} %get-tuple-element.11), kind=kOutput, calls=%fused_computation.57 | convolution fusion | flops 2162163712 | bytes 6291456 | tf_op jit(solution)/shard_map/fpsi,fpsj->fij/dot_general | solution.py:101
  153.3 0.4 maximum_multiply_fusion
  153.8 34.7 %collective-permute-done.3 = bf16[2,2,512,512]{3,2,1,0:T(8,128)(2,1)S(1)} collective-permute-done((bf16[2,2,512,512]{3,2,1,0:T(8,128)(2,1)S(1)}, bf16[2,2,512,512]{3,2,1,0:T(8,128)(2,1)S(1)}, u32[]{:S(2)}, u32[]{:S(2)}) %collective-permute-start.3) | collective-permute-done | bytes 2097184 | tf_op jit(solution)/shard_map/ppermute | solution.py:22
  188.4 1.6 collective-permute-start.4
  190.5 2.6 %fusion.60 = bf16[1,2,512,1024]{3,2,1,0:T(8,128)(2,1)S(1)} fusion(bf16[2,2,512,512]{3,2,1,0:T(8,128)(2,1)S(1)} %bitcast.95, bf16[2,1,512,512]{3,2,1,0:T(8,128)(2,1)S(1)} %get-tuple-element.14, bf16[2,1,512,512]{3,2,1,0:T(8,128)(2,1)S(1)} %get-tuple-element.13, bf16[2,2,512,512]{3,2,1,0:T(8,128)(2,1)S(1)} %broadcast_select_fusion.1), kind=kOutput, calls=%fused_computation.58 | convolution fusion | flops 2162163712 | bytes 8388608 | tf_op jit(solution)/shard_map/fpsi,fpsj->fij/dot_general | solution.py:101
  193.3 2.6 %fusion.69 = bf16[1,2,512,1024]{3,2,1,0:T(8,128)(2,1)S(1)} fusion(bf16[2,2,512,512]{3,2,1,0:T(8,128)(2,1)S(1)} %bitcast.100, bf16[2,1,512,512]{3,2,1,0:T(8,128)(2,1)S(1)} %get-tuple-element.20, bf16[2,1,512,512]{3,2,1,0:T(8,128)(2,1)S(1)} %get-tuple-element.19, bf16[2,2,512,512]{3,2,1,0:T(8,128)(2,1)S(1)} %collective-permute-done.3), kind=kOutput, calls=%fused_computation.61 | convolution fusion | flops 2162163712 | bytes 8388608 | tf_op jit(solution)/shard_map/fpsi,fpsj->fij/dot_general | solution.py:101
  195.9 0.4 maximum_multiply_fusion.2
  196.7 2.6 %fusion.63 = bf16[1,2,512,1024]{3,2,1,0:T(8,128)(2,1)S(1)} fusion(bf16[2,2,512,512]{3,2,1,0:T(8,128)(2,1)S(1)} %bitcast.101, bf16[2,1,512,512]{3,2,1,0:T(8,128)(2,1)S(1)} %get-tuple-element.16, bf16[2,1,512,512]{3,2,1,0:T(8,128)(2,1)S(1)} %get-tuple-element.15, bf16[2,2,512,512]{3,2,1,0:T(8,128)(2,1)S(1)} %broadcast_select_fusion), kind=kOutput, calls=%fused_computation.59 | convolution fusion | flops 2162163712 | bytes 8388608 | tf_op jit(solution)/shard_map/fpsi,fpsj->fij/dot_general | solution.py:101
  199.3 0.4 maximum_multiply_fusion.1
  199.7 5.5 %pad_maximum_fusion = bf16[3,4,512,1024]{3,2,1,0:T(8,128)(2,1)} fusion(bf16[1,4,512,1024]{3,2,1,0:T(8,128)(2,1)S(1)} %maximum_multiply_fusion.2, bf16[1,4,512,1024]{3,2,1,0:T(8,128)(2,1)S(1)} %maximum_multiply_fusion.1, bf16[1,4,512,1024]{3,2,1,0:T(8,128)(2,1)S(1)} %maximum_multiply_fusion), kind=kLoop, calls=%fused_computation | loop fusion | flops 12582912 | bytes 25165824 | tf_op jit(solution)/shard_map/stack | solution.py:142
  (25 shorter events, 1.8 us)
Async XLA Ops:
  62.4 8.1 %collective-permute-start = (bf16[2,2,512,512]{3,2,1,0:T(8,128)(2,1)S(1)}, bf16[2,2,512,512]{3,2,1,0:T(8,128)(2,1)S(1)}, u32[]{:S(2)}, u32[]{:S(2)}) collective-permute-start(bf16[2,2,512,512]{3,2,1,0:T(8,128)(2,1)S(1)} %bitcast.90), channel_id=1, source_target_pairs={{8,0},{24,16},{40,32},{56,48},{72,64},{88,80},{104,96},{120,112},{... | collective-permute-start | bytes 6291464 | tf_op jit(solution)/shard_map/ppermute | solution.py:111
  63.7 51.1 %collective-permute-start.1 = (bf16[2,2,512,512]{3,2,1,0:T(8,128)(2,1)S(1)}, bf16[2,2,512,512]{3,2,1,0:T(8,128)(2,1)}, u32[]{:S(2)}, u32[]{:S(2)}) collective-permute-start(bf16[2,2,512,512]{3,2,1,0:T(8,128)(2,1)S(1)} %bitcast.91), channel_id=1, source_target_pairs={{16,0},{24,8},{32,16},{40,24},{48,32},{56,40},{64,48},{72,56},{80,... | collective-permute-start | bytes 6291464 | tf_op jit(solution)/shard_map/ppermute | solution.py:22
  70.5 1.3 copy-start
  71.8 64.1 %all-to-all-start.1 = ((bf16[16,2,64,512]{3,1,2,0:T(2,128)(2,1)}), bf16[16,2,64,512]{3,1,2,0:T(2,128)(2,1)}, u32[]{:S(2)}, u32[]{:S(2)}) async-start(bf16[16,2,64,512]{3,1,2,0:T(2,128)(2,1)} %bitcast.102), calls=%async_computation.1 | async-start | bytes 4194304 | tf_op jit(solution)/shard_map/all_to_all | solution.py:131
  114.8 75.3 %collective-permute-start.2 = (bf16[2,2,512,512]{3,2,1,0:T(8,128)(2,1)}, bf16[2,2,512,512]{3,2,1,0:T(8,128)(2,1)}, u32[]{:S(2)}, u32[]{:S(2)}) collective-permute-start(bf16[2,2,512,512]{3,2,1,0:T(8,128)(2,1)} %collective-permute-done.1), channel_id=1, source_target_pairs={{0,8},{16,24},{32,40},{48,56},{64,72},{80,88},{96,104},{112,120},{... | collective-permute-start | bytes 6291464 | tf_op jit(solution)/shard_map/ppermute | solution.py:112
  135.9 5.1 %copy-start.2 = (bf16[2,1,512,512]{3,2,1,0:T(8,128)(2,1)S(1)}, bf16[2,1,512,512]{3,2,1,0:T(8,128)(2,1)}, u32[]{:S(2)}) copy-start(bf16[2,1,512,512]{3,2,1,0:T(8,128)(2,1)} %get-tuple-element.10) | copy-start | bytes 3145732
  138.0 50.4 %collective-permute-start.3 = (bf16[2,2,512,512]{3,2,1,0:T(8,128)(2,1)S(1)}, bf16[2,2,512,512]{3,2,1,0:T(8,128)(2,1)S(1)}, u32[]{:S(2)}, u32[]{:S(2)}) collective-permute-start(bf16[2,2,512,512]{3,2,1,0:T(8,128)(2,1)S(1)} %bitcast.96), channel_id=1, source_target_pairs={{16,0},{24,8},{32,16},{40,24},{48,32},{56,40},{64,48},{72,56},{80,... | collective-permute-start | bytes 6291464 | tf_op jit(solution)/shard_map/ppermute | solution.py:22
  149.2 47.1 %collective-permute-start.5 = (bf16[2,2,512,512]{3,2,1,0:T(8,128)(2,1)S(1)}, bf16[2,2,512,512]{3,2,1,0:T(8,128)(2,1)S(1)}, u32[]{:S(2)}, u32[]{:S(2)}) collective-permute-start(bf16[2,2,512,512]{3,2,1,0:T(8,128)(2,1)S(1)} %bitcast.97), channel_id=1, source_target_pairs={{8,0},{24,16},{40,32},{56,48},{72,64},{88,80},{104,96},{120,112},{... | collective-permute-start | bytes 6291464 | tf_op jit(solution)/shard_map/ppermute | solution.py:111
  153.3 36.8 %copy-start.1 = (bf16[2,2,512,512]{3,2,1,0:T(8,128)(2,1)S(1)}, bf16[2,2,512,512]{3,2,1,0:T(8,128)(2,1)}, u32[]{:S(2)}) copy-start(bf16[2,2,512,512]{3,2,1,0:T(8,128)(2,1)} %copy-done) | copy-start | bytes 6291460
  188.4 7.9 %collective-permute-start.4 = (bf16[2,2,512,512]{3,2,1,0:T(8,128)(2,1)S(1)}, bf16[2,2,512,512]{3,2,1,0:T(8,128)(2,1)S(1)}, u32[]{:S(2)}, u32[]{:S(2)}) collective-permute-start(bf16[2,2,512,512]{3,2,1,0:T(8,128)(2,1)S(1)} %collective-permute-done.3), channel_id=1, source_target_pairs={{0,8},{16,24},{32,40},{48,56},{64,72},{80,88},{96,104},{112,120},{... | collective-permute-start | bytes 6291464 | tf_op jit(solution)/shard_map/ppermute | solution.py:112

commit v17 on v16

--- a/solution.py
+++ b/solution.py
@@ -134,12 +134,14 @@
             _, parts[k + 1] = lax.optimization_barrier((from_sibling, parts[k + 1]))
         chunk_products.append(local_products(own_panel, [own_panel, upper_panel, second_panel]))
     band_limit = band_blocks[0]
-    results = []
-    for offset_index in range(BAND + 1):
-        product = jnp.concatenate([p[offset_index] for p in chunk_products], axis=0)
-        keep_flag = (offset_index <= band_limit).astype(jnp.bfloat16)
-        results.append(product.astype(jnp.bfloat16) * keep_flag)
-    return jnp.stack(results, axis=0)
+    first = chunk_products[0][0]
+    cross = jnp.zeros((BAND + 1, per_device) + first.shape[1:], jnp.bfloat16)
+    for k, products in enumerate(chunk_products):
+        for offset_index, product in enumerate(products):
+            keep_flag = (offset_index <= band_limit).astype(jnp.bfloat16)
+            block = (product.astype(jnp.bfloat16) * keep_flag)[None]
+            cross = lax.dynamic_update_slice(cross, block, (offset_index, k * per_chunk, 0, 0))
+    return cross
 
 
 def solution(mesh):

time: 208 us -> 222 us (1.067)
  local copies, waits for them, and re-layouts: 12.6 us -> 26.6 us
  matrix products: 17 us -> 25.2 us
  other arithmetic: 13 us -> 8.6 us
  waiting for transfers between devices: 88.6 us -> 85.7 us
    dot_general x6, matrix products: 17 us -> 25.2 us  [local_products(): jnp.einsum('fpsi,fpsj->fij', left_panel, both, preferred_element_type=jnp...]
    dynamic_update_slice x0 -> x1, local copies, waits for them, and re-layouts: none -> 7.95 us  [shards(): lax.dynamic_update_slice(cross, block, (offset_index, k * per_chunk, 0, 0))]
    another operation x1 -> x0, other arithmetic: 5.47 us -> none  [shards(): return jnp.stack(results, axis=0)]
    unnamed x8 -> x10, local copies, waits for them, and re-layouts: 6.97 us -> 11.7 us
    neg x6, other arithmetic: 3.42 us -> 5.76 us  [local_products(): turned = jnp.stack([-right_panel[:, 1], right_panel[:, 0]], axis=1)]
  transfers between devices with their start and end apart: 7 -> 7, of which waited for: 3 -> 3; matrix products, arithmetic and copies ran while one was open for 12% -> 16% of each run, Pallas kernels for 0% -> 0%
where the time goes in v17:
time: 222 us; the launch traced here: 220 us
  waiting for transfers between devices  85.7 us (39%)
  blocking collectives  34.5 us (16%)
  local copies, waits for them, and re-layouts  26.6 us (12%)
  matrix products  25.2 us (11%)
  Pallas kernels  19.8 us (9%)
  starting transfers between devices  18.6 us (8%)
  other arithmetic  8.6 us (4%)
    ppermute x2, waiting for transfers between devices, from_behind(): return lax.ppermute(block, axis, route)  69.3 us
    all_to_all x1, blocking collectives, shards(): lax.all_to_all(parts[k], 'freq', split_axis=0, concat_axis=2, tiled=True)  34.5 us
    dot_general x6, matrix products, local_products(): jnp.einsum('fpsi,fpsj->fij', left_panel, both, preferred_element_type=jnp...  25.2 us
    pallas_call x1, Pallas kernels, whitened_spectra(): pl.pallas_call(functools.partial(spectra_kernel, seg_count, window), out_...  19.8 us
    all_to_all x1, waiting for transfers between devices, shards(): lax.all_to_all(parts[k], 'freq', split_axis=0, concat_axis=2, tiled=True)  16.4 us
    unnamed x10, local copies, waits for them, and re-layouts  11.7 us
    dynamic_update_slice x1, local copies, waits for them, and re-layouts, shards(): lax.dynamic_update_slice(cross, block, (offset_index, k * per_chunk, 0, 0))  7.95 us
    ppermute x2, starting transfers between devices, from_behind(): return lax.ppermute(block, axis, route)  6.26 us
  transfers between devices with their start and end apart: 7, of which 3 were waited for; matrix products, arithmetic and copies ran while one was open for 16% of the time, Pallas kernels for 0%

profile of v17, /device:TPU:34, one launch (start us, length us, event | category | flops | bytes accessed | tf_op | source)
XLA Modules:
  0.0 220.0 jit_solution(18219221413475058143)
XLA Ops:
  0.4 0.3 multiply_convert_fusion
  0.8 0.7 pad_convert_fusion.dft_ref
  1.5 1.2 convert_element_type.67
  2.7 19.8 %shard_map.46 = bf16[64,64,512]{2,1,0:T(8,128)(2,1)} custom-call(s32[64]{0:T(128)} %offs_ref.1, f32[64,384]{1,0:T(8,128)} %pad_convert_fusion.dft_ref, f32[1,512]{1,0:T(1,128)} %bitcast.99, bf16[8448,512]{1,0:T(8,128)(2,1)} %rec_hbm.1), custom_call_target="tpu_custom_call" | custom-call | flops 1140850688 | bytes 22020096 | tf_op jit(solution)/shard_map/pallas_call | solution.py:69
  22.5 2.8 %fusion.82 = (bf16[64,2,1,16,512]{4,3,2,1,0:T(8,128)(2,1)S(1)}, bf16[64,2,1,16,512]{4,3,2,1,0:T(8,128)(2,1)S(1)}) fusion(bf16[64,2,2,16,512]{4,3,2,1,0:T(8,128)(2,1)} %bitcast.89), kind=kLoop, calls=%fused_computation.90 | loop fusion | bytes 8388608 | tf_op jit(solution)/shard_map/slice | solution.py:128
  25.3 2.2 copy.48
  27.5 34.5 %all_to_all.36 = bf16[16,2,64,512]{3,1,2,0:T(2,128)(2,1)S(1)} all-to-all(bf16[16,2,64,512]{3,1,2,0:T(2,128)(2,1)S(1)} %bitcast.97), channel_id=1, replica_groups=mesh['chan'=16,'freq'=8] {'freq'}, dimensions={0} | all-to-all | bytes 4194304 | tf_op jit(solution)/shard_map/all_to_all | solution.py:131
  61.9 0.4 copy.22
  62.4 1.3 collective-permute-start.2
  63.7 3.3 %collective-permute-start = (bf16[2,2,512,512]{3,2,1,0:T(8,128)(2,1)S(1)}, bf16[2,2,512,512]{3,2,1,0:T(8,128)(2,1)}, u32[]{:S(2)}, u32[]{:S(2)}) collective-permute-start(bf16[2,2,512,512]{3,2,1,0:T(8,128)(2,1)S(1)} %bitcast.91), channel_id=1, source_target_pairs={{16,0},{24,8},{32,16},{40,24},{48,32},{56,40},{64,48},{72,56},{80,... | collective-permute-start | bytes 6291464 | tf_op jit(solution)/shard_map/ppermute | solution.py:22
  67.0 3.5 %copy.47 = bf16[64,2,1,16,512]{4,1,0,3,2:T(2,128)(2,1)} copy(bf16[64,2,1,16,512]{4,3,2,1,0:T(8,128)(2,1)S(1)} %get-tuple-element.7) | data formatting | bytes 4194304
  70.5 1.3 copy-done.2
  71.8 4.4 %all-to-all-start.1 = ((bf16[16,2,64,512]{3,1,2,0:T(2,128)(2,1)}), bf16[16,2,64,512]{3,1,2,0:T(2,128)(2,1)}, u32[]{:S(2)}, u32[]{:S(2)}) async-start(bf16[16,2,64,512]{3,1,2,0:T(2,128)(2,1)} %bitcast.96), calls=%async_computation.1 | async-start | bytes 4194304 | tf_op jit(solution)/shard_map/all_to_all | solution.py:131
  76.2 38.6 %collective-permute-done = bf16[2,2,512,512]{3,2,1,0:T(8,128)(2,1)} collective-permute-done((bf16[2,2,512,512]{3,2,1,0:T(8,128)(2,1)S(1)}, bf16[2,2,512,512]{3,2,1,0:T(8,128)(2,1)}, u32[]{:S(2)}, u32[]{:S(2)}) %collective-permute-start) | collective-permute-done | bytes 2097184 | tf_op jit(solution)/shard_map/ppermute | solution.py:22
  114.8 4.0 %collective-permute-start.1 = (bf16[2,2,512,512]{3,2,1,0:T(8,128)(2,1)}, bf16[2,2,512,512]{3,2,1,0:T(8,128)(2,1)}, u32[]{:S(2)}, u32[]{:S(2)}) collective-permute-start(bf16[2,2,512,512]{3,2,1,0:T(8,128)(2,1)} %collective-permute-done), channel_id=1, source_target_pairs={{0,8},{16,24},{32,40},{48,56},{64,72},{80,88},{96,104},{112,120},{... | collective-permute-start | bytes 6291464 | tf_op jit(solution)/shard_map/ppermute | solution.py:112
  119.4 16.4 %all-to-all-done.1 = bf16[16,2,64,512]{3,1,2,0:T(2,128)(2,1)} async-done(((bf16[16,2,64,512]{3,1,2,0:T(2,128)(2,1)}), bf16[16,2,64,512]{3,1,2,0:T(2,128)(2,1)}, u32[]{:S(2)}, u32[]{:S(2)}) %all-to-all-start.1) | async-done | bytes 2097184 | tf_op jit(solution)/shard_map/all_to_all | solution.py:131
  135.9 3.4 %copy.27 = bf16[8,2,2,64,512]{4,3,0,2,1:T(8,128)(2,1)} copy(bf16[8,2,2,64,512]{4,2,3,1,0:T(2,128)(2,1)} %bitcast.22) | data formatting | bytes 4194304 | tf_op jit(solution)/shard_map/all_to_all | solution.py:131
  139.3 3.0 %collective-permute-start.3 = (bf16[2,2,512,512]{3,2,1,0:T(8,128)(2,1)}, bf16[2,2,512,512]{3,2,1,0:T(8,128)(2,1)}, u32[]{:S(2)}, u32[]{:S(2)}) collective-permute-start(bf16[2,2,512,512]{3,2,1,0:T(8,128)(2,1)} %bitcast.24), channel_id=1, source_target_pairs={{16,0},{24,8},{32,16},{40,24},{48,32},{56,40},{64,48},{72,56},{80,... | collective-permute-start | bytes 6291464 | tf_op jit(solution)/shard_map/ppermute | solution.py:22
  142.4 3.6 %multiply_bitcast_fusion = bf16[1,2,512,1024]{3,2,1,0:T(8,128)(2,1)} fusion(bf16[2,2,512,512]{3,2,1,0:T(8,128)(2,1)S(1)} %bitcast.93, bf16[2,1,512,512]{3,2,1,0:T(8,128)(2,1)S(1)} %get-tuple-element.20, bf16[2,1,512,512]{3,2,1,0:T(8,128)(2,1)S(1)} %get-tuple-element.19, bf16[]{:T(256)} %bitcast.10), kind=kOutput, calls=%fused_computation.55 | convolution fusion | flops 2163212288 | bytes 6291458 | tf_op jit(solution)/shard_map/fpsi,fpsj->fij/dot_general | solution.py:101
  146.0 7.9 %dynamic_update_slice.18 = bf16[3,4,512,1024]{3,2,1,0:T(8,128)(2,1)} pad(bf16[1,2,512,1024]{3,2,1,0:T(8,128)(2,1)} %multiply_bitcast_fusion, bf16[]{:T(256)} %constant.85.clone.1), padding=0_2x0_2x0_0x0_0 | pad | bytes 14680066 | tf_op jit(solution)/shard_map/dynamic_update_slice | solution.py:143
  154.0 1.8 slice_negate_fusion.3
  155.8 1.3 collective-permute-start.5
  157.1 1.8 slice_negate_fusion.2
  159.4 30.7 %collective-permute-done.3 = bf16[2,2,512,512]{3,2,1,0:T(8,128)(2,1)} collective-permute-done((bf16[2,2,512,512]{3,2,1,0:T(8,128)(2,1)}, bf16[2,2,512,512]{3,2,1,0:T(8,128)(2,1)}, u32[]{:S(2)}, u32[]{:S(2)}) %collective-permute-start.3) | collective-permute-done | bytes 2097184 | tf_op jit(solution)/shard_map/ppermute | solution.py:22
  190.1 1.4 collective-permute-start.4
  191.5 2.6 %bitcast_dynamic-update-slice_fusion.4 = bf16[3,4,512,1024]{3,2,1,0:T(8,128)(2,1)S(1)} fusion(bf16[3,4,512,1024]{3,2,1,0:T(8,128)(2,1)S(1)} %copy-done, bf16[2,2,512,512]{3,2,1,0:T(8,128)(2,1)S(1)} %bitcast.94, bf16[2,1,512,512]{3,2,1,0:T(8,128)(2,1)S(1)} %get-tuple-element.18, bf16[2,1,512,512]{3,2,1,0:T(8,128)(2,1)S(1)} %get-tuple-element.17, ...), kind=kOutput, calls=%fused_computation.54 | convolution fusion | flops 2166358016 | bytes 8388610 | tf_op jit(solution)/shard_map/fpsi,fpsj->fij/dot_general | solution.py:101
  194.1 4.0 %bitcast_dynamic-update-slice_fusion.3 = bf16[3,4,512,1024]{3,2,1,0:T(8,128)(2,1)S(1)} fusion(bf16[3,4,512,1024]{3,2,1,0:T(8,128)(2,1)S(1)} %bitcast_dynamic-update-slice_fusion.4, bf16[2,2,512,512]{3,2,1,0:T(8,128)(2,1)S(1)} %bitcast.95, bf16[2,1,512,512]{3,2,1,0:T(8,128)(2,1)S(1)} %get-tuple-element.16, ...), kind=kOutput, calls=%fused_computation.53 | convolution fusion | flops 2166358016 | bytes 8388610 | tf_op jit(solution)/shard_map/fpsi,fpsj->fij/dot_general | solution.py:101
  198.1 4.6 %bitcast_dynamic-update-slice_fusion.2 = bf16[3,4,512,1024]{3,2,1,0:T(8,128)(2,1)S(1)} fusion(bf16[3,4,512,1024]{3,2,1,0:T(8,128)(2,1)S(1)} %bitcast_dynamic-update-slice_fusion.3, bf16[2,2,512,512]{3,2,1,0:T(8,128)(2,1)} %bitcast.24, bf16[2,1,512,512]{3,2,1,0:T(8,128)(2,1)S(1)} %get-tuple-element.14, bf16[2,1,512,512]{3,2,1,0:T(8,128)(2,1)S(1)} %get-tuple-element.13, ...), kind=kOutput, calls=%fused_computation.52 | convolution fusion | flops 2166358016 | bytes 8389120 | tf_op jit(solution)/shard_map/fpsi,fpsj->fij/dot_general | solution.py:101
  202.7 1.7 slice_negate_fusion
  204.8 4.5 %bitcast_dynamic-update-slice_fusion.1 = bf16[3,4,512,1024]{3,2,1,0:T(8,128)(2,1)S(1)} fusion(bf16[3,4,512,1024]{3,2,1,0:T(8,128)(2,1)S(1)} %bitcast_dynamic-update-slice_fusion.2, bf16[2,2,512,512]{3,2,1,0:T(8,128)(2,1)} %bitcast.24, bf16[2,1,512,512]{3,2,1,0:T(8,128)(2,1)S(1)} %get-tuple-element.12, bf16[2,1,512,512]{3,2,1,0:T(8,128)(2,1)S(1)} %get-tuple-element.11, ...), kind=kOutput, calls=%fused_computation.51 | convolution fusion | flops 2166358016 | bytes 8388610 | tf_op jit(solution)/shard_map/fpsi,fpsj->fij/dot_general | solution.py:101
  209.3 4.8 %copy-done.1 = bf16[3,4,512,1024]{3,2,1,0:T(8,128)(2,1)} copy-done((bf16[3,4,512,1024]{3,2,1,0:T(8,128)(2,1)}, bf16[3,4,512,1024]{3,2,1,0:T(8,128)(2,1)S(1)}, u32[]{:S(2)}) %copy-start.1) | copy-done | bytes 12582936
  214.1 5.9 %bitcast_dynamic-update-slice_fusion = bf16[3,4,512,1024]{3,2,1,0:T(8,128)(2,1)} fusion(bf16[3,4,512,1024]{3,2,1,0:T(8,128)(2,1)} %copy-done.1, bf16[2,2,512,512]{3,2,1,0:T(8,128)(2,1)} %bitcast.24, bf16[2,1,512,512]{3,2,1,0:T(8,128)(2,1)S(1)} %get-tuple-element.10, bf16[2,1,512,512]{3,2,1,0:T(8,128)(2,1)S(1)} %get-tuple-element.9, ...), kind=kOutput, calls=%fused_computation.50 | convolution fusion | flops 2166358016 | bytes 8389120 | tf_op jit(solution)/shard_map/fpsi,fpsj->fij/dot_general | solution.py:101
  (24 shorter events, 1.4 us)
Async XLA Ops:
  62.4 8.1 %collective-permute-start.2 = (bf16[2,2,512,512]{3,2,1,0:T(8,128)(2,1)S(1)}, bf16[2,2,512,512]{3,2,1,0:T(8,128)(2,1)S(1)}, u32[]{:S(2)}, u32[]{:S(2)}) collective-permute-start(bf16[2,2,512,512]{3,2,1,0:T(8,128)(2,1)S(1)} %bitcast.90), channel_id=1, source_target_pairs={{8,0},{24,16},{40,32},{56,48},{72,64},{88,80},{104,96},{120,112},{... | collective-permute-start | bytes 6291464 | tf_op jit(solution)/shard_map/ppermute | solution.py:111
  63.7 51.1 %collective-permute-start = (bf16[2,2,512,512]{3,2,1,0:T(8,128)(2,1)S(1)}, bf16[2,2,512,512]{3,2,1,0:T(8,128)(2,1)}, u32[]{:S(2)}, u32[]{:S(2)}) collective-permute-start(bf16[2,2,512,512]{3,2,1,0:T(8,128)(2,1)S(1)} %bitcast.91), channel_id=1, source_target_pairs={{16,0},{24,8},{32,16},{40,24},{48,32},{56,40},{64,48},{72,56},{80,... | collective-permute-start | bytes 6291464 | tf_op jit(solution)/shard_map/ppermute | solution.py:22
  70.5 1.3 copy-start.2
  71.8 64.1 %all-to-all-start.1 = ((bf16[16,2,64,512]{3,1,2,0:T(2,128)(2,1)}), bf16[16,2,64,512]{3,1,2,0:T(2,128)(2,1)}, u32[]{:S(2)}, u32[]{:S(2)}) async-start(bf16[16,2,64,512]{3,1,2,0:T(2,128)(2,1)} %bitcast.96), calls=%async_computation.1 | async-start | bytes 4194304 | tf_op jit(solution)/shard_map/all_to_all | solution.py:131
  114.8 44.1 %collective-permute-start.1 = (bf16[2,2,512,512]{3,2,1,0:T(8,128)(2,1)}, bf16[2,2,512,512]{3,2,1,0:T(8,128)(2,1)}, u32[]{:S(2)}, u32[]{:S(2)}) collective-permute-start(bf16[2,2,512,512]{3,2,1,0:T(8,128)(2,1)} %collective-permute-done), channel_id=1, source_target_pairs={{0,8},{16,24},{32,40},{48,56},{64,72},{80,88},{96,104},{112,120},{... | collective-permute-start | bytes 6291464 | tf_op jit(solution)/shard_map/ppermute | solution.py:112
  139.3 50.7 %collective-permute-start.3 = (bf16[2,2,512,512]{3,2,1,0:T(8,128)(2,1)}, bf16[2,2,512,512]{3,2,1,0:T(8,128)(2,1)}, u32[]{:S(2)}, u32[]{:S(2)}) collective-permute-start(bf16[2,2,512,512]{3,2,1,0:T(8,128)(2,1)} %bitcast.24), channel_id=1, source_target_pairs={{16,0},{24,8},{32,16},{40,24},{48,32},{56,40},{64,48},{72,56},{80,... | collective-permute-start | bytes 6291464 | tf_op jit(solution)/shard_map/ppermute | solution.py:22
  154.0 5.0 %copy-start.3 = (bf16[2,2,512,512]{3,2,1,0:T(8,128)(2,1)S(1)}, bf16[2,2,512,512]{3,2,1,0:T(8,128)(2,1)}, u32[]{:S(2)}) copy-start(bf16[2,2,512,512]{3,2,1,0:T(8,128)(2,1)} %copy-done.2) | copy-start | bytes 6291460
  155.8 48.6 %collective-permute-start.5 = (bf16[2,2,512,512]{3,2,1,0:T(8,128)(2,1)}, bf16[2,2,512,512]{3,2,1,0:T(8,128)(2,1)S(1)}, u32[]{:S(2)}, u32[]{:S(2)}) collective-permute-start(bf16[2,2,512,512]{3,2,1,0:T(8,128)(2,1)} %bitcast.24), channel_id=1, source_target_pairs={{8,0},{24,16},{40,32},{56,48},{72,64},{88,80},{104,96},{120,112},{... | collective-permute-start | bytes 6291464 | tf_op jit(solution)/shard_map/ppermute | solution.py:111
  157.1 34.4 %copy-start = (bf16[3,4,512,1024]{3,2,1,0:T(8,128)(2,1)S(1)}, bf16[3,4,512,1024]{3,2,1,0:T(8,128)(2,1)}, u32[]{:S(2)}) copy-start(bf16[3,4,512,1024]{3,2,1,0:T(8,128)(2,1)} %dynamic_update_slice.18) | copy-start | bytes 37748740
  190.1 14.3 %collective-permute-start.4 = (bf16[2,2,512,512]{3,2,1,0:T(8,128)(2,1)}, bf16[2,2,512,512]{3,2,1,0:T(8,128)(2,1)S(1)}, u32[]{:S(2)}, u32[]{:S(2)}) collective-permute-start(bf16[2,2,512,512]{3,2,1,0:T(8,128)(2,1)} %collective-permute-done.3), channel_id=1, source_target_pairs={{0,8},{16,24},{32,40},{48,56},{64,72},{80,88},{96,104},{112,120},{... | collective-permute-start | bytes 6291464 | tf_op jit(solution)/shard_map/ppermute | solution.py:112
  209.3 4.8 %copy-start.1 = (bf16[3,4,512,1024]{3,2,1,0:T(8,128)(2,1)}, bf16[3,4,512,1024]{3,2,1,0:T(8,128)(2,1)S(1)}, u32[]{:S(2)}) copy-start(bf16[3,4,512,1024]{3,2,1,0:T(8,128)(2,1)S(1)} %bitcast_dynamic-update-slice_fusion.1) | copy-start | bytes 37748740

commit v18 on v13

--- a/solution.py
+++ b/solution.py
@@ -51,7 +51,7 @@
     dft = dft_ref[...]
     live = mask_ref[...]
     for j in range(seg_count):
-        shifted = pltpu.roll(dft, starts[j], 1).astype(jnp.bfloat16)
+        shifted = pltpu.roll(dft, starts[j], 1)[:, :window].astype(jnp.bfloat16)
         copies[j].wait()
         spec = jnp.dot(shifted, frames[j], preferred_element_type=jnp.float32)
         power = jnp.sum(spec * spec, axis=0, keepdims=True) * (1.0 / BINS)
@@ -62,9 +62,9 @@
 def whitened_spectra(records, offsets, dead_mask, dft_rows):
     seg_count = offsets.shape[0]
     channels = records.shape[1]
-    window = SEG_LEN + 128
+    window = SEG_LEN + 16
     rows = dft_rows.shape[0]
-    padded = jnp.pad(dft_rows.astype(jnp.float32), ((0, 0), (0, window - SEG_LEN)))
+    padded = jnp.pad(dft_rows.astype(jnp.float32), ((0, 0), (0, 128)))
     live = dead_mask.astype(jnp.float32).reshape(1, channels)
     return pl.pallas_call(
         functools.partial(spectra_kernel, seg_count, window),
@@ -73,7 +73,7 @@
             num_scalar_prefetch=1,
             grid=(1,),
             in_specs=[
-                pl.BlockSpec((rows, window), lambda i, offs: (0, 0)),
+                pl.BlockSpec((rows, SEG_LEN + 128), lambda i, offs: (0, 0)),
                 pl.BlockSpec((1, channels), lambda i, offs: (0, 0)),
                 pl.BlockSpec(memory_space=pl.ANY),
             ],
@@ -118,7 +118,7 @@
 def shards(records, offsets, dead_mask, band_blocks):
     n_freq = lax.axis_size("freq")
     per_device = BINS // n_freq
-    sizes = [per_device - 1, 1]
+    sizes = [2, 1, 1]
     chunks = len(sizes)
     bounds = [sum(sizes[:k]) for k in range(chunks + 1)]
     table = dft_table(SEG_LEN, BINS, FIRST_BIN).reshape(n_freq, per_device, 2, SEG_LEN)

time: 211 us -> 211 us (level)
  blocking collectives: 46.1 us -> 34.4 us
  starting transfers between devices: 21.1 us -> 32.5 us
  waiting for transfers between devices: 67.1 us -> 62.5 us
  local copies, waits for them, and re-layouts: 10.7 us -> 15.1 us
    all_to_all x1, blocking collectives: 46.1 us -> 34.4 us  [shards(): lax.all_to_all(parts[k], 'freq', split_axis=0, concat_axis=2, tiled=True)]
    ppermute x2 -> x3, waiting for transfers between devices: 67.1 us -> 62.3 us  [from_behind(): return lax.ppermute(block, axis, route)]
    all_to_all x1 -> x2, starting transfers between devices: 4.23 us -> 8.49 us  [shards(): lax.all_to_all(parts[k], 'freq', split_axis=0, concat_axis=2, tiled=True)]
    unnamed x6 -> x17, local copies, waits for them, and re-layouts: 4.61 us -> 8.44 us
    ppermute x2 -> x3, starting transfers between devices: 5.17 us -> 8.17 us  [from_behind(): return lax.ppermute(block, axis, route)]
    ppermute x2 -> x3, starting transfers between devices: 9.08 us -> 11.7 us  [neighbour_panels(): lax.ppermute(second_panel, 'chan', [(c - 1, c) for c in range(1, n_chan,...]
    dot_general x6 -> x9, matrix products: 23.5 us -> 25.3 us  [local_products(): jnp.einsum('fpsi,fpsj->fij', left_panel, both, preferred_element_type=jnp...]
    neg x6 -> x9, other arithmetic: 7.67 us -> 5.91 us  [local_products(): turned = jnp.stack([-right_panel[:, 1], right_panel[:, 0]], axis=1)]
  transfers between devices with their start and end apart: 7 -> 11, of which waited for: 2 -> 4; matrix products, arithmetic and copies ran while one was open for 15% -> 19% of each run, Pallas kernels for 0% -> 0%
where the time goes in v18:
time: 211 us; the launch traced here: 209 us
  waiting for transfers between devices  62.5 us (30%)
  blocking collectives  34.4 us (16%)
  starting transfers between devices  32.5 us (15%)
  matrix products  25.3 us (12%)
  Pallas kernels  19.9 us (9%)
  other arithmetic  18.3 us (9%)
  local copies, waits for them, and re-layouts  15.1 us (7%)
    ppermute x3, waiting for transfers between devices, from_behind(): return lax.ppermute(block, axis, route)  62.3 us
    all_to_all x1, blocking collectives, shards(): lax.all_to_all(parts[k], 'freq', split_axis=0, concat_axis=2, tiled=True)  34.4 us
    dot_general x9, matrix products, local_products(): jnp.einsum('fpsi,fpsj->fij', left_panel, both, preferred_element_type=jnp...  25.3 us
    pallas_call x1, Pallas kernels, whitened_spectra(): pl.pallas_call(functools.partial(spectra_kernel, seg_count, window), out_...  19.9 us
    ppermute x3, starting transfers between devices, neighbour_panels(): lax.ppermute(second_panel, 'chan', [(c - 1, c) for c in range(1, n_chan,...  11.7 us
    all_to_all x2, starting transfers between devices, shards(): lax.all_to_all(parts[k], 'freq', split_axis=0, concat_axis=2, tiled=True)  8.49 us
    unnamed x17, local copies, waits for them, and re-layouts  8.44 us
    ppermute x3, starting transfers between devices, from_behind(): return lax.ppermute(block, axis, route)  8.17 us
  transfers between devices with their start and end apart: 11, of which 4 were waited for; matrix products, arithmetic and copies ran while one was open for 19% of the time, Pallas kernels for 0%

profile of v18, /device:TPU:34, one launch (start us, length us, event | category | flops | bytes accessed | tf_op | source)
XLA Modules:
  0.0 209.1 jit_solution(9095947451569711137)
XLA Ops:
  1.4 1.3 convert_element_type.86
  3.4 19.9 %shard_map.46 = bf16[64,64,512]{2,1,0:T(8,128)(2,1)} custom-call(s32[64]{0:T(128)} %offs_ref.1, f32[64,384]{1,0:T(8,128)} %pad_convert_fusion.dft_ref, f32[1,512]{1,0:T(1,128)} %bitcast.193, bf16[8448,512]{1,0:T(8,128)(2,1)} %rec_hbm.1), custom_call_target="tpu_custom_call" | custom-call | flops 1140850688 | bytes 22020096 | tf_op jit(solution)/shard_map/pallas_call | solution.py:69
  23.3 1.8 slice.99
  25.2 2.2 %copy.62 = bf16[64,2,16,512]{3,1,0,2:T(2,128)(2,1)S(1)} copy(bf16[64,2,16,512]{3,2,1,0:T(8,128)(2,1)S(1)} %slice.99) | data formatting | bytes 4194304
  27.3 34.4 %all_to_all.54 = bf16[16,2,64,512]{3,1,2,0:T(2,128)(2,1)S(1)} all-to-all(bf16[16,2,64,512]{3,1,2,0:T(2,128)(2,1)S(1)} %bitcast.174), channel_id=1, replica_groups=mesh['chan'=16,'freq'=8] {'freq'}, dimensions={0} | all-to-all | bytes 4194304 | tf_op jit(solution)/shard_map/all_to_all | solution.py:137
  62.2 1.3 collective-permute-start
  63.5 3.3 %collective-permute-start.2 = (bf16[2,2,512,512]{3,2,1,0:T(8,128)(2,1)S(1)}, bf16[2,2,512,512]{3,2,1,0:T(8,128)(2,1)}, u32[]{:S(2)}, u32[]{:S(2)}) collective-permute-start(bf16[2,2,512,512]{3,2,1,0:T(8,128)(2,1)S(1)} %bitcast.169), channel_id=1, source_target_pairs={{16,0},{24,8},{32,16},{40,24},{48,32},{56,40},{64,48},{72,56},{80,... | collective-permute-start | bytes 6291464 | tf_op jit(solution)/shard_map/ppermute | solution.py:22
  67.5 1.7 fusion.97
  69.2 1.6 copy.63
  70.8 1.5 copy.64
  73.5 4.2 %all-to-all-start.1 = ((bf16[8,2,64,512]{3,2,1,0:T(8,128)(2,1)}), bf16[8,2,64,512]{3,2,1,0:T(8,128)(2,1)}, u32[]{:S(2)}, u32[]{:S(2)}) async-start(bf16[8,2,64,512]{3,2,1,0:T(8,128)(2,1)} %bitcast.165), calls=%async_computation.1 | async-start | bytes 2097152 | tf_op jit(solution)/shard_map/all_to_all | solution.py:137
  77.7 5.0 %fusion.63 = bf16[1,2,512,1024]{3,2,1,0:T(8,128)(2,1)} fusion(bf16[2,2,512,512]{3,2,1,0:T(8,128)(2,1)S(1)} %bitcast.171, bf16[2,1,512,512]{3,2,1,0:T(8,128)(2,1)} %get-tuple-element.12, bf16[2,1,512,512]{3,2,1,0:T(8,128)(2,1)S(1)} %get-tuple-element.11), kind=kOutput, calls=%fused_computation.78 | convolution fusion | flops 2162163712 | bytes 6291456 | tf_op jit(solution)/shard_map/fpsi,fpsj->fij/dot_general | solution.py:101
  82.7 30.6 %collective-permute-done.2 = bf16[2,2,512,512]{3,2,1,0:T(8,128)(2,1)} collective-permute-done((bf16[2,2,512,512]{3,2,1,0:T(8,128)(2,1)S(1)}, bf16[2,2,512,512]{3,2,1,0:T(8,128)(2,1)}, u32[]{:S(2)}, u32[]{:S(2)}) %collective-permute-start.2) | collective-permute-done | bytes 2097184 | tf_op jit(solution)/shard_map/ppermute | solution.py:22
  113.4 6.5 %collective-permute-start.3 = (bf16[2,2,512,512]{3,2,1,0:T(8,128)(2,1)}, bf16[2,2,512,512]{3,2,1,0:T(8,128)(2,1)}, u32[]{:S(2)}, u32[]{:S(2)}) collective-permute-start(bf16[2,2,512,512]{3,2,1,0:T(8,128)(2,1)} %collective-permute-done.2), channel_id=1, source_target_pairs={{0,8},{16,24},{32,40},{48,56},{64,72},{80,88},{96,104},{112,120},{... | collective-permute-start | bytes 6291464 | tf_op jit(solution)/shard_map/ppermute | solution.py:112
  119.9 3.1 %slice_negate_fusion = (bf16[2,1,512,512]{3,2,1,0:T(8,128)(2,1)}, bf16[2,1,512,512]{3,2,1,0:T(8,128)(2,1)}) fusion(bf16[2,2,512,512]{3,2,1,0:T(8,128)(2,1)} %collective-permute-done.2), kind=kLoop, calls=%fused_computation.87 | loop fusion | flops 524288 | bytes 4194304 | tf_op jit(solution)/shard_map/neg | solution.py:99
  123.2 1.3 copy.33
  124.5 1.3 collective-permute-start.1
  125.8 3.0 %collective-permute-start.4 = (bf16[1,2,512,512]{3,2,1,0:T(8,128)(2,1)S(1)}, bf16[1,2,512,512]{3,2,1,0:T(8,128)(2,1)}, u32[]{:S(2)}, u32[]{:S(2)}) collective-permute-start(bf16[1,2,512,512]{3,2,1,0:T(8,128)(2,1)S(1)} %bitcast.177), channel_id=1, source_target_pairs={{16,0},{24,8},{32,16},{40,24},{48,32},{56,40},{64,48},{72,56},{80,... | collective-permute-start | bytes 3145736 | tf_op jit(solution)/shard_map/ppermute | solution.py:22
  128.8 5.9 %fusion.69 = bf16[1,2,512,1024]{3,2,1,0:T(8,128)(2,1)} fusion(bf16[2,2,512,512]{3,2,1,0:T(8,128)(2,1)S(1)} %bitcast.172, bf16[2,1,512,512]{3,2,1,0:T(8,128)(2,1)} %get-tuple-element.16, bf16[2,1,512,512]{3,2,1,0:T(8,128)(2,1)} %get-tuple-element.15, bf16[2,2,512,512]{3,2,1,0:T(8,128)(2,1)} %collective-permute-done.2), kind=kOutput, calls=%fused_computation.80 | convolution fusion | flops 2162163712 | bytes 8388608 | tf_op jit(solution)/shard_map/fpsi,fpsj->fij/dot_general | solution.py:101
  134.8 2.3 %fusion.72 = bf16[1,1,512,1024]{3,2,1,0:T(8,128)(2,1)} fusion(bf16[2,512,512]{2,1,0:T(8,128)(2,1)S(1)} %bitcast.179, bf16[1,1,512,512]{3,2,1,0:T(8,128)(2,1)S(1)} %get-tuple-element.18, bf16[1,1,512,512]{3,2,1,0:T(8,128)(2,1)S(1)} %get-tuple-element.17, bf16[1,2,512,512]{3,2,1,0:T(8,128)(2,1)S(1)} %bitcast.180), kind=kOutput, calls=%fused_computation.81 | convolution fusion | flops 1081081856 | bytes 4194304 | tf_op jit(solution)/shard_map/fpsi,fpsj->fij/dot_general | solution.py:101
  138.0 4.2 %all-to-all-start.2 = ((bf16[8,2,64,512]{3,2,1,0:T(8,128)(2,1)}), bf16[8,2,64,512]{3,2,1,0:T(8,128)(2,1)}, u32[]{:S(2)}, u32[]{:S(2)}) async-start(bf16[8,2,64,512]{3,2,1,0:T(8,128)(2,1)} %bitcast.183), calls=%async_computation.2 | async-start | bytes 2097152 | tf_op jit(solution)/shard_map/all_to_all | solution.py:137
  142.3 12.1 %collective-permute-done.4 = bf16[1,2,512,512]{3,2,1,0:T(8,128)(2,1)} collective-permute-done((bf16[1,2,512,512]{3,2,1,0:T(8,128)(2,1)S(1)}, bf16[1,2,512,512]{3,2,1,0:T(8,128)(2,1)}, u32[]{:S(2)}, u32[]{:S(2)}) %collective-permute-start.4) | collective-permute-done | bytes 1048608 | tf_op jit(solution)/shard_map/ppermute | solution.py:22
  154.3 3.8 %collective-permute-start.5 = (bf16[1,2,512,512]{3,2,1,0:T(8,128)(2,1)}, bf16[1,2,512,512]{3,2,1,0:T(8,128)(2,1)}, u32[]{:S(2)}, u32[]{:S(2)}) collective-permute-start(bf16[1,2,512,512]{3,2,1,0:T(8,128)(2,1)} %collective-permute-done.4), channel_id=1, source_target_pairs={{0,8},{16,24},{32,40},{48,56},{64,72},{80,88},{96,104},{112,120},{... | collective-permute-start | bytes 3145736 | tf_op jit(solution)/shard_map/ppermute | solution.py:112
  159.4 3.5 %fusion.76 = bf16[1,1,512,1024]{3,2,1,0:T(8,128)(2,1)} fusion(bf16[2,512,512]{2,1,0:T(8,128)(2,1)S(1)} %bitcast.181, bf16[1,1,512,512]{3,2,1,0:T(8,128)(2,1)S(1)} %get-tuple-element.26, bf16[1,1,512,512]{3,2,1,0:T(8,128)(2,1)S(1)} %get-tuple-element.25, bf16[1,2,512,512]{3,2,1,0:T(8,128)(2,1)} %collective-permute-done.4), kind=kOutput, calls=%fused_computation.85 | convolution fusion | flops 1081081856 | bytes 4194304 | tf_op jit(solution)/shard_map/fpsi,fpsj->fij/dot_general | solution.py:101
  162.9 1.8 broadcast_select_fusion
  164.9 3.6 %fusion.66 = bf16[1,2,512,1024]{3,2,1,0:T(8,128)(2,1)} fusion(bf16[2,2,512,512]{3,2,1,0:T(8,128)(2,1)S(1)} %bitcast.173, bf16[2,1,512,512]{3,2,1,0:T(8,128)(2,1)S(1)} %get-tuple-element.14, bf16[2,1,512,512]{3,2,1,0:T(8,128)(2,1)S(1)} %get-tuple-element.13, bf16[2,2,512,512]{3,2,1,0:T(8,128)(2,1)S(1)} %broadcast_select_fusion), kind=kOutput, calls=%fused_computation.79 | convolution fusion | flops 2162163712 | bytes 8388608 | tf_op jit(solution)/shard_map/fpsi,fpsj->fij/dot_general | solution.py:101
  168.5 1.3 copy.36
  169.8 1.9 collective-permute-start.6
  171.7 1.5 collective-permute-start.8
  176.6 19.6 %collective-permute-done.6 = bf16[1,2,512,512]{3,2,1,0:T(8,128)(2,1)S(1)} collective-permute-done((bf16[1,2,512,512]{3,2,1,0:T(8,128)(2,1)S(1)}, bf16[1,2,512,512]{3,2,1,0:T(8,128)(2,1)S(1)}, u32[]{:S(2)}, u32[]{:S(2)}) %collective-permute-start.6) | collective-permute-done | bytes 1048608 | tf_op jit(solution)/shard_map/ppermute | solution.py:22
  196.2 1.3 collective-permute-start.7
  203.6 5.5 %pad_maximum_fusion = bf16[3,4,512,1024]{3,2,1,0:T(8,128)(2,1)} fusion(bf16[1,4,512,1024]{3,2,1,0:T(8,128)(2,1)S(1)} %maximum_multiply_fusion.2, bf16[1,4,512,1024]{3,2,1,0:T(8,128)(2,1)S(1)} %maximum_multiply_fusion.1, bf16[1,4,512,1024]{3,2,1,0:T(8,128)(2,1)S(1)} %maximum_multiply_fusion), kind=kLoop, calls=%fused_computation | loop fusion | flops 12582912 | bytes 25165824 | tf_op jit(solution)/shard_map/stack | solution.py:148
  (50 shorter events, 15.6 us)
Async XLA Ops:
  62.2 11.3 %collective-permute-start = (bf16[2,2,512,512]{3,2,1,0:T(8,128)(2,1)S(1)}, bf16[2,2,512,512]{3,2,1,0:T(8,128)(2,1)}, u32[]{:S(2)}, u32[]{:S(2)}) collective-permute-start(bf16[2,2,512,512]{3,2,1,0:T(8,128)(2,1)S(1)} %bitcast.168), channel_id=1, source_target_pairs={{8,0},{24,16},{40,32},{56,48},{72,64},{88,80},{104,96},{120,112},{... | collective-permute-start | bytes 6291464 | tf_op jit(solution)/shard_map/ppermute | solution.py:111
  63.5 49.8 %collective-permute-start.2 = (bf16[2,2,512,512]{3,2,1,0:T(8,128)(2,1)S(1)}, bf16[2,2,512,512]{3,2,1,0:T(8,128)(2,1)}, u32[]{:S(2)}, u32[]{:S(2)}) collective-permute-start(bf16[2,2,512,512]{3,2,1,0:T(8,128)(2,1)S(1)} %bitcast.169), channel_id=1, source_target_pairs={{16,0},{24,8},{32,16},{40,24},{48,32},{56,40},{64,48},{72,56},{80,... | collective-permute-start | bytes 6291464 | tf_op jit(solution)/shard_map/ppermute | solution.py:22
  73.5 49.7 %all-to-all-start.1 = ((bf16[8,2,64,512]{3,2,1,0:T(8,128)(2,1)}), bf16[8,2,64,512]{3,2,1,0:T(8,128)(2,1)}, u32[]{:S(2)}, u32[]{:S(2)}) async-start(bf16[8,2,64,512]{3,2,1,0:T(8,128)(2,1)} %bitcast.165), calls=%async_computation.1 | async-start | bytes 2097152 | tf_op jit(solution)/shard_map/all_to_all | solution.py:137
  113.4 49.6 %collective-permute-start.3 = (bf16[2,2,512,512]{3,2,1,0:T(8,128)(2,1)}, bf16[2,2,512,512]{3,2,1,0:T(8,128)(2,1)}, u32[]{:S(2)}, u32[]{:S(2)}) collective-permute-start(bf16[2,2,512,512]{3,2,1,0:T(8,128)(2,1)} %collective-permute-done.2), channel_id=1, source_target_pairs={{0,8},{16,24},{32,40},{48,56},{64,72},{80,88},{96,104},{112,120},{... | collective-permute-start | bytes 6291464 | tf_op jit(solution)/shard_map/ppermute | solution.py:112
  124.5 12.5 %collective-permute-start.1 = (bf16[1,2,512,512]{3,2,1,0:T(8,128)(2,1)S(1)}, bf16[1,2,512,512]{3,2,1,0:T(8,128)(2,1)S(1)}, u32[]{:S(2)}, u32[]{:S(2)}) collective-permute-start(bf16[1,2,512,512]{3,2,1,0:T(8,128)(2,1)S(1)} %bitcast.176), channel_id=1, source_target_pairs={{8,0},{24,16},{40,32},{56,48},{72,64},{88,80},{104,96},{120,112},{... | collective-permute-start | bytes 3145736 | tf_op jit(solution)/shard_map/ppermute | solution.py:111
  125.8 28.5 %collective-permute-start.4 = (bf16[1,2,512,512]{3,2,1,0:T(8,128)(2,1)S(1)}, bf16[1,2,512,512]{3,2,1,0:T(8,128)(2,1)}, u32[]{:S(2)}, u32[]{:S(2)}) collective-permute-start(bf16[1,2,512,512]{3,2,1,0:T(8,128)(2,1)S(1)} %bitcast.177), channel_id=1, source_target_pairs={{16,0},{24,8},{32,16},{40,24},{48,32},{56,40},{64,48},{72,56},{80,... | collective-permute-start | bytes 3145736 | tf_op jit(solution)/shard_map/ppermute | solution.py:22
  137.0 1.0 copy-start.5
  138.0 30.5 %all-to-all-start.2 = ((bf16[8,2,64,512]{3,2,1,0:T(8,128)(2,1)}), bf16[8,2,64,512]{3,2,1,0:T(8,128)(2,1)}, u32[]{:S(2)}, u32[]{:S(2)}) async-start(bf16[8,2,64,512]{3,2,1,0:T(8,128)(2,1)} %bitcast.183), calls=%async_computation.2 | async-start | bytes 2097152 | tf_op jit(solution)/shard_map/all_to_all | solution.py:137
  154.3 21.4 %collective-permute-start.5 = (bf16[1,2,512,512]{3,2,1,0:T(8,128)(2,1)}, bf16[1,2,512,512]{3,2,1,0:T(8,128)(2,1)}, u32[]{:S(2)}, u32[]{:S(2)}) collective-permute-start(bf16[1,2,512,512]{3,2,1,0:T(8,128)(2,1)} %collective-permute-done.4), channel_id=1, source_target_pairs={{0,8},{16,24},{32,40},{48,56},{64,72},{80,88},{96,104},{112,120},{... | collective-permute-start | bytes 3145736 | tf_op jit(solution)/shard_map/ppermute | solution.py:112
  169.8 26.4 %collective-permute-start.6 = (bf16[1,2,512,512]{3,2,1,0:T(8,128)(2,1)S(1)}, bf16[1,2,512,512]{3,2,1,0:T(8,128)(2,1)S(1)}, u32[]{:S(2)}, u32[]{:S(2)}) collective-permute-start(bf16[1,2,512,512]{3,2,1,0:T(8,128)(2,1)S(1)} %bitcast.184), channel_id=1, source_target_pairs={{16,0},{24,8},{32,16},{40,24},{48,32},{56,40},{64,48},{72,56},{80,... | collective-permute-start | bytes 3145736 | tf_op jit(solution)/shard_map/ppermute | solution.py:22
  171.7 29.6 %collective-permute-start.8 = (bf16[1,2,512,512]{3,2,1,0:T(8,128)(2,1)S(1)}, bf16[1,2,512,512]{3,2,1,0:T(8,128)(2,1)S(1)}, u32[]{:S(2)}, u32[]{:S(2)}) collective-permute-start(bf16[1,2,512,512]{3,2,1,0:T(8,128)(2,1)S(1)} %bitcast.185), channel_id=1, source_target_pairs={{8,0},{24,16},{40,32},{56,48},{72,64},{88,80},{104,96},{120,112},{... | collective-permute-start | bytes 3145736 | tf_op jit(solution)/shard_map/ppermute | solution.py:111
  173.3 1.6 copy-start.1
  173.3 1.8 copy-start.4
  175.2 1.2 copy-start.6
  196.2 5.1 %collective-permute-start.7 = (bf16[1,2,512,512]{3,2,1,0:T(8,128)(2,1)S(1)}, bf16[1,2,512,512]{3,2,1,0:T(8,128)(2,1)S(1)}, u32[]{:S(2)}, u32[]{:S(2)}) collective-permute-start(bf16[1,2,512,512]{3,2,1,0:T(8,128)(2,1)S(1)} %collective-permute-done.6), channel_id=1, source_target_pairs={{0,8},{16,24},{32,40},{48,56},{64,72},{80,88},{96,104},{112,120},{... | collective-permute-start | bytes 3145736 | tf_op jit(solution)/shard_map/ppermute | solution.py:112
  198.9 1.6 copy-start
  198.9 1.8 copy-start.3
  201.5 1.6 copy-start.2

commit v19 on v16

--- a/solution.py
+++ b/solution.py
@@ -105,9 +105,15 @@
     return results
 
 
-def neighbour_panels(own_panel):
+def neighbour_panels(own_panel, merged=False):
     n_chan = lax.axis_size("chan")
     second_panel = from_behind(own_panel, "chan", -2)
+    odd = lax.axis_index("chan") % 2 == 1
+    if merged:
+        outgoing = jnp.where(odd, own_panel, second_panel)
+        pairs = [(c, c - 1) for c in range(1, n_chan, 2)] + [(c, c + 1) for c in range(0, n_chan - 1, 2)]
+        upper_panel = lax.ppermute(outgoing, "chan", pairs)
+        return upper_panel, second_panel, upper_panel
     from_sibling = lax.ppermute(own_panel, "chan", [(c + 1, c) for c in range(0, n_chan, 2)])
     from_forward = lax.ppermute(second_panel, "chan", [(c - 1, c) for c in range(1, n_chan, 2)])
     odd = lax.axis_index("chan") % 2 == 1
@@ -129,7 +135,7 @@
     chunk_products = []
     for k in range(chunks):
         own_panel = lax.all_to_all(parts[k], "freq", split_axis=0, concat_axis=2, tiled=True)
-        upper_panel, second_panel, from_sibling = neighbour_panels(own_panel)
+        upper_panel, second_panel, from_sibling = neighbour_panels(own_panel, merged=k + 1 == chunks)
         if k + 1 < chunks:
             _, parts[k + 1] = lax.optimization_barrier((from_sibling, parts[k + 1]))
         chunk_products.append(local_products(own_panel, [own_panel, upper_panel, second_panel]))

time: 208 us -> 207 us (level)
  waiting for transfers between devices: 88.6 us -> 94.2 us
  starting transfers between devices: 18.7 us -> 13.6 us
    all_to_all x1, waiting for transfers between devices: 17.1 us -> 22.9 us  [shards(): lax.all_to_all(parts[k], 'freq', split_axis=0, concat_axis=2, tiled=True)]
    ppermute x2 -> x1, starting transfers between devices: 5.58 us -> 1.41 us  [neighbour_panels(): lax.ppermute(second_panel, 'chan', [(c - 1, c) for c in range(1, n_chan,...]
  transfers between devices with their start and end apart: 7 -> 6, of which waited for: 3 -> 4; matrix products, arithmetic and copies ran while one was open for 12% -> 12% of each run, Pallas kernels for 0% -> 0%
where the time goes in v19:
time: 207 us; the launch traced here: 206 us
  waiting for transfers between devices  94.2 us (46%)
  blocking collectives  34.5 us (17%)
  Pallas kernels  19.8 us (10%)
  matrix products  17 us (8%)
  starting transfers between devices  13.6 us (7%)
  other arithmetic  13.1 us (6%)
  local copies, waits for them, and re-layouts  12.6 us (6%)
    ppermute x2, waiting for transfers between devices, from_behind(): return lax.ppermute(block, axis, route)  70.2 us
    all_to_all x1, blocking collectives, shards(): lax.all_to_all(parts[k], 'freq', split_axis=0, concat_axis=2, tiled=True)  34.5 us
    all_to_all x1, waiting for transfers between devices, shards(): lax.all_to_all(parts[k], 'freq', split_axis=0, concat_axis=2, tiled=True)  22.9 us
    pallas_call x1, Pallas kernels, whitened_spectra(): pl.pallas_call(functools.partial(spectra_kernel, seg_count, window), out_...  19.8 us
    dot_general x6, matrix products, local_products(): jnp.einsum('fpsi,fpsj->fij', left_panel, both, preferred_element_type=jnp...  17 us
    unnamed x8, local copies, waits for them, and re-layouts  6.97 us
    ppermute x2, starting transfers between devices, from_behind(): return lax.ppermute(block, axis, route)  6.1 us
    another operation x1, other arithmetic, shards(): return jnp.stack(results, axis=0)  5.47 us
  transfers between devices with their start and end apart: 6, of which 4 were waited for; matrix products, arithmetic and copies ran while one was open for 12% of the time, Pallas kernels for 0%

profile of v19, /device:TPU:34, one launch (start us, length us, event | category | flops | bytes accessed | tf_op | source)
XLA Modules:
  0.0 205.9 jit_solution(18296498190668790958)
XLA Ops:
  0.1 1.3 convert_element_type.70
  2.1 0.7 pad_convert_fusion.dft_ref
  2.7 19.8 %shard_map.46 = bf16[64,64,512]{2,1,0:T(8,128)(2,1)} custom-call(s32[64]{0:T(128)} %offs_ref.1, f32[64,384]{1,0:T(8,128)} %pad_convert_fusion.dft_ref, f32[1,512]{1,0:T(1,128)} %bitcast.105, bf16[8448,512]{1,0:T(8,128)(2,1)} %rec_hbm.1), custom_call_target="tpu_custom_call" | custom-call | flops 1140850688 | bytes 22020096 | tf_op jit(solution)/shard_map/pallas_call | solution.py:69
  22.6 2.8 %fusion.88 = (bf16[64,2,1,16,512]{4,3,2,1,0:T(8,128)(2,1)S(1)}, bf16[64,2,1,16,512]{4,3,2,1,0:T(8,128)(2,1)S(1)}) fusion(bf16[64,2,2,16,512]{4,3,2,1,0:T(8,128)(2,1)} %bitcast.95), kind=kLoop, calls=%fused_computation.94 | loop fusion | bytes 8388608 | tf_op jit(solution)/shard_map/slice | solution.py:134
  25.3 2.2 %copy.48 = bf16[64,2,1,16,512]{4,1,0,3,2:T(2,128)(2,1)S(1)} copy(bf16[64,2,1,16,512]{4,3,2,1,0:T(8,128)(2,1)S(1)} %get-tuple-element.8) | data formatting | bytes 4194304
  27.5 34.5 %all_to_all.36 = bf16[16,2,64,512]{3,1,2,0:T(2,128)(2,1)S(1)} all-to-all(bf16[16,2,64,512]{3,1,2,0:T(2,128)(2,1)S(1)} %bitcast.103), channel_id=1, replica_groups=mesh['chan'=16,'freq'=8] {'freq'}, dimensions={0} | all-to-all | bytes 4194304 | tf_op jit(solution)/shard_map/all_to_all | solution.py:137
  62.0 0.4 copy.22
  62.4 1.5 collective-permute-start
  63.9 3.5 %copy.47 = bf16[64,2,1,16,512]{4,1,0,3,2:T(2,128)(2,1)} copy(bf16[64,2,1,16,512]{4,3,2,1,0:T(8,128)(2,1)S(1)} %get-tuple-element.7) | data formatting | bytes 4194304
  67.4 1.1 collective-permute-done
  68.5 1.3 copy-done
  69.8 4.3 %all-to-all-start.1 = ((bf16[16,2,64,512]{3,1,2,0:T(2,128)(2,1)}), bf16[16,2,64,512]{3,1,2,0:T(2,128)(2,1)}, u32[]{:S(2)}, u32[]{:S(2)}) async-start(bf16[16,2,64,512]{3,1,2,0:T(2,128)(2,1)} %bitcast.102), calls=%async_computation.1 | async-start | bytes 4194304 | tf_op jit(solution)/shard_map/all_to_all | solution.py:137
  74.2 3.1 %collective-permute-start.1 = (bf16[2,2,512,512]{3,2,1,0:T(8,128)(2,1)S(1)}, bf16[2,2,512,512]{3,2,1,0:T(8,128)(2,1)}, u32[]{:S(2)}, u32[]{:S(2)}) collective-permute-start(bf16[2,2,512,512]{3,2,1,0:T(8,128)(2,1)S(1)} %bitcast.97), channel_id=1, source_target_pairs={{16,0},{24,8},{32,16},{40,24},{48,32},{56,40},{64,48},{72,56},{80,... | collective-permute-start | bytes 6291464 | tf_op jit(solution)/shard_map/ppermute | solution.py:22
  77.9 1.1 slice_negate_fusion.5
  79.1 22.9 %all-to-all-done.1 = bf16[16,2,64,512]{3,1,2,0:T(2,128)(2,1)} async-done(((bf16[16,2,64,512]{3,1,2,0:T(2,128)(2,1)}), bf16[16,2,64,512]{3,1,2,0:T(2,128)(2,1)}, u32[]{:S(2)}, u32[]{:S(2)}) %all-to-all-start.1) | async-done | bytes 2097184 | tf_op jit(solution)/shard_map/all_to_all | solution.py:137
  101.9 2.1 %copy.25 = bf16[8,2,2,64,512]{4,3,0,2,1:T(8,128)(2,1)S(1)} copy(bf16[8,2,2,64,512]{4,2,3,1,0:T(2,128)(2,1)} %bitcast.13) | data formatting | bytes 4194304 | tf_op jit(solution)/shard_map/all_to_all | solution.py:137
  104.1 3.0 %collective-permute-start.3 = (bf16[2,2,512,512]{3,2,1,0:T(8,128)(2,1)S(1)}, bf16[2,2,512,512]{3,2,1,0:T(8,128)(2,1)S(1)}, u32[]{:S(2)}, u32[]{:S(2)}) collective-permute-start(bf16[2,2,512,512]{3,2,1,0:T(8,128)(2,1)S(1)} %bitcast.90), channel_id=1, source_target_pairs={{16,0},{24,8},{32,16},{40,24},{48,32},{56,40},{64,48},{72,56},{80,... | collective-permute-start | bytes 6291464 | tf_op jit(solution)/shard_map/ppermute | solution.py:22
  107.1 2.6 %fusion.54 = bf16[1,2,512,1024]{3,2,1,0:T(8,128)(2,1)S(1)} fusion(bf16[2,2,512,512]{3,2,1,0:T(8,128)(2,1)S(1)} %bitcast.99, bf16[2,1,512,512]{3,2,1,0:T(8,128)(2,1)S(1)} %copy-done.2, bf16[2,1,512,512]{3,2,1,0:T(8,128)(2,1)S(1)} %get-tuple-element.9), kind=kOutput, calls=%fused_computation.56 | convolution fusion | flops 2162163712 | bytes 6291456 | tf_op jit(solution)/shard_map/fpsi,fpsj->fij/dot_general | solution.py:101
  109.7 36.1 %collective-permute-done.1 = bf16[2,2,512,512]{3,2,1,0:T(8,128)(2,1)} collective-permute-done((bf16[2,2,512,512]{3,2,1,0:T(8,128)(2,1)S(1)}, bf16[2,2,512,512]{3,2,1,0:T(8,128)(2,1)}, u32[]{:S(2)}, u32[]{:S(2)}) %collective-permute-start.1) | collective-permute-done | bytes 2097184 | tf_op jit(solution)/shard_map/ppermute | solution.py:22
  145.8 1.4 collective-permute-start.2
  147.3 1.7 slice_negate_fusion.1
  149.0 4.0 %fusion.66 = bf16[1,2,512,1024]{3,2,1,0:T(8,128)(2,1)S(1)} fusion(bf16[2,2,512,512]{3,2,1,0:T(8,128)(2,1)S(1)} %bitcast.100, bf16[2,1,512,512]{3,2,1,0:T(8,128)(2,1)S(1)} %get-tuple-element.18, bf16[2,1,512,512]{3,2,1,0:T(8,128)(2,1)S(1)} %get-tuple-element.17, bf16[2,2,512,512]{3,2,1,0:T(8,128)(2,1)} %collective-permute-done.1), kind=kOutput, calls=%fused_computation.60 | convolution fusion | flops 2162163712 | bytes 8388608 | tf_op jit(solution)/shard_map/fpsi,fpsj->fij/dot_general | solution.py:101
  153.1 2.6 %fusion.57 = bf16[1,2,512,1024]{3,2,1,0:T(8,128)(2,1)S(1)} fusion(bf16[2,2,512,512]{3,2,1,0:T(8,128)(2,1)S(1)} %bitcast.92, bf16[2,1,512,512]{3,2,1,0:T(8,128)(2,1)S(1)} %get-tuple-element.12, bf16[2,1,512,512]{3,2,1,0:T(8,128)(2,1)S(1)} %get-tuple-element.11), kind=kOutput, calls=%fused_computation.57 | convolution fusion | flops 2162163712 | bytes 6291456 | tf_op jit(solution)/shard_map/fpsi,fpsj->fij/dot_general | solution.py:101
  155.7 0.4 maximum_multiply_fusion
  156.1 34.1 %collective-permute-done.3 = bf16[2,2,512,512]{3,2,1,0:T(8,128)(2,1)S(1)} collective-permute-done((bf16[2,2,512,512]{3,2,1,0:T(8,128)(2,1)S(1)}, bf16[2,2,512,512]{3,2,1,0:T(8,128)(2,1)S(1)}, u32[]{:S(2)}, u32[]{:S(2)}) %collective-permute-start.3) | collective-permute-done | bytes 2097184 | tf_op jit(solution)/shard_map/ppermute | solution.py:22
  190.2 0.4 broadcast_select_fusion
  191.4 2.6 %fusion.60 = bf16[1,2,512,1024]{3,2,1,0:T(8,128)(2,1)S(1)} fusion(bf16[2,2,512,512]{3,2,1,0:T(8,128)(2,1)S(1)} %bitcast.101, bf16[2,1,512,512]{3,2,1,0:T(8,128)(2,1)S(1)} %get-tuple-element.14, bf16[2,1,512,512]{3,2,1,0:T(8,128)(2,1)S(1)} %get-tuple-element.13, bf16[2,2,512,512]{3,2,1,0:T(8,128)(2,1)S(1)} %broadcast_select_fusion.1), kind=kOutput, calls=%fused_computation.58 | convolution fusion | flops 2162163712 | bytes 8388608 | tf_op jit(solution)/shard_map/fpsi,fpsj->fij/dot_general | solution.py:101
  194.2 2.6 %fusion.69 = bf16[1,2,512,1024]{3,2,1,0:T(8,128)(2,1)S(1)} fusion(bf16[2,2,512,512]{3,2,1,0:T(8,128)(2,1)S(1)} %bitcast.93, bf16[2,1,512,512]{3,2,1,0:T(8,128)(2,1)S(1)} %get-tuple-element.20, bf16[2,1,512,512]{3,2,1,0:T(8,128)(2,1)S(1)} %get-tuple-element.19, bf16[2,2,512,512]{3,2,1,0:T(8,128)(2,1)S(1)} %collective-permute-done.3), kind=kOutput, calls=%fused_computation.61 | convolution fusion | flops 2162163712 | bytes 8388608 | tf_op jit(solution)/shard_map/fpsi,fpsj->fij/dot_general | solution.py:101
  196.8 0.4 maximum_multiply_fusion.2
  197.4 2.6 %fusion.63 = bf16[1,2,512,1024]{3,2,1,0:T(8,128)(2,1)S(1)} fusion(bf16[2,2,512,512]{3,2,1,0:T(8,128)(2,1)S(1)} %bitcast.94, bf16[2,1,512,512]{3,2,1,0:T(8,128)(2,1)S(1)} %get-tuple-element.16, bf16[2,1,512,512]{3,2,1,0:T(8,128)(2,1)S(1)} %get-tuple-element.15, bf16[2,2,512,512]{3,2,1,0:T(8,128)(2,1)S(1)} %collective-permute-done.4), kind=kOutput, calls=%fused_computation.59 | convolution fusion | flops 2162163712 | bytes 8388608 | tf_op jit(solution)/shard_map/fpsi,fpsj->fij/dot_general | solution.py:101
  200.0 0.4 maximum_multiply_fusion.1
  200.4 5.5 %pad_maximum_fusion = bf16[3,4,512,1024]{3,2,1,0:T(8,128)(2,1)} fusion(bf16[1,4,512,1024]{3,2,1,0:T(8,128)(2,1)S(1)} %maximum_multiply_fusion.2, bf16[1,4,512,1024]{3,2,1,0:T(8,128)(2,1)S(1)} %maximum_multiply_fusion.1, bf16[1,4,512,1024]{3,2,1,0:T(8,128)(2,1)S(1)} %maximum_multiply_fusion), kind=kLoop, calls=%fused_computation | loop fusion | flops 12582912 | bytes 25165824 | tf_op jit(solution)/shard_map/stack | solution.py:148
  (23 shorter events, 1.9 us)
Async XLA Ops:
  62.4 6.1 %collective-permute-start = (bf16[2,2,512,512]{3,2,1,0:T(8,128)(2,1)S(1)}, bf16[2,2,512,512]{3,2,1,0:T(8,128)(2,1)S(1)}, u32[]{:S(2)}, u32[]{:S(2)}) collective-permute-start(bf16[2,2,512,512]{3,2,1,0:T(8,128)(2,1)S(1)} %bitcast.96), channel_id=1, source_target_pairs={{8,0},{24,16},{40,32},{56,48},{72,64},{88,80},{104,96},{120,112},{... | collective-permute-start | bytes 6291464 | tf_op jit(solution)/shard_map/ppermute | solution.py:117
  68.5 1.3 copy-start
  69.8 32.1 %all-to-all-start.1 = ((bf16[16,2,64,512]{3,1,2,0:T(2,128)(2,1)}), bf16[16,2,64,512]{3,1,2,0:T(2,128)(2,1)}, u32[]{:S(2)}, u32[]{:S(2)}) async-start(bf16[16,2,64,512]{3,1,2,0:T(2,128)(2,1)} %bitcast.102), calls=%async_computation.1 | async-start | bytes 4194304 | tf_op jit(solution)/shard_map/all_to_all | solution.py:137
  74.2 71.7 %collective-permute-start.1 = (bf16[2,2,512,512]{3,2,1,0:T(8,128)(2,1)S(1)}, bf16[2,2,512,512]{3,2,1,0:T(8,128)(2,1)}, u32[]{:S(2)}, u32[]{:S(2)}) collective-permute-start(bf16[2,2,512,512]{3,2,1,0:T(8,128)(2,1)S(1)} %bitcast.97), channel_id=1, source_target_pairs={{16,0},{24,8},{32,16},{40,24},{48,32},{56,40},{64,48},{72,56},{80,... | collective-permute-start | bytes 6291464 | tf_op jit(solution)/shard_map/ppermute | solution.py:22
  101.9 5.2 %copy-start.2 = (bf16[2,1,512,512]{3,2,1,0:T(8,128)(2,1)S(1)}, bf16[2,1,512,512]{3,2,1,0:T(8,128)(2,1)}, u32[]{:S(2)}) copy-start(bf16[2,1,512,512]{3,2,1,0:T(8,128)(2,1)} %get-tuple-element.10) | copy-start | bytes 3145732
  104.1 86.2 %collective-permute-start.3 = (bf16[2,2,512,512]{3,2,1,0:T(8,128)(2,1)S(1)}, bf16[2,2,512,512]{3,2,1,0:T(8,128)(2,1)S(1)}, u32[]{:S(2)}, u32[]{:S(2)}) collective-permute-start(bf16[2,2,512,512]{3,2,1,0:T(8,128)(2,1)S(1)} %bitcast.90), channel_id=1, source_target_pairs={{16,0},{24,8},{32,16},{40,24},{48,32},{56,40},{64,48},{72,56},{80,... | collective-permute-start | bytes 6291464 | tf_op jit(solution)/shard_map/ppermute | solution.py:22
  145.8 45.1 %collective-permute-start.2 = (bf16[2,2,512,512]{3,2,1,0:T(8,128)(2,1)}, bf16[2,2,512,512]{3,2,1,0:T(8,128)(2,1)S(1)}, u32[]{:S(2)}, u32[]{:S(2)}) collective-permute-start(bf16[2,2,512,512]{3,2,1,0:T(8,128)(2,1)} %collective-permute-done.1), channel_id=1, source_target_pairs={{0,8},{16,24},{32,40},{48,56},{64,72},{80,88},{96,104},{112,120},{... | collective-permute-start | bytes 6291464 | tf_op jit(solution)/shard_map/ppermute | solution.py:118
  156.1 34.9 %copy-start.1 = (bf16[2,2,512,512]{3,2,1,0:T(8,128)(2,1)S(1)}, bf16[2,2,512,512]{3,2,1,0:T(8,128)(2,1)}, u32[]{:S(2)}) copy-start(bf16[2,2,512,512]{3,2,1,0:T(8,128)(2,1)} %copy-done) | copy-start | bytes 6291460
  190.6 6.6 %collective-permute-start.4 = (bf16[2,2,512,512]{3,2,1,0:T(8,128)(2,1)S(1)}, bf16[2,2,512,512]{3,2,1,0:T(8,128)(2,1)S(1)}, u32[]{:S(2)}, u32[]{:S(2)}) collective-permute-start(bf16[2,2,512,512]{3,2,1,0:T(8,128)(2,1)S(1)} %broadcast_select_fusion), channel_id=1, source_target_pairs={{8,0},{24,16},{40,32},{56,48},{72,64},{88,80},{104,96},{120,112},{... | collective-permute-start | bytes 6291464 | tf_op jit(solution)/shard_map/ppermute | solution.py:115

commit v20 on v19

--- a/solution.py
+++ b/solution.py
@@ -35,7 +35,8 @@
     return (hann_taper[None, :] * wave_rows).astype(jnp.bfloat16)
 
 
-def spectra_kernel(seg_count, window, offs_ref, dft_ref, mask_ref, rec_hbm, out_ref, frames, sems):
+def spectra_kernel(seg_count, window, chunks, offs_ref, dft_ref, mask_ref, rec_hbm, *refs):
+    out_refs, (frames, sems) = refs[:chunks], refs[chunks:]
     last_start = rec_hbm.shape[0] - window
     starts = []
     copies = []
@@ -56,10 +57,15 @@
         spec = jnp.dot(shifted, frames[j], preferred_element_type=jnp.float32)
         power = jnp.sum(spec * spec, axis=0, keepdims=True) * (1.0 / BINS)
         scale = live / jnp.sqrt(power + EPS_POWER)
-        out_ref[j] = (spec * scale).astype(out_ref.dtype)
+        white = (spec * scale).astype(jnp.bfloat16)
+        slab = white.shape[0] // (2 * chunks)
+        for k, out_ref in enumerate(out_refs):
+            for part in range(2):
+                first = (part * chunks + k) * slab
+                out_ref[j, part] = white[first:first + slab]
 
 
-def whitened_spectra(records, offsets, dead_mask, dft_rows):
+def whitened_spectra(records, offsets, dead_mask, dft_rows, chunks):
     seg_count = offsets.shape[0]
     channels = records.shape[1]
     window = SEG_LEN + 16
@@ -67,8 +73,11 @@
     padded = jnp.pad(dft_rows.astype(jnp.float32), ((0, 0), (0, 128)))
     live = dead_mask.astype(jnp.float32).reshape(1, channels)
     return pl.pallas_call(
-        functools.partial(spectra_kernel, seg_count, window),
-        out_shape=jax.ShapeDtypeStruct((seg_count, rows, channels), jnp.bfloat16),
+        functools.partial(spectra_kernel, seg_count, window, chunks),
+        out_shape=[
+            jax.ShapeDtypeStruct((seg_count, 2, rows // (2 * chunks), channels), jnp.bfloat16)
+            for _ in range(chunks)
+        ],
         grid_spec=pltpu.PrefetchScalarGridSpec(
             num_scalar_prefetch=1,
             grid=(1,),
@@ -77,7 +86,10 @@
                 pl.BlockSpec((1, channels), lambda i, offs: (0, 0)),
                 pl.BlockSpec(memory_space=pl.ANY),
             ],
-            out_specs=pl.BlockSpec((seg_count, rows, channels), lambda i, offs: (0, 0, 0)),
+            out_specs=[
+                pl.BlockSpec((seg_count, 2, rows // (2 * chunks), channels), lambda i, offs: (0, 0, 0, 0))
+                for _ in range(chunks)
+            ],
             scratch_shapes=[
                 pltpu.VMEM((seg_count, window, channels), records.dtype),
                 pltpu.SemaphoreType.DMA((seg_count,)),
@@ -128,10 +140,9 @@
     per_chunk = per_device // chunks
     table = dft_table(SEG_LEN, BINS, FIRST_BIN).reshape(n_freq, chunks, per_chunk, 2, SEG_LEN)
     table = table.transpose(3, 1, 0, 2, 4).reshape(2 * BINS, SEG_LEN)
-    per_segment = whitened_spectra(records, offsets, dead_mask, table)
-    seg_count, rows, channels = per_segment.shape
-    slabs = per_segment.reshape(seg_count, 2, chunks, n_freq * per_chunk, channels)
-    parts = [slabs[:, :, k].transpose(2, 1, 0, 3) for k in range(chunks)]
+    slabs = whitened_spectra(records, offsets, dead_mask, table, chunks)
+    seg_count, _, _, channels = slabs[0].shape
+    parts = [slab.transpose(2, 1, 0, 3) for slab in slabs]
     chunk_products = []
     for k in range(chunks):
         own_panel = lax.all_to_all(parts[k], "freq", split_axis=0, concat_axis=2, tiled=True)

time: 207 us -> 210 us (1.014)
  waiting for transfers between devices: 94.2 us -> 97.5 us
    unnamed x8, local copies, waits for them, and re-layouts: 6.97 us -> 1.35 us
    transpose x0 -> x1, local copies, waits for them, and re-layouts: none -> 3.75 us  [shards(): parts = [slab.transpose(2, 1, 0, 3) for slab in slabs]]
    ppermute x1, waiting for transfers between devices: 1.09 us -> 4.57 us  [neighbour_panels(): lax.ppermute(own_panel, 'chan', [(c + 1, c) for c in range(0, n_chan, 2)])]
    optimization_barrier x0 -> x1, local copies, waits for them, and re-layouts: none -> 3.48 us  [shards(): _, parts[k + 1] = lax.optimization_barrier((from_sibling, parts[k + 1]))]
    slice x1 -> x0, local copies, waits for them, and re-layouts: 2.76 us -> none  [shards(): parts = [slabs[:, :, k].transpose(2, 1, 0, 3) for k in range(chunks)]]
  transfers between devices with their start and end apart: 6 -> 6, of which waited for: 4 -> 4; matrix products, arithmetic and copies ran while one was open for 12% -> 10% of each run, Pallas kernels for 0% -> 0%
where the time goes in v20:
time: 210 us; the launch traced here: 208 us
  waiting for transfers between devices  97.5 us (46%)
  blocking collectives  34.6 us (16%)
  Pallas kernels  19.8 us (9%)
  matrix products  17 us (8%)
  starting transfers between devices  13.8 us (7%)
  other arithmetic  13.1 us (6%)
  local copies, waits for them, and re-layouts  11.5 us (5%)
    ppermute x2, waiting for transfers between devices, from_behind(): return lax.ppermute(block, axis, route)  70.1 us
    all_to_all x1, blocking collectives, shards(): lax.all_to_all(parts[k], 'freq', split_axis=0, concat_axis=2, tiled=True)  34.6 us
    all_to_all x1, waiting for transfers between devices, shards(): lax.all_to_all(parts[k], 'freq', split_axis=0, concat_axis=2, tiled=True)  22.8 us
    pallas_call x1, Pallas kernels, whitened_spectra(): pl.pallas_call(functools.partial(spectra_kernel, seg_count, window, chunk...  19.8 us
    dot_general x6, matrix products, local_products(): jnp.einsum('fpsi,fpsj->fij', left_panel, both, preferred_element_type=jnp...  17 us
    ppermute x2, starting transfers between devices, from_behind(): return lax.ppermute(block, axis, route)  6.21 us
    another operation x1, other arithmetic, shards(): return jnp.stack(results, axis=0)  5.47 us
    ppermute x1, waiting for transfers between devices, neighbour_panels(): lax.ppermute(own_panel, 'chan', [(c + 1, c) for c in range(0, n_chan, 2)])  4.57 us
  transfers between devices with their start and end apart: 6, of which 4 were waited for; matrix products, arithmetic and copies ran while one was open for 10% of the time, Pallas kernels for 0%

profile of v20, /device:TPU:34, one launch (start us, length us, event | category | flops | bytes accessed | tf_op | source)
XLA Modules:
  0.0 208.2 jit_solution(16814948235709563085)
XLA Ops:
  0.1 1.3 convert_element_type.70
  1.7 0.3 multiply_convert_fusion
  2.1 0.7 pad_convert_fusion.dft_ref
  2.7 19.8 %shard_map.46 = (bf16[64,2,16,512]{3,2,1,0:T(8,128)(2,1)}, bf16[64,2,16,512]{3,2,1,0:T(8,128)(2,1)}) custom-call(s32[64]{0:T(128)} %offs_ref.1, f32[64,384]{1,0:T(8,128)} %pad_convert_fusion.dft_ref, f32[1,512]{1,0:T(1,128)} %bitcast.95, bf16[8448,512]{1,0:T(8,128)(2,1)} %rec_hbm.1), custom_call_target="tpu_custom_call" | custom-call | flops 1140850688 | bytes 22020096 | tf_op jit(solution)/shard_map/pallas_call | solution.py:75
  22.5 3.8 %copy.21 = bf16[16,2,64,512]{3,1,2,0:T(2,128)(2,1)S(1)} copy(bf16[16,2,64,512]{3,0,1,2:T(8,128)(2,1)} %bitcast.94) | data formatting | bytes 4194304 | tf_op jit(solution)/shard_map/transpose | solution.py:145
  26.3 34.6 %all_to_all.36 = bf16[16,2,64,512]{3,1,2,0:T(2,128)(2,1)S(1)} all-to-all(bf16[16,2,64,512]{3,1,2,0:T(2,128)(2,1)S(1)} %copy.21), channel_id=1, replica_groups=mesh['chan'=16,'freq'=8] {'freq'}, dimensions={0} | all-to-all | bytes 4194304 | tf_op jit(solution)/shard_map/all_to_all | solution.py:148
  60.9 0.4 copy.22
  61.4 1.5 collective-permute-start
  62.8 4.6 %collective-permute-done = bf16[2,2,512,512]{3,2,1,0:T(8,128)(2,1)S(1)} collective-permute-done((bf16[2,2,512,512]{3,2,1,0:T(8,128)(2,1)S(1)}, bf16[2,2,512,512]{3,2,1,0:T(8,128)(2,1)S(1)}, u32[]{:S(2)}, u32[]{:S(2)}) %collective-permute-start) | collective-permute-done | bytes 2097184 | tf_op jit(solution)/shard_map/ppermute | solution.py:129
  67.4 1.3 copy-done
  68.8 3.5 %copy.24 = bf16[16,2,64,512]{3,1,2,0:T(2,128)(2,1)} copy(bf16[16,2,64,512]{3,0,1,2:T(8,128)(2,1)S(1)} %bitcast.93) | data formatting | bytes 4194304 | tf_op jit(solution)/shard_map/optimization_barrier | solution.py:151
  72.2 4.4 %all-to-all-start.1 = ((bf16[16,2,64,512]{3,1,2,0:T(2,128)(2,1)}), bf16[16,2,64,512]{3,1,2,0:T(2,128)(2,1)}, u32[]{:S(2)}, u32[]{:S(2)}) async-start(bf16[16,2,64,512]{3,1,2,0:T(2,128)(2,1)} %copy.24), calls=%async_computation.1 | async-start | bytes 4194304 | tf_op jit(solution)/shard_map/all_to_all | solution.py:148
  76.6 3.1 %collective-permute-start.1 = (bf16[2,2,512,512]{3,2,1,0:T(8,128)(2,1)S(1)}, bf16[2,2,512,512]{3,2,1,0:T(8,128)(2,1)}, u32[]{:S(2)}, u32[]{:S(2)}) collective-permute-start(bf16[2,2,512,512]{3,2,1,0:T(8,128)(2,1)S(1)} %bitcast.87), channel_id=1, source_target_pairs={{16,0},{24,8},{32,16},{40,24},{48,32},{56,40},{64,48},{72,56},{80,... | collective-permute-start | bytes 6291464 | tf_op jit(solution)/shard_map/ppermute | solution.py:22
  80.4 1.1 slice_negate_fusion.5
  81.5 22.8 %all-to-all-done.1 = bf16[16,2,64,512]{3,1,2,0:T(2,128)(2,1)} async-done(((bf16[16,2,64,512]{3,1,2,0:T(2,128)(2,1)}), bf16[16,2,64,512]{3,1,2,0:T(2,128)(2,1)}, u32[]{:S(2)}, u32[]{:S(2)}) %all-to-all-start.1) | async-done | bytes 2097184 | tf_op jit(solution)/shard_map/all_to_all | solution.py:148
  104.3 2.1 %copy.25 = bf16[8,2,2,64,512]{4,3,0,2,1:T(8,128)(2,1)S(1)} copy(bf16[8,2,2,64,512]{4,2,3,1,0:T(2,128)(2,1)} %bitcast.10) | data formatting | bytes 4194304 | tf_op jit(solution)/shard_map/all_to_all | solution.py:148
  106.5 3.1 %collective-permute-start.3 = (bf16[2,2,512,512]{3,2,1,0:T(8,128)(2,1)S(1)}, bf16[2,2,512,512]{3,2,1,0:T(8,128)(2,1)S(1)}, u32[]{:S(2)}, u32[]{:S(2)}) collective-permute-start(bf16[2,2,512,512]{3,2,1,0:T(8,128)(2,1)S(1)} %bitcast.81), channel_id=1, source_target_pairs={{16,0},{24,8},{32,16},{40,24},{48,32},{56,40},{64,48},{72,56},{80,... | collective-permute-start | bytes 6291464 | tf_op jit(solution)/shard_map/ppermute | solution.py:22
  109.6 2.6 %fusion.54 = bf16[1,2,512,1024]{3,2,1,0:T(8,128)(2,1)S(1)} fusion(bf16[2,2,512,512]{3,2,1,0:T(8,128)(2,1)S(1)} %bitcast.89, bf16[2,1,512,512]{3,2,1,0:T(8,128)(2,1)S(1)} %copy-done.3, bf16[2,1,512,512]{3,2,1,0:T(8,128)(2,1)S(1)} %get-tuple-element.11), kind=kOutput, calls=%fused_computation.54 | convolution fusion | flops 2162163712 | bytes 6291456 | tf_op jit(solution)/shard_map/fpsi,fpsj->fij/dot_general | solution.py:113
  112.2 36.1 %collective-permute-done.1 = bf16[2,2,512,512]{3,2,1,0:T(8,128)(2,1)} collective-permute-done((bf16[2,2,512,512]{3,2,1,0:T(8,128)(2,1)S(1)}, bf16[2,2,512,512]{3,2,1,0:T(8,128)(2,1)}, u32[]{:S(2)}, u32[]{:S(2)}) %collective-permute-start.1) | collective-permute-done | bytes 2097184 | tf_op jit(solution)/shard_map/ppermute | solution.py:22
  148.3 1.4 collective-permute-start.2
  149.7 1.7 slice_negate_fusion.1
  151.4 4.0 %fusion.66 = bf16[1,2,512,1024]{3,2,1,0:T(8,128)(2,1)S(1)} fusion(bf16[2,2,512,512]{3,2,1,0:T(8,128)(2,1)S(1)} %bitcast.90, bf16[2,1,512,512]{3,2,1,0:T(8,128)(2,1)S(1)} %get-tuple-element.20, bf16[2,1,512,512]{3,2,1,0:T(8,128)(2,1)S(1)} %get-tuple-element.19, bf16[2,2,512,512]{3,2,1,0:T(8,128)(2,1)} %collective-permute-done.1), kind=kOutput, calls=%fused_computation.58 | convolution fusion | flops 2162163712 | bytes 8388608 | tf_op jit(solution)/shard_map/fpsi,fpsj->fij/dot_general | solution.py:113
  155.5 2.6 %fusion.57 = bf16[1,2,512,1024]{3,2,1,0:T(8,128)(2,1)S(1)} fusion(bf16[2,2,512,512]{3,2,1,0:T(8,128)(2,1)S(1)} %bitcast.83, bf16[2,1,512,512]{3,2,1,0:T(8,128)(2,1)S(1)} %get-tuple-element.14, bf16[2,1,512,512]{3,2,1,0:T(8,128)(2,1)S(1)} %get-tuple-element.13), kind=kOutput, calls=%fused_computation.55 | convolution fusion | flops 2162163712 | bytes 6291456 | tf_op jit(solution)/shard_map/fpsi,fpsj->fij/dot_general | solution.py:113
  158.1 0.4 maximum_multiply_fusion
  158.5 34.1 %collective-permute-done.3 = bf16[2,2,512,512]{3,2,1,0:T(8,128)(2,1)S(1)} collective-permute-done((bf16[2,2,512,512]{3,2,1,0:T(8,128)(2,1)S(1)}, bf16[2,2,512,512]{3,2,1,0:T(8,128)(2,1)S(1)}, u32[]{:S(2)}, u32[]{:S(2)}) %collective-permute-start.3) | collective-permute-done | bytes 2097184 | tf_op jit(solution)/shard_map/ppermute | solution.py:22
  192.6 0.4 broadcast_select_fusion
  193.8 2.6 %fusion.60 = bf16[1,2,512,1024]{3,2,1,0:T(8,128)(2,1)S(1)} fusion(bf16[2,2,512,512]{3,2,1,0:T(8,128)(2,1)S(1)} %bitcast.91, bf16[2,1,512,512]{3,2,1,0:T(8,128)(2,1)S(1)} %get-tuple-element.16, bf16[2,1,512,512]{3,2,1,0:T(8,128)(2,1)S(1)} %get-tuple-element.15, bf16[2,2,512,512]{3,2,1,0:T(8,128)(2,1)S(1)} %broadcast_select_fusion.1), kind=kOutput, calls=%fused_computation.56 | convolution fusion | flops 2162163712 | bytes 8388608 | tf_op jit(solution)/shard_map/fpsi,fpsj->fij/dot_general | solution.py:113
  196.5 2.6 %fusion.69 = bf16[1,2,512,1024]{3,2,1,0:T(8,128)(2,1)S(1)} fusion(bf16[2,2,512,512]{3,2,1,0:T(8,128)(2,1)S(1)} %bitcast.84, bf16[2,1,512,512]{3,2,1,0:T(8,128)(2,1)S(1)} %get-tuple-element.22, bf16[2,1,512,512]{3,2,1,0:T(8,128)(2,1)S(1)} %get-tuple-element.21, bf16[2,2,512,512]{3,2,1,0:T(8,128)(2,1)S(1)} %collective-permute-done.3), kind=kOutput, calls=%fused_computation.59 | convolution fusion | flops 2162163712 | bytes 8388608 | tf_op jit(solution)/shard_map/fpsi,fpsj->fij/dot_general | solution.py:113
  199.2 0.4 maximum_multiply_fusion.2
  199.7 2.6 %fusion.63 = bf16[1,2,512,1024]{3,2,1,0:T(8,128)(2,1)S(1)} fusion(bf16[2,2,512,512]{3,2,1,0:T(8,128)(2,1)S(1)} %bitcast.85, bf16[2,1,512,512]{3,2,1,0:T(8,128)(2,1)S(1)} %get-tuple-element.18, bf16[2,1,512,512]{3,2,1,0:T(8,128)(2,1)S(1)} %get-tuple-element.17, bf16[2,2,512,512]{3,2,1,0:T(8,128)(2,1)S(1)} %collective-permute-done.4), kind=kOutput, calls=%fused_computation.57 | convolution fusion | flops 2162163712 | bytes 8388608 | tf_op jit(solution)/shard_map/fpsi,fpsj->fij/dot_general | solution.py:113
  202.4 0.4 maximum_multiply_fusion.1
  202.8 5.5 %pad_maximum_fusion = bf16[3,4,512,1024]{3,2,1,0:T(8,128)(2,1)} fusion(bf16[1,4,512,1024]{3,2,1,0:T(8,128)(2,1)S(1)} %maximum_multiply_fusion.2, bf16[1,4,512,1024]{3,2,1,0:T(8,128)(2,1)S(1)} %maximum_multiply_fusion.1, bf16[1,4,512,1024]{3,2,1,0:T(8,128)(2,1)S(1)} %maximum_multiply_fusion), kind=kLoop, calls=%fused_computation | loop fusion | flops 12582912 | bytes 25165824 | tf_op jit(solution)/shard_map/stack | solution.py:159
  (24 shorter events, 1.6 us)
Async XLA Ops:
  26.3 42.5 %copy-start.2 = (bf16[64,2,16,512]{3,2,1,0:T(8,128)(2,1)S(1)}, bf16[64,2,16,512]{3,2,1,0:T(8,128)(2,1)}, u32[]{:S(2)}) copy-start(bf16[64,2,16,512]{3,2,1,0:T(8,128)(2,1)} %get-tuple-element.9) | copy-start | bytes 6291460
  61.4 6.1 %collective-permute-start = (bf16[2,2,512,512]{3,2,1,0:T(8,128)(2,1)S(1)}, bf16[2,2,512,512]{3,2,1,0:T(8,128)(2,1)S(1)}, u32[]{:S(2)}, u32[]{:S(2)}) collective-permute-start(bf16[2,2,512,512]{3,2,1,0:T(8,128)(2,1)S(1)} %bitcast.86), channel_id=1, source_target_pairs={{8,0},{24,16},{40,32},{56,48},{72,64},{88,80},{104,96},{120,112},{... | collective-permute-start | bytes 6291464 | tf_op jit(solution)/shard_map/ppermute | solution.py:129
  67.4 1.3 copy-start
  72.2 32.1 %all-to-all-start.1 = ((bf16[16,2,64,512]{3,1,2,0:T(2,128)(2,1)}), bf16[16,2,64,512]{3,1,2,0:T(2,128)(2,1)}, u32[]{:S(2)}, u32[]{:S(2)}) async-start(bf16[16,2,64,512]{3,1,2,0:T(2,128)(2,1)} %copy.24), calls=%async_computation.1 | async-start | bytes 4194304 | tf_op jit(solution)/shard_map/all_to_all | solution.py:148
  76.6 71.7 %collective-permute-start.1 = (bf16[2,2,512,512]{3,2,1,0:T(8,128)(2,1)S(1)}, bf16[2,2,512,512]{3,2,1,0:T(8,128)(2,1)}, u32[]{:S(2)}, u32[]{:S(2)}) collective-permute-start(bf16[2,2,512,512]{3,2,1,0:T(8,128)(2,1)S(1)} %bitcast.87), channel_id=1, source_target_pairs={{16,0},{24,8},{32,16},{40,24},{48,32},{56,40},{64,48},{72,56},{80,... | collective-permute-start | bytes 6291464 | tf_op jit(solution)/shard_map/ppermute | solution.py:22
  104.3 5.3 %copy-start.3 = (bf16[2,1,512,512]{3,2,1,0:T(8,128)(2,1)S(1)}, bf16[2,1,512,512]{3,2,1,0:T(8,128)(2,1)}, u32[]{:S(2)}) copy-start(bf16[2,1,512,512]{3,2,1,0:T(8,128)(2,1)} %get-tuple-element.12) | copy-start | bytes 3145732
  106.5 86.1 %collective-permute-start.3 = (bf16[2,2,512,512]{3,2,1,0:T(8,128)(2,1)S(1)}, bf16[2,2,512,512]{3,2,1,0:T(8,128)(2,1)S(1)}, u32[]{:S(2)}, u32[]{:S(2)}) collective-permute-start(bf16[2,2,512,512]{3,2,1,0:T(8,128)(2,1)S(1)} %bitcast.81), channel_id=1, source_target_pairs={{16,0},{24,8},{32,16},{40,24},{48,32},{56,40},{64,48},{72,56},{80,... | collective-permute-start | bytes 6291464 | tf_op jit(solution)/shard_map/ppermute | solution.py:22
  148.3 45.1 %collective-permute-start.2 = (bf16[2,2,512,512]{3,2,1,0:T(8,128)(2,1)}, bf16[2,2,512,512]{3,2,1,0:T(8,128)(2,1)S(1)}, u32[]{:S(2)}, u32[]{:S(2)}) collective-permute-start(bf16[2,2,512,512]{3,2,1,0:T(8,128)(2,1)} %collective-permute-done.1), channel_id=1, source_target_pairs={{0,8},{16,24},{32,40},{48,56},{64,72},{80,88},{96,104},{112,120},{... | collective-permute-start | bytes 6291464 | tf_op jit(solution)/shard_map/ppermute | solution.py:130
  158.5 34.8 %copy-start.1 = (bf16[2,2,512,512]{3,2,1,0:T(8,128)(2,1)S(1)}, bf16[2,2,512,512]{3,2,1,0:T(8,128)(2,1)}, u32[]{:S(2)}) copy-start(bf16[2,2,512,512]{3,2,1,0:T(8,128)(2,1)} %copy-done) | copy-start | bytes 6291460
  193.0 6.6 %collective-permute-start.4 = (bf16[2,2,512,512]{3,2,1,0:T(8,128)(2,1)S(1)}, bf16[2,2,512,512]{3,2,1,0:T(8,128)(2,1)S(1)}, u32[]{:S(2)}, u32[]{:S(2)}) collective-permute-start(bf16[2,2,512,512]{3,2,1,0:T(8,128)(2,1)S(1)} %broadcast_select_fusion), channel_id=1, source_target_pairs={{8,0},{24,16},{40,32},{56,48},{72,64},{88,80},{104,96},{120,112},{... | collective-permute-start | bytes 6291464 | tf_op jit(solution)/shard_map/ppermute | solution.py:127

commit v21 on v19

--- a/solution.py
+++ b/solution.py
@@ -94,14 +94,12 @@
 
 def local_products(left_panel, partner_panels):
     seg_count = left_panel.shape[2]
+    turned = jnp.stack([left_panel[:, 1], -left_panel[:, 0]], axis=1)
     results = []
     for right_panel in partner_panels:
-        turned = jnp.stack([-right_panel[:, 1], right_panel[:, 0]], axis=1)
-        both = jnp.concatenate([right_panel, turned], axis=3)
-        product = jnp.einsum(
-            "fpsi,fpsj->fij", left_panel, both, preferred_element_type=jnp.float32
-        )
-        results.append(product * (1.0 / seg_count))
+        real_part = jnp.einsum("fpsi,fpsj->fij", left_panel, right_panel, preferred_element_type=jnp.float32)
+        imag_part = jnp.einsum("fpsi,fpsj->fij", turned, right_panel, preferred_element_type=jnp.float32)
+        results.append(jnp.concatenate([real_part, imag_part], axis=2) * (1.0 / seg_count))
     return results
 
 

time: 207 us -> 237 us (1.14)
  local copies, waits for them, and re-layouts: 12.6 us -> 38.6 us
  waiting for transfers between devices: 94.2 us -> 85.1 us
  starting transfers between devices: 13.6 us -> 18.9 us
  matrix products: 17 us -> 21.6 us
    another operation x0 -> x1, local copies, waits for them, and re-layouts: none -> 16.9 us  [shards(): return jnp.stack(results, axis=0)]
    all_to_all x1, waiting for transfers between devices: 22.9 us -> 14.6 us  [shards(): lax.all_to_all(parts[k], 'freq', split_axis=0, concat_axis=2, tiled=True)]
    all_to_all x2 -> x4, local copies, waits for them, and re-layouts: 2.58 us -> 9.96 us  [shards(): lax.all_to_all(parts[k], 'freq', split_axis=0, concat_axis=2, tiled=True)]
    concatenate x0 -> x6, other arithmetic: none -> 5.06 us  [shards(): product = jnp.concatenate([p[offset_index] for p in chunk_products], axis=0)]
    ppermute x1, starting transfers between devices: 1.41 us -> 6.44 us  [neighbour_panels(): lax.ppermute(second_panel, 'chan', [(c - 1, c) for c in range(1, n_chan,...]
    dot_general x6 -> x12, matrix products: 17 us -> 21.6 us  [the longest x6 10.8 us: local_products(): jnp.einsum('fpsi,fpsj->fij', left_panel, right_panel, preferred_element_t...]
    neg x6 -> x0, other arithmetic: 3.37 us -> none  [local_products(): turned = jnp.stack([-right_panel[:, 1], right_panel[:, 0]], axis=1)]
    unnamed x8 -> x12, local copies, waits for them, and re-layouts: 6.97 us -> 7.16 us
  transfers between devices with their start and end apart: 6 -> 6, of which waited for: 4 -> 3; matrix products, arithmetic and copies ran while one was open for 12% -> 15% of each run, Pallas kernels for 0% -> 0%
where the time goes in v21:
time: 237 us; the launch traced here: 234 us
  waiting for transfers between devices  85.1 us (36%)
  local copies, waits for them, and re-layouts  38.6 us (16%)
  blocking collectives  34.5 us (15%)
  matrix products  21.6 us (9%)
  Pallas kernels  19.8 us (8%)
  starting transfers between devices  18.9 us (8%)
  other arithmetic  14.4 us (6%)
    ppermute x2, waiting for transfers between devices, from_behind(): return lax.ppermute(block, axis, route)  70.5 us
    all_to_all x1, blocking collectives, shards(): lax.all_to_all(parts[k], 'freq', split_axis=0, concat_axis=2, tiled=True)  34.5 us
    pallas_call x1, Pallas kernels, whitened_spectra(): pl.pallas_call(functools.partial(spectra_kernel, seg_count, window), out_...  19.8 us
    another operation x1, local copies, waits for them, and re-layouts, shards(): return jnp.stack(results, axis=0)  16.9 us
    all_to_all x1, waiting for transfers between devices, shards(): lax.all_to_all(parts[k], 'freq', split_axis=0, concat_axis=2, tiled=True)  14.6 us
    dot_general x6, matrix products, local_products(): jnp.einsum('fpsi,fpsj->fij', left_panel, right_panel, preferred_element_t...  10.8 us
    dot_general x6, matrix products, local_products(): jnp.einsum('fpsi,fpsj->fij', turned, right_panel, preferred_element_type=...  10.8 us
    all_to_all x4, local copies, waits for them, and re-layouts, shards(): lax.all_to_all(parts[k], 'freq', split_axis=0, concat_axis=2, tiled=True)  9.96 us
  transfers between devices with their start and end apart: 6, of which 3 were waited for; matrix products, arithmetic and copies ran while one was open for 15% of the time, Pallas kernels for 0%

profile of v21, /device:TPU:34, one launch (start us, length us, event | category | flops | bytes accessed | tf_op | source)
XLA Modules:
  0.0 233.8 jit_solution(3388076392581287795)
XLA Ops:
  0.1 1.2 convert_element_type.70
  2.7 19.8 %shard_map.46 = bf16[64,64,512]{2,1,0:T(8,128)(2,1)} custom-call(s32[64]{0:T(128)} %offs_ref.1, f32[64,384]{1,0:T(8,128)} %pad_convert_fusion.dft_ref, f32[1,512]{1,0:T(1,128)} %bitcast.109, bf16[8448,512]{1,0:T(8,128)(2,1)} %rec_hbm.1), custom_call_target="tpu_custom_call" | custom-call | flops 1140850688 | bytes 22020096 | tf_op jit(solution)/shard_map/pallas_call | solution.py:69
  22.5 4.2 %fusion.28 = (bf16[64,2,1,16,512]{4,3,2,1,0:T(8,128)(2,1)}, bf16[64,2,1,16,512]{4,3,2,1,0:T(8,128)(2,1)S(1)}) fusion(bf16[64,2,2,16,512]{4,3,2,1,0:T(8,128)(2,1)} %bitcast.105), kind=kLoop, calls=%fused_computation.68 | loop fusion | bytes 8388608 | tf_op jit(solution)/shard_map/slice | solution.py:132
  26.8 1.2 copy.63
  27.9 34.5 %all_to_all.36 = bf16[16,2,64,512]{3,2,1,0:T(8,128)(2,1)S(1)} all-to-all(bf16[16,2,64,512]{3,2,1,0:T(8,128)(2,1)S(1)} %bitcast.107), channel_id=1, replica_groups=mesh['chan'=16,'freq'=8] {'freq'}, dimensions={0} | all-to-all | bytes 4194304 | tf_op jit(solution)/shard_map/all_to_all | solution.py:135
  62.7 2.4 %copy.33 = bf16[2,2,512,512]{2,3,1,0:T(8,128)(2,1)} copy(bf16[2,2,512,512]{3,2,1,0:T(8,128)(2,1)S(1)} %bitcast.93) | data formatting | bytes 4194304 | tf_op jit(solution)/shard_map/all_to_all | solution.py:135
  65.1 1.3 collective-permute-start
  66.4 3.1 %collective-permute-start.1 = (bf16[2,2,512,512]{2,3,1,0:T(8,128)(2,1)}, bf16[2,2,512,512]{2,3,1,0:T(8,128)(2,1)}, u32[]{:S(2)}, u32[]{:S(2)}) collective-permute-start(bf16[2,2,512,512]{2,3,1,0:T(8,128)(2,1)} %copy.33), channel_id=1, source_target_pairs={{16,0},{24,8},{32,16},{40,24},{48,32},{56,40},{64,48},{72,56},{80,... | collective-permute-start | bytes 6291464 | tf_op jit(solution)/shard_map/ppermute | solution.py:22
  69.5 4.1 %copy.62 = bf16[64,2,1,16,512]{4,0,1,3,2:T(8,128)(2,1)} copy(bf16[64,2,1,16,512]{4,3,2,1,0:T(8,128)(2,1)} %get-tuple-element.7) | data formatting | bytes 4194304
  73.6 4.5 %all-to-all-start.1 = ((bf16[16,2,64,512]{3,2,1,0:T(8,128)(2,1)}), bf16[16,2,64,512]{3,2,1,0:T(8,128)(2,1)}, u32[]{:S(2)}, u32[]{:S(2)}) async-start(bf16[16,2,64,512]{3,2,1,0:T(8,128)(2,1)} %bitcast.106), calls=%async_computation.1 | async-start | bytes 4194304 | tf_op jit(solution)/shard_map/all_to_all | solution.py:135
  78.9 1.3 convolution_bitcast_fusion.10
  80.3 1.3 convolution_bitcast_fusion.11
  81.6 2.0 fusion.11
  83.5 32.9 %collective-permute-done.1 = bf16[2,2,512,512]{2,3,1,0:T(8,128)(2,1)} collective-permute-done((bf16[2,2,512,512]{2,3,1,0:T(8,128)(2,1)}, bf16[2,2,512,512]{2,3,1,0:T(8,128)(2,1)}, u32[]{:S(2)}, u32[]{:S(2)}) %collective-permute-start.1) | collective-permute-done | bytes 2097184 | tf_op jit(solution)/shard_map/ppermute | solution.py:22
  116.4 6.4 %collective-permute-start.2 = (bf16[2,2,512,512]{2,3,1,0:T(8,128)(2,1)}, bf16[2,2,512,512]{2,3,1,0:T(8,128)(2,1)}, u32[]{:S(2)}, u32[]{:S(2)}) collective-permute-start(bf16[2,2,512,512]{2,3,1,0:T(8,128)(2,1)} %collective-permute-done.1), channel_id=1, source_target_pairs={{0,8},{16,24},{32,40},{48,56},{64,72},{80,88},{96,104},{112,120},{... | collective-permute-start | bytes 6291464 | tf_op jit(solution)/shard_map/ppermute | solution.py:116
  122.9 14.6 %all-to-all-done.1 = bf16[16,2,64,512]{3,2,1,0:T(8,128)(2,1)} async-done(((bf16[16,2,64,512]{3,2,1,0:T(8,128)(2,1)}), bf16[16,2,64,512]{3,2,1,0:T(8,128)(2,1)}, u32[]{:S(2)}, u32[]{:S(2)}) %all-to-all-start.1) | async-done | bytes 2097184 | tf_op jit(solution)/shard_map/all_to_all | solution.py:135
  137.5 3.1 %copy.35 = bf16[2,2,8,64,512]{4,3,2,1,0:T(8,128)(2,1)} copy(bf16[2,2,8,64,512]{4,3,1,0,2:T(8,128)(2,1)} %bitcast.15) | data formatting | bytes 4194304 | tf_op jit(solution)/shard_map/all_to_all | solution.py:135
  140.6 4.2 %copy.40 = bf16[2,2,512,512]{2,3,1,0:T(8,128)(2,1)} copy(bf16[2,2,512,512]{3,2,1,0:T(8,128)(2,1)} %bitcast.99) | data formatting | bytes 4194304 | tf_op jit(solution)/shard_map/all_to_all | solution.py:135
  144.8 3.1 %collective-permute-start.3 = (bf16[2,2,512,512]{2,3,1,0:T(8,128)(2,1)}, bf16[2,2,512,512]{2,3,1,0:T(8,128)(2,1)S(1)}, u32[]{:S(2)}, u32[]{:S(2)}) collective-permute-start(bf16[2,2,512,512]{2,3,1,0:T(8,128)(2,1)} %copy.40), channel_id=1, source_target_pairs={{16,0},{24,8},{32,16},{40,24},{48,32},{56,40},{64,48},{72,56},{80,... | collective-permute-start | bytes 6291464 | tf_op jit(solution)/shard_map/ppermute | solution.py:22
  147.9 2.8 %convolution_bitcast_fusion.3 = f32[2,512,512]{1,2,0:T(8,128)S(1)} fusion(bf16[2,2,512,512]{2,3,1,0:T(8,128)(2,1)} %collective-permute-done.1, bf16[2,2,512,512]{3,2,1,0:T(8,128)(2,1)S(1)} %bitcast.97), kind=kOutput, calls=%fused_computation.31 | convolution fusion | flops 1073741824 | bytes 6291456 | tf_op jit(solution)/shard_map/fpsi,fpsj->fij/dot_general | solution.py:100
  150.8 2.8 %convolution_bitcast_fusion.2 = f32[2,512,512]{1,2,0:T(8,128)S(1)} fusion(bf16[2,2,512,512]{2,3,1,0:T(8,128)(2,1)} %collective-permute-done.1, bf16[2,1,512,512]{3,2,1,0:T(8,128)(2,1)S(1)} %copy-done.4, bf16[2,1,512,512]{3,2,1,0:T(8,128)(2,1)S(1)} %get-tuple-element.9), kind=kOutput, calls=%fused_computation.30 | convolution fusion | flops 1077936128 | bytes 6291456 | tf_op jit(solution)/shard_map/fpsi,fpsj->fij/dot_general | solution.py:101
  155.3 1.3 convolution_bitcast_fusion.8
  156.6 1.3 convolution_bitcast_fusion.9
  158.6 37.6 %collective-permute-done.3 = bf16[2,2,512,512]{2,3,1,0:T(8,128)(2,1)S(1)} collective-permute-done((bf16[2,2,512,512]{2,3,1,0:T(8,128)(2,1)}, bf16[2,2,512,512]{2,3,1,0:T(8,128)(2,1)S(1)}, u32[]{:S(2)}, u32[]{:S(2)}) %collective-permute-start.3) | collective-permute-done | bytes 2097184 | tf_op jit(solution)/shard_map/ppermute | solution.py:22
  196.8 2.8 %convolution_bitcast_fusion.6 = f32[2,512,512]{1,2,0:T(8,128)S(1)} fusion(bf16[2,2,512,512]{2,3,1,0:T(8,128)(2,1)} %collective-permute-done.2, bf16[2,2,512,512]{2,3,1,0:T(8,128)(2,1)} %collective-permute-done, pred[]{:T(512)S(6)} %eq.22, bf16[2,1,512,512]{3,2,1,0:T(8,128)(2,1)S(1)} %copy-done.4, bf16[2,1,512,512]{3,2,1,0:T(8,128)(2,1)S(1)} %get-tuple-element.9), kind=kOutput, calls=%fused_computation.34 | convolution fusion | flops 1078984704 | bytes 8388609 | tf_op jit(solution)/shard_map/fpsi,fpsj->fij/dot_general | solution.py:101
  199.6 2.9 %convolution_bitcast_fusion.7 = f32[2,512,512]{1,2,0:T(8,128)S(1)} fusion(bf16[2,2,512,512]{3,2,1,0:T(8,128)(2,1)S(1)} %bitcast.98, bf16[2,2,512,512]{2,3,1,0:T(8,128)(2,1)} %collective-permute-done.2, bf16[2,2,512,512]{2,3,1,0:T(8,128)(2,1)} %collective-permute-done, pred[]{:T(512)S(6)} %eq.22), kind=kOutput, calls=%fused_computation.35 | convolution fusion | flops 1074790400 | bytes 8388609 | tf_op jit(solution)/shard_map/fpsi,fpsj->fij/dot_general | solution.py:100
  203.1 1.3 convolution_bitcast_fusion
  204.4 1.3 convolution_bitcast_fusion.1
  206.7 1.3 convolution_bitcast_fusion.5
  208.0 1.3 convolution_bitcast_fusion.4
  211.6 5.3 %pad_maximum_fusion = bf16[3,4,512,1024]{2,3,1,0:T(8,128)(2,1)} fusion(bf16[1,4,512,1024]{2,3,1,0:T(8,128)(2,1)S(1)} %maximum_multiply_fusion.8, bf16[1,4,512,1024]{2,3,1,0:T(8,128)(2,1)S(1)} %get-tuple-element.14, bf16[1,4,512,1024]{2,3,1,0:T(8,128)(2,1)S(1)} %get-tuple-element.13), kind=kLoop, calls=%fused_computation | loop fusion | flops 12582912 | bytes 25165824 | tf_op jit(solution)/shard_map/stack | solution.py:146
  216.9 16.9 %copy.41 = bf16[3,4,512,1024]{3,2,1,0:T(8,128)(2,1)} copy(bf16[3,4,512,1024]{2,3,1,0:T(8,128)(2,1)} %pad_maximum_fusion) | data formatting | bytes 25165824 | tf_op jit(solution)/shard_map/stack | solution.py:146
  (36 shorter events, 8.7 us)
Async XLA Ops:
  65.1 8.5 %collective-permute-start = (bf16[2,2,512,512]{2,3,1,0:T(8,128)(2,1)}, bf16[2,2,512,512]{2,3,1,0:T(8,128)(2,1)}, u32[]{:S(2)}, u32[]{:S(2)}) collective-permute-start(bf16[2,2,512,512]{2,3,1,0:T(8,128)(2,1)} %copy.33), channel_id=1, source_target_pairs={{8,0},{24,16},{40,32},{56,48},{72,64},{88,80},{104,96},{120,112},{... | collective-permute-start | bytes 6291464 | tf_op jit(solution)/shard_map/ppermute | solution.py:115
  66.4 50.1 %collective-permute-start.1 = (bf16[2,2,512,512]{2,3,1,0:T(8,128)(2,1)}, bf16[2,2,512,512]{2,3,1,0:T(8,128)(2,1)}, u32[]{:S(2)}, u32[]{:S(2)}) collective-permute-start(bf16[2,2,512,512]{2,3,1,0:T(8,128)(2,1)} %copy.33), channel_id=1, source_target_pairs={{16,0},{24,8},{32,16},{40,24},{48,32},{56,40},{64,48},{72,56},{80,... | collective-permute-start | bytes 6291464 | tf_op jit(solution)/shard_map/ppermute | solution.py:22
  73.6 63.9 %all-to-all-start.1 = ((bf16[16,2,64,512]{3,2,1,0:T(8,128)(2,1)}), bf16[16,2,64,512]{3,2,1,0:T(8,128)(2,1)}, u32[]{:S(2)}, u32[]{:S(2)}) async-start(bf16[16,2,64,512]{3,2,1,0:T(8,128)(2,1)} %bitcast.106), calls=%async_computation.1 | async-start | bytes 4194304 | tf_op jit(solution)/shard_map/all_to_all | solution.py:135
  78.9 1.3 copy-start.3
  116.4 80.4 %collective-permute-start.2 = (bf16[2,2,512,512]{2,3,1,0:T(8,128)(2,1)}, bf16[2,2,512,512]{2,3,1,0:T(8,128)(2,1)}, u32[]{:S(2)}, u32[]{:S(2)}) collective-permute-start(bf16[2,2,512,512]{2,3,1,0:T(8,128)(2,1)} %collective-permute-done.1), channel_id=1, source_target_pairs={{0,8},{16,24},{32,40},{48,56},{64,72},{80,88},{96,104},{112,120},{... | collective-permute-start | bytes 6291464 | tf_op jit(solution)/shard_map/ppermute | solution.py:116
  144.8 5.9 %copy-start.4 = (bf16[2,1,512,512]{3,2,1,0:T(8,128)(2,1)S(1)}, bf16[2,1,512,512]{3,2,1,0:T(8,128)(2,1)}, u32[]{:S(2)}) copy-start(bf16[2,1,512,512]{3,2,1,0:T(8,128)(2,1)} %copy-done.3) | copy-start | bytes 3145732
  144.8 51.3 %collective-permute-start.3 = (bf16[2,2,512,512]{2,3,1,0:T(8,128)(2,1)}, bf16[2,2,512,512]{2,3,1,0:T(8,128)(2,1)S(1)}, u32[]{:S(2)}, u32[]{:S(2)}) collective-permute-start(bf16[2,2,512,512]{2,3,1,0:T(8,128)(2,1)} %copy.40), channel_id=1, source_target_pairs={{16,0},{24,8},{32,16},{40,24},{48,32},{56,40},{64,48},{72,56},{80,... | collective-permute-start | bytes 6291464 | tf_op jit(solution)/shard_map/ppermute | solution.py:22
  153.6 1.6 copy-start
  157.9 38.2 %copy-start.2 = (bf16[2,2,512,512]{2,3,1,0:T(8,128)(2,1)S(1)}, bf16[2,2,512,512]{2,3,1,0:T(8,128)(2,1)}, u32[]{:S(2)}) copy-start(bf16[2,2,512,512]{2,3,1,0:T(8,128)(2,1)} %copy.40) | copy-start | bytes 6291460
  196.4 10.3 %collective-permute-start.4 = (bf16[2,2,512,512]{2,3,1,0:T(8,128)(2,1)S(1)}, bf16[2,2,512,512]{2,3,1,0:T(8,128)(2,1)S(1)}, u32[]{:S(2)}, u32[]{:S(2)}) collective-permute-start(bf16[2,2,512,512]{2,3,1,0:T(8,128)(2,1)S(1)} %broadcast_select_fusion), channel_id=1, source_target_pairs={{8,0},{24,16},{40,32},{56,48},{72,64},{88,80},{104,96},{120,112},{... | collective-permute-start | bytes 6291464 | tf_op jit(solution)/shard_map/ppermute | solution.py:113
  209.2 1.6 copy-start.1

commit v22 on v19

--- a/solution.py
+++ b/solution.py
@@ -135,9 +135,9 @@
     chunk_products = []
     for k in range(chunks):
         own_panel = lax.all_to_all(parts[k], "freq", split_axis=0, concat_axis=2, tiled=True)
-        upper_panel, second_panel, from_sibling = neighbour_panels(own_panel, merged=k + 1 == chunks)
+        upper_panel, second_panel, _ = neighbour_panels(own_panel, merged=True)
         if k + 1 < chunks:
-            _, parts[k + 1] = lax.optimization_barrier((from_sibling, parts[k + 1]))
+            _, parts[k + 1] = lax.optimization_barrier((own_panel, parts[k + 1]))
         chunk_products.append(local_products(own_panel, [own_panel, upper_panel, second_panel]))
     band_limit = band_blocks[0]
     results = []

time: 207 us -> 208 us (level)
  blocking collectives: 34.5 us -> 0 us
  waiting for transfers between devices: 94.2 us -> 117 us
  local copies, waits for them, and re-layouts: 12.6 us -> 18.8 us
  starting transfers between devices: 13.6 us -> 17.8 us
    all_to_all x1 -> x0, blocking collectives: 34.5 us -> none  [shards(): lax.all_to_all(parts[k], 'freq', split_axis=0, concat_axis=2, tiled=True)]
    all_to_all x1 -> x2, waiting for transfers between devices: 22.9 us -> 44.2 us  [shards(): lax.all_to_all(parts[k], 'freq', split_axis=0, concat_axis=2, tiled=True)]
    all_to_all x1 -> x2, starting transfers between devices: 4.35 us -> 10.8 us  [shards(): lax.all_to_all(parts[k], 'freq', split_axis=0, concat_axis=2, tiled=True)]
    ppermute x2, waiting for transfers between devices: 70.2 us -> 73.2 us  [from_behind(): return lax.ppermute(block, axis, route)]
    unnamed x8 -> x6, local copies, waits for them, and re-layouts: 6.97 us -> 9.89 us
    ppermute x2 -> x0, starting transfers between devices: 2.88 us -> none  [the longest x1 1.47 us: neighbour_panels(): lax.ppermute(own_panel, 'chan', [(c + 1, c) for c in range(0, n_chan, 2)])]
  transfers between devices with their start and end apart: 6 -> 6, of which waited for: 4 -> 4; matrix products, arithmetic and copies ran while one was open for 12% -> 14% of each run, Pallas kernels for 0% -> 0%
where the time goes in v22:
time: 208 us; the launch traced here: 206 us
  waiting for transfers between devices  117 us (56%)
  Pallas kernels  19.8 us (10%)
  local copies, waits for them, and re-layouts  18.8 us (9%)
  starting transfers between devices  17.8 us (9%)
  matrix products  17 us (8%)
  other arithmetic  14.6 us (7%)
    ppermute x2, waiting for transfers between devices, from_behind(): return lax.ppermute(block, axis, route)  73.2 us
    all_to_all x2, waiting for transfers between devices, shards(): lax.all_to_all(parts[k], 'freq', split_axis=0, concat_axis=2, tiled=True)  44.2 us
    pallas_call x1, Pallas kernels, whitened_spectra(): pl.pallas_call(functools.partial(spectra_kernel, seg_count, window), out_...  19.8 us
    dot_general x6, matrix products, local_products(): jnp.einsum('fpsi,fpsj->fij', left_panel, both, preferred_element_type=jnp...  17 us
    all_to_all x2, starting transfers between devices, shards(): lax.all_to_all(parts[k], 'freq', split_axis=0, concat_axis=2, tiled=True)  10.8 us
    unnamed x6, local copies, waits for them, and re-layouts  9.89 us
    ppermute x2, starting transfers between devices, from_behind(): return lax.ppermute(block, axis, route)  6.62 us
    another operation x1, other arithmetic, shards(): return jnp.stack(results, axis=0)  5.47 us
  transfers between devices with their start and end apart: 6, of which 4 were waited for; matrix products, arithmetic and copies ran while one was open for 14% of the time, Pallas kernels for 0%

profile of v22, /device:TPU:34, one launch (start us, length us, event | category | flops | bytes accessed | tf_op | source)
XLA Modules:
  0.0 206.4 jit_solution(15797146021554376620)
XLA Ops:
  0.1 1.3 convert_element_type.70
  1.7 0.3 multiply_convert_fusion
  2.1 0.7 pad_convert_fusion.dft_ref
  2.7 19.8 %shard_map.46 = bf16[64,64,512]{2,1,0:T(8,128)(2,1)} custom-call(s32[64]{0:T(128)} %offs_ref.1, f32[64,384]{1,0:T(8,128)} %pad_convert_fusion.dft_ref, f32[1,512]{1,0:T(1,128)} %bitcast.105, bf16[8448,512]{1,0:T(8,128)(2,1)} %rec_hbm.1), custom_call_target="tpu_custom_call" | custom-call | flops 1140850688 | bytes 22020096 | tf_op jit(solution)/shard_map/pallas_call | solution.py:69
  22.6 4.4 %fusion.88 = (bf16[64,2,1,16,512]{4,3,2,1,0:T(8,128)(2,1)}, bf16[64,2,1,16,512]{4,3,2,1,0:T(8,128)(2,1)S(1)}) fusion(bf16[64,2,2,16,512]{4,3,2,1,0:T(8,128)(2,1)} %bitcast.101), kind=kLoop, calls=%fused_computation.94 | loop fusion | bytes 8388608 | tf_op jit(solution)/shard_map/slice | solution.py:134
  27.0 3.5 %copy.48 = bf16[64,2,1,16,512]{4,1,0,3,2:T(2,128)(2,1)} copy(bf16[64,2,1,16,512]{4,3,2,1,0:T(8,128)(2,1)S(1)} %get-tuple-element.8) | data formatting | bytes 4194304
  30.5 6.0 %all-to-all-start = ((bf16[16,2,64,512]{3,1,2,0:T(2,128)(2,1)}), bf16[16,2,64,512]{3,1,2,0:T(2,128)(2,1)S(1)}, u32[]{:S(2)}, u32[]{:S(2)}) async-start(bf16[16,2,64,512]{3,1,2,0:T(2,128)(2,1)} %bitcast.104), calls=%async_computation | async-start | bytes 4194304 | tf_op jit(solution)/shard_map/all_to_all | solution.py:137
  36.5 5.1 %copy.47 = bf16[64,2,1,16,512]{4,1,0,3,2:T(2,128)(2,1)} copy(bf16[64,2,1,16,512]{4,3,2,1,0:T(8,128)(2,1)} %get-tuple-element.7) | data formatting | bytes 4194304
  41.6 21.4 %all-to-all-done = bf16[16,2,64,512]{3,1,2,0:T(2,128)(2,1)S(1)} async-done(((bf16[16,2,64,512]{3,1,2,0:T(2,128)(2,1)}), bf16[16,2,64,512]{3,1,2,0:T(2,128)(2,1)S(1)}, u32[]{:S(2)}, u32[]{:S(2)}) %all-to-all-start) | async-done | bytes 2097184 | tf_op jit(solution)/shard_map/all_to_all | solution.py:137
  62.9 1.3 copy-done
  64.3 2.0 copy.22
  66.3 4.8 %all-to-all-start.1 = ((bf16[16,2,64,512]{3,1,2,0:T(2,128)(2,1)}), bf16[16,2,64,512]{3,1,2,0:T(2,128)(2,1)}, u32[]{:S(2)}, u32[]{:S(2)}) async-start(bf16[16,2,64,512]{3,1,2,0:T(2,128)(2,1)} %bitcast.102), calls=%async_computation.1 | async-start | bytes 4194304 | tf_op jit(solution)/shard_map/all_to_all | solution.py:137
  71.1 3.3 %collective-permute-start = (bf16[2,2,512,512]{3,2,1,0:T(8,128)(2,1)S(1)}, bf16[2,2,512,512]{3,2,1,0:T(8,128)(2,1)}, u32[]{:S(2)}, u32[]{:S(2)}) collective-permute-start(bf16[2,2,512,512]{3,2,1,0:T(8,128)(2,1)S(1)} %bitcast.91), channel_id=1, source_target_pairs={{16,0},{24,8},{32,16},{40,24},{48,32},{56,40},{64,48},{72,56},{80,... | collective-permute-start | bytes 6291464 | tf_op jit(solution)/shard_map/ppermute | solution.py:22
  75.1 1.1 slice_negate_fusion.5
  76.2 22.8 %all-to-all-done.1 = bf16[16,2,64,512]{3,1,2,0:T(2,128)(2,1)} async-done(((bf16[16,2,64,512]{3,1,2,0:T(2,128)(2,1)}), bf16[16,2,64,512]{3,1,2,0:T(2,128)(2,1)}, u32[]{:S(2)}, u32[]{:S(2)}) %all-to-all-start.1) | async-done | bytes 2097184 | tf_op jit(solution)/shard_map/all_to_all | solution.py:137
  99.0 2.1 %copy.25 = bf16[8,2,2,64,512]{4,3,0,2,1:T(8,128)(2,1)S(1)} copy(bf16[8,2,2,64,512]{4,2,3,1,0:T(2,128)(2,1)} %bitcast.13) | data formatting | bytes 4194304 | tf_op jit(solution)/shard_map/all_to_all | solution.py:137
  101.1 3.3 %collective-permute-start.2 = (bf16[2,2,512,512]{3,2,1,0:T(8,128)(2,1)S(1)}, bf16[2,2,512,512]{3,2,1,0:T(8,128)(2,1)S(1)}, u32[]{:S(2)}, u32[]{:S(2)}) collective-permute-start(bf16[2,2,512,512]{3,2,1,0:T(8,128)(2,1)S(1)} %bitcast.96), channel_id=1, source_target_pairs={{16,0},{24,8},{32,16},{40,24},{48,32},{56,40},{64,48},{72,56},{80,... | collective-permute-start | bytes 6291464 | tf_op jit(solution)/shard_map/ppermute | solution.py:22
  104.5 2.6 %fusion.54 = bf16[1,2,512,1024]{3,2,1,0:T(8,128)(2,1)S(1)} fusion(bf16[2,2,512,512]{3,2,1,0:T(8,128)(2,1)S(1)} %bitcast.93, bf16[2,1,512,512]{3,2,1,0:T(8,128)(2,1)S(1)} %copy-done.1, bf16[2,1,512,512]{3,2,1,0:T(8,128)(2,1)S(1)} %get-tuple-element.9), kind=kOutput, calls=%fused_computation.56 | convolution fusion | flops 2162163712 | bytes 6291456 | tf_op jit(solution)/shard_map/fpsi,fpsj->fij/dot_general | solution.py:101
  107.2 2.6 %fusion.57 = bf16[1,2,512,1024]{3,2,1,0:T(8,128)(2,1)S(1)} fusion(bf16[2,2,512,512]{3,2,1,0:T(8,128)(2,1)S(1)} %bitcast.98, bf16[2,1,512,512]{3,2,1,0:T(8,128)(2,1)S(1)} %get-tuple-element.12, bf16[2,1,512,512]{3,2,1,0:T(8,128)(2,1)S(1)} %get-tuple-element.11), kind=kOutput, calls=%fused_computation.57 | convolution fusion | flops 2162163712 | bytes 6291456 | tf_op jit(solution)/shard_map/fpsi,fpsj->fij/dot_general | solution.py:101
  109.9 0.4 maximum_multiply_fusion
  110.3 32.9 %collective-permute-done = bf16[2,2,512,512]{3,2,1,0:T(8,128)(2,1)} collective-permute-done((bf16[2,2,512,512]{3,2,1,0:T(8,128)(2,1)S(1)}, bf16[2,2,512,512]{3,2,1,0:T(8,128)(2,1)}, u32[]{:S(2)}, u32[]{:S(2)}) %collective-permute-start) | collective-permute-done | bytes 2097184 | tf_op jit(solution)/shard_map/ppermute | solution.py:22
  143.2 1.8 broadcast_select_fusion.1
  145.1 1.7 slice_negate_fusion.1
  146.8 40.3 %collective-permute-done.2 = bf16[2,2,512,512]{3,2,1,0:T(8,128)(2,1)S(1)} collective-permute-done((bf16[2,2,512,512]{3,2,1,0:T(8,128)(2,1)S(1)}, bf16[2,2,512,512]{3,2,1,0:T(8,128)(2,1)S(1)}, u32[]{:S(2)}, u32[]{:S(2)}) %collective-permute-start.2) | collective-permute-done | bytes 2097184 | tf_op jit(solution)/shard_map/ppermute | solution.py:22
  187.1 0.4 broadcast_select_fusion
  187.8 4.0 %fusion.66 = bf16[1,2,512,1024]{3,2,1,0:T(8,128)(2,1)S(1)} fusion(bf16[2,2,512,512]{3,2,1,0:T(8,128)(2,1)S(1)} %bitcast.94, bf16[2,1,512,512]{3,2,1,0:T(8,128)(2,1)S(1)} %get-tuple-element.18, bf16[2,1,512,512]{3,2,1,0:T(8,128)(2,1)S(1)} %get-tuple-element.17, bf16[2,2,512,512]{3,2,1,0:T(8,128)(2,1)} %collective-permute-done), kind=kOutput, calls=%fused_computation.60 | convolution fusion | flops 2162163712 | bytes 8388608 | tf_op jit(solution)/shard_map/fpsi,fpsj->fij/dot_general | solution.py:101
  191.9 2.6 %fusion.69 = bf16[1,2,512,1024]{3,2,1,0:T(8,128)(2,1)S(1)} fusion(bf16[2,2,512,512]{3,2,1,0:T(8,128)(2,1)S(1)} %bitcast.99, bf16[2,1,512,512]{3,2,1,0:T(8,128)(2,1)S(1)} %get-tuple-element.20, bf16[2,1,512,512]{3,2,1,0:T(8,128)(2,1)S(1)} %get-tuple-element.19, bf16[2,2,512,512]{3,2,1,0:T(8,128)(2,1)S(1)} %collective-permute-done.2), kind=kOutput, calls=%fused_computation.61 | convolution fusion | flops 2162163712 | bytes 8388608 | tf_op jit(solution)/shard_map/fpsi,fpsj->fij/dot_general | solution.py:101
  194.5 0.4 maximum_multiply_fusion.2
  195.1 2.6 %fusion.60 = bf16[1,2,512,1024]{3,2,1,0:T(8,128)(2,1)S(1)} fusion(bf16[2,2,512,512]{3,2,1,0:T(8,128)(2,1)S(1)} %bitcast.95, bf16[2,1,512,512]{3,2,1,0:T(8,128)(2,1)S(1)} %get-tuple-element.14, bf16[2,1,512,512]{3,2,1,0:T(8,128)(2,1)S(1)} %get-tuple-element.13, bf16[2,2,512,512]{3,2,1,0:T(8,128)(2,1)S(1)} %collective-permute-done.1), kind=kOutput, calls=%fused_computation.58 | convolution fusion | flops 2162163712 | bytes 8388608 | tf_op jit(solution)/shard_map/fpsi,fpsj->fij/dot_general | solution.py:101
  197.9 2.6 %fusion.63 = bf16[1,2,512,1024]{3,2,1,0:T(8,128)(2,1)S(1)} fusion(bf16[2,2,512,512]{3,2,1,0:T(8,128)(2,1)S(1)} %bitcast.100, bf16[2,1,512,512]{3,2,1,0:T(8,128)(2,1)S(1)} %get-tuple-element.16, bf16[2,1,512,512]{3,2,1,0:T(8,128)(2,1)S(1)} %get-tuple-element.15, bf16[2,2,512,512]{3,2,1,0:T(8,128)(2,1)S(1)} %collective-permute-done.3), kind=kOutput, calls=%fused_computation.59 | convolution fusion | flops 2162163712 | bytes 8388608 | tf_op jit(solution)/shard_map/fpsi,fpsj->fij/dot_general | solution.py:101
  200.5 0.4 maximum_multiply_fusion.1
  200.9 5.5 %pad_maximum_fusion = bf16[3,4,512,1024]{3,2,1,0:T(8,128)(2,1)} fusion(bf16[1,4,512,1024]{3,2,1,0:T(8,128)(2,1)S(1)} %maximum_multiply_fusion.2, bf16[1,4,512,1024]{3,2,1,0:T(8,128)(2,1)S(1)} %maximum_multiply_fusion.1, bf16[1,4,512,1024]{3,2,1,0:T(8,128)(2,1)S(1)} %maximum_multiply_fusion), kind=kLoop, calls=%fused_computation | loop fusion | flops 12582912 | bytes 25165824 | tf_op jit(solution)/shard_map/stack | solution.py:148
  (20 shorter events, 1.4 us)
Async XLA Ops:
  30.5 32.5 %all-to-all-start = ((bf16[16,2,64,512]{3,1,2,0:T(2,128)(2,1)}), bf16[16,2,64,512]{3,1,2,0:T(2,128)(2,1)S(1)}, u32[]{:S(2)}, u32[]{:S(2)}) async-start(bf16[16,2,64,512]{3,1,2,0:T(2,128)(2,1)} %bitcast.104), calls=%async_computation | async-start | bytes 4194304 | tf_op jit(solution)/shard_map/all_to_all | solution.py:137
  62.9 1.3 copy-start
  66.3 32.7 %all-to-all-start.1 = ((bf16[16,2,64,512]{3,1,2,0:T(2,128)(2,1)}), bf16[16,2,64,512]{3,1,2,0:T(2,128)(2,1)}, u32[]{:S(2)}, u32[]{:S(2)}) async-start(bf16[16,2,64,512]{3,1,2,0:T(2,128)(2,1)} %bitcast.102), calls=%async_computation.1 | async-start | bytes 4194304 | tf_op jit(solution)/shard_map/all_to_all | solution.py:137
  71.1 72.1 %collective-permute-start = (bf16[2,2,512,512]{3,2,1,0:T(8,128)(2,1)S(1)}, bf16[2,2,512,512]{3,2,1,0:T(8,128)(2,1)}, u32[]{:S(2)}, u32[]{:S(2)}) collective-permute-start(bf16[2,2,512,512]{3,2,1,0:T(8,128)(2,1)S(1)} %bitcast.91), channel_id=1, source_target_pairs={{16,0},{24,8},{32,16},{40,24},{48,32},{56,40},{64,48},{72,56},{80,... | collective-permute-start | bytes 6291464 | tf_op jit(solution)/shard_map/ppermute | solution.py:22
  99.0 5.5 %copy-start.1 = (bf16[2,1,512,512]{3,2,1,0:T(8,128)(2,1)S(1)}, bf16[2,1,512,512]{3,2,1,0:T(8,128)(2,1)}, u32[]{:S(2)}) copy-start(bf16[2,1,512,512]{3,2,1,0:T(8,128)(2,1)} %get-tuple-element.10) | copy-start | bytes 3145732
  101.1 85.9 %collective-permute-start.2 = (bf16[2,2,512,512]{3,2,1,0:T(8,128)(2,1)S(1)}, bf16[2,2,512,512]{3,2,1,0:T(8,128)(2,1)S(1)}, u32[]{:S(2)}, u32[]{:S(2)}) collective-permute-start(bf16[2,2,512,512]{3,2,1,0:T(8,128)(2,1)S(1)} %bitcast.96), channel_id=1, source_target_pairs={{16,0},{24,8},{32,16},{40,24},{48,32},{56,40},{64,48},{72,56},{80,... | collective-permute-start | bytes 6291464 | tf_op jit(solution)/shard_map/ppermute | solution.py:22
  145.0 50.0 %collective-permute-start.1 = (bf16[2,2,512,512]{3,2,1,0:T(8,128)(2,1)S(1)}, bf16[2,2,512,512]{3,2,1,0:T(8,128)(2,1)S(1)}, u32[]{:S(2)}, u32[]{:S(2)}) collective-permute-start(bf16[2,2,512,512]{3,2,1,0:T(8,128)(2,1)S(1)} %broadcast_select_fusion.1), channel_id=1, source_target_pairs={{8,0},{24,16},{40,32},{56,48},{72,64},{88,80},{104,96},{120,112},{... | collective-permute-start | bytes 6291464 | tf_op jit(solution)/shard_map/ppermute | solution.py:115
  187.5 10.2 %collective-permute-start.3 = (bf16[2,2,512,512]{3,2,1,0:T(8,128)(2,1)S(1)}, bf16[2,2,512,512]{3,2,1,0:T(8,128)(2,1)S(1)}, u32[]{:S(2)}, u32[]{:S(2)}) collective-permute-start(bf16[2,2,512,512]{3,2,1,0:T(8,128)(2,1)S(1)} %broadcast_select_fusion), channel_id=1, source_target_pairs={{8,0},{24,16},{40,32},{56,48},{72,64},{88,80},{104,96},{120,112},{... | collective-permute-start | bytes 6291464 | tf_op jit(solution)/shard_map/ppermute | solution.py:115

commit v23 on v19

--- a/solution.py
+++ b/solution.py
@@ -83,7 +83,7 @@
                 pltpu.SemaphoreType.DMA((seg_count,)),
             ],
         ),
-        compiler_params=pltpu.CompilerParams(vmem_limit_bytes=56 * 1024 * 1024),
+        compiler_params=pltpu.CompilerParams(vmem_limit_bytes=32 * 1024 * 1024),
         cost_estimate=pl.CostEstimate(
             flops=2 * seg_count * rows * window * channels,
             bytes_accessed=seg_count * (window + rows) * channels * 2,

time: 207 us -> 208 us (level)
    unnamed x8 -> x12, local copies, waits for them, and re-layouts: 6.97 us -> 11.1 us
    slice x1, local copies, waits for them, and re-layouts: 2.76 us -> 0.64 us  [shards(): parts = [slabs[:, :, k].transpose(2, 1, 0, 3) for k in range(chunks)]]
where the time goes in v23:
time: 208 us; the launch traced here: 206 us
  waiting for transfers between devices  94.3 us (45%)
  blocking collectives  34.5 us (17%)
  Pallas kernels  19.2 us (9%)
  matrix products  17 us (8%)
  local copies, waits for them, and re-layouts  14.6 us (7%)
  starting transfers between devices  13.5 us (6%)
  other arithmetic  11.9 us (6%)
    ppermute x2, waiting for transfers between devices, from_behind(): return lax.ppermute(block, axis, route)  70.2 us
    all_to_all x1, blocking collectives, shards(): lax.all_to_all(parts[k], 'freq', split_axis=0, concat_axis=2, tiled=True)  34.5 us
    all_to_all x1, waiting for transfers between devices, shards(): lax.all_to_all(parts[k], 'freq', split_axis=0, concat_axis=2, tiled=True)  22.8 us
    pallas_call x1, Pallas kernels, whitened_spectra(): pl.pallas_call(functools.partial(spectra_kernel, seg_count, window), out_...  19.2 us
    dot_general x6, matrix products, local_products(): jnp.einsum('fpsi,fpsj->fij', left_panel, both, preferred_element_type=jnp...  17 us
    unnamed x12, local copies, waits for them, and re-layouts  11.1 us
    ppermute x2, starting transfers between devices, from_behind(): return lax.ppermute(block, axis, route)  6.16 us
    another operation x1, other arithmetic, shards(): return jnp.stack(results, axis=0)  5.47 us
  transfers between devices with their start and end apart: 6, of which 4 were waited for; matrix products, arithmetic and copies ran while one was open for 12% of the time, Pallas kernels for 0%

profile of v23, /device:TPU:34, one launch (start us, length us, event | category | flops | bytes accessed | tf_op | source)
XLA Modules:
  0.0 206.0 jit_solution(18247369829137284596)
XLA Ops:
  0.1 0.7 convert_element_type.70
  1.5 3.4 %copy-done = bf16[8448,512]{1,0:T(8,128)(2,1)S(1)} copy-done((bf16[8448,512]{1,0:T(8,128)(2,1)S(1)}, bf16[8448,512]{1,0:T(8,128)(2,1)}, u32[]{:S(2)}) %copy-start) | copy-done | bytes 8650776
  5.0 0.7 copy-done.1
  5.6 19.2 %shard_map.46 = bf16[64,64,512]{2,1,0:T(8,128)(2,1)S(1)} custom-call(s32[64]{0:T(128)S(1)} %copy-done.1, f32[64,384]{1,0:T(8,128)S(1)} %pad_convert_fusion.dft_ref, f32[1,512]{1,0:T(1,128)S(1)} %bitcast.91, bf16[8448,512]{1,0:T(8,128)(2,1)S(1)} %copy-done), custom_call_target="tpu_custom_call" | custom-call | flops 1140850688 | bytes 22020096 | tf_op jit(solution)/shard_map/pallas_call | solution.py:69
  24.8 0.6 fusion.88
  25.5 2.2 %copy.48 = bf16[64,2,1,16,512]{4,1,0,3,2:T(2,128)(2,1)S(1)} copy(bf16[64,2,1,16,512]{4,3,2,1,0:T(8,128)(2,1)S(1)} %get-tuple-element.8) | data formatting | bytes 4194304
  27.6 34.5 %all_to_all.36 = bf16[16,2,64,512]{3,1,2,0:T(2,128)(2,1)S(1)} all-to-all(bf16[16,2,64,512]{3,1,2,0:T(2,128)(2,1)S(1)} %bitcast.104), channel_id=1, replica_groups=mesh['chan'=16,'freq'=8] {'freq'}, dimensions={0} | all-to-all | bytes 4194304 | tf_op jit(solution)/shard_map/all_to_all | solution.py:137
  62.1 0.4 copy.22
  62.6 1.3 collective-permute-start
  63.9 3.5 %copy.47 = bf16[64,2,1,16,512]{4,1,0,3,2:T(2,128)(2,1)} copy(bf16[64,2,1,16,512]{4,3,2,1,0:T(8,128)(2,1)S(1)} %get-tuple-element.7) | data formatting | bytes 4194304
  67.4 1.3 collective-permute-done
  68.6 1.3 copy-done.2
  70.0 4.4 %all-to-all-start.1 = ((bf16[16,2,64,512]{3,1,2,0:T(2,128)(2,1)}), bf16[16,2,64,512]{3,1,2,0:T(2,128)(2,1)}, u32[]{:S(2)}, u32[]{:S(2)}) async-start(bf16[16,2,64,512]{3,1,2,0:T(2,128)(2,1)} %bitcast.103), calls=%async_computation.1 | async-start | bytes 4194304 | tf_op jit(solution)/shard_map/all_to_all | solution.py:137
  74.3 3.1 %collective-permute-start.1 = (bf16[2,2,512,512]{3,2,1,0:T(8,128)(2,1)S(1)}, bf16[2,2,512,512]{3,2,1,0:T(8,128)(2,1)}, u32[]{:S(2)}, u32[]{:S(2)}) collective-permute-start(bf16[2,2,512,512]{3,2,1,0:T(8,128)(2,1)S(1)} %bitcast.98), channel_id=1, source_target_pairs={{16,0},{24,8},{32,16},{40,24},{48,32},{56,40},{64,48},{72,56},{80,... | collective-permute-start | bytes 6291464 | tf_op jit(solution)/shard_map/ppermute | solution.py:22
  78.1 1.1 slice_negate_fusion.5
  79.2 22.8 %all-to-all-done.1 = bf16[16,2,64,512]{3,1,2,0:T(2,128)(2,1)} async-done(((bf16[16,2,64,512]{3,1,2,0:T(2,128)(2,1)}), bf16[16,2,64,512]{3,1,2,0:T(2,128)(2,1)}, u32[]{:S(2)}, u32[]{:S(2)}) %all-to-all-start.1) | async-done | bytes 2097184 | tf_op jit(solution)/shard_map/all_to_all | solution.py:137
  102.1 2.1 %copy.25 = bf16[8,2,2,64,512]{4,3,0,2,1:T(8,128)(2,1)S(1)} copy(bf16[8,2,2,64,512]{4,2,3,1,0:T(2,128)(2,1)} %bitcast.13) | data formatting | bytes 4194304 | tf_op jit(solution)/shard_map/all_to_all | solution.py:137
  104.2 3.1 %collective-permute-start.3 = (bf16[2,2,512,512]{3,2,1,0:T(8,128)(2,1)S(1)}, bf16[2,2,512,512]{3,2,1,0:T(8,128)(2,1)S(1)}, u32[]{:S(2)}, u32[]{:S(2)}) collective-permute-start(bf16[2,2,512,512]{3,2,1,0:T(8,128)(2,1)S(1)} %bitcast.92), channel_id=1, source_target_pairs={{16,0},{24,8},{32,16},{40,24},{48,32},{56,40},{64,48},{72,56},{80,... | collective-permute-start | bytes 6291464 | tf_op jit(solution)/shard_map/ppermute | solution.py:22
  107.3 2.6 %fusion.54 = bf16[1,2,512,1024]{3,2,1,0:T(8,128)(2,1)S(1)} fusion(bf16[2,2,512,512]{3,2,1,0:T(8,128)(2,1)S(1)} %bitcast.100, bf16[2,1,512,512]{3,2,1,0:T(8,128)(2,1)S(1)} %copy-done.4, bf16[2,1,512,512]{3,2,1,0:T(8,128)(2,1)S(1)} %get-tuple-element.9), kind=kOutput, calls=%fused_computation.56 | convolution fusion | flops 2162163712 | bytes 6291456 | tf_op jit(solution)/shard_map/fpsi,fpsj->fij/dot_general | solution.py:101
  109.9 36.1 %collective-permute-done.1 = bf16[2,2,512,512]{3,2,1,0:T(8,128)(2,1)} collective-permute-done((bf16[2,2,512,512]{3,2,1,0:T(8,128)(2,1)S(1)}, bf16[2,2,512,512]{3,2,1,0:T(8,128)(2,1)}, u32[]{:S(2)}, u32[]{:S(2)}) %collective-permute-start.1) | collective-permute-done | bytes 2097184 | tf_op jit(solution)/shard_map/ppermute | solution.py:22
  146.0 1.4 collective-permute-start.2
  147.4 1.7 slice_negate_fusion.1
  149.1 4.0 %fusion.66 = bf16[1,2,512,1024]{3,2,1,0:T(8,128)(2,1)S(1)} fusion(bf16[2,2,512,512]{3,2,1,0:T(8,128)(2,1)S(1)} %bitcast.101, bf16[2,1,512,512]{3,2,1,0:T(8,128)(2,1)S(1)} %get-tuple-element.18, bf16[2,1,512,512]{3,2,1,0:T(8,128)(2,1)S(1)} %get-tuple-element.17, bf16[2,2,512,512]{3,2,1,0:T(8,128)(2,1)} %collective-permute-done.1), kind=kOutput, calls=%fused_computation.60 | convolution fusion | flops 2162163712 | bytes 8388608 | tf_op jit(solution)/shard_map/fpsi,fpsj->fij/dot_general | solution.py:101
  153.2 2.6 %fusion.57 = bf16[1,2,512,1024]{3,2,1,0:T(8,128)(2,1)S(1)} fusion(bf16[2,2,512,512]{3,2,1,0:T(8,128)(2,1)S(1)} %bitcast.94, bf16[2,1,512,512]{3,2,1,0:T(8,128)(2,1)S(1)} %get-tuple-element.12, bf16[2,1,512,512]{3,2,1,0:T(8,128)(2,1)S(1)} %get-tuple-element.11), kind=kOutput, calls=%fused_computation.57 | convolution fusion | flops 2162163712 | bytes 6291456 | tf_op jit(solution)/shard_map/fpsi,fpsj->fij/dot_general | solution.py:101
  155.8 0.4 maximum_multiply_fusion
  156.3 34.1 %collective-permute-done.3 = bf16[2,2,512,512]{3,2,1,0:T(8,128)(2,1)S(1)} collective-permute-done((bf16[2,2,512,512]{3,2,1,0:T(8,128)(2,1)S(1)}, bf16[2,2,512,512]{3,2,1,0:T(8,128)(2,1)S(1)}, u32[]{:S(2)}, u32[]{:S(2)}) %collective-permute-start.3) | collective-permute-done | bytes 2097184 | tf_op jit(solution)/shard_map/ppermute | solution.py:22
  191.5 2.6 %fusion.60 = bf16[1,2,512,1024]{3,2,1,0:T(8,128)(2,1)S(1)} fusion(bf16[2,2,512,512]{3,2,1,0:T(8,128)(2,1)S(1)} %bitcast.102, bf16[2,1,512,512]{3,2,1,0:T(8,128)(2,1)S(1)} %get-tuple-element.14, bf16[2,1,512,512]{3,2,1,0:T(8,128)(2,1)S(1)} %get-tuple-element.13, bf16[2,2,512,512]{3,2,1,0:T(8,128)(2,1)S(1)} %broadcast_select_fusion.1), kind=kOutput, calls=%fused_computation.58 | convolution fusion | flops 2162163712 | bytes 8388608 | tf_op jit(solution)/shard_map/fpsi,fpsj->fij/dot_general | solution.py:101
  194.3 2.6 %fusion.69 = bf16[1,2,512,1024]{3,2,1,0:T(8,128)(2,1)S(1)} fusion(bf16[2,2,512,512]{3,2,1,0:T(8,128)(2,1)S(1)} %bitcast.95, bf16[2,1,512,512]{3,2,1,0:T(8,128)(2,1)S(1)} %get-tuple-element.20, bf16[2,1,512,512]{3,2,1,0:T(8,128)(2,1)S(1)} %get-tuple-element.19, bf16[2,2,512,512]{3,2,1,0:T(8,128)(2,1)S(1)} %collective-permute-done.3), kind=kOutput, calls=%fused_computation.61 | convolution fusion | flops 2162163712 | bytes 8388608 | tf_op jit(solution)/shard_map/fpsi,fpsj->fij/dot_general | solution.py:101
  196.9 0.4 maximum_multiply_fusion.2
  197.5 2.6 %fusion.63 = bf16[1,2,512,1024]{3,2,1,0:T(8,128)(2,1)S(1)} fusion(bf16[2,2,512,512]{3,2,1,0:T(8,128)(2,1)S(1)} %bitcast.96, bf16[2,1,512,512]{3,2,1,0:T(8,128)(2,1)S(1)} %get-tuple-element.16, bf16[2,1,512,512]{3,2,1,0:T(8,128)(2,1)S(1)} %get-tuple-element.15, bf16[2,2,512,512]{3,2,1,0:T(8,128)(2,1)S(1)} %collective-permute-done.4), kind=kOutput, calls=%fused_computation.59 | convolution fusion | flops 2162163712 | bytes 8388608 | tf_op jit(solution)/shard_map/fpsi,fpsj->fij/dot_general | solution.py:101
  200.1 0.4 maximum_multiply_fusion.1
  200.5 5.5 %pad_maximum_fusion = bf16[3,4,512,1024]{3,2,1,0:T(8,128)(2,1)} fusion(bf16[1,4,512,1024]{3,2,1,0:T(8,128)(2,1)S(1)} %maximum_multiply_fusion.2, bf16[1,4,512,1024]{3,2,1,0:T(8,128)(2,1)S(1)} %maximum_multiply_fusion.1, bf16[1,4,512,1024]{3,2,1,0:T(8,128)(2,1)S(1)} %maximum_multiply_fusion), kind=kLoop, calls=%fused_computation | loop fusion | flops 12582912 | bytes 25165824 | tf_op jit(solution)/shard_map/stack | solution.py:148
  (27 shorter events, 2.3 us)
Async XLA Ops:
  1.5 3.5 %copy-start = (bf16[8448,512]{1,0:T(8,128)(2,1)S(1)}, bf16[8448,512]{1,0:T(8,128)(2,1)}, u32[]{:S(2)}) copy-start(bf16[8448,512]{1,0:T(8,128)(2,1)} %rec_hbm.1) | copy-start | bytes 25952260
  5.0 0.7 copy-start.1
  62.6 6.1 %collective-permute-start = (bf16[2,2,512,512]{3,2,1,0:T(8,128)(2,1)S(1)}, bf16[2,2,512,512]{3,2,1,0:T(8,128)(2,1)S(1)}, u32[]{:S(2)}, u32[]{:S(2)}) collective-permute-start(bf16[2,2,512,512]{3,2,1,0:T(8,128)(2,1)S(1)} %bitcast.97), channel_id=1, source_target_pairs={{8,0},{24,16},{40,32},{56,48},{72,64},{88,80},{104,96},{120,112},{... | collective-permute-start | bytes 6291464 | tf_op jit(solution)/shard_map/ppermute | solution.py:117
  68.6 1.3 copy-start.2
  70.0 32.1 %all-to-all-start.1 = ((bf16[16,2,64,512]{3,1,2,0:T(2,128)(2,1)}), bf16[16,2,64,512]{3,1,2,0:T(2,128)(2,1)}, u32[]{:S(2)}, u32[]{:S(2)}) async-start(bf16[16,2,64,512]{3,1,2,0:T(2,128)(2,1)} %bitcast.103), calls=%async_computation.1 | async-start | bytes 4194304 | tf_op jit(solution)/shard_map/all_to_all | solution.py:137
  74.3 71.7 %collective-permute-start.1 = (bf16[2,2,512,512]{3,2,1,0:T(8,128)(2,1)S(1)}, bf16[2,2,512,512]{3,2,1,0:T(8,128)(2,1)}, u32[]{:S(2)}, u32[]{:S(2)}) collective-permute-start(bf16[2,2,512,512]{3,2,1,0:T(8,128)(2,1)S(1)} %bitcast.98), channel_id=1, source_target_pairs={{16,0},{24,8},{32,16},{40,24},{48,32},{56,40},{64,48},{72,56},{80,... | collective-permute-start | bytes 6291464 | tf_op jit(solution)/shard_map/ppermute | solution.py:22
  102.1 5.2 %copy-start.4 = (bf16[2,1,512,512]{3,2,1,0:T(8,128)(2,1)S(1)}, bf16[2,1,512,512]{3,2,1,0:T(8,128)(2,1)}, u32[]{:S(2)}) copy-start(bf16[2,1,512,512]{3,2,1,0:T(8,128)(2,1)} %get-tuple-element.10) | copy-start | bytes 3145732
  104.2 86.1 %collective-permute-start.3 = (bf16[2,2,512,512]{3,2,1,0:T(8,128)(2,1)S(1)}, bf16[2,2,512,512]{3,2,1,0:T(8,128)(2,1)S(1)}, u32[]{:S(2)}, u32[]{:S(2)}) collective-permute-start(bf16[2,2,512,512]{3,2,1,0:T(8,128)(2,1)S(1)} %bitcast.92), channel_id=1, source_target_pairs={{16,0},{24,8},{32,16},{40,24},{48,32},{56,40},{64,48},{72,56},{80,... | collective-permute-start | bytes 6291464 | tf_op jit(solution)/shard_map/ppermute | solution.py:22
  146.0 45.1 %collective-permute-start.2 = (bf16[2,2,512,512]{3,2,1,0:T(8,128)(2,1)}, bf16[2,2,512,512]{3,2,1,0:T(8,128)(2,1)S(1)}, u32[]{:S(2)}, u32[]{:S(2)}) collective-permute-start(bf16[2,2,512,512]{3,2,1,0:T(8,128)(2,1)} %collective-permute-done.1), channel_id=1, source_target_pairs={{0,8},{16,24},{32,40},{48,56},{64,72},{80,88},{96,104},{112,120},{... | collective-permute-start | bytes 6291464 | tf_op jit(solution)/shard_map/ppermute | solution.py:118
  156.3 34.8 %copy-start.3 = (bf16[2,2,512,512]{3,2,1,0:T(8,128)(2,1)S(1)}, bf16[2,2,512,512]{3,2,1,0:T(8,128)(2,1)}, u32[]{:S(2)}) copy-start(bf16[2,2,512,512]{3,2,1,0:T(8,128)(2,1)} %copy-done.2) | copy-start | bytes 6291460
  190.8 6.6 %collective-permute-start.4 = (bf16[2,2,512,512]{3,2,1,0:T(8,128)(2,1)S(1)}, bf16[2,2,512,512]{3,2,1,0:T(8,128)(2,1)S(1)}, u32[]{:S(2)}, u32[]{:S(2)}) collective-permute-start(bf16[2,2,512,512]{3,2,1,0:T(8,128)(2,1)S(1)} %broadcast_select_fusion), channel_id=1, source_target_pairs={{8,0},{24,16},{40,32},{56,48},{72,64},{88,80},{104,96},{120,112},{... | collective-permute-start | bytes 6291464 | tf_op jit(solution)/shard_map/ppermute | solution.py:115
